TPU v7x, 128 devices: a whole 4x4x4 slice. The times are simulated.
128 devices in a mesh: grp: 4 (over y), slab: 32 (over z, x, core).
Axes of the slice: x: 4, y: 4, z: 4, core: 2. Of those that a mesh axis runs over, the one named last changes fastest.
Arguments:
- vessel_start: float32 [16384, 128], P(('grp', 'slab')), may hold values from -6 to 6
- drive: float32 [16384, 128], P(('grp', 'slab')), may hold values from -6 to 6
- junction_gain: float32 [16384], P(('grp', 'slab')), may hold values from 0.5 to 2
- parent: int32 [16384], P(('grp', 'slab')), may hold values from 0 to 16383, as said below
- inverse_blocks: bfloat16 [16384, 128, 128], P(('grp', 'slab')), as said below
- wall_perm: float32 [16384, 128], P(('grp', 'slab')), may hold values from 0.2 to 2
- outside: float32 [16384, 128], P(('grp', 'slab')), may hold values from -6 to 6
- owner: int32 [16384, 1], P(('grp', 'slab')), may hold values from 0 to 127; in each aligned block of 128 rows (0 to 127, 128 to 255, ...) at most 2 rows name the same one
- target: int32 [16384], P(('grp', 'slab')), may hold values from 0 to 4095
- kernel_id: int32 [16384], P(('grp', 'slab')), may hold values from 0 to 3
- kernels: bfloat16 [4, 128, 128], replicated, may hold values from -0.5 to 0.5
- tissue_start: float32 [512, 256, 512], P(('grp', 'slab')), may hold values from -6 to 6
- conduct: float32 [512, 256, 512], P(('grp', 'slab')), may hold values from 0.1 to 10
- base_source: float32 [512, 256, 512], P(('grp', 'slab')), may hold values from -6 to 6
Outputs:
- vessel_pressure: float32 [16384, 128], P(('grp', 'slab'))
- tissue_pressure: float32 [512, 256, 512], P(('grp', 'slab'))
Inputs may be any that keep to these rules, and one draw needn't show every extreme that they name: Block 0's parent is the last block and the last block's parent is block 0. Within the blocks of one device no owner is named by more than 2 blocks. `inverse_blocks`: each block is the identity plus entries of order 0.05, except the first column below the diagonal, whose entries lie between 0.5 and 1.
All inputs are finite; a program needn't handle non-finite values.
Results may differ from a plain program's by a relative error of at most 0.0042.
Values sent between devices are 32-bit elements; how exact they have to be, the bound alone decides.
No kernel may reach another device: no remote copies, remote signals or barrier semaphores. Data moves between devices by JAX's collectives and lax.ppermute only.
A program may use at most 64 MiB of HBM per device.

v0:
```python
import jax
import jax.numpy as jnp
from jax import lax
from jax.sharding import PartitionSpec as P

SWEEPS = 3


UPTAKE = 0.5


def padded(cells, sides, width):
    for axis, dim in sides:
        count = lax.axis_size(axis)
        ends = count - 1
        head = lax.slice_in_dim(cells, 0, width, axis=dim)
        tail = lax.slice_in_dim(cells, cells.shape[dim] - width, cells.shape[dim], axis=dim)
        cells = jnp.concatenate(
            [
                lax.ppermute(tail, axis, [(i, (i + 1) % count) for i in range(ends)]),
                cells,
                lax.ppermute(head, axis, [((i + 1) % count, i) for i in range(ends)]),
            ],
            axis=dim,
        )
    return cells


def neighbours(values):
    return [
        values[2:, 1:-1, 1:-1],
        values[:-2, 1:-1, 1:-1],
        values[1:-1, 2:, 1:-1],
        values[1:-1, :-2, 1:-1],
        values[1:-1, 1:-1, 2:],
        values[1:-1, 1:-1, :-2],
    ]


def relax(padded_p, padded_k, source):
    centre = padded_k[1:-1, 1:-1, 1:-1]
    numerator = source
    denominator = jnp.full(centre.shape, UPTAKE, jnp.float32)
    for p_side, k_side in zip(neighbours(padded_p), neighbours(padded_k)):
        facing = 0.5 * (centre + k_side)
        numerator = numerator + facing * p_side
        denominator = denominator + facing
    return numerator / denominator


def pad_sides(values):
    return jnp.pad(values, ((0, 0), (1, 1), (1, 1)))


def on_device(
    vessel_start,
    drive,
    junction_gain,
    parent,
    inverse_blocks,
    wall_perm,
    outside,
    owner,
    target,
    kernel_id,
    kernels,
    tissue_start,
    conduct,
    base_source,
):
    devices = lax.axis_size(("grp", "slab"))
    pressure = vessel_start
    for sweep_index in range(SWEEPS):
        exit_values = lax.all_gather(pressure[:, -1], ("grp", "slab"), axis=0, tiled=True)
        inflow = exit_values[parent]
        right_side = drive.at[:, 0].add(junction_gain * inflow).astype(jnp.bfloat16)
        pressure = jnp.einsum(
            "bij,bj->bi", inverse_blocks, right_side, preferred_element_type=jnp.float32
        )
    leak = (wall_perm * (pressure - outside)).astype(jnp.bfloat16)
    spread = jnp.einsum("bs,ksc->kbc", leak, kernels, preferred_element_type=jnp.float32)
    picks = kernel_id[None, :] == jnp.arange(kernels.shape[0], dtype=jnp.int32)[:, None]
    cells = jnp.sum(jnp.where(picks[:, :, None], spread, 0.0), axis=0)
    blocks_here = pressure.shape[0]
    capacity = max(2, 2 * blocks_here // devices)
    destination = owner[:, 0]
    owner_hits = (destination[:, None] == jnp.arange(devices, dtype=jnp.int32)[None, :]).astype(
        jnp.int32
    )
    earlier = jnp.cumsum(owner_hits, axis=0) - owner_hits
    slot_index = jnp.sum(earlier * owner_hits, axis=1)
    send_rows = (
        jnp.zeros((devices, capacity, 128), jnp.float32).at[destination, slot_index].set(cells)
    )
    send_index = jnp.zeros((devices, capacity), jnp.int32).at[destination, slot_index].set(target)
    got_rows, got_index = (
        lax.all_to_all(send_rows, ("grp", "slab"), split_axis=0, concat_axis=0, tiled=True),
        lax.all_to_all(send_index, ("grp", "slab"), split_axis=0, concat_axis=0, tiled=True),
    )
    cell_blocks = tissue_start.size // 128
    leakage = jax.ops.segment_sum(
        got_rows.reshape(-1, 128), got_index.reshape(-1), num_segments=cell_blocks
    )
    source = base_source + leakage.reshape(base_source.shape)
    stacked = jnp.stack([tissue_start, conduct])
    wide = padded(stacked, ((("grp", "slab"), 1),), 1)
    padded_k = pad_sides(wide[1])
    first = relax(pad_sides(wide[0]), padded_k, source)
    second = padded(first, ((("grp", "slab"), 0),), 1)
    tissue = relax(pad_sides(second), padded_k, source)
    return (pressure, tissue)


def solution(mesh):
    in_specs = (
        P(("grp", "slab"), None),
        P(("grp", "slab"), None),
        P(("grp", "slab")),
        P(("grp", "slab")),
        P(("grp", "slab"), None, None),
        P(("grp", "slab"), None),
        P(("grp", "slab"), None),
        P(("grp", "slab"), None),
        P(("grp", "slab")),
        P(("grp", "slab")),
        P(),
        P(("grp", "slab"), None, None),
        P(("grp", "slab"), None, None),
        P(("grp", "slab"), None, None),
    )
    out_specs = (P(("grp", "slab"), None), P(("grp", "slab"), None, None))
    return jax.shard_map(
        on_device, mesh=mesh, in_specs=in_specs, out_specs=out_specs, check_vma=False
    )
```

profile of v0, /device:TPU:8, one launch (start us, length us, event | category | flops | bytes accessed | tf_op | source)
XLA Modules:
  0.0 244.3 jit_solution(10301380788214489369)
XLA Ops:
  0.6 0.0 copy-start
  0.6 0.9 copy.49
  1.5 3.0 %pad_maximum_fusion.7 = (f32[2,1,256,512]{3,2,1,0:T(8,128)}, f32[2,1,256,512]{3,2,1,0:T(8,128)}) fusion(f32[1,4,256,512]{3,2,1,0:T(8,128)} %bitcast.84, f32[1,4,256,512]{3,2,1,0:T(8,128)} %bitcast.88), kind=kLoop, calls=%fused_computation.78 | loop fusion | flops 524288 | bytes 6291456 | tf_op jit(solution)/shard_map/stack | solution.py:105
  4.6 7.5 %collective-permute-start = (f32[2,1,256,512]{3,2,1,0:T(8,128)}, f32[2,1,256,512]{3,2,1,0:T(8,128)S(1)}, u32[]{:S(2)}, u32[]{:S(2)}) collective-permute-start(f32[2,1,256,512]{3,2,1,0:T(8,128)} %get-tuple-element.43), channel_id=1, source_target_pairs={{1,0},{2,1},{3,2},{4,3},{5,4},{6,5},{7,6},{8,7},{9,8},{10,9},{11,1... | collective-permute-start | bytes 3145736 | tf_op jit(solution)/shard_map/ppermute | solution.py:22
  12.0 1.9 collective-permute-start.1
  14.0 0.1 fusion.49
  14.1 0.2 reduce_window_sum.11
  14.2 0.2 select_reduce_fusion
  14.4 6.4 %scatter_fusion = s32[128,2]{0,1:T(2,128)S(1)} fusion(s32[128,2]{0,1:T(2,128)S(1)} %broadcast_in_dim.36, s32[128]{0:T(128)S(1)} %fusion.53, s32[128]{0:T(128)S(1)} %copy-done.11), kind=kCustom, calls=%fused_computation.3 | custom fusion | bytes 2560 | tf_op jit(solution)/shard_map/scatter | solution.py:95
  20.8 0.7 copy.29
  21.5 10.0 %all-to-all-start = ((s32[128,1,2]{2,1,0:T(1,128)}), s32[128,1,2]{2,1,0:T(1,128)S(1)}, u32[]{:S(2)}, u32[]{:S(2)}) async-start(s32[128,1,2]{2,1,0:T(1,128)} %copy.29), calls=%async_computation | async-start | bytes 131072 | tf_op jit(solution)/shard_map/all_to_all | solution.py:98
  31.6 0.6 compare_reduce_fusion
  32.2 0.1 copy.36
  32.3 0.1 slice.167
  32.4 0.0 copy-start.12
  32.4 45.5 %all-gather = f32[16384,1]{1,0:T(8,128)} all-gather(f32[128,1]{1,0:T(8,128)S(1)} %slice.167), channel_id=2, replica_groups=mesh['grp'=4,'slab'=32] {'grp','slab'}, dimensions={0}, use_global_device_ids=true | all-gather | bytes 66048 | tf_op jit(solution)/shard_map/all_gather | solution.py:74
  77.9 0.0 copy-start.9
  77.9 4.6 %reduce.11 = f32[16384]{0:T(1024)S(1)} reduce(f32[16384,1]{1,0:T(8,128)} %all-gather, f32[]{:T(128)} %constant.129), dimensions={1}, to_apply=%all-gather.reduce_sub_computation | reduce | bytes 131076 | tf_op jit(solution)/shard_map/all_gather | solution.py:74
  82.6 1.1 gather_fusion
  83.7 0.7 broadcast_select_fusion.2
  84.4 0.1 copy.26
  84.5 0.3 scatter-add.16
  84.8 4.4 %fusion.47 = f32[128,1,128]{2,1,0:T(1,128)S(1)} fusion(bf16[128,128,128]{2,1,0:T(8,128)(2,1)} %param.24, bf16[128,128,1]{1,0,2:T(8,128)(2,1)S(1)} %convert_bitcast_fusion.2), kind=kOutput, calls=%fused_computation.86 | convolution fusion | flops 4194304 | bytes 4292608 | tf_op jit(solution)/shard_map/bij,bj->bi/dot_general | solution.py:77
  89.2 0.1 copy.31
  89.4 29.5 %all-gather.1 = f32[16384,1]{0,1:T(1,128)S(1)} all-gather(f32[128,1]{0,1:T(1,128)S(1)} %slice.208), channel_id=3, replica_groups=mesh['grp'=4,'slab'=32] {'grp','slab'}, dimensions={0}, use_global_device_ids=true | all-gather | bytes 66048 | tf_op jit(solution)/shard_map/all_gather | solution.py:74
  118.9 1.1 gather_fusion.1
  120.0 0.7 broadcast_select_fusion.1
  120.7 0.1 copy.27
  120.8 0.3 scatter-add.19
  121.1 0.0 copy-start.13
  121.1 4.4 %fusion.45 = f32[128,1,128]{2,1,0:T(1,128)S(1)} fusion(bf16[128,128,128]{2,1,0:T(8,128)(2,1)} %param.24, bf16[128,128,1]{1,0,2:T(8,128)(2,1)S(1)} %convert_bitcast_fusion.1), kind=kOutput, calls=%fused_computation.84 | convolution fusion | flops 4194304 | bytes 4292608 | tf_op jit(solution)/shard_map/bij,bj->bi/dot_general | solution.py:77
  125.5 0.1 copy.33
  125.7 29.9 %all-gather.2 = f32[16384,1]{0,1:T(1,128)S(1)} all-gather(f32[128,1]{0,1:T(1,128)S(1)} %slice.209), channel_id=4, replica_groups=mesh['grp'=4,'slab'=32] {'grp','slab'}, dimensions={0}, use_global_device_ids=true | all-gather | bytes 66048 | tf_op jit(solution)/shard_map/all_gather | solution.py:74
  155.5 1.1 gather_fusion.2
  156.7 0.7 broadcast_select_fusion
  157.3 0.1 copy.28
  157.5 0.4 scatter-add.24
  157.9 0.0 copy-start.7
  158.0 0.0 copy-start.8
  158.0 4.5 %fusion.43 = f32[128,1,128]{2,1,0:T(1,128)S(1)} fusion(bf16[128,128,128]{2,1,0:T(8,128)(2,1)} %param.24, bf16[128,128,1]{1,0,2:T(8,128)(2,1)S(1)} %convert_bitcast_fusion), kind=kOutput, calls=%fused_computation.82 | convolution fusion | flops 4194304 | bytes 4292608 | tf_op jit(solution)/shard_map/bij,bj->bi/dot_general | solution.py:77
  162.4 0.0 copy-done.8
  162.5 0.2 fusion.40
  162.7 0.7 broadcast_in_dim.37
  163.4 13.8 %scatter_fusion.1 = f32[128,2,128]{2,1,0:T(2,128)} fusion(f32[128,2,128]{2,1,0:T(2,128)} %broadcast_in_dim.37, s32[128]{0:T(128)S(1)} %fusion.53, f32[128,128]{1,0:T(8,128)S(1)} %fusion.40), kind=kCustom, calls=%fused_computation.4 | custom fusion | bytes 197632 | tf_op jit(solution)/shard_map/scatter | solution.py:93
  177.1 0.0 all-to-all-done
  177.1 5.8 %all-to-all-start.1 = ((f32[128,2,128]{2,1,0:T(2,128)}), f32[128,2,128]{2,1,0:T(2,128)S(1)}, u32[]{:S(2)}, u32[]{:S(2)}) async-start(f32[128,2,128]{2,1,0:T(2,128)} %scatter_fusion.1), calls=%async_computation.1 | async-start | bytes 262144 | tf_op jit(solution)/shard_map/all_to_all | solution.py:97
  183.0 0.5 broadcast.209
  183.5 0.8 reduce.16
  184.3 0.1 reshape.168
  184.4 7.5 %all-to-all-done.1 = f32[128,2,128]{2,1,0:T(2,128)S(1)} async-done(((f32[128,2,128]{2,1,0:T(2,128)}), f32[128,2,128]{2,1,0:T(2,128)S(1)}, u32[]{:S(2)}, u32[]{:S(2)}) %all-to-all-start.1) | async-done | bytes 131104 | tf_op jit(solution)/shard_map/all_to_all | solution.py:97
  191.9 2.9 %scatter_custom_fusion.2 = f32[4096,128]{1,0:T(8,128)} fusion(s32[256]{0:T(256)S(1)} %reshape.168, f32[256,128]{1,0:T(8,128)S(1)} %bitcast.97, f32[]{:T(128)} %constant.84.clone.1), kind=kCustom, calls=%fused_computation.80 | custom fusion | flops 32768 | bytes 2097156 | tf_op jit(solution)/shard_map/scatter-add | solution.py:101
  194.8 2.9 %reshape.129 = f32[4,256,512]{2,1,0:T(8,128)} reshape(f32[4096,128]{1,0:T(8,128)} %scatter_custom_fusion.2) | data formatting | bytes 4194304 | tf_op jit(solution)/shard_map/reshape | solution.py:104
  197.7 0.0 collective-permute-done
  197.7 2.2 pad_maximum_fusion
  199.9 0.0 copy-start.2
  199.9 3.4 %slice_bitcast_fusion.1 = (f32[6,256,512]{2,1,0:T(8,128)}, f32[6,256,512]{2,1,0:T(8,128)}) fusion(f32[2,6,256,512]{3,2,1,0:T(8,128)S(1)} %pad_maximum_fusion), kind=kLoop, calls=%fused_computation.25 | loop fusion | bytes 12582912 | tf_op jit(solution)/shard_map/squeeze | solution.py:107
  203.3 11.4 %fusion.16 = (f32[4,256,512]{2,1,0:T(8,128)}, f32[4,256,512]{2,1,0:T(8,128)}) fusion(f32[6,256,512]{2,1,0:T(8,128)} %get-tuple-element.41, f32[2,1,256,512]{3,2,1,0:T(8,128)} %collective-permute-done.1, f32[1,4,256,512]{3,2,1,0:T(8,128)S(1)} %bitcast.86, f32[1,4,256,512]{3,2,1,0:T(8,128)S(1)} %bitcast.90, f32[2,1,256,512]{3,2,1,0:T(8,128)S(1)} %collective-permute-done, ...), kind=kLoop, calls=%fused_computation.39 | loop fusion | flops 20971520 | bytes 23068672 | tf_op jit(solution)/shard_map/div | solution.py:48
  214.8 1.4 fusion.54
  216.2 4.0 %collective-permute-start.2 = (f32[1,256,512]{2,1,0:T(8,128)S(1)}, f32[1,256,512]{2,1,0:T(8,128)S(1)}, u32[]{:S(2)}, u32[]{:S(2)}) collective-permute-start(f32[1,256,512]{2,1,0:T(8,128)S(1)} %get-tuple-element.45), channel_id=1, source_target_pairs={{1,0},{2,1},{3,2},{4,3},{5,4},{6,5},{7,6},{8,7},{9,8},{10,9},{11,1... | collective-permute-start | bytes 1572872 | tf_op jit(solution)/shard_map/ppermute | solution.py:22
  220.2 2.2 collective-permute-start.3
  222.4 4.5 %collective-permute-done.2 = f32[1,256,512]{2,1,0:T(8,128)S(1)} collective-permute-done((f32[1,256,512]{2,1,0:T(8,128)S(1)}, f32[1,256,512]{2,1,0:T(8,128)S(1)}, u32[]{:S(2)}, u32[]{:S(2)}) %collective-permute-start.2) | collective-permute-done | bytes 524320 | tf_op jit(solution)/shard_map/ppermute | solution.py:22
  226.9 8.3 %collective-permute-done.3 = f32[1,256,512]{2,1,0:T(8,128)S(1)} collective-permute-done((f32[1,256,512]{2,1,0:T(8,128)S(1)}, f32[1,256,512]{2,1,0:T(8,128)S(1)}, u32[]{:S(2)}, u32[]{:S(2)}) %collective-permute-start.3) | collective-permute-done | bytes 524320 | tf_op jit(solution)/shard_map/ppermute | solution.py:20
  235.2 2.3 select_maximum_fusion
  237.5 6.8 %fusion.21 = f32[4,256,512]{2,1,0:T(8,128)} fusion(f32[6,258,514]{2,1,0:T(8,128)S(1)} %select_maximum_fusion, f32[4,256,512]{2,1,0:T(8,128)} %get-tuple-element.38, f32[1,256,512]{2,1,0:T(8,128)S(1)} %collective-permute-done.3, f32[4,256,512]{2,1,0:T(8,128)} %get-tuple-element.39, f32[1,256,512]{2,1,0:T(8,128)S(1)} %collective-permute-done.2, ...), kind=kLoop, calls=%fused_computation.45 | loop fusion | flops 19398656 | bytes 27262976 | tf_op jit(solution)/shard_map/div | solution.py:48
  (33 shorter events, 0.1 us)
Async XLA Ops:
  0.6 161.8 %copy-start = (bf16[4,128,128]{2,1,0:T(8,128)(2,1)S(1)}, bf16[4,128,128]{2,1,0:T(8,128)(2,1)}, u32[]{:S(2)}) copy-start(bf16[4,128,128]{2,1,0:T(8,128)(2,1)} %param.30) | copy-start | bytes 393220
  1.5 12.4 %copy-start.10 = (s32[128,1]{0,1:T(1,128)S(1)}, s32[128,1]{0,1:T(1,128)}, u32[]{:S(2)}) copy-start(s32[128,1]{0,1:T(1,128)} %param.27) | copy-start | bytes 1540
  1.5 12.9 %copy-start.11 = (s32[128]{0:T(128)S(1)}, s32[128]{0:T(128)}, u32[]{:S(2)}) copy-start(s32[128]{0:T(128)} %param.28) | copy-start | bytes 1540
  1.5 30.8 %copy-start.6 = (f32[128,128]{1,0:T(8,128)S(1)}, f32[128,128]{1,0:T(8,128)}, u32[]{:S(2)}) copy-start(f32[128,128]{1,0:T(8,128)} %param.20) | copy-start | bytes 196612
  4.6 193.2 %collective-permute-start = (f32[2,1,256,512]{3,2,1,0:T(8,128)}, f32[2,1,256,512]{3,2,1,0:T(8,128)S(1)}, u32[]{:S(2)}, u32[]{:S(2)}) collective-permute-start(f32[2,1,256,512]{3,2,1,0:T(8,128)} %get-tuple-element.43), channel_id=1, source_target_pairs={{1,0},{2,1},{3,2},{4,3},{5,4},{6,5},{7,6},{8,7},{9,8},{10,9},{11,1... | collective-permute-start | bytes 3145736 | tf_op jit(solution)/shard_map/ppermute | solution.py:22
  12.0 185.7 %collective-permute-start.1 = (f32[2,1,256,512]{3,2,1,0:T(8,128)}, f32[2,1,256,512]{3,2,1,0:T(8,128)}, u32[]{:S(2)}, u32[]{:S(2)}) collective-permute-start(f32[2,1,256,512]{3,2,1,0:T(8,128)} %get-tuple-element.42), channel_id=1, source_target_pairs={{0,1},{1,2},{2,3},{3,4},{4,5},{5,6},{6,7},{7,8},{8,9},{9,10},{10,1... | collective-permute-start | bytes 3145736 | tf_op jit(solution)/shard_map/ppermute | solution.py:20
  21.5 155.6 %all-to-all-start = ((s32[128,1,2]{2,1,0:T(1,128)}), s32[128,1,2]{2,1,0:T(1,128)S(1)}, u32[]{:S(2)}, u32[]{:S(2)}) async-start(s32[128,1,2]{2,1,0:T(1,128)} %copy.29), calls=%async_computation | async-start | bytes 131072 | tf_op jit(solution)/shard_map/all_to_all | solution.py:98
  32.4 45.5 %copy-start.12 = (s32[128]{0:T(128)S(1)}, s32[128]{0:T(128)}, u32[]{:S(2)}) copy-start(s32[128]{0:T(128)} %param.23) | copy-start | bytes 1540
  77.9 5.8 %copy-start.9 = (f32[128]{0:T(128)S(1)}, f32[128]{0:T(128)}, u32[]{:S(2)}) copy-start(f32[128]{0:T(128)} %param.22) | copy-start | bytes 1540
  121.1 36.8 %copy-start.13 = (s32[128]{0:T(128)S(1)}, s32[128]{0:T(128)}, u32[]{:S(2)}) copy-start(s32[128]{0:T(128)} %param.29) | copy-start | bytes 1540
  157.9 4.5 %copy-start.7 = (f32[128,128]{1,0:T(8,128)S(1)}, f32[128,128]{1,0:T(8,128)}, u32[]{:S(2)}) copy-start(f32[128,128]{1,0:T(8,128)} %param.25) | copy-start | bytes 196612
  158.0 4.5 %copy-start.8 = (f32[128,128]{1,0:T(8,128)S(1)}, f32[128,128]{1,0:T(8,128)}, u32[]{:S(2)}) copy-start(f32[128,128]{1,0:T(8,128)} %param.26) | copy-start | bytes 196612
  162.4 32.4 %copy-start.5 = (f32[128,1,128]{2,1,0:T(1,128)}, f32[128,1,128]{2,1,0:T(1,128)S(1)}, u32[]{:S(2)}) copy-start(f32[128,1,128]{2,1,0:T(1,128)S(1)} %fusion.43) | copy-start | bytes 196612
  177.1 14.8 %all-to-all-start.1 = ((f32[128,2,128]{2,1,0:T(2,128)}), f32[128,2,128]{2,1,0:T(2,128)S(1)}, u32[]{:S(2)}, u32[]{:S(2)}) async-start(f32[128,2,128]{2,1,0:T(2,128)} %scatter_fusion.1), calls=%async_computation.1 | async-start | bytes 262144 | tf_op jit(solution)/shard_map/all_to_all | solution.py:97
  194.8 2.9 %copy-start.1 = (f32[4,256,512]{2,1,0:T(8,128)S(1)}, f32[4,256,512]{2,1,0:T(8,128)}, u32[]{:S(2)}) copy-start(f32[4,256,512]{2,1,0:T(8,128)} %param.32) | copy-start | bytes 6291460
  199.9 3.4 %copy-start.2 = (f32[4,256,512]{2,1,0:T(8,128)S(1)}, f32[4,256,512]{2,1,0:T(8,128)}, u32[]{:S(2)}) copy-start(f32[4,256,512]{2,1,0:T(8,128)} %param.31) | copy-start | bytes 6291460
  214.7 20.4 %copy-start.4 = (f32[4,256,512]{2,1,0:T(8,128)S(1)}, f32[4,256,512]{2,1,0:T(8,128)}, u32[]{:S(2)}) copy-start(f32[4,256,512]{2,1,0:T(8,128)} %get-tuple-element.38) | copy-start | bytes 6291460
  216.2 10.7 %collective-permute-start.2 = (f32[1,256,512]{2,1,0:T(8,128)S(1)}, f32[1,256,512]{2,1,0:T(8,128)S(1)}, u32[]{:S(2)}, u32[]{:S(2)}) collective-permute-start(f32[1,256,512]{2,1,0:T(8,128)S(1)} %get-tuple-element.45), channel_id=1, source_target_pairs={{1,0},{2,1},{3,2},{4,3},{5,4},{6,5},{7,6},{8,7},{9,8},{10,9},{11,1... | collective-permute-start | bytes 1572872 | tf_op jit(solution)/shard_map/ppermute | solution.py:22
  220.2 17.3 %copy-start.3 = (f32[6,256,512]{2,1,0:T(8,128)S(1)}, f32[6,256,512]{2,1,0:T(8,128)}, u32[]{:S(2)}) copy-start(f32[6,256,512]{2,1,0:T(8,128)} %get-tuple-element.40) | copy-start | bytes 9437188
  220.2 15.0 %collective-permute-start.3 = (f32[1,256,512]{2,1,0:T(8,128)S(1)}, f32[1,256,512]{2,1,0:T(8,128)S(1)}, u32[]{:S(2)}, u32[]{:S(2)}) collective-permute-start(f32[1,256,512]{2,1,0:T(8,128)S(1)} %get-tuple-element.44), channel_id=1, source_target_pairs={{0,1},{1,2},{2,3},{3,4},{4,5},{5,6},{6,7},{7,8},{8,9},{9,10},{10,1... | collective-permute-start | bytes 1572872 | tf_op jit(solution)/shard_map/ppermute | solution.py:20
where the time goes:
time: 245 us; the launch traced here: 244 us
  blocking collectives  105 us (43%)
  other arithmetic  37.1 us (15%)
  local copies, waits for them, and re-layouts  36.1 us (15%)
  starting transfers between devices  31.4 us (13%)
  waiting for transfers between devices  20.3 us (8%)
  matrix products  13.5 us (6%)
    all_gather x3, blocking collectives, on_device(): lax.all_gather(pressure[:, -1], ('grp', 'slab'), axis=0, tiled=True)  105 us
    div x2, other arithmetic, relax(): return numerator / denominator  18.3 us
    scatter x1, local copies, waits for them, and re-layouts, on_device(): jnp.zeros((devices, capacity, 128), jnp.float32).at[destination, slot_index]  13.8 us
    dot_general x3, matrix products, on_device(): jnp.einsum('bij,bj->bi', inverse_blocks, right_side, preferred_element_ty...  13.3 us
    ppermute x2, starting transfers between devices, padded(): lax.ppermute(head, axis, [((i + 1) % count, i) for i in range(ends)])  11.5 us
    all_to_all x1, starting transfers between devices, on_device(): lax.all_to_all(send_index, ('grp', 'slab'), split_axis=0, concat_axis=0,...  10 us
    ppermute x2, waiting for transfers between devices, padded(): lax.ppermute(tail, axis, [(i, (i + 1) % count) for i in range(ends)])  8.32 us
    all_to_all x1, waiting for transfers between devices, on_device(): lax.all_to_all(send_rows, ('grp', 'slab'), split_axis=0, concat_axis=0, t...  7.5 us
  transfers between devices with their start and end apart: 6, of which 3 were waited for; matrix products, arithmetic and copies ran while one was open for 23% of the time, Pallas kernels for 0%

commit v1 on v0

v1 whole, which is shorter than its diff:
```python
import jax
import jax.numpy as jnp
from jax import lax
from jax.sharding import PartitionSpec as P

UPTAKE = 0.5
AXES = ("grp", "slab")


def padded(cells, sides, width):
    for axis, dim in sides:
        count = lax.axis_size(axis)
        ends = count - 1
        head = lax.slice_in_dim(cells, 0, width, axis=dim)
        tail = lax.slice_in_dim(cells, cells.shape[dim] - width, cells.shape[dim], axis=dim)
        cells = jnp.concatenate(
            [
                lax.ppermute(tail, axis, [(i, (i + 1) % count) for i in range(ends)]),
                cells,
                lax.ppermute(head, axis, [((i + 1) % count, i) for i in range(ends)]),
            ],
            axis=dim,
        )
    return cells


def neighbours(values):
    return [
        values[2:, 1:-1, 1:-1],
        values[:-2, 1:-1, 1:-1],
        values[1:-1, 2:, 1:-1],
        values[1:-1, :-2, 1:-1],
        values[1:-1, 1:-1, 2:],
        values[1:-1, 1:-1, :-2],
    ]


def relax(padded_p, padded_k, source):
    centre = padded_k[1:-1, 1:-1, 1:-1]
    numerator = source
    denominator = jnp.full(centre.shape, UPTAKE, jnp.float32)
    for p_side, k_side in zip(neighbours(padded_p), neighbours(padded_k)):
        facing = 0.5 * (centre + k_side)
        numerator = numerator + facing * p_side
        denominator = denominator + facing
    return numerator / denominator


def pad_sides(values):
    return jnp.pad(values, ((0, 0), (1, 1), (1, 1)))


def bf16_round(x):
    return x.astype(jnp.bfloat16).astype(jnp.float32)


def on_device(
    vessel_start,
    drive,
    junction_gain,
    parent,
    inverse_blocks,
    wall_perm,
    outside,
    owner,
    target,
    kernel_id,
    kernels,
    tissue_start,
    conduct,
    base_source,
):
    devices = lax.axis_size(AXES)
    nb = drive.shape[0]
    seg = drive.shape[1]
    lane = jnp.arange(seg, dtype=jnp.int32)[None, :]
    fixed_rhs = jnp.where(lane == 0, 0.0, drive).astype(jnp.bfloat16)
    base = jnp.einsum(
        "bij,bj->bi", inverse_blocks, fixed_rhs, preferred_element_type=jnp.float32
    )
    first_col = inverse_blocks[:, :, 0].astype(jnp.float32)
    exit_base = base[:, -1]
    exit_col = first_col[:, -1]
    drive0 = drive[:, 0]
    packed = jnp.stack(
        [
            exit_base,
            exit_col,
            drive0,
            junction_gain,
            vessel_start[:, -1],
            parent.astype(jnp.float32),
        ]
    ).reshape(1, 6 * nb)
    sent = jnp.broadcast_to(packed, (devices, 6 * nb))
    got = lax.all_to_all(sent, AXES, 0, 0, tiled=True)
    table = got.reshape(devices, 6, nb).transpose(1, 0, 2).reshape(6, devices * nb)
    all_parent = table[5].astype(jnp.int32)
    p1 = parent
    p2 = all_parent[p1]
    p3 = all_parent[p2]
    at2 = table[:, p2]
    at1 = table[:, p1]
    x0 = table[4][p3]
    exit1 = at2[0] + at2[1] * bf16_round(at2[2] + at2[3] * x0)
    exit2 = at1[0] + at1[1] * bf16_round(at1[2] + at1[3] * exit1)
    r0 = bf16_round(drive0 + junction_gain * exit2)
    pressure = base + first_col * r0[:, None]
    leak = (wall_perm * (pressure - outside)).astype(jnp.bfloat16)
    destination = owner[:, 0]
    same = destination[:, None] == destination[None, :]
    earlier = jnp.arange(nb)[None, :] < jnp.arange(nb)[:, None]
    slot = jnp.sum((same & earlier).astype(jnp.int32), axis=1)
    capacity = 2
    row_of = destination * capacity + slot
    slots = devices * capacity
    onehot = row_of[None, :] == jnp.arange(slots, dtype=jnp.int32)[:, None]
    leak_sent = jnp.dot(
        onehot.astype(jnp.bfloat16), leak, preferred_element_type=jnp.float32
    ).astype(jnp.bfloat16)
    kid_sent = jnp.sum(jnp.where(onehot, kernel_id[None, :], 0), axis=1)
    tgt_sent = jnp.sum(jnp.where(onehot, target[None, :], 0), axis=1)
    cells = jnp.zeros((slots, seg), jnp.float32)
    for k in range(kernels.shape[0]):
        part = jnp.dot(leak_sent, kernels[k], preferred_element_type=jnp.float32)
        cells = jnp.where((kid_sent == k)[:, None], part, cells)
    tgt_row = jnp.pad(
        tgt_sent.astype(jnp.float32).reshape(devices, capacity), ((0, 0), (0, seg - capacity))
    )
    send = jnp.concatenate(
        [cells.reshape(devices, capacity, seg), tgt_row[:, None, :]], axis=1
    )
    recv = lax.all_to_all(send, AXES, 0, 0, tiled=True)
    got_rows = recv[:, :capacity, :].reshape(slots, seg)
    got_index = recv[:, capacity, :capacity].reshape(slots).astype(jnp.int32)
    cell_blocks = tissue_start.size // seg
    leakage = jax.ops.segment_sum(got_rows, got_index, num_segments=cell_blocks)
    source = base_source + leakage.reshape(base_source.shape)
    stacked = jnp.stack([tissue_start, conduct])
    wide = padded(stacked, ((AXES, 1),), 1)
    padded_k = pad_sides(wide[1])
    first = relax(pad_sides(wide[0]), padded_k, source)
    second = padded(first, ((AXES, 0),), 1)
    tissue = relax(pad_sides(second), padded_k, source)
    return (pressure, tissue)


def solution(mesh):
    in_specs = (
        P(AXES, None),
        P(AXES, None),
        P(AXES),
        P(AXES),
        P(AXES, None, None),
        P(AXES, None),
        P(AXES, None),
        P(AXES, None),
        P(AXES),
        P(AXES),
        P(),
        P(AXES, None, None),
        P(AXES, None, None),
        P(AXES, None, None),
    )
    out_specs = (P(AXES, None), P(AXES, None, None))
    return jax.shard_map(
        on_device, mesh=mesh, in_specs=in_specs, out_specs=out_specs, check_vma=False
    )
```

time: 245 us -> 141 us (0.58)
  blocking collectives: 105 us -> 19.9 us
  waiting for transfers between devices: 20.3 us -> 12.8 us
  starting transfers between devices: 31.4 us -> 26.3 us
  other arithmetic: 37.1 us -> 32.5 us
  matrix products: 13.5 us -> 9.16 us
  local copies, waits for them, and re-layouts: 36.1 us -> 38.7 us
    all_gather x3 -> x0, blocking collectives: 105 us -> none  [on_device(): lax.all_gather(pressure[:, -1], ('grp', 'slab'), axis=0, tiled=True)]
    scatter x2 -> x0, local copies, waits for them, and re-layouts: 20.2 us -> none  [the longest x1 13.8 us: on_device(): jnp.zeros((devices, capacity, 128), jnp.float32).at[destination, slot_index]]
    all_to_all x0 -> x1, blocking collectives: none -> 19.9 us  [on_device(): recv = lax.all_to_all(send, AXES, 0, 0, tiled=True)]
    transpose x0 -> x1, local copies, waits for them, and re-layouts: none -> 8.43 us  [on_device(): got.reshape(devices, 6, nb).transpose(1, 0, 2).reshape(6, devices * nb)]
    gather x3 -> x5, local copies, waits for them, and re-layouts: 3.44 us -> 11.5 us  [the longest x1 4.03 us: on_device(): at1 = table[:, p1]]
    all_to_all x2 -> x1, waiting for transfers between devices: 7.5 us -> 0.01 us  [on_device(): got = lax.all_to_all(sent, AXES, 0, 0, tiled=True)]
    all_to_all x2 -> x1, starting transfers between devices: 15.8 us -> 10.8 us  [on_device(): got = lax.all_to_all(sent, AXES, 0, 0, tiled=True)]
    all_gather x1 -> x0, other arithmetic: 4.63 us -> none  [on_device(): lax.all_gather(pressure[:, -1], ('grp', 'slab'), axis=0, tiled=True)]
  transfers between devices with their start and end apart: 6 -> 5, of which waited for: 3 -> 2; matrix products, arithmetic and copies ran while one was open for 23% -> 29% of each run, Pallas kernels for 0% -> 0%
where the time goes in v1:
time: 141 us; the launch traced here: 140 us
  local copies, waits for them, and re-layouts  38.7 us (27%)
  other arithmetic  32.5 us (23%)
  starting transfers between devices  26.3 us (19%)
  blocking collectives  19.9 us (14%)
  waiting for transfers between devices  12.8 us (9%)
  matrix products  9.16 us (6%)
    all_to_all x1, blocking collectives, on_device(): recv = lax.all_to_all(send, AXES, 0, 0, tiled=True)  19.9 us
    div x2, other arithmetic, relax(): return numerator / denominator  18.2 us
    ppermute x2, starting transfers between devices, padded(): lax.ppermute(head, axis, [((i + 1) % count, i) for i in range(ends)])  11.3 us
    all_to_all x1, starting transfers between devices, on_device(): got = lax.all_to_all(sent, AXES, 0, 0, tiled=True)  10.8 us
    transpose x1, local copies, waits for them, and re-layouts, on_device(): got.reshape(devices, 6, nb).transpose(1, 0, 2).reshape(6, devices * nb)  8.43 us
    ppermute x2, waiting for transfers between devices, padded(): lax.ppermute(tail, axis, [(i, (i + 1) % count) for i in range(ends)])  8.32 us
    ppermute x2, waiting for transfers between devices, padded(): lax.ppermute(head, axis, [((i + 1) % count, i) for i in range(ends)])  4.48 us
    concatenate x2, other arithmetic, padded(): jnp.concatenate([lax.ppermute(tail, axis, [(i, (i + 1) % count) for i in...  4.44 us
  transfers between devices with their start and end apart: 5, of which 2 were waited for; matrix products, arithmetic and copies ran while one was open for 29% of the time, Pallas kernels for 0%

profile of v1, /device:TPU:8, one launch (start us, length us, event | category | flops | bytes accessed | tf_op | source)
XLA Modules:
  0.0 140.4 jit_solution(18128661748867660331)
XLA Ops:
  0.6 0.9 slice_reduce_fusion.11
  1.6 0.9 fusion.49
  2.4 4.4 %fusion.45 = f32[128,1,128]{2,1,0:T(1,128)S(1)} fusion(bf16[128,128,128]{2,1,0:T(8,128)(2,1)} %param.18, bf16[128,128,1]{1,0,2:T(8,128)(2,1)S(1)} %fusion.49), kind=kOutput, calls=%fused_computation.101 | convolution fusion | flops 4194304 | bytes 4292608 | tf_op jit(solution)/shard_map/bij,bj->bi/dot_general | solution.py:78
  6.9 0.2 slice_reduce_fusion.9
  7.1 0.0 copy-start.5
  7.1 0.0 copy-start.9
  7.1 0.0 copy-start.6
  7.1 0.0 copy-start
  7.1 3.8 %copy.41 = bf16[128,128,1]{1,0,2:T(8,128)(2,1)S(1)} copy(bf16[128,128,1]{2,1,0:T(8,128)(2,1)} %bitcast.110) | data formatting | bytes 65536
  11.0 0.2 slice_reduce_fusion.8
  11.2 0.2 slice_reduce_fusion.10
  11.4 1.0 broadcast_in_dim.92
  12.4 10.8 %all-to-all-start = ((f32[128,1,768]{2,1,0:T(1,128)}), f32[128,1,768]{2,1,0:T(1,128)}, u32[]{:S(2)}, u32[]{:S(2)}) async-start(f32[128,1,768]{2,1,0:T(1,128)} %broadcast_in_dim.92), calls=%async_computation | async-start | bytes 786432 | tf_op jit(solution)/shard_map/all_to_all | solution.py:96
  23.2 0.0 copy-start.10
  23.2 0.0 copy-start.7
  23.2 0.0 copy-start.8
  23.3 2.8 %pad_maximum_fusion.7 = (f32[2,1,256,512]{3,2,1,0:T(8,128)}, f32[2,1,256,512]{3,2,1,0:T(8,128)}) fusion(f32[1,4,256,512]{3,2,1,0:T(8,128)S(1)} %bitcast.100, f32[1,4,256,512]{3,2,1,0:T(8,128)} %bitcast.104), kind=kLoop, calls=%fused_computation.80 | loop fusion | flops 524288 | bytes 6291456 | tf_op jit(solution)/shard_map/stack | solution.py:139
  26.0 7.1 %collective-permute-start = (f32[2,1,256,512]{3,2,1,0:T(8,128)}, f32[2,1,256,512]{3,2,1,0:T(8,128)S(1)}, u32[]{:S(2)}, u32[]{:S(2)}) collective-permute-start(f32[2,1,256,512]{3,2,1,0:T(8,128)} %get-tuple-element.17), channel_id=1, source_target_pairs={{1,0},{2,1},{3,2},{4,3},{5,4},{6,5},{7,6},{8,7},{9,8},{10,9},{11,1... | collective-permute-start | bytes 3145736 | tf_op jit(solution)/shard_map/ppermute | solution.py:20
  33.1 1.9 %collective-permute-start.1 = (f32[2,1,256,512]{3,2,1,0:T(8,128)}, f32[2,1,256,512]{3,2,1,0:T(8,128)}, u32[]{:S(2)}, u32[]{:S(2)}) collective-permute-start(f32[2,1,256,512]{3,2,1,0:T(8,128)} %get-tuple-element.16), channel_id=1, source_target_pairs={{0,1},{1,2},{2,3},{3,4},{4,5},{5,6},{6,7},{7,8},{8,9},{9,10},{10,1... | collective-permute-start | bytes 3145736 | tf_op jit(solution)/shard_map/ppermute | solution.py:18
  35.1 0.2 convert_reduce_fusion
  35.3 0.0 copy-done.7
  35.3 0.0 copy-done.8
  35.3 0.1 select_reduce_fusion.1
  35.4 0.1 convert_element_type.88
  35.6 0.0 all-to-all-done
  35.6 1.9 %copy.34 = f32[128,1,768]{0,2,1:T(8,128)} copy(f32[128,1,768]{2,1,0:T(1,128)} %all-to-all-done) | data formatting | bytes 786432 | tf_op jit(solution)/shard_map/all_to_all | solution.py:96
  37.5 8.4 %copy.35 = f32[6,128,128]{0,2,1:T(8,128)} copy(f32[6,128,128]{1,2,0:T(8,128)} %bitcast.114) | data formatting | bytes 786432 | tf_op jit(solution)/shard_map/transpose | solution.py:97
  46.0 1.5 %fusion.64 = (f32[1,128,128]{1,2,0:T(8,128)}, s32[1,128,128]{1,2,0:T(8,128)S(1)}) fusion(f32[6,128,128]{1,2,0:T(8,128)} %bitcast.115), kind=kLoop, calls=%fused_computation.142 | loop fusion | flops 16384 | bytes 262144 | tf_op jit(solution)/shard_map/slice | solution.py:104
  47.5 0.1 copy.36
  47.6 1.2 gather_fusion.1
  48.7 4.0 %gather_fusion = f32[128,6]{1,0:T(8,128)S(1)} fusion(f32[6,16384]{0,1:T(8,128)} %bitcast.111, s32[1024]{0:T(1024)S(1)} %pad_clamp_fusion.2), kind=kCustom, calls=%fused_computation | custom fusion | bytes 6656 | tf_op jit(solution)/shard_map/gather | solution.py:103
  52.8 4.0 %gather_fusion.2 = f32[128,6]{1,0:T(8,128)S(1)} fusion(f32[6,16384]{0,1:T(8,128)} %bitcast.112, s32[1024]{0:T(1024)S(1)} %pad_clamp_fusion.1), kind=kCustom, calls=%fused_computation.2 | custom fusion | bytes 6656 | tf_op jit(solution)/shard_map/gather | solution.py:102
  56.8 1.1 gather_fusion.3
  58.0 0.9 copy.37
  58.9 0.9 slice_reduce_fusion
  59.9 1.1 gather_fusion.4
  61.0 0.7 convert_convert_fusion
  61.8 0.1 multiply_add_fusion
  61.8 0.0 copy-start.4
  61.9 1.1 convolution_convert_fusion
  62.9 0.9 fusion.55
  63.8 0.9 fusion.53
  64.7 0.9 fusion.51
  65.6 1.0 fusion.41
  66.6 0.1 pad_maximum_fusion.9
  66.8 19.9 %all_to_all.11 = f32[128,3,128]{2,1,0:T(4,128)S(1)} all-to-all(f32[128,3,128]{2,1,0:T(4,128)S(1)} %pad_maximum_fusion.9), channel_id=1, replica_groups=mesh['grp'=4,'slab'=32] {'grp','slab'}, dimensions={0} | all-to-all | bytes 393216 | tf_op jit(solution)/shard_map/all_to_all | solution.py:133
  86.7 0.2 fusion.44
  86.9 0.1 reshape.159
  87.1 0.7 slice.249
  87.8 3.2 %scatter_custom_fusion = f32[4096,128]{1,0:T(8,128)} fusion(s32[256]{0:T(256)S(1)} %reshape.159, f32[256,128]{1,0:T(8,128)} %bitcast.122, f32[]{:T(128)} %constant.8.clone.1), kind=kCustom, calls=%fused_computation.82 | custom fusion | flops 32768 | bytes 2097664 | tf_op jit(solution)/shard_map/scatter-add | solution.py:137
  90.9 2.7 %reshape.115 = f32[4,256,512]{2,1,0:T(8,128)} reshape(f32[4096,128]{1,0:T(8,128)} %scatter_custom_fusion) | data formatting | bytes 4194304 | tf_op jit(solution)/shard_map/reshape | solution.py:138
  93.7 0.0 collective-permute-done
  93.7 0.0 collective-permute-done.1
  93.7 2.2 %pad_maximum_fusion = f32[2,6,256,512]{3,2,1,0:T(8,128)S(1)} fusion(f32[2,1,256,512]{3,2,1,0:T(8,128)S(1)} %collective-permute-done, f32[1,4,256,512]{3,2,1,0:T(8,128)S(1)} %bitcast.101, f32[1,4,256,512]{3,2,1,0:T(8,128)} %bitcast.105, f32[2,1,256,512]{3,2,1,0:T(8,128)} %collective-permute-done.1), kind=kLoop, calls=%fused_computation.6 | loop fusion | flops 4718592 | bytes 12582912 | tf_op jit(solution)/shard_map/concatenate | solution.py:16
  95.9 0.0 copy-start.1
  95.9 3.4 %slice_bitcast_fusion.1 = (f32[6,256,512]{2,1,0:T(8,128)}, f32[6,256,512]{2,1,0:T(8,128)}) fusion(f32[2,6,256,512]{3,2,1,0:T(8,128)S(1)} %pad_maximum_fusion), kind=kLoop, calls=%fused_computation.25 | loop fusion | bytes 12582912 | tf_op jit(solution)/shard_map/squeeze | solution.py:141
  99.3 11.3 %fusion.16 = (f32[4,256,512]{2,1,0:T(8,128)}, f32[4,256,512]{2,1,0:T(8,128)}) fusion(f32[6,256,512]{2,1,0:T(8,128)} %get-tuple-element.15, f32[2,1,256,512]{3,2,1,0:T(8,128)} %collective-permute-done.1, f32[1,4,256,512]{3,2,1,0:T(8,128)S(1)} %bitcast.102, f32[1,4,256,512]{3,2,1,0:T(8,128)S(1)} %bitcast.106, f32[2,1,256,512]{3,2,1,0:T(8,128)S(1)} %collective-permute-done, ...), kind=kLoop, calls=%fused_computation.39 | loop fusion | flops 20971520 | bytes 23068672 | tf_op jit(solution)/shard_map/div | solution.py:46
  110.6 1.4 %fusion.63 = (f32[1,256,512]{2,1,0:T(8,128)S(1)}, f32[1,256,512]{2,1,0:T(8,128)S(1)}) fusion(f32[4,256,512]{2,1,0:T(8,128)} %get-tuple-element.12), kind=kLoop, calls=%fused_computation.141 | loop fusion | bytes 2097152 | tf_op jit(solution)/shard_map/slice | solution.py:15
  112.0 4.2 %collective-permute-start.2 = (f32[1,256,512]{2,1,0:T(8,128)S(1)}, f32[1,256,512]{2,1,0:T(8,128)S(1)}, u32[]{:S(2)}, u32[]{:S(2)}) collective-permute-start(f32[1,256,512]{2,1,0:T(8,128)S(1)} %get-tuple-element.19), channel_id=1, source_target_pairs={{1,0},{2,1},{3,2},{4,3},{5,4},{6,5},{7,6},{8,7},{9,8},{10,9},{11,1... | collective-permute-start | bytes 1572872 | tf_op jit(solution)/shard_map/ppermute | solution.py:20
  116.2 2.2 %collective-permute-start.3 = (f32[1,256,512]{2,1,0:T(8,128)S(1)}, f32[1,256,512]{2,1,0:T(8,128)S(1)}, u32[]{:S(2)}, u32[]{:S(2)}) collective-permute-start(f32[1,256,512]{2,1,0:T(8,128)S(1)} %get-tuple-element.18), channel_id=1, source_target_pairs={{0,1},{1,2},{2,3},{3,4},{4,5},{5,6},{6,7},{7,8},{8,9},{9,10},{10,1... | collective-permute-start | bytes 1572872 | tf_op jit(solution)/shard_map/ppermute | solution.py:18
  118.4 4.5 %collective-permute-done.2 = f32[1,256,512]{2,1,0:T(8,128)S(1)} collective-permute-done((f32[1,256,512]{2,1,0:T(8,128)S(1)}, f32[1,256,512]{2,1,0:T(8,128)S(1)}, u32[]{:S(2)}, u32[]{:S(2)}) %collective-permute-start.2) | collective-permute-done | bytes 524320 | tf_op jit(solution)/shard_map/ppermute | solution.py:20
  122.9 8.3 %collective-permute-done.3 = f32[1,256,512]{2,1,0:T(8,128)S(1)} collective-permute-done((f32[1,256,512]{2,1,0:T(8,128)S(1)}, f32[1,256,512]{2,1,0:T(8,128)S(1)}, u32[]{:S(2)}, u32[]{:S(2)}) %collective-permute-start.3) | collective-permute-done | bytes 524320 | tf_op jit(solution)/shard_map/ppermute | solution.py:18
  131.2 2.3 %select_maximum_fusion = f32[6,258,514]{2,1,0:T(8,128)S(1)} fusion(f32[1,256,512]{2,1,0:T(8,128)S(1)} %collective-permute-done.2, f32[4,256,512]{2,1,0:T(8,128)S(1)} %copy-done.3, f32[1,256,512]{2,1,0:T(8,128)S(1)} %collective-permute-done.3), kind=kLoop, calls=%fused_computation.19 | loop fusion | flops 11935080 | bytes 6328416 | tf_op jit(solution)/shard_map/concatenate | solution.py:16
  133.5 6.9 %fusion.21 = f32[4,256,512]{2,1,0:T(8,128)} fusion(f32[6,258,514]{2,1,0:T(8,128)S(1)} %select_maximum_fusion, f32[4,256,512]{2,1,0:T(8,128)} %get-tuple-element.12, f32[1,256,512]{2,1,0:T(8,128)S(1)} %collective-permute-done.3, f32[4,256,512]{2,1,0:T(8,128)} %get-tuple-element.13, f32[1,256,512]{2,1,0:T(8,128)S(1)} %collective-permute-done.2, ...), kind=kLoop, calls=%fused_computation.45 | loop fusion | flops 19398656 | bytes 27262976 | tf_op jit(solution)/shard_map/div | solution.py:46
  (24 shorter events, 0.1 us)
Async XLA Ops:
  7.1 4.1 %copy-start.5 = (f32[128,128]{1,0:T(8,128)S(1)}, f32[128,128]{1,0:T(8,128)}, u32[]{:S(2)}) copy-start(f32[128,128]{1,0:T(8,128)} %param.14) | copy-start | bytes 196612
  7.1 4.3 %copy-start.9 = (s32[128]{0:T(128)S(1)}, s32[128]{0:T(128)}, u32[]{:S(2)}) copy-start(s32[128]{0:T(128)} %param.17) | copy-start | bytes 1540
  7.1 4.3 %copy-start.6 = (f32[128]{0:T(128)S(1)}, f32[128]{0:T(128)}, u32[]{:S(2)}) copy-start(f32[128]{0:T(128)} %param.16) | copy-start | bytes 1540
  7.1 16.1 %copy-start = (f32[4,256,512]{2,1,0:T(8,128)S(1)}, f32[4,256,512]{2,1,0:T(8,128)}, u32[]{:S(2)}) copy-start(f32[4,256,512]{2,1,0:T(8,128)} %param.26) | copy-start | bytes 6291460
  12.4 23.3 %all-to-all-start = ((f32[128,1,768]{2,1,0:T(1,128)}), f32[128,1,768]{2,1,0:T(1,128)}, u32[]{:S(2)}, u32[]{:S(2)}) async-start(f32[128,1,768]{2,1,0:T(1,128)} %broadcast_in_dim.92), calls=%async_computation | async-start | bytes 786432 | tf_op jit(solution)/shard_map/all_to_all | solution.py:96
  23.2 11.8 %copy-start.10 = (s32[128,1]{0,1:T(1,128)S(1)}, s32[128,1]{0,1:T(1,128)}, u32[]{:S(2)}) copy-start(s32[128,1]{0,1:T(1,128)} %param.21) | copy-start | bytes 1540
  23.2 12.0 %copy-start.7 = (s32[128]{0:T(128)S(1)}, s32[128]{0:T(128)}, u32[]{:S(2)}) copy-start(s32[128]{0:T(128)} %param.23) | copy-start | bytes 1540
  23.2 12.0 %copy-start.8 = (s32[128]{0:T(128)S(1)}, s32[128]{0:T(128)}, u32[]{:S(2)}) copy-start(s32[128]{0:T(128)} %param.22) | copy-start | bytes 1540
  26.0 67.7 %collective-permute-start = (f32[2,1,256,512]{3,2,1,0:T(8,128)}, f32[2,1,256,512]{3,2,1,0:T(8,128)S(1)}, u32[]{:S(2)}, u32[]{:S(2)}) collective-permute-start(f32[2,1,256,512]{3,2,1,0:T(8,128)} %get-tuple-element.17), channel_id=1, source_target_pairs={{1,0},{2,1},{3,2},{4,3},{5,4},{6,5},{7,6},{8,7},{9,8},{10,9},{11,1... | collective-permute-start | bytes 3145736 | tf_op jit(solution)/shard_map/ppermute | solution.py:20
  33.1 60.6 %collective-permute-start.1 = (f32[2,1,256,512]{3,2,1,0:T(8,128)}, f32[2,1,256,512]{3,2,1,0:T(8,128)}, u32[]{:S(2)}, u32[]{:S(2)}) collective-permute-start(f32[2,1,256,512]{3,2,1,0:T(8,128)} %get-tuple-element.16), channel_id=1, source_target_pairs={{0,1},{1,2},{2,3},{3,4},{4,5},{5,6},{6,7},{7,8},{8,9},{9,10},{10,1... | collective-permute-start | bytes 3145736 | tf_op jit(solution)/shard_map/ppermute | solution.py:18
  61.8 4.8 %copy-start.4 = (f32[128,128]{1,0:T(8,128)}, f32[128,128]{1,0:T(8,128)S(1)}, u32[]{:S(2)}) copy-start(f32[128,128]{1,0:T(8,128)S(1)} %multiply_add_fusion) | copy-start | bytes 196612
  95.9 3.4 %copy-start.1 = (f32[4,256,512]{2,1,0:T(8,128)S(1)}, f32[4,256,512]{2,1,0:T(8,128)}, u32[]{:S(2)}) copy-start(f32[4,256,512]{2,1,0:T(8,128)} %param.25) | copy-start | bytes 6291460
  110.6 20.6 %copy-start.3 = (f32[4,256,512]{2,1,0:T(8,128)S(1)}, f32[4,256,512]{2,1,0:T(8,128)}, u32[]{:S(2)}) copy-start(f32[4,256,512]{2,1,0:T(8,128)} %get-tuple-element.12) | copy-start | bytes 6291460
  112.0 10.9 %collective-permute-start.2 = (f32[1,256,512]{2,1,0:T(8,128)S(1)}, f32[1,256,512]{2,1,0:T(8,128)S(1)}, u32[]{:S(2)}, u32[]{:S(2)}) collective-permute-start(f32[1,256,512]{2,1,0:T(8,128)S(1)} %get-tuple-element.19), channel_id=1, source_target_pairs={{1,0},{2,1},{3,2},{4,3},{5,4},{6,5},{7,6},{8,7},{9,8},{10,9},{11,1... | collective-permute-start | bytes 1572872 | tf_op jit(solution)/shard_map/ppermute | solution.py:20
  116.2 17.3 %copy-start.2 = (f32[6,256,512]{2,1,0:T(8,128)S(1)}, f32[6,256,512]{2,1,0:T(8,128)}, u32[]{:S(2)}) copy-start(f32[6,256,512]{2,1,0:T(8,128)} %get-tuple-element.14) | copy-start | bytes 9437188
  116.2 15.0 %collective-permute-start.3 = (f32[1,256,512]{2,1,0:T(8,128)S(1)}, f32[1,256,512]{2,1,0:T(8,128)S(1)}, u32[]{:S(2)}, u32[]{:S(2)}) collective-permute-start(f32[1,256,512]{2,1,0:T(8,128)S(1)} %get-tuple-element.18), channel_id=1, source_target_pairs={{0,1},{1,2},{2,3},{3,4},{4,5},{5,6},{6,7},{7,8},{8,9},{9,10},{10,1... | collective-permute-start | bytes 1572872 | tf_op jit(solution)/shard_map/ppermute | solution.py:18

commit v2 on v1

--- a/solution.py
+++ b/solution.py
@@ -44,6 +44,17 @@
         numerator = numerator + facing * p_side
         denominator = denominator + facing
     return numerator / denominator
+
+
+def relax_parts(padded_p, padded_k, source):
+    centre = padded_k[1:-1, 1:-1, 1:-1]
+    numerator = source
+    denominator = jnp.full(centre.shape, UPTAKE, jnp.float32)
+    for p_side, k_side in zip(neighbours(padded_p), neighbours(padded_k)):
+        facing = 0.5 * (centre + k_side)
+        numerator = numerator + facing * p_side
+        denominator = denominator + facing
+    return numerator, denominator
 
 
 def pad_sides(values):
@@ -93,15 +104,18 @@
         ]
     ).reshape(1, 6 * nb)
     sent = jnp.broadcast_to(packed, (devices, 6 * nb))
-    got = lax.all_to_all(sent, AXES, 0, 0, tiled=True)
-    table = got.reshape(devices, 6, nb).transpose(1, 0, 2).reshape(6, devices * nb)
-    all_parent = table[5].astype(jnp.int32)
-    p1 = parent
-    p2 = all_parent[p1]
-    p3 = all_parent[p2]
-    at2 = table[:, p2]
-    at1 = table[:, p1]
-    x0 = table[4][p3]
+    got = lax.all_to_all(sent, AXES, 0, 0, tiled=True).reshape(-1)
+    fields = jnp.arange(6, dtype=jnp.int32)[:, None] * nb
+
+    def fetch(index):
+        flat = (index // nb) * (6 * nb) + index % nb
+        return got[flat[None, :] + fields]
+
+    at1 = fetch(parent)
+    p2 = at1[5].astype(jnp.int32)
+    at2 = fetch(p2)
+    p3 = at2[5].astype(jnp.int32)
+    x0 = got[(p3 // nb) * (6 * nb) + 4 * nb + p3 % nb]
     exit1 = at2[0] + at2[1] * bf16_round(at2[2] + at2[3] * x0)
     exit2 = at1[0] + at1[1] * bf16_round(at1[2] + at1[3] * exit1)
     r0 = bf16_round(drive0 + junction_gain * exit2)
@@ -130,16 +144,20 @@
     send = jnp.concatenate(
         [cells.reshape(devices, capacity, seg), tgt_row[:, None, :]], axis=1
     )
-    recv = lax.all_to_all(send, AXES, 0, 0, tiled=True)
+    recv = lax.all_to_all(
+        send.reshape(devices, (capacity + 1) * seg), AXES, 0, 0, tiled=True
+    ).reshape(devices, capacity + 1, seg)
     got_rows = recv[:, :capacity, :].reshape(slots, seg)
     got_index = recv[:, capacity, :capacity].reshape(slots).astype(jnp.int32)
     cell_blocks = tissue_start.size // seg
     leakage = jax.ops.segment_sum(got_rows, got_index, num_segments=cell_blocks)
-    source = base_source + leakage.reshape(base_source.shape)
+    leak_field = leakage.reshape(base_source.shape)
+    source = base_source + leak_field
     stacked = jnp.stack([tissue_start, conduct])
     wide = padded(stacked, ((AXES, 1),), 1)
     padded_k = pad_sides(wide[1])
-    first = relax(pad_sides(wide[0]), padded_k, source)
+    partial, denominator = relax_parts(pad_sides(wide[0]), padded_k, base_source)
+    first = (partial + leak_field) / denominator
     second = padded(first, ((AXES, 0),), 1)
     tissue = relax(pad_sides(second), padded_k, source)
     return (pressure, tissue)

time: 141 us -> 130 us (0.922); the launches traced: 140 us -> 128 us
  local copies, waits for them, and re-layouts: 38.7 us -> 32.2 us
  waiting for transfers between devices: 12.8 us -> 6.5 us
  blocking collectives: 19.9 us -> 15 us
  starting transfers between devices: 26.3 us -> 30.2 us
    div x2 -> x1, other arithmetic: 18.2 us -> 7.43 us  [relax(): return numerator / denominator]
    div x0 -> x1, other arithmetic: none -> 8.8 us  [on_device(): first = (partial + leak_field) / denominator]
    transpose x1 -> x0, local copies, waits for them, and re-layouts: 8.43 us -> none  [on_device(): got.reshape(devices, 6, nb).transpose(1, 0, 2).reshape(6, devices * nb)]
    all_to_all x1, blocking collectives: 19.9 us -> 15 us  [on_device(): lax.all_to_all(send.reshape(devices, (capacity + 1) * seg), AXES, 0, 0, t...]
    ppermute x2, starting transfers between devices: 11.3 us -> 15.8 us  [padded(): lax.ppermute(head, axis, [((i + 1) % count, i) for i in range(ends)])]
    ppermute x2, waiting for transfers between devices: 8.32 us -> 4.74 us  [padded(): lax.ppermute(tail, axis, [(i, (i + 1) % count) for i in range(ends)])]
    broadcast_in_dim x0 -> x2, local copies, waits for them, and re-layouts: none -> 3.01 us  [on_device(): tgt_row[:, None, :]]
    ppermute x2, waiting for transfers between devices: 4.48 us -> 1.76 us  [padded(): lax.ppermute(head, axis, [((i + 1) % count, i) for i in range(ends)])]
  transfers between devices with their start and end apart: 5 -> 5, of which waited for: 2 -> 2; matrix products, arithmetic and copies ran while one was open for 29% -> 27% of each run, Pallas kernels for 0% -> 0%
where the time goes in v2:
time: 130 us; the launch traced here: 128 us
  other arithmetic  33.7 us (26%)
  local copies, waits for them, and re-layouts  32.2 us (25%)
  starting transfers between devices  30.2 us (23%)
  blocking collectives  15 us (12%)
  matrix products  9.31 us (7%)
  waiting for transfers between devices  6.5 us (5%)
    ppermute x2, starting transfers between devices, padded(): lax.ppermute(head, axis, [((i + 1) % count, i) for i in range(ends)])  15.8 us
    all_to_all x1, blocking collectives, on_device(): lax.all_to_all(send.reshape(devices, (capacity + 1) * seg), AXES, 0, 0, t...  15 us
    all_to_all x1, starting transfers between devices, on_device(): got = lax.all_to_all(sent, AXES, 0, 0, tiled=True).reshape(-1)  10.4 us
    gather x2, local copies, waits for them, and re-layouts, fetch(): return got[flat[None, :] + fields]  8.91 us
    div x1, other arithmetic, on_device(): first = (partial + leak_field) / denominator  8.8 us
    div x1, other arithmetic, relax(): return numerator / denominator  7.43 us
    unnamed x27, local copies, waits for them, and re-layouts  6.47 us
    ppermute x2, waiting for transfers between devices, padded(): lax.ppermute(tail, axis, [(i, (i + 1) % count) for i in range(ends)])  4.74 us
  transfers between devices with their start and end apart: 5, of which 2 were waited for; matrix products, arithmetic and copies ran while one was open for 27% of the time, Pallas kernels for 0%

profile of v2, /device:TPU:8, one launch (start us, length us, event | category | flops | bytes accessed | tf_op | source)
XLA Modules:
  0.0 127.9 jit_solution(2989818631683950294)
XLA Ops:
  0.6 0.9 slice_reduce_fusion.3
  1.6 1.0 slice_reduce_fusion.2
  2.6 1.3 fusion.63
  3.9 0.8 fusion.49
  4.7 3.7 %copy.42 = bf16[128,128,1]{1,0,2:T(8,128)(2,1)S(1)} copy(bf16[128,128,1]{2,1,0:T(8,128)(2,1)} %bitcast.137) | data formatting | bytes 65536
  8.4 0.0 copy-start.8
  8.4 0.0 copy-start
  8.4 4.6 %fusion.45 = f32[128,1,128]{2,1,0:T(1,128)S(1)} fusion(bf16[128,128,128]{2,1,0:T(8,128)(2,1)} %param.18, bf16[128,128,1]{1,0,2:T(8,128)(2,1)S(1)} %fusion.49), kind=kOutput, calls=%fused_computation.89 | convolution fusion | flops 4194304 | bytes 4292608 | tf_op jit(solution)/shard_map/bij,bj->bi/dot_general | solution.py:89
  13.0 0.7 copy-done.4
  13.7 0.2 slice_reduce_fusion.1
  13.9 0.2 slice_reduce_fusion
  14.1 1.0 broadcast_in_dim.91
  15.0 10.4 %all-to-all-start = ((f32[128,1,768]{2,1,0:T(1,128)}), f32[128,1,768]{2,1,0:T(1,128)S(1)}, u32[]{:S(2)}, u32[]{:S(2)}) async-start(f32[128,1,768]{2,1,0:T(1,128)} %broadcast_in_dim.91), calls=%async_computation | async-start | bytes 786432 | tf_op jit(solution)/shard_map/all_to_all | solution.py:107
  25.5 0.0 copy-start.12
  25.5 0.0 copy-start.10
  25.5 0.0 copy-start.11
  25.5 2.7 %pad_maximum_fusion.7 = (f32[2,1,256,512]{3,2,1,0:T(8,128)}, f32[2,1,256,512]{3,2,1,0:T(8,128)}) fusion(f32[1,4,256,512]{3,2,1,0:T(8,128)S(1)} %bitcast.129, f32[1,4,256,512]{3,2,1,0:T(8,128)} %bitcast.133), kind=kLoop, calls=%fused_computation.79 | loop fusion | flops 524288 | bytes 6291456 | tf_op jit(solution)/shard_map/stack | solution.py:156
  28.2 2.0 %collective-permute-start.1 = (f32[2,1,256,512]{3,2,1,0:T(8,128)}, f32[2,1,256,512]{3,2,1,0:T(8,128)S(1)}, u32[]{:S(2)}, u32[]{:S(2)}) collective-permute-start(f32[2,1,256,512]{3,2,1,0:T(8,128)} %get-tuple-element.6), channel_id=1, source_target_pairs={{0,1},{1,2},{2,3},{3,4},{4,5},{5,6},{6,7},{7,8},{8,9},{9,10},{10,1... | collective-permute-start | bytes 3145736 | tf_op jit(solution)/shard_map/ppermute | solution.py:18
  30.3 7.8 %collective-permute-start = (f32[2,1,256,512]{3,2,1,0:T(8,128)}, f32[2,1,256,512]{3,2,1,0:T(8,128)}, u32[]{:S(2)}, u32[]{:S(2)}) collective-permute-start(f32[2,1,256,512]{3,2,1,0:T(8,128)} %get-tuple-element.7), channel_id=1, source_target_pairs={{1,0},{2,1},{3,2},{4,3},{5,4},{6,5},{7,6},{8,7},{9,8},{10,9},{11,1... | collective-permute-start | bytes 3145736 | tf_op jit(solution)/shard_map/ppermute | solution.py:20
  38.0 0.5 iota_multiply_fusion
  38.6 0.2 convert_reduce_fusion
  38.8 0.1 select_reduce_fusion.1
  38.9 0.4 copy-done.7
  39.4 0.8 convert_element_type.100
  40.1 0.7 fusion.61
  40.8 1.5 %pad_bitcast_fusion = f32[128,1,128]{2,0,1:T(8,128)} fusion(f32[128,2]{1,0:T(8,128)} %convert_element_type.100), kind=kLoop, calls=%fused_computation.91 | loop fusion | bytes 66560 | tf_op jit(solution)/shard_map/broadcast_in_dim | solution.py:145
  42.3 1.6 %copy.35 = f32[128,1,128]{0,2,1:T(8,128)} copy(f32[128,1,128]{2,0,1:T(8,128)} %pad_bitcast_fusion) | data formatting | bytes 131072 | tf_op jit(solution)/shard_map/broadcast_in_dim | solution.py:145
  43.8 0.6 broadcast_compare_fusion.3
  44.4 0.0 all-to-all-done
  44.4 4.5 %gather_fusion = f32[768]{0:T(1024)S(1)} fusion(f32[98304]{0:T(1024)S(1)} %bitcast.126, s32[1024]{0:T(1024)S(1)} %pad_clamp_fusion.2), kind=kCustom, calls=%fused_computation | custom fusion | bytes 9216 | tf_op jit(solution)/shard_map/gather | solution.py:112
  48.9 0.1 fusion.62
  49.0 4.5 %gather_fusion.1 = f32[768]{0:T(1024)S(1)} fusion(f32[98304]{0:T(1024)S(1)} %bitcast.127, s32[1024]{0:T(1024)S(1)} %pad_clamp_fusion.1), kind=kCustom, calls=%fused_computation.1 | custom fusion | bytes 9216 | tf_op jit(solution)/shard_map/gather | solution.py:112
  53.5 1.7 %gather_fusion.2 = f32[128]{0:T(128)} fusion(f32[98304]{0:T(1024)S(1)} %bitcast.128, s32[1024]{0:T(1024)S(1)} %pad_clamp_fusion), kind=kCustom, calls=%fused_computation.2 | custom fusion | bytes 1536 | tf_op jit(solution)/shard_map/gather | solution.py:118
  55.2 0.7 convert_convert_fusion
  55.9 0.9 multiply_add_fusion
  56.8 0.0 copy-start.6
  56.8 0.6 copy-done.6
  57.4 1.0 convolution_convert_fusion
  58.5 0.9 fusion.51
  59.4 0.9 fusion.53
  60.3 0.9 fusion.55
  61.2 1.0 fusion.42
  62.2 0.1 copy.34
  62.3 0.9 pad_maximum_fusion.9
  63.1 0.2 copy.36
  63.3 15.0 %all_to_all.15 = f32[128,1,384]{2,1,0:T(1,128)S(1)} all-to-all(f32[128,1,384]{2,1,0:T(1,128)S(1)} %copy.36), channel_id=1, replica_groups=mesh['grp'=4,'slab'=32] {'grp','slab'}, dimensions={0} | all-to-all | bytes 393216 | tf_op jit(solution)/shard_map/all_to_all | solution.py:147
  78.3 0.2 copy.37
  78.5 0.7 copy.39
  79.2 0.1 copy.38
  79.3 0.1 reshape.327
  79.5 3.4 %scatter_custom_fusion = f32[4096,128]{1,0:T(8,128)} fusion(s32[256]{0:T(256)S(1)} %reshape.327, f32[256,128]{1,0:T(8,128)} %bitcast.144, f32[]{:T(128)} %constant.66.clone.1), kind=kCustom, calls=%fused_computation.81 | custom fusion | flops 32768 | bytes 2097664 | tf_op jit(solution)/shard_map/scatter-add | solution.py:153
  82.9 2.8 %reshape.299 = f32[4,256,512]{2,1,0:T(8,128)} reshape(f32[4096,128]{1,0:T(8,128)} %scatter_custom_fusion) | data formatting | bytes 4194304 | tf_op jit(solution)/shard_map/reshape | solution.py:154
  85.6 1.0 copy-done.3
  86.7 2.2 %pad_maximum_fusion = f32[2,6,256,512]{3,2,1,0:T(8,128)S(1)} fusion(f32[2,1,256,512]{3,2,1,0:T(8,128)} %collective-permute-done, f32[1,4,256,512]{3,2,1,0:T(8,128)S(1)} %bitcast.130, f32[1,4,256,512]{3,2,1,0:T(8,128)} %bitcast.134, f32[2,1,256,512]{3,2,1,0:T(8,128)S(1)} %collective-permute-done.1), kind=kLoop, calls=%fused_computation.4 | loop fusion | flops 4718592 | bytes 12582912 | tf_op jit(solution)/shard_map/concatenate | solution.py:16
  88.9 0.0 copy-start.1
  88.9 2.5 %slice_bitcast_fusion.1 = (f32[6,256,512]{2,1,0:T(8,128)S(1)}, f32[6,256,512]{2,1,0:T(8,128)}) fusion(f32[2,6,256,512]{3,2,1,0:T(8,128)S(1)} %pad_maximum_fusion), kind=kLoop, calls=%fused_computation.23 | loop fusion | bytes 12582912 | tf_op jit(solution)/shard_map/squeeze | solution.py:158
  91.4 8.8 %fusion.17 = f32[4,256,512]{2,1,0:T(8,128)} fusion(f32[4,256,512]{2,1,0:T(8,128)} %reshape.299, f32[6,256,512]{2,1,0:T(8,128)} %get-tuple-element.5, f32[2,1,256,512]{3,2,1,0:T(8,128)} %copy-done.3, f32[1,4,256,512]{3,2,1,0:T(8,128)S(1)} %bitcast.131, f32[1,4,256,512]{3,2,1,0:T(8,128)S(1)} %bitcast.135, f32[4,256,512]{2,1,0:T(8,128)} %param.27, ...), kind=kLoop, calls=%fused_computation.38 | loop fusion | flops 20971520 | bytes 20971520 | tf_op jit(solution)/shard_map/div | solution.py:160
  100.2 1.4 %fusion.75 = (f32[1,256,512]{2,1,0:T(8,128)S(1)}, f32[1,256,512]{2,1,0:T(8,128)S(1)}) fusion(f32[4,256,512]{2,1,0:T(8,128)} %fusion.17), kind=kLoop, calls=%fused_computation.164 | loop fusion | bytes 2097152 | tf_op jit(solution)/shard_map/slice | solution.py:15
  101.7 1.9 %collective-permute-start.3 = (f32[1,256,512]{2,1,0:T(8,128)S(1)}, f32[1,256,512]{2,1,0:T(8,128)S(1)}, u32[]{:S(2)}, u32[]{:S(2)}) collective-permute-start(f32[1,256,512]{2,1,0:T(8,128)S(1)} %get-tuple-element.8), channel_id=1, source_target_pairs={{0,1},{1,2},{2,3},{3,4},{4,5},{5,6},{6,7},{7,8},{8,9},{9,10},{10,1... | collective-permute-start | bytes 1572872 | tf_op jit(solution)/shard_map/ppermute | solution.py:18
  103.6 8.0 %collective-permute-start.2 = (f32[1,256,512]{2,1,0:T(8,128)S(1)}, f32[1,256,512]{2,1,0:T(8,128)S(1)}, u32[]{:S(2)}, u32[]{:S(2)}) collective-permute-start(f32[1,256,512]{2,1,0:T(8,128)S(1)} %get-tuple-element.9), channel_id=1, source_target_pairs={{1,0},{2,1},{3,2},{4,3},{5,4},{6,5},{7,6},{8,7},{9,8},{10,9},{11,1... | collective-permute-start | bytes 1572872 | tf_op jit(solution)/shard_map/ppermute | solution.py:20
  111.6 4.7 %collective-permute-done.3 = f32[1,256,512]{2,1,0:T(8,128)S(1)} collective-permute-done((f32[1,256,512]{2,1,0:T(8,128)S(1)}, f32[1,256,512]{2,1,0:T(8,128)S(1)}, u32[]{:S(2)}, u32[]{:S(2)}) %collective-permute-start.3) | collective-permute-done | bytes 524320 | tf_op jit(solution)/shard_map/ppermute | solution.py:18
  116.4 1.8 %collective-permute-done.2 = f32[1,256,512]{2,1,0:T(8,128)S(1)} collective-permute-done((f32[1,256,512]{2,1,0:T(8,128)S(1)}, f32[1,256,512]{2,1,0:T(8,128)S(1)}, u32[]{:S(2)}, u32[]{:S(2)}) %collective-permute-start.2) | collective-permute-done | bytes 524320 | tf_op jit(solution)/shard_map/ppermute | solution.py:20
  118.1 2.3 %select_maximum_fusion = f32[6,258,514]{2,1,0:T(8,128)S(1)} fusion(f32[1,256,512]{2,1,0:T(8,128)S(1)} %collective-permute-done.2, f32[4,256,512]{2,1,0:T(8,128)S(1)} %copy-done.2, f32[1,256,512]{2,1,0:T(8,128)S(1)} %collective-permute-done.3), kind=kLoop, calls=%fused_computation.17 | loop fusion | flops 11935080 | bytes 6328416 | tf_op jit(solution)/shard_map/concatenate | solution.py:16
  120.4 7.4 %fusion.22 = f32[4,256,512]{2,1,0:T(8,128)} fusion(f32[6,258,514]{2,1,0:T(8,128)S(1)} %select_maximum_fusion, f32[4,256,512]{2,1,0:T(8,128)} %fusion.17, f32[1,256,512]{2,1,0:T(8,128)S(1)} %collective-permute-done.3, f32[1,256,512]{2,1,0:T(8,128)S(1)} %collective-permute-done.2, f32[4,256,512]{2,1,0:T(8,128)} %param.27, f32[4,256,512]{2,1,0:T(8,128)} %reshape.299, ...), kind=kLoop, calls=%fused_computation.44 | loop fusion | flops 19922944 | bytes 29360128 | tf_op jit(solution)/shard_map/div | solution.py:46
  (29 shorter events, 0.2 us)
Async XLA Ops:
  8.4 5.4 %copy-start.5 = (bf16[128,128,1]{1,0,2:T(8,128)(2,1)}, bf16[128,128,1]{1,0,2:T(8,128)(2,1)S(1)}, u32[]{:S(2)}) copy-start(bf16[128,128,1]{1,0,2:T(8,128)(2,1)S(1)} %copy.42) | copy-start | bytes 98308
  8.4 5.6 %copy-start.8 = (f32[128]{0:T(128)S(1)}, f32[128]{0:T(128)}, u32[]{:S(2)}) copy-start(f32[128]{0:T(128)} %param.16) | copy-start | bytes 1540
  8.4 17.1 %copy-start = (f32[4,256,512]{2,1,0:T(8,128)S(1)}, f32[4,256,512]{2,1,0:T(8,128)}, u32[]{:S(2)}) copy-start(f32[4,256,512]{2,1,0:T(8,128)} %param.26) | copy-start | bytes 6291460
  13.0 0.7 copy-start.4
  15.0 29.4 %all-to-all-start = ((f32[128,1,768]{2,1,0:T(1,128)}), f32[128,1,768]{2,1,0:T(1,128)S(1)}, u32[]{:S(2)}, u32[]{:S(2)}) async-start(f32[128,1,768]{2,1,0:T(1,128)} %broadcast_in_dim.91), calls=%async_computation | async-start | bytes 786432 | tf_op jit(solution)/shard_map/all_to_all | solution.py:107
  25.5 13.1 %copy-start.12 = (s32[128,1]{0,1:T(1,128)S(1)}, s32[128,1]{0,1:T(1,128)}, u32[]{:S(2)}) copy-start(s32[128,1]{0,1:T(1,128)} %param.21) | copy-start | bytes 1540
  25.5 13.3 %copy-start.10 = (s32[128]{0:T(128)S(1)}, s32[128]{0:T(128)}, u32[]{:S(2)}) copy-start(s32[128]{0:T(128)} %param.23) | copy-start | bytes 1540
  25.5 13.3 %copy-start.11 = (s32[128]{0:T(128)S(1)}, s32[128]{0:T(128)}, u32[]{:S(2)}) copy-start(s32[128]{0:T(128)} %param.22) | copy-start | bytes 1540
  28.2 57.4 %collective-permute-start.1 = (f32[2,1,256,512]{3,2,1,0:T(8,128)}, f32[2,1,256,512]{3,2,1,0:T(8,128)S(1)}, u32[]{:S(2)}, u32[]{:S(2)}) collective-permute-start(f32[2,1,256,512]{3,2,1,0:T(8,128)} %get-tuple-element.6), channel_id=1, source_target_pairs={{0,1},{1,2},{2,3},{3,4},{4,5},{5,6},{6,7},{7,8},{8,9},{9,10},{10,1... | collective-permute-start | bytes 3145736 | tf_op jit(solution)/shard_map/ppermute | solution.py:18
  30.3 55.4 %collective-permute-start = (f32[2,1,256,512]{3,2,1,0:T(8,128)}, f32[2,1,256,512]{3,2,1,0:T(8,128)}, u32[]{:S(2)}, u32[]{:S(2)}) collective-permute-start(f32[2,1,256,512]{3,2,1,0:T(8,128)} %get-tuple-element.7), channel_id=1, source_target_pairs={{1,0},{2,1},{3,2},{4,3},{5,4},{6,5},{7,6},{8,7},{9,8},{10,9},{11,1... | collective-permute-start | bytes 3145736 | tf_op jit(solution)/shard_map/ppermute | solution.py:20
  38.8 0.6 copy-start.7
  44.4 4.5 %copy-start.9 = (s32[6]{0:T(128)S(1)}, s32[6]{0:T(128)}, u32[]{:S(2)}) copy-start(s32[6]{0:T(128)} %iota_multiply_fusion) | copy-start | bytes 76
  56.8 0.6 copy-start.6
  85.6 1.0 copy-start.3
  88.9 2.6 %copy-start.1 = (f32[4,256,512]{2,1,0:T(8,128)S(1)}, f32[4,256,512]{2,1,0:T(8,128)}, u32[]{:S(2)}) copy-start(f32[4,256,512]{2,1,0:T(8,128)} %param.25) | copy-start | bytes 6291460
  100.2 17.9 %copy-start.2 = (f32[4,256,512]{2,1,0:T(8,128)S(1)}, f32[4,256,512]{2,1,0:T(8,128)}, u32[]{:S(2)}) copy-start(f32[4,256,512]{2,1,0:T(8,128)} %fusion.17) | copy-start | bytes 6291460
  101.7 14.7 %collective-permute-start.3 = (f32[1,256,512]{2,1,0:T(8,128)S(1)}, f32[1,256,512]{2,1,0:T(8,128)S(1)}, u32[]{:S(2)}, u32[]{:S(2)}) collective-permute-start(f32[1,256,512]{2,1,0:T(8,128)S(1)} %get-tuple-element.8), channel_id=1, source_target_pairs={{0,1},{1,2},{2,3},{3,4},{4,5},{5,6},{6,7},{7,8},{8,9},{9,10},{10,1... | collective-permute-start | bytes 1572872 | tf_op jit(solution)/shard_map/ppermute | solution.py:18
  103.6 14.5 %collective-permute-start.2 = (f32[1,256,512]{2,1,0:T(8,128)S(1)}, f32[1,256,512]{2,1,0:T(8,128)S(1)}, u32[]{:S(2)}, u32[]{:S(2)}) collective-permute-start(f32[1,256,512]{2,1,0:T(8,128)S(1)} %get-tuple-element.9), channel_id=1, source_target_pairs={{1,0},{2,1},{3,2},{4,3},{5,4},{6,5},{7,6},{8,7},{9,8},{10,9},{11,1... | collective-permute-start | bytes 1572872 | tf_op jit(solution)/shard_map/ppermute | solution.py:20

commit v3 on v2

--- a/solution.py
+++ b/solution.py
@@ -86,10 +86,15 @@
     seg = drive.shape[1]
     lane = jnp.arange(seg, dtype=jnp.int32)[None, :]
     fixed_rhs = jnp.where(lane == 0, 0.0, drive).astype(jnp.bfloat16)
-    base = jnp.einsum(
-        "bij,bj->bi", inverse_blocks, fixed_rhs, preferred_element_type=jnp.float32
+    unit = jnp.broadcast_to((lane == 0).astype(jnp.bfloat16), (nb, seg))
+    both = jnp.einsum(
+        "bij,cbj->cbi",
+        inverse_blocks,
+        jnp.stack([fixed_rhs, unit]),
+        preferred_element_type=jnp.float32,
     )
-    first_col = inverse_blocks[:, :, 0].astype(jnp.float32)
+    base = both[0]
+    first_col = both[1]
     exit_base = base[:, -1]
     exit_col = first_col[:, -1]
     drive0 = drive[:, 0]
@@ -104,18 +109,23 @@
         ]
     ).reshape(1, 6 * nb)
     sent = jnp.broadcast_to(packed, (devices, 6 * nb))
-    got = lax.all_to_all(sent, AXES, 0, 0, tiled=True).reshape(-1)
-    fields = jnp.arange(6, dtype=jnp.int32)[:, None] * nb
+    got = lax.all_to_all(sent, AXES, 0, 0, tiled=True)
+    owners = jnp.arange(devices, dtype=jnp.int32)[None, :]
+    within = jnp.arange(nb, dtype=jnp.int32)[None, :]
 
     def fetch(index):
-        flat = (index // nb) * (6 * nb) + index % nb
-        return got[flat[None, :] + fields]
+        pick = (index // nb)[:, None] == owners
+        rows = jnp.dot(
+            pick.astype(jnp.float32), got, precision=lax.Precision.HIGHEST
+        ).reshape(index.shape[0], 6, nb)
+        lanes = ((index % nb)[:, None] == within)[:, None, :]
+        return jnp.sum(jnp.where(lanes, rows, 0.0), axis=2).T
 
     at1 = fetch(parent)
-    p2 = at1[5].astype(jnp.int32)
+    p2 = jnp.round(at1[5]).astype(jnp.int32)
     at2 = fetch(p2)
-    p3 = at2[5].astype(jnp.int32)
-    x0 = got[(p3 // nb) * (6 * nb) + 4 * nb + p3 % nb]
+    p3 = jnp.round(at2[5]).astype(jnp.int32)
+    x0 = fetch(p3)[4]
     exit1 = at2[0] + at2[1] * bf16_round(at2[2] + at2[3] * x0)
     exit2 = at1[0] + at1[1] * bf16_round(at1[2] + at1[3] * exit1)
     r0 = bf16_round(drive0 + junction_gain * exit2)

time: 130 us -> 112 us (0.86)
  local copies, waits for them, and re-layouts: 32.2 us -> 16.2 us
  other arithmetic: 33.7 us -> 31.5 us
    gather x3 -> x0, local copies, waits for them, and re-layouts: 10.6 us -> none  [the longest x2 8.91 us: fetch(): return got[flat[None, :] + fields]]
    unnamed x27 -> x38, local copies, waits for them, and re-layouts: 6.47 us -> 2.5 us
    broadcast_in_dim x2, local copies, waits for them, and re-layouts: 3.01 us -> 0.72 us  [on_device(): tgt_row[:, None, :]]
    dot_general x1 -> x4, matrix products: 4.58 us -> 6.46 us  [the longest x1 4.58 us: on_device(): jnp.einsum('bij,cbj->cbi', inverse_blocks, jnp.stack([fixed_rhs, unit]),...]
    dot_general x4, matrix products: 3.69 us -> 2.15 us  [on_device(): part = jnp.dot(leak_sent, kernels[k], preferred_element_type=jnp.float32)]
  transfers between devices with their start and end apart: 5 -> 5, of which waited for: 2 -> 2; matrix products, arithmetic and copies ran while one was open for 27% -> 18% of each run, Pallas kernels for 0% -> 0%
where the time goes in v3:
time: 112 us; the launch traced here: 111 us
  other arithmetic  31.5 us (28%)
  starting transfers between devices  30.6 us (27%)
  local copies, waits for them, and re-layouts  16.2 us (14%)
  blocking collectives  15 us (13%)
  matrix products  9.64 us (9%)
  waiting for transfers between devices  6.5 us (6%)
  between operations  1.17 us (1%)
    ppermute x2, starting transfers between devices, padded(): lax.ppermute(head, axis, [((i + 1) % count, i) for i in range(ends)])  15.8 us
    all_to_all x1, blocking collectives, on_device(): lax.all_to_all(send.reshape(devices, (capacity + 1) * seg), AXES, 0, 0, t...  15 us
    all_to_all x1, starting transfers between devices, on_device(): got = lax.all_to_all(sent, AXES, 0, 0, tiled=True)  10.8 us
    div x1, other arithmetic, on_device(): first = (partial + leak_field) / denominator  8.8 us
    div x1, other arithmetic, relax(): return numerator / denominator  7.43 us
    ppermute x2, waiting for transfers between devices, padded(): lax.ppermute(tail, axis, [(i, (i + 1) % count) for i in range(ends)])  4.74 us
    dot_general x1, matrix products, on_device(): jnp.einsum('bij,cbj->cbi', inverse_blocks, jnp.stack([fixed_rhs, unit]),...  4.58 us
    concatenate x2, other arithmetic, padded(): jnp.concatenate([lax.ppermute(tail, axis, [(i, (i + 1) % count) for i in...  4.47 us
  transfers between devices with their start and end apart: 5, of which 2 were waited for; matrix products, arithmetic and copies ran while one was open for 18% of the time, Pallas kernels for 0%

profile of v3, /device:TPU:8, one launch (start us, length us, event | category | flops | bytes accessed | tf_op | source)
XLA Modules:
  0.0 110.5 jit_solution(1269403274291056043)
XLA Ops:
  0.7 0.9 slice_reduce_fusion.3
  1.6 1.0 slice_reduce_fusion.2
  2.6 1.3 %and_select_fusion.4 = (s32[128]{0:T(128)}, s32[128]{0:T(128)S(1)}, f32[1,128]{1,0:T(1,128)S(1)}) fusion(s32[128]{0:T(128)} %param.17), kind=kLoop, calls=%fused_computation.134 | loop fusion | flops 2560 | bytes 2048 | tf_op jit(solution)/shard_map/jit(floor_divide)/jit(_where)/select_n | solution.py:117
  3.9 0.8 fusion.59
  4.8 0.1 copy.37
  4.9 0.0 copy-start.15
  4.9 0.0 copy-start
  4.9 4.6 %convolution_bitcast_fusion = f32[2,128,128]{2,0,1:T(2,128)S(1)} fusion(bf16[128,128,128]{2,1,0:T(8,128)(2,1)} %param.18, bf16[1,128,128]{2,0,1:T(2,128)(2,1)S(1)} %stack_broadcast_in_dim.2, bf16[1,128,128]{2,0,1:T(2,128)(2,1)S(1)} %copy.37), kind=kOutput, calls=%fused_computation.77 | convolution fusion | flops 8519680 | bytes 4390912 | tf_op jit(solution)/shard_map/bij,cbj->cbi/dot_general | solution.py:90
  9.5 0.1 fusion.80
  9.6 0.0 copy-start.5
  9.6 0.2 slice_reduce_fusion.1
  9.8 0.4 copy-done.4
  10.2 0.2 slice_reduce_fusion
  10.5 1.0 broadcast_in_dim.121
  11.4 10.8 %all-to-all-start = ((f32[128,1,768]{2,1,0:T(1,128)}), f32[128,1,768]{2,1,0:T(1,128)}, u32[]{:S(2)}, u32[]{:S(2)}) async-start(f32[128,1,768]{2,1,0:T(1,128)} %broadcast_in_dim.121), calls=%async_computation | async-start | bytes 786432 | tf_op jit(solution)/shard_map/all_to_all | solution.py:112
  22.3 0.0 copy-start.18
  22.3 0.0 copy-start.16
  22.3 0.0 copy-start.17
  22.3 2.7 %pad_maximum_fusion.7 = (f32[2,1,256,512]{3,2,1,0:T(8,128)}, f32[2,1,256,512]{3,2,1,0:T(8,128)}) fusion(f32[1,4,256,512]{3,2,1,0:T(8,128)S(1)} %bitcast.138, f32[1,4,256,512]{3,2,1,0:T(8,128)} %bitcast.142), kind=kLoop, calls=%fused_computation.83 | loop fusion | flops 524288 | bytes 6291456 | tf_op jit(solution)/shard_map/stack | solution.py:166
  25.0 2.0 %collective-permute-start.1 = (f32[2,1,256,512]{3,2,1,0:T(8,128)}, f32[2,1,256,512]{3,2,1,0:T(8,128)S(1)}, u32[]{:S(2)}, u32[]{:S(2)}) collective-permute-start(f32[2,1,256,512]{3,2,1,0:T(8,128)} %get-tuple-element.10), channel_id=1, source_target_pairs={{0,1},{1,2},{2,3},{3,4},{4,5},{5,6},{6,7},{7,8},{8,9},{9,10},{10,1... | collective-permute-start | bytes 3145736 | tf_op jit(solution)/shard_map/ppermute | solution.py:18
  27.0 7.8 %collective-permute-start = (f32[2,1,256,512]{3,2,1,0:T(8,128)}, f32[2,1,256,512]{3,2,1,0:T(8,128)}, u32[]{:S(2)}, u32[]{:S(2)}) collective-permute-start(f32[2,1,256,512]{3,2,1,0:T(8,128)} %get-tuple-element.11), channel_id=1, source_target_pairs={{1,0},{2,1},{3,2},{4,3},{5,4},{6,5},{7,6},{8,7},{9,8},{10,9},{11,1... | collective-permute-start | bytes 3145736 | tf_op jit(solution)/shard_map/ppermute | solution.py:20
  34.8 0.2 convert_reduce_fusion
  35.0 0.1 select_reduce_fusion.1
  35.2 0.3 copy-done.10
  35.5 0.1 convert_element_type.119
  35.7 0.7 copy.41
  36.4 0.6 broadcast_compare_fusion.3
  37.0 1.2 %copy.48 = f32[128,1,768]{0,2,1:T(8,128)S(1)} copy(f32[128,1,768]{2,1,0:T(1,128)} %all-to-all-done) | data formatting | bytes 786432 | tf_op jit(solution)/shard_map/dot_general | solution.py:118
  38.2 0.0 copy-start.8
  38.3 1.1 fusion.40
  39.4 0.4 fusion.41
  39.9 0.4 fusion.42
  40.3 0.7 fusion.76
  41.0 0.9 multiply_add_fusion
  42.0 0.0 copy-start.6
  42.0 0.6 copy-done.6
  42.6 1.0 convolution_convert_fusion
  43.6 0.9 fusion.61
  44.5 0.9 fusion.63
  45.5 0.1 fusion.65
  45.6 0.2 fusion.45
  45.9 0.1 copy.40
  46.0 0.2 copy.42
  46.2 15.0 %all_to_all.18 = f32[128,1,384]{2,1,0:T(1,128)S(1)} all-to-all(f32[128,1,384]{2,1,0:T(1,128)S(1)} %copy.42), channel_id=1, replica_groups=mesh['grp'=4,'slab'=32] {'grp','slab'}, dimensions={0} | all-to-all | bytes 393216 | tf_op jit(solution)/shard_map/all_to_all | solution.py:157
  61.2 0.2 copy.43
  61.4 0.7 copy.45
  62.1 0.1 copy.44
  62.2 0.1 reshape.232
  62.3 3.2 %scatter_custom_fusion = f32[4096,128]{1,0:T(8,128)} fusion(s32[256]{0:T(256)S(1)} %reshape.232, f32[256,128]{1,0:T(8,128)} %bitcast.157, f32[]{:T(128)} %constant.59.clone.1), kind=kCustom, calls=%fused_computation.85 | custom fusion | flops 32768 | bytes 2097664 | tf_op jit(solution)/shard_map/scatter-add | solution.py:163
  65.5 2.8 %reshape.225 = f32[4,256,512]{2,1,0:T(8,128)} reshape(f32[4096,128]{1,0:T(8,128)} %scatter_custom_fusion) | data formatting | bytes 4194304 | tf_op jit(solution)/shard_map/reshape | solution.py:164
  68.3 0.0 collective-permute-done.1
  68.3 0.0 collective-permute-done
  68.3 1.0 copy-done.3
  69.4 2.2 %pad_maximum_fusion = f32[2,6,256,512]{3,2,1,0:T(8,128)S(1)} fusion(f32[2,1,256,512]{3,2,1,0:T(8,128)} %collective-permute-done, f32[1,4,256,512]{3,2,1,0:T(8,128)S(1)} %bitcast.139, f32[1,4,256,512]{3,2,1,0:T(8,128)} %bitcast.143, f32[2,1,256,512]{3,2,1,0:T(8,128)S(1)} %collective-permute-done.1), kind=kLoop, calls=%fused_computation.1 | loop fusion | flops 4718592 | bytes 12582912 | tf_op jit(solution)/shard_map/concatenate | solution.py:16
  71.6 0.0 copy-start.1
  71.6 2.5 %slice_bitcast_fusion.1 = (f32[6,256,512]{2,1,0:T(8,128)S(1)}, f32[6,256,512]{2,1,0:T(8,128)}) fusion(f32[2,6,256,512]{3,2,1,0:T(8,128)S(1)} %pad_maximum_fusion), kind=kLoop, calls=%fused_computation.20 | loop fusion | bytes 12582912 | tf_op jit(solution)/shard_map/squeeze | solution.py:168
  74.1 8.8 %fusion.17 = f32[4,256,512]{2,1,0:T(8,128)} fusion(f32[4,256,512]{2,1,0:T(8,128)} %reshape.225, f32[6,256,512]{2,1,0:T(8,128)} %get-tuple-element.9, f32[2,1,256,512]{3,2,1,0:T(8,128)} %copy-done.3, f32[1,4,256,512]{3,2,1,0:T(8,128)S(1)} %bitcast.140, f32[1,4,256,512]{3,2,1,0:T(8,128)S(1)} %bitcast.144, f32[4,256,512]{2,1,0:T(8,128)} %param.27, ...), kind=kLoop, calls=%fused_computation.35 | loop fusion | flops 20971520 | bytes 20971520 | tf_op jit(solution)/shard_map/div | solution.py:170
  82.9 1.4 %fusion.79 = (f32[1,256,512]{2,1,0:T(8,128)S(1)}, f32[1,256,512]{2,1,0:T(8,128)S(1)}) fusion(f32[4,256,512]{2,1,0:T(8,128)} %fusion.17), kind=kLoop, calls=%fused_computation.163 | loop fusion | bytes 2097152 | tf_op jit(solution)/shard_map/slice | solution.py:15
  84.3 2.0 %collective-permute-start.3 = (f32[1,256,512]{2,1,0:T(8,128)S(1)}, f32[1,256,512]{2,1,0:T(8,128)S(1)}, u32[]{:S(2)}, u32[]{:S(2)}) collective-permute-start(f32[1,256,512]{2,1,0:T(8,128)S(1)} %get-tuple-element.12), channel_id=1, source_target_pairs={{0,1},{1,2},{2,3},{3,4},{4,5},{5,6},{6,7},{7,8},{8,9},{9,10},{10,1... | collective-permute-start | bytes 1572872 | tf_op jit(solution)/shard_map/ppermute | solution.py:18
  86.3 8.0 %collective-permute-start.2 = (f32[1,256,512]{2,1,0:T(8,128)S(1)}, f32[1,256,512]{2,1,0:T(8,128)S(1)}, u32[]{:S(2)}, u32[]{:S(2)}) collective-permute-start(f32[1,256,512]{2,1,0:T(8,128)S(1)} %get-tuple-element.13), channel_id=1, source_target_pairs={{1,0},{2,1},{3,2},{4,3},{5,4},{6,5},{7,6},{8,7},{9,8},{10,9},{11,1... | collective-permute-start | bytes 1572872 | tf_op jit(solution)/shard_map/ppermute | solution.py:20
  94.3 4.7 %collective-permute-done.3 = f32[1,256,512]{2,1,0:T(8,128)S(1)} collective-permute-done((f32[1,256,512]{2,1,0:T(8,128)S(1)}, f32[1,256,512]{2,1,0:T(8,128)S(1)}, u32[]{:S(2)}, u32[]{:S(2)}) %collective-permute-start.3) | collective-permute-done | bytes 524320 | tf_op jit(solution)/shard_map/ppermute | solution.py:18
  99.1 1.8 %collective-permute-done.2 = f32[1,256,512]{2,1,0:T(8,128)S(1)} collective-permute-done((f32[1,256,512]{2,1,0:T(8,128)S(1)}, f32[1,256,512]{2,1,0:T(8,128)S(1)}, u32[]{:S(2)}, u32[]{:S(2)}) %collective-permute-start.2) | collective-permute-done | bytes 524320 | tf_op jit(solution)/shard_map/ppermute | solution.py:20
  100.8 2.3 %select_maximum_fusion = f32[6,258,514]{2,1,0:T(8,128)S(1)} fusion(f32[1,256,512]{2,1,0:T(8,128)S(1)} %collective-permute-done.2, f32[4,256,512]{2,1,0:T(8,128)S(1)} %copy-done.2, f32[1,256,512]{2,1,0:T(8,128)S(1)} %collective-permute-done.3), kind=kLoop, calls=%fused_computation.14 | loop fusion | flops 11935080 | bytes 6328416 | tf_op jit(solution)/shard_map/concatenate | solution.py:16
  103.1 7.4 %fusion.22 = f32[4,256,512]{2,1,0:T(8,128)} fusion(f32[6,258,514]{2,1,0:T(8,128)S(1)} %select_maximum_fusion, f32[4,256,512]{2,1,0:T(8,128)} %fusion.17, f32[1,256,512]{2,1,0:T(8,128)S(1)} %collective-permute-done.3, f32[1,256,512]{2,1,0:T(8,128)S(1)} %collective-permute-done.2, f32[4,256,512]{2,1,0:T(8,128)} %param.27, f32[4,256,512]{2,1,0:T(8,128)} %reshape.225, ...), kind=kLoop, calls=%fused_computation.41 | loop fusion | flops 19922944 | bytes 29360128 | tf_op jit(solution)/shard_map/div | solution.py:46
  (43 shorter events, 0.3 us)
Async XLA Ops:
  1.6 8.8 %copy-start.9 = (f32[128]{0:T(128)}, f32[128]{0:T(128)S(1)}, u32[]{:S(2)}) copy-start(f32[128]{0:T(128)S(1)} %slice_reduce_fusion.3) | copy-start | bytes 1540
  4.9 5.6 %copy-start.15 = (f32[128]{0:T(128)S(1)}, f32[128]{0:T(128)}, u32[]{:S(2)}) copy-start(f32[128]{0:T(128)} %param.16) | copy-start | bytes 1540
  4.9 17.4 %copy-start = (f32[4,256,512]{2,1,0:T(8,128)S(1)}, f32[4,256,512]{2,1,0:T(8,128)}, u32[]{:S(2)}) copy-start(f32[4,256,512]{2,1,0:T(8,128)} %param.26) | copy-start | bytes 6291460
  9.6 0.6 copy-start.4
  9.6 0.8 copy-start.5
  11.4 25.6 %all-to-all-start = ((f32[128,1,768]{2,1,0:T(1,128)}), f32[128,1,768]{2,1,0:T(1,128)}, u32[]{:S(2)}, u32[]{:S(2)}) async-start(f32[128,1,768]{2,1,0:T(1,128)} %broadcast_in_dim.121), calls=%async_computation | async-start | bytes 786432 | tf_op jit(solution)/shard_map/all_to_all | solution.py:112
  22.3 12.5 %copy-start.18 = (s32[128,1]{0,1:T(1,128)S(1)}, s32[128,1]{0,1:T(1,128)}, u32[]{:S(2)}) copy-start(s32[128,1]{0,1:T(1,128)} %param.21) | copy-start | bytes 1540
  22.3 12.7 %copy-start.16 = (s32[128]{0:T(128)S(1)}, s32[128]{0:T(128)}, u32[]{:S(2)}) copy-start(s32[128]{0:T(128)} %param.23) | copy-start | bytes 1540
  22.3 12.7 %copy-start.17 = (s32[128]{0:T(128)S(1)}, s32[128]{0:T(128)}, u32[]{:S(2)}) copy-start(s32[128]{0:T(128)} %param.22) | copy-start | bytes 1540
  25.0 43.3 %collective-permute-start.1 = (f32[2,1,256,512]{3,2,1,0:T(8,128)}, f32[2,1,256,512]{3,2,1,0:T(8,128)S(1)}, u32[]{:S(2)}, u32[]{:S(2)}) collective-permute-start(f32[2,1,256,512]{3,2,1,0:T(8,128)} %get-tuple-element.10), channel_id=1, source_target_pairs={{0,1},{1,2},{2,3},{3,4},{4,5},{5,6},{6,7},{7,8},{8,9},{9,10},{10,1... | collective-permute-start | bytes 3145736 | tf_op jit(solution)/shard_map/ppermute | solution.py:18
  27.0 41.3 %collective-permute-start = (f32[2,1,256,512]{3,2,1,0:T(8,128)}, f32[2,1,256,512]{3,2,1,0:T(8,128)}, u32[]{:S(2)}, u32[]{:S(2)}) collective-permute-start(f32[2,1,256,512]{3,2,1,0:T(8,128)} %get-tuple-element.11), channel_id=1, source_target_pairs={{1,0},{2,1},{3,2},{4,3},{5,4},{6,5},{7,6},{8,7},{9,8},{10,9},{11,1... | collective-permute-start | bytes 3145736 | tf_op jit(solution)/shard_map/ppermute | solution.py:20
  35.0 0.5 copy-start.10
  38.2 7.2 %copy-start.8 = (bf16[4,128,128]{2,1,0:T(8,128)(2,1)S(1)}, bf16[4,128,128]{2,1,0:T(8,128)(2,1)}, u32[]{:S(2)}) copy-start(bf16[4,128,128]{2,1,0:T(8,128)(2,1)} %param.24) | copy-start | bytes 393220
  38.3 7.4 %copy-start.11 = (pred[256]{0:T(512)(128)(4,1)S(1)}, pred[256]{0:T(512)(128)(4,1)}, u32[]{:S(2)}) copy-start(pred[256]{0:T(512)(128)(4,1)} %get-tuple-element.16) | copy-start | bytes 772
  38.3 7.4 %copy-start.12 = (pred[256]{0:T(512)(128)(4,1)S(1)}, pred[256]{0:T(512)(128)(4,1)}, u32[]{:S(2)}) copy-start(pred[256]{0:T(512)(128)(4,1)} %get-tuple-element.17) | copy-start | bytes 772
  38.3 7.4 %copy-start.13 = (pred[256]{0:T(512)(128)(4,1)S(1)}, pred[256]{0:T(512)(128)(4,1)}, u32[]{:S(2)}) copy-start(pred[256]{0:T(512)(128)(4,1)} %get-tuple-element.18) | copy-start | bytes 772
  38.3 7.4 %copy-start.14 = (pred[256]{0:T(512)(128)(4,1)S(1)}, pred[256]{0:T(512)(128)(4,1)}, u32[]{:S(2)}) copy-start(pred[256]{0:T(512)(128)(4,1)} %get-tuple-element.19) | copy-start | bytes 772
  40.3 5.7 %copy-start.7 = (f32[128,1,128]{0,2,1:T(8,128)S(1)}, f32[128,1,128]{0,2,1:T(8,128)}, u32[]{:S(2)}) copy-start(f32[128,1,128]{0,2,1:T(8,128)} %copy.41) | copy-start | bytes 196612
  42.0 0.6 copy-start.6
  68.3 1.0 copy-start.3
  71.6 2.6 %copy-start.1 = (f32[4,256,512]{2,1,0:T(8,128)S(1)}, f32[4,256,512]{2,1,0:T(8,128)}, u32[]{:S(2)}) copy-start(f32[4,256,512]{2,1,0:T(8,128)} %param.25) | copy-start | bytes 6291460
  82.9 17.9 %copy-start.2 = (f32[4,256,512]{2,1,0:T(8,128)S(1)}, f32[4,256,512]{2,1,0:T(8,128)}, u32[]{:S(2)}) copy-start(f32[4,256,512]{2,1,0:T(8,128)} %fusion.17) | copy-start | bytes 6291460
  84.3 14.7 %collective-permute-start.3 = (f32[1,256,512]{2,1,0:T(8,128)S(1)}, f32[1,256,512]{2,1,0:T(8,128)S(1)}, u32[]{:S(2)}, u32[]{:S(2)}) collective-permute-start(f32[1,256,512]{2,1,0:T(8,128)S(1)} %get-tuple-element.12), channel_id=1, source_target_pairs={{0,1},{1,2},{2,3},{3,4},{4,5},{5,6},{6,7},{7,8},{8,9},{9,10},{10,1... | collective-permute-start | bytes 1572872 | tf_op jit(solution)/shard_map/ppermute | solution.py:18
  86.3 14.5 %collective-permute-start.2 = (f32[1,256,512]{2,1,0:T(8,128)S(1)}, f32[1,256,512]{2,1,0:T(8,128)S(1)}, u32[]{:S(2)}, u32[]{:S(2)}) collective-permute-start(f32[1,256,512]{2,1,0:T(8,128)S(1)} %get-tuple-element.13), channel_id=1, source_target_pairs={{1,0},{2,1},{3,2},{4,3},{5,4},{6,5},{7,6},{8,7},{9,8},{10,9},{11,1... | collective-permute-start | bytes 1572872 | tf_op jit(solution)/shard_map/ppermute | solution.py:20

commit v4 on v3

--- a/solution.py
+++ b/solution.py
@@ -95,8 +95,9 @@
     )
     base = both[0]
     first_col = both[1]
-    exit_base = base[:, -1]
-    exit_col = first_col[:, -1]
+    last_row = inverse_blocks[:, -1, :].astype(jnp.float32)
+    exit_base = jnp.sum(last_row * fixed_rhs.astype(jnp.float32), axis=1)
+    exit_col = last_row[:, 0]
     drive0 = drive[:, 0]
     packed = jnp.stack(
         [

time: 112 us -> 104 us (0.929)
  local copies, waits for them, and re-layouts: 16.2 us -> 12.8 us
  matrix products: 9.64 us -> 6.45 us
    unnamed x38 -> x22, local copies, waits for them, and re-layouts: 2.5 us -> 0.08 us
    dot_general x4, matrix products: 2.15 us -> 0.65 us  [on_device(): part = jnp.dot(leak_sent, kernels[k], preferred_element_type=jnp.float32)]
    slice x1, local copies, waits for them, and re-layouts: 1.42 us -> 0.07 us  [padded(): lax.slice_in_dim(cells, cells.shape[dim] - width, cells.shape[dim], axis=...]
    div x1, other arithmetic: 8.8 us -> 10 us  [on_device(): first = (partial + leak_field) / denominator]
  transfers between devices with their start and end apart: 5 -> 5, of which waited for: 2 -> 2; matrix products, arithmetic and copies ran while one was open for 18% -> 17% of each run, Pallas kernels for 0% -> 0%
where the time goes in v4:
time: 104 us; the launch traced here: 103 us
  other arithmetic  31.3 us (30%)
  starting transfers between devices  30.2 us (29%)
  blocking collectives  15 us (14%)
  local copies, waits for them, and re-layouts  12.8 us (12%)
  waiting for transfers between devices  6.5 us (6%)
  matrix products  6.45 us (6%)
  between operations  1.11 us (1%)
    ppermute x2, starting transfers between devices, padded(): lax.ppermute(head, axis, [((i + 1) % count, i) for i in range(ends)])  15.8 us
    all_to_all x1, blocking collectives, on_device(): lax.all_to_all(send.reshape(devices, (capacity + 1) * seg), AXES, 0, 0, t...  15 us
    all_to_all x1, starting transfers between devices, on_device(): got = lax.all_to_all(sent, AXES, 0, 0, tiled=True)  10.4 us
    div x1, other arithmetic, on_device(): first = (partial + leak_field) / denominator  10 us
    div x1, other arithmetic, relax(): return numerator / denominator  8.41 us
    ppermute x2, waiting for transfers between devices, padded(): lax.ppermute(tail, axis, [(i, (i + 1) % count) for i in range(ends)])  4.74 us
    concatenate x2, other arithmetic, padded(): jnp.concatenate([lax.ppermute(tail, axis, [(i, (i + 1) % count) for i in...  4.48 us
    dot_general x1, matrix products, on_device(): jnp.einsum('bij,cbj->cbi', inverse_blocks, jnp.stack([fixed_rhs, unit]),...  4.43 us
  transfers between devices with their start and end apart: 5, of which 2 were waited for; matrix products, arithmetic and copies ran while one was open for 17% of the time, Pallas kernels for 0%

profile of v4, /device:TPU:8, one launch (start us, length us, event | category | flops | bytes accessed | tf_op | source)
XLA Modules:
  0.0 103.3 jit_solution(3726560301166070979)
XLA Ops:
  0.6 0.9 slice_reduce_fusion.2
  1.6 1.0 slice_reduce_fusion.1
  2.6 0.7 and_select_fusion.4
  3.4 1.0 slice.184
  4.4 0.9 multiply_reduce_fusion
  5.4 0.1 slice_reduce_fusion
  5.5 0.7 stack.32
  6.2 1.0 broadcast_in_dim.121
  7.1 10.4 %all-to-all-start = ((f32[128,1,768]{2,1,0:T(1,128)}), f32[128,1,768]{2,1,0:T(1,128)S(1)}, u32[]{:S(2)}, u32[]{:S(2)}) async-start(f32[128,1,768]{2,1,0:T(1,128)} %broadcast_in_dim.121), calls=%async_computation | async-start | bytes 786432 | tf_op jit(solution)/shard_map/all_to_all | solution.py:113
  17.6 0.0 copy-start.2
  17.6 0.0 copy-start.10
  17.6 0.0 copy-start.8
  17.6 0.0 copy-start.9
  17.6 3.1 %pad_maximum_fusion.7 = (f32[2,1,256,512]{3,2,1,0:T(8,128)}, f32[2,1,256,512]{3,2,1,0:T(8,128)}) fusion(f32[1,4,256,512]{3,2,1,0:T(8,128)} %bitcast.145, f32[1,4,256,512]{3,2,1,0:T(8,128)} %bitcast.149), kind=kLoop, calls=%fused_computation.83 | loop fusion | flops 524288 | bytes 6291456 | tf_op jit(solution)/shard_map/stack | solution.py:167
  20.7 2.0 %collective-permute-start.1 = (f32[2,1,256,512]{3,2,1,0:T(8,128)}, f32[2,1,256,512]{3,2,1,0:T(8,128)S(1)}, u32[]{:S(2)}, u32[]{:S(2)}) collective-permute-start(f32[2,1,256,512]{3,2,1,0:T(8,128)} %get-tuple-element.10), channel_id=1, source_target_pairs={{0,1},{1,2},{2,3},{3,4},{4,5},{5,6},{6,7},{7,8},{8,9},{9,10},{10,1... | collective-permute-start | bytes 3145736 | tf_op jit(solution)/shard_map/ppermute | solution.py:18
  22.7 7.8 %collective-permute-start = (f32[2,1,256,512]{3,2,1,0:T(8,128)}, f32[2,1,256,512]{3,2,1,0:T(8,128)}, u32[]{:S(2)}, u32[]{:S(2)}) collective-permute-start(f32[2,1,256,512]{3,2,1,0:T(8,128)} %get-tuple-element.11), channel_id=1, source_target_pairs={{1,0},{2,1},{3,2},{4,3},{5,4},{6,5},{7,6},{8,7},{9,8},{10,9},{11,1... | collective-permute-start | bytes 3145736 | tf_op jit(solution)/shard_map/ppermute | solution.py:20
  30.5 0.0 copy-done.2
  30.5 0.2 convert_reduce_fusion
  30.7 0.1 select_reduce_fusion.1
  30.9 0.1 copy.41
  31.0 0.1 convert_element_type.131
  31.1 0.1 copy.46
  31.3 4.4 %convolution_bitcast_fusion = f32[2,128,128]{2,0,1:T(2,128)S(1)} fusion(bf16[128,128,128]{2,1,0:T(8,128)(2,1)} %param.18, bf16[1,128,128]{2,0,1:T(2,128)(2,1)S(1)} %stack_broadcast_in_dim.2, bf16[1,128,128]{2,0,1:T(2,128)(2,1)S(1)} %copy.41), kind=kOutput, calls=%fused_computation.77 | convolution fusion | flops 8519680 | bytes 4390912 | tf_op jit(solution)/shard_map/bij,cbj->cbi/dot_general | solution.py:90
  35.7 0.0 copy-start.4
  35.7 0.1 fusion.81
  35.9 0.0 all-to-all-done
  35.9 0.4 copy.54
  36.3 0.4 fusion.40
  36.7 0.4 fusion.41
  37.2 0.4 fusion.42
  37.6 0.0 copy-done.7
  37.6 0.1 multiply_add_fusion
  37.7 0.0 copy-done.5
  37.7 0.0 copy-done.6
  37.7 0.0 copy-start.3
  37.7 0.2 convolution_convert_fusion
  37.9 0.0 copy-done.4
  37.9 0.1 fusion.61
  38.1 0.1 fusion.63
  38.2 0.1 fusion.65
  38.4 0.2 fusion.45
  38.6 0.1 copy.45
  38.7 0.2 copy.47
  38.9 15.0 %all_to_all.18 = f32[128,1,384]{2,1,0:T(1,128)S(1)} all-to-all(f32[128,1,384]{2,1,0:T(1,128)S(1)} %copy.47), channel_id=1, replica_groups=mesh['grp'=4,'slab'=32] {'grp','slab'}, dimensions={0} | all-to-all | bytes 393216 | tf_op jit(solution)/shard_map/all_to_all | solution.py:158
  53.9 0.2 copy.48
  54.1 0.1 copy.50
  54.2 0.1 copy.49
  54.3 0.1 reshape.235
  54.4 3.0 %scatter_custom_fusion = f32[4096,128]{1,0:T(8,128)} fusion(s32[256]{0:T(256)S(1)} %reshape.235, f32[256,128]{1,0:T(8,128)S(1)} %bitcast.162, f32[]{:T(128)} %constant.59.clone.1), kind=kCustom, calls=%fused_computation.85 | custom fusion | flops 32768 | bytes 2097156 | tf_op jit(solution)/shard_map/scatter-add | solution.py:164
  57.5 0.0 copy-done.3
  57.5 2.9 %reshape.227 = f32[4,256,512]{2,1,0:T(8,128)} reshape(f32[4096,128]{1,0:T(8,128)} %scatter_custom_fusion) | data formatting | bytes 4194304 | tf_op jit(solution)/shard_map/reshape | solution.py:165
  60.4 0.0 collective-permute-done.1
  60.4 0.0 collective-permute-done
  60.4 2.2 %pad_maximum_fusion = f32[2,6,256,512]{3,2,1,0:T(8,128)S(1)} fusion(f32[2,1,256,512]{3,2,1,0:T(8,128)} %collective-permute-done, f32[1,4,256,512]{3,2,1,0:T(8,128)S(1)} %bitcast.146, f32[1,4,256,512]{3,2,1,0:T(8,128)} %bitcast.150, f32[2,1,256,512]{3,2,1,0:T(8,128)S(1)} %collective-permute-done.1), kind=kLoop, calls=%fused_computation.1 | loop fusion | flops 4718592 | bytes 12582912 | tf_op jit(solution)/shard_map/concatenate | solution.py:16
  62.6 0.0 copy-start.1
  62.6 3.4 %slice_bitcast_fusion.1 = (f32[6,256,512]{2,1,0:T(8,128)}, f32[6,256,512]{2,1,0:T(8,128)}) fusion(f32[2,6,256,512]{3,2,1,0:T(8,128)S(1)} %pad_maximum_fusion), kind=kLoop, calls=%fused_computation.20 | loop fusion | bytes 12582912 | tf_op jit(solution)/shard_map/squeeze | solution.py:169
  66.0 10.0 %fusion.17 = f32[4,256,512]{2,1,0:T(8,128)S(1)} fusion(f32[4,256,512]{2,1,0:T(8,128)} %reshape.227, f32[6,256,512]{2,1,0:T(8,128)} %get-tuple-element.9, f32[2,1,256,512]{3,2,1,0:T(8,128)S(1)} %collective-permute-done.1, f32[1,4,256,512]{3,2,1,0:T(8,128)S(1)} %bitcast.147, f32[1,4,256,512]{3,2,1,0:T(8,128)S(1)} %bitcast.151, f32[4,256,512]{2,1,0:T(8,128)} %param.27, ...), kind=kLoop, calls=%fused_computation.35 | loop fusion | flops 20971520 | bytes 20971520 | tf_op jit(solution)/shard_map/div | solution.py:171
  76.1 0.1 fusion.80
  76.1 1.9 %collective-permute-start.3 = (f32[1,256,512]{2,1,0:T(8,128)S(1)}, f32[1,256,512]{2,1,0:T(8,128)S(1)}, u32[]{:S(2)}, u32[]{:S(2)}) collective-permute-start(f32[1,256,512]{2,1,0:T(8,128)S(1)} %get-tuple-element.12), channel_id=1, source_target_pairs={{0,1},{1,2},{2,3},{3,4},{4,5},{5,6},{6,7},{7,8},{8,9},{9,10},{10,1... | collective-permute-start | bytes 1572872 | tf_op jit(solution)/shard_map/ppermute | solution.py:18
  78.1 8.0 %collective-permute-start.2 = (f32[1,256,512]{2,1,0:T(8,128)S(1)}, f32[1,256,512]{2,1,0:T(8,128)S(1)}, u32[]{:S(2)}, u32[]{:S(2)}) collective-permute-start(f32[1,256,512]{2,1,0:T(8,128)S(1)} %get-tuple-element.13), channel_id=1, source_target_pairs={{1,0},{2,1},{3,2},{4,3},{5,4},{6,5},{7,6},{8,7},{9,8},{10,9},{11,1... | collective-permute-start | bytes 1572872 | tf_op jit(solution)/shard_map/ppermute | solution.py:20
  86.1 4.7 %collective-permute-done.3 = f32[1,256,512]{2,1,0:T(8,128)S(1)} collective-permute-done((f32[1,256,512]{2,1,0:T(8,128)S(1)}, f32[1,256,512]{2,1,0:T(8,128)S(1)}, u32[]{:S(2)}, u32[]{:S(2)}) %collective-permute-start.3) | collective-permute-done | bytes 524320 | tf_op jit(solution)/shard_map/ppermute | solution.py:18
  90.9 1.8 %collective-permute-done.2 = f32[1,256,512]{2,1,0:T(8,128)S(1)} collective-permute-done((f32[1,256,512]{2,1,0:T(8,128)S(1)}, f32[1,256,512]{2,1,0:T(8,128)S(1)}, u32[]{:S(2)}, u32[]{:S(2)}) %collective-permute-start.2) | collective-permute-done | bytes 524320 | tf_op jit(solution)/shard_map/ppermute | solution.py:20
  92.6 2.3 %select_maximum_fusion = f32[6,258,514]{2,1,0:T(8,128)S(1)} fusion(f32[1,256,512]{2,1,0:T(8,128)S(1)} %collective-permute-done.2, f32[4,256,512]{2,1,0:T(8,128)S(1)} %fusion.17, f32[1,256,512]{2,1,0:T(8,128)S(1)} %collective-permute-done.3), kind=kLoop, calls=%fused_computation.14 | loop fusion | flops 11935080 | bytes 6328416 | tf_op jit(solution)/shard_map/concatenate | solution.py:16
  94.9 8.4 %fusion.22 = f32[4,256,512]{2,1,0:T(8,128)} fusion(f32[6,258,514]{2,1,0:T(8,128)S(1)} %select_maximum_fusion, f32[4,256,512]{2,1,0:T(8,128)S(1)} %fusion.17, f32[1,256,512]{2,1,0:T(8,128)S(1)} %collective-permute-done.3, f32[1,256,512]{2,1,0:T(8,128)S(1)} %collective-permute-done.2, f32[4,256,512]{2,1,0:T(8,128)} %param.27, f32[4,256,512]{2,1,0:T(8,128)} %reshape.227, ...), kind=kLoop, calls=%fused_computation.41 | loop fusion | flops 19922944 | bytes 29360128 | tf_op jit(solution)/shard_map/div | solution.py:46
  (29 shorter events, 0.2 us)
Async XLA Ops:
  7.1 28.8 %all-to-all-start = ((f32[128,1,768]{2,1,0:T(1,128)}), f32[128,1,768]{2,1,0:T(1,128)S(1)}, u32[]{:S(2)}, u32[]{:S(2)}) async-start(f32[128,1,768]{2,1,0:T(1,128)} %broadcast_in_dim.121), calls=%async_computation | async-start | bytes 786432 | tf_op jit(solution)/shard_map/all_to_all | solution.py:113
  17.6 12.9 %copy-start.2 = (f32[128,128]{1,0:T(8,128)S(1)}, f32[128,128]{1,0:T(8,128)}, u32[]{:S(2)}) copy-start(f32[128,128]{1,0:T(8,128)} %param.15) | copy-start | bytes 196612
  17.6 12.9 %copy-start.10 = (s32[128,1]{0,1:T(1,128)S(1)}, s32[128,1]{0,1:T(1,128)}, u32[]{:S(2)}) copy-start(s32[128,1]{0,1:T(1,128)} %param.21) | copy-start | bytes 1540
  17.6 13.1 %copy-start.8 = (s32[128]{0:T(128)S(1)}, s32[128]{0:T(128)}, u32[]{:S(2)}) copy-start(s32[128]{0:T(128)} %param.23) | copy-start | bytes 1540
  17.6 13.1 %copy-start.9 = (s32[128]{0:T(128)S(1)}, s32[128]{0:T(128)}, u32[]{:S(2)}) copy-start(s32[128]{0:T(128)} %param.22) | copy-start | bytes 1540
  20.7 39.7 %collective-permute-start.1 = (f32[2,1,256,512]{3,2,1,0:T(8,128)}, f32[2,1,256,512]{3,2,1,0:T(8,128)S(1)}, u32[]{:S(2)}, u32[]{:S(2)}) collective-permute-start(f32[2,1,256,512]{3,2,1,0:T(8,128)} %get-tuple-element.10), channel_id=1, source_target_pairs={{0,1},{1,2},{2,3},{3,4},{4,5},{5,6},{6,7},{7,8},{8,9},{9,10},{10,1... | collective-permute-start | bytes 3145736 | tf_op jit(solution)/shard_map/ppermute | solution.py:18
  22.7 37.7 %collective-permute-start = (f32[2,1,256,512]{3,2,1,0:T(8,128)}, f32[2,1,256,512]{3,2,1,0:T(8,128)}, u32[]{:S(2)}, u32[]{:S(2)}) collective-permute-start(f32[2,1,256,512]{3,2,1,0:T(8,128)} %get-tuple-element.11), channel_id=1, source_target_pairs={{1,0},{2,1},{3,2},{4,3},{5,4},{6,5},{7,6},{8,7},{9,8},{10,9},{11,1... | collective-permute-start | bytes 3145736 | tf_op jit(solution)/shard_map/ppermute | solution.py:20
  35.7 1.9 %copy-start.7 = (f32[128]{0:T(128)S(1)}, f32[128]{0:T(128)}, u32[]{:S(2)}) copy-start(f32[128]{0:T(128)} %param.16) | copy-start | bytes 1540
  35.7 2.0 %copy-start.5 = (f32[128,128]{1,0:T(8,128)S(1)}, f32[128,128]{1,0:T(8,128)}, u32[]{:S(2)}) copy-start(f32[128,128]{1,0:T(8,128)} %param.19) | copy-start | bytes 196612
  35.7 2.0 %copy-start.6 = (f32[128,128]{1,0:T(8,128)S(1)}, f32[128,128]{1,0:T(8,128)}, u32[]{:S(2)}) copy-start(f32[128,128]{1,0:T(8,128)} %param.20) | copy-start | bytes 196612
  35.7 2.2 %copy-start.4 = (bf16[4,128,128]{2,1,0:T(8,128)(2,1)S(1)}, bf16[4,128,128]{2,1,0:T(8,128)(2,1)}, u32[]{:S(2)}) copy-start(bf16[4,128,128]{2,1,0:T(8,128)(2,1)} %param.24) | copy-start | bytes 393220
  37.7 19.7 %copy-start.3 = (f32[128,128]{1,0:T(8,128)}, f32[128,128]{1,0:T(8,128)S(1)}, u32[]{:S(2)}) copy-start(f32[128,128]{1,0:T(8,128)S(1)} %multiply_add_fusion) | copy-start | bytes 196612
  57.5 2.9 %copy-start = (f32[4,256,512]{2,1,0:T(8,128)S(1)}, f32[4,256,512]{2,1,0:T(8,128)}, u32[]{:S(2)}) copy-start(f32[4,256,512]{2,1,0:T(8,128)} %param.26) | copy-start | bytes 6291460
  62.6 3.4 %copy-start.1 = (f32[4,256,512]{2,1,0:T(8,128)S(1)}, f32[4,256,512]{2,1,0:T(8,128)}, u32[]{:S(2)}) copy-start(f32[4,256,512]{2,1,0:T(8,128)} %param.25) | copy-start | bytes 6291460
  76.1 14.7 %collective-permute-start.3 = (f32[1,256,512]{2,1,0:T(8,128)S(1)}, f32[1,256,512]{2,1,0:T(8,128)S(1)}, u32[]{:S(2)}, u32[]{:S(2)}) collective-permute-start(f32[1,256,512]{2,1,0:T(8,128)S(1)} %get-tuple-element.12), channel_id=1, source_target_pairs={{0,1},{1,2},{2,3},{3,4},{4,5},{5,6},{6,7},{7,8},{8,9},{9,10},{10,1... | collective-permute-start | bytes 1572872 | tf_op jit(solution)/shard_map/ppermute | solution.py:18
  78.1 14.5 %collective-permute-start.2 = (f32[1,256,512]{2,1,0:T(8,128)S(1)}, f32[1,256,512]{2,1,0:T(8,128)S(1)}, u32[]{:S(2)}, u32[]{:S(2)}) collective-permute-start(f32[1,256,512]{2,1,0:T(8,128)S(1)} %get-tuple-element.13), channel_id=1, source_target_pairs={{1,0},{2,1},{3,2},{4,3},{5,4},{6,5},{7,6},{8,7},{9,8},{10,9},{11,1... | collective-permute-start | bytes 1572872 | tf_op jit(solution)/shard_map/ppermute | solution.py:20

commit v5 on v4

--- a/solution.py
+++ b/solution.py
@@ -65,7 +65,7 @@
     return x.astype(jnp.bfloat16).astype(jnp.float32)
 
 
-def on_device(
+def on_device_body(
     vessel_start,
     drive,
     junction_gain,
@@ -149,17 +149,12 @@
     for k in range(kernels.shape[0]):
         part = jnp.dot(leak_sent, kernels[k], preferred_element_type=jnp.float32)
         cells = jnp.where((kid_sent == k)[:, None], part, cells)
-    tgt_row = jnp.pad(
-        tgt_sent.astype(jnp.float32).reshape(devices, capacity), ((0, 0), (0, seg - capacity))
-    )
-    send = jnp.concatenate(
-        [cells.reshape(devices, capacity, seg), tgt_row[:, None, :]], axis=1
-    )
-    recv = lax.all_to_all(
-        send.reshape(devices, (capacity + 1) * seg), AXES, 0, 0, tiled=True
-    ).reshape(devices, capacity + 1, seg)
-    got_rows = recv[:, :capacity, :].reshape(slots, seg)
-    got_index = recv[:, capacity, :capacity].reshape(slots).astype(jnp.int32)
+    got_rows = lax.all_to_all(
+        cells.reshape(devices, capacity, seg), AXES, 0, 0, tiled=True
+    ).reshape(slots, seg)
+    got_index = lax.all_to_all(
+        tgt_sent.astype(jnp.float32).reshape(devices, 1, capacity), AXES, 0, 0, tiled=True
+    ).reshape(slots).astype(jnp.int32)
     cell_blocks = tissue_start.size // seg
     leakage = jax.ops.segment_sum(got_rows, got_index, num_segments=cell_blocks)
     leak_field = leakage.reshape(base_source.shape)
@@ -167,7 +162,9 @@
     stacked = jnp.stack([tissue_start, conduct])
     wide = padded(stacked, ((AXES, 1),), 1)
     padded_k = pad_sides(wide[1])
-    partial, denominator = relax_parts(pad_sides(wide[0]), padded_k, base_source)
+    partial, denominator = lax.optimization_barrier(
+        relax_parts(pad_sides(wide[0]), padded_k, base_source)
+    )
     first = (partial + leak_field) / denominator
     second = padded(first, ((AXES, 0),), 1)
     tissue = relax(pad_sides(second), padded_k, source)
@@ -193,5 +190,5 @@
     )
     out_specs = (P(AXES, None), P(AXES, None, None))
     return jax.shard_map(
-        on_device, mesh=mesh, in_specs=in_specs, out_specs=out_specs, check_vma=False
+        on_device_body, mesh=mesh, in_specs=in_specs, out_specs=out_specs, check_vma=False
     )

time: 104 us -> 122 us (1.17)
  waiting for transfers between devices: 6.5 us -> 32.6 us
  blocking collectives: 15 us -> 0 us
  starting transfers between devices: 30.2 us -> 36 us
  other arithmetic: 31.3 us -> 35 us
  local copies, waits for them, and re-layouts: 12.8 us -> 9.32 us
    all_to_all x1 -> x3, waiting for transfers between devices: 0.01 us -> 19.8 us  [the longest x1 8.64 us: on_device_body(): lax.all_to_all(cells.reshape(devices, capacity, seg), AXES, 0, 0, tiled=T...]
    all_to_all x1 -> x0, blocking collectives: 15 us -> none  [on_device(): lax.all_to_all(send.reshape(devices, (capacity + 1) * seg), AXES, 0, 0, t...]
    add x2 -> x4, other arithmetic: 0.09 us -> 13.7 us  [the longest x1 9.23 us: relax_parts(): numerator = numerator + facing * p_side]
    all_to_all x1 -> x3, starting transfers between devices: 10.4 us -> 20.9 us  [the longest x1 10 us: on_device_body(): got = lax.all_to_all(sent, AXES, 0, 0, tiled=True)]
    div x1, other arithmetic: 10 us -> 2.97 us  [on_device_body(): first = (partial + leak_field) / denominator]
    ppermute x2, starting transfers between devices: 15.8 us -> 11.3 us  [padded(): lax.ppermute(head, axis, [((i + 1) % count, i) for i in range(ends)])]
    ppermute x2, waiting for transfers between devices: 4.74 us -> 8.04 us  [padded(): lax.ppermute(tail, axis, [(i, (i + 1) % count) for i in range(ends)])]
    ppermute x2, waiting for transfers between devices: 1.76 us -> 4.75 us  [padded(): lax.ppermute(head, axis, [((i + 1) % count, i) for i in range(ends)])]
  transfers between devices with their start and end apart: 5 -> 7, of which waited for: 2 -> 5; matrix products, arithmetic and copies ran while one was open for 17% -> 15% of each run, Pallas kernels for 0% -> 0%
where the time goes in v5:
time: 122 us; the launch traced here: 121 us
  starting transfers between devices  36 us (30%)
  other arithmetic  35 us (29%)
  waiting for transfers between devices  32.6 us (27%)
  local copies, waits for them, and re-layouts  9.32 us (8%)
  matrix products  7.11 us (6%)
    ppermute x2, starting transfers between devices, padded(): lax.ppermute(head, axis, [((i + 1) % count, i) for i in range(ends)])  11.3 us
    all_to_all x1, starting transfers between devices, on_device_body(): got = lax.all_to_all(sent, AXES, 0, 0, tiled=True)  10 us
    add x1, other arithmetic, relax_parts(): numerator = numerator + facing * p_side  9.23 us
    all_to_all x1, waiting for transfers between devices, on_device_body(): lax.all_to_all(cells.reshape(devices, capacity, seg), AXES, 0, 0, tiled=T...  8.64 us
    ppermute x2, waiting for transfers between devices, padded(): lax.ppermute(tail, axis, [(i, (i + 1) % count) for i in range(ends)])  8.04 us
    div x1, other arithmetic, relax(): return numerator / denominator  6.97 us
    all_to_all x1, starting transfers between devices, on_device_body(): lax.all_to_all(tgt_sent.astype(jnp.float32).reshape(devices, 1, capacity)...  5.66 us
    all_to_all x1, waiting for transfers between devices, on_device_body(): lax.all_to_all(tgt_sent.astype(jnp.float32).reshape(devices, 1, capacity)...  5.65 us
  transfers between devices with their start and end apart: 7, of which 5 were waited for; matrix products, arithmetic and copies ran while one was open for 15% of the time, Pallas kernels for 0%

profile of v5, /device:TPU:8, one launch (start us, length us, event | category | flops | bytes accessed | tf_op | source)
XLA Modules:
  0.0 121.2 jit_solution(6984086006932011164)
XLA Ops:
  0.6 0.0 copy-start.4
  0.6 0.0 copy-start.13
  0.7 0.0 copy-start.7
  0.7 0.0 copy-start.10
  0.7 0.0 copy-start.14
  0.7 0.0 copy-start.11
  0.7 0.0 copy-start.12
  0.7 3.1 %pad_maximum_fusion.7 = (f32[2,1,256,512]{3,2,1,0:T(8,128)}, f32[2,1,256,512]{3,2,1,0:T(8,128)}) fusion(f32[1,4,256,512]{3,2,1,0:T(8,128)} %bitcast.134, f32[1,4,256,512]{3,2,1,0:T(8,128)} %bitcast.138), kind=kLoop, calls=%fused_computation.82 | loop fusion | flops 524288 | bytes 6291456 | tf_op jit(solution)/shard_map/stack | solution.py:162
  3.8 7.5 %collective-permute-start = (f32[2,1,256,512]{3,2,1,0:T(8,128)}, f32[2,1,256,512]{3,2,1,0:T(8,128)S(1)}, u32[]{:S(2)}, u32[]{:S(2)}) collective-permute-start(f32[2,1,256,512]{3,2,1,0:T(8,128)} %get-tuple-element.18), channel_id=1, source_target_pairs={{1,0},{2,1},{3,2},{4,3},{5,4},{6,5},{7,6},{8,7},{9,8},{10,9},{11,1... | collective-permute-start | bytes 3145736 | tf_op jit(solution)/shard_map/ppermute | solution.py:20
  11.3 1.9 %collective-permute-start.1 = (f32[2,1,256,512]{3,2,1,0:T(8,128)}, f32[2,1,256,512]{3,2,1,0:T(8,128)}, u32[]{:S(2)}, u32[]{:S(2)}) collective-permute-start(f32[2,1,256,512]{3,2,1,0:T(8,128)} %get-tuple-element.17), channel_id=1, source_target_pairs={{0,1},{1,2},{2,3},{3,4},{4,5},{5,6},{6,7},{7,8},{8,9},{9,10},{10,1... | collective-permute-start | bytes 3145736 | tf_op jit(solution)/shard_map/ppermute | solution.py:18
  13.2 1.0 slice.178
  14.3 0.0 copy-done.4
  14.3 0.1 slice_reduce_fusion.2
  14.4 0.1 multiply_reduce_fusion
  14.5 0.0 copy-done.13
  14.5 0.1 slice_reduce_fusion
  14.6 0.0 copy-done.7
  14.6 0.2 slice_reduce_fusion.1
  14.8 1.0 broadcast_in_dim.118
  15.8 10.0 %all-to-all-start = ((f32[128,1,768]{2,1,0:T(1,128)}), f32[128,1,768]{2,1,0:T(1,128)S(1)}, u32[]{:S(2)}, u32[]{:S(2)}) async-start(f32[128,1,768]{2,1,0:T(1,128)} %broadcast_in_dim.118), calls=%async_computation | async-start | bytes 786432 | tf_op jit(solution)/shard_map/all_to_all | solution.py:113
  25.9 0.1 copy.26
  25.9 0.0 copy-done.14
  25.9 0.2 convert_reduce_fusion.1
  26.2 0.1 select_reduce_fusion
  26.3 0.8 convert_element_type.133
  27.1 4.4 %convolution_bitcast_fusion = f32[2,128,128]{2,0,1:T(2,128)S(1)} fusion(bf16[128,128,128]{2,1,0:T(8,128)(2,1)} %param.18, bf16[1,128,128]{2,0,1:T(2,128)(2,1)S(1)} %stack_broadcast_in_dim.2, bf16[1,128,128]{2,0,1:T(2,128)(2,1)S(1)} %copy.26), kind=kOutput, calls=%fused_computation.76 | convolution fusion | flops 8519680 | bytes 4390912 | tf_op jit(solution)/shard_map/bij,cbj->cbi/dot_general | solution.py:90
  31.6 0.1 fusion.81
  31.7 5.6 %all-to-all-done = f32[128,1,768]{2,1,0:T(1,128)S(1)} async-done(((f32[128,1,768]{2,1,0:T(1,128)}), f32[128,1,768]{2,1,0:T(1,128)S(1)}, u32[]{:S(2)}, u32[]{:S(2)}) %all-to-all-start) | async-done | bytes 393248 | tf_op jit(solution)/shard_map/all_to_all | solution.py:113
  37.3 5.7 %all-to-all-start.1 = ((f32[128,1,2]{2,1,0:T(1,128)}), f32[128,1,2]{2,1,0:T(1,128)S(1)}, u32[]{:S(2)}, u32[]{:S(2)}) async-start(f32[128,1,2]{2,1,0:T(1,128)} %bitcast.22), calls=%async_computation.1 | async-start | bytes 131072 | tf_op jit(solution)/shard_map/all_to_all | solution.py:155
  42.9 0.4 copy.34
  43.3 0.4 fusion.38
  43.8 0.4 fusion.39
  44.3 0.4 fusion.40
  44.7 0.1 multiply_add_fusion
  44.8 0.0 copy-start.5
  44.8 0.2 convolution_convert_fusion
  45.0 0.0 copy-done.6
  45.0 0.1 fusion.59
  45.1 0.1 fusion.61
  45.3 0.1 fusion.63
  45.4 0.9 fusion.43
  46.3 5.6 %all-to-all-done.1 = f32[128,1,2]{2,1,0:T(1,128)S(1)} async-done(((f32[128,1,2]{2,1,0:T(1,128)}), f32[128,1,2]{2,1,0:T(1,128)S(1)}, u32[]{:S(2)}, u32[]{:S(2)}) %all-to-all-start.1) | async-done | bytes 1056 | tf_op jit(solution)/shard_map/all_to_all | solution.py:155
  51.9 5.2 %all-to-all-start.2 = ((f32[128,2,128]{2,1,0:T(2,128)}), f32[128,2,128]{2,1,0:T(2,128)S(1)}, u32[]{:S(2)}, u32[]{:S(2)}) async-start(f32[128,2,128]{2,1,0:T(2,128)} %bitcast.27), calls=%async_computation.2 | async-start | bytes 262144 | tf_op jit(solution)/shard_map/all_to_all | solution.py:152
  57.1 0.2 convert_reduce_fusion
  57.3 0.1 reshape.236
  57.5 8.6 %all-to-all-done.2 = f32[128,2,128]{2,1,0:T(2,128)S(1)} async-done(((f32[128,2,128]{2,1,0:T(2,128)}), f32[128,2,128]{2,1,0:T(2,128)S(1)}, u32[]{:S(2)}, u32[]{:S(2)}) %all-to-all-start.2) | async-done | bytes 131104 | tf_op jit(solution)/shard_map/all_to_all | solution.py:152
  66.1 3.0 %scatter_custom_fusion = f32[4096,128]{1,0:T(8,128)} fusion(s32[256]{0:T(256)S(1)} %reshape.236, f32[256,128]{1,0:T(8,128)S(1)} %bitcast.147, f32[]{:T(128)} %constant.59.clone.1), kind=kCustom, calls=%fused_computation.84 | custom fusion | flops 32768 | bytes 2097156 | tf_op jit(solution)/shard_map/scatter-add | solution.py:159
  69.1 2.9 %reshape.228 = f32[4,256,512]{2,1,0:T(8,128)} reshape(f32[4096,128]{1,0:T(8,128)} %scatter_custom_fusion) | data formatting | bytes 4194304 | tf_op jit(solution)/shard_map/reshape | solution.py:160
  72.1 0.0 collective-permute-done
  72.1 0.0 collective-permute-done.1
  72.1 2.2 %pad_maximum_fusion = f32[2,6,256,512]{3,2,1,0:T(8,128)S(1)} fusion(f32[2,1,256,512]{3,2,1,0:T(8,128)S(1)} %collective-permute-done, f32[1,4,256,512]{3,2,1,0:T(8,128)S(1)} %bitcast.135, f32[1,4,256,512]{3,2,1,0:T(8,128)} %bitcast.139, f32[2,1,256,512]{3,2,1,0:T(8,128)} %collective-permute-done.1), kind=kLoop, calls=%fused_computation.1 | loop fusion | flops 4718592 | bytes 12582912 | tf_op jit(solution)/shard_map/concatenate | solution.py:16
  74.3 0.0 copy-start.1
  74.3 2.4 %slice_bitcast_fusion.1 = (f32[6,256,512]{2,1,0:T(8,128)S(1)}, f32[6,256,512]{2,1,0:T(8,128)}) fusion(f32[2,6,256,512]{3,2,1,0:T(8,128)S(1)} %pad_maximum_fusion), kind=kLoop, calls=%fused_computation.20 | loop fusion | bytes 12582912 | tf_op jit(solution)/shard_map/squeeze | solution.py:164
  76.7 0.0 copy-done.1
  76.7 4.4 %add_add_fusion = (f32[4,256,512]{2,1,0:T(8,128)}, f32[4,256,512]{2,1,0:T(8,128)S(1)}, f32[4,256,512]{2,1,0:T(8,128)}) fusion(f32[4,256,512]{2,1,0:T(8,128)S(1)} %copy-done, f32[6,256,512]{2,1,0:T(8,128)S(1)} %get-tuple-element.15, f32[2,1,256,512]{3,2,1,0:T(8,128)S(1)} %collective-permute-done, f32[1,4,256,512]{3,2,1,0:T(8,128)S(1)} %bitcast.136, ...), kind=kLoop, calls=%fused_computation.69 | loop fusion | flops 11534336 | bytes 17825792 | tf_op jit(solution)/shard_map/add | solution.py:56
  81.1 9.2 %fusion.15 = f32[4,256,512]{2,1,0:T(8,128)} fusion(f32[6,256,512]{2,1,0:T(8,128)} %get-tuple-element.16, f32[4,256,512]{2,1,0:T(8,128)} %get-tuple-element.10, f32[2,1,256,512]{3,2,1,0:T(8,128)} %collective-permute-done.1, f32[1,4,256,512]{3,2,1,0:T(8,128)S(1)} %bitcast.137, f32[1,4,256,512]{3,2,1,0:T(8,128)S(1)} %bitcast.141, f32[4,256,512]{2,1,0:T(8,128)} %param.27, ...), kind=kLoop, calls=%fused_computation.33 | loop fusion | flops 12582912 | bytes 23068672 | tf_op jit(solution)/shard_map/add | solution.py:55
  90.3 3.0 %add_divide_fusion = f32[4,256,512]{2,1,0:T(8,128)S(1)} fusion(f32[4,256,512]{2,1,0:T(8,128)} %get-tuple-element.5, f32[4,256,512]{2,1,0:T(8,128)} %fusion.15, f32[4,256,512]{2,1,0:T(8,128)S(1)} %copy-done.2), kind=kLoop, calls=%fused_computation.68 | loop fusion | flops 1048576 | bytes 8388608 | tf_op jit(solution)/shard_map/div | solution.py:168
  93.3 0.1 fusion.80
  93.4 3.9 %collective-permute-start.2 = (f32[1,256,512]{2,1,0:T(8,128)S(1)}, f32[1,256,512]{2,1,0:T(8,128)S(1)}, u32[]{:S(2)}, u32[]{:S(2)}) collective-permute-start(f32[1,256,512]{2,1,0:T(8,128)S(1)} %get-tuple-element.20), channel_id=1, source_target_pairs={{1,0},{2,1},{3,2},{4,3},{5,4},{6,5},{7,6},{8,7},{9,8},{10,9},{11,1... | collective-permute-start | bytes 1572872 | tf_op jit(solution)/shard_map/ppermute | solution.py:20
  97.3 1.9 %collective-permute-start.3 = (f32[1,256,512]{2,1,0:T(8,128)S(1)}, f32[1,256,512]{2,1,0:T(8,128)S(1)}, u32[]{:S(2)}, u32[]{:S(2)}) collective-permute-start(f32[1,256,512]{2,1,0:T(8,128)S(1)} %get-tuple-element.19), channel_id=1, source_target_pairs={{0,1},{1,2},{2,3},{3,4},{4,5},{5,6},{6,7},{7,8},{8,9},{9,10},{10,1... | collective-permute-start | bytes 1572872 | tf_op jit(solution)/shard_map/ppermute | solution.py:18
  99.2 4.7 %collective-permute-done.2 = f32[1,256,512]{2,1,0:T(8,128)S(1)} collective-permute-done((f32[1,256,512]{2,1,0:T(8,128)S(1)}, f32[1,256,512]{2,1,0:T(8,128)S(1)}, u32[]{:S(2)}, u32[]{:S(2)}) %collective-permute-start.2) | collective-permute-done | bytes 524320 | tf_op jit(solution)/shard_map/ppermute | solution.py:20
  104.0 8.0 %collective-permute-done.3 = f32[1,256,512]{2,1,0:T(8,128)S(1)} collective-permute-done((f32[1,256,512]{2,1,0:T(8,128)S(1)}, f32[1,256,512]{2,1,0:T(8,128)S(1)}, u32[]{:S(2)}, u32[]{:S(2)}) %collective-permute-start.3) | collective-permute-done | bytes 524320 | tf_op jit(solution)/shard_map/ppermute | solution.py:18
  112.0 2.3 %select_maximum_fusion = f32[6,258,514]{2,1,0:T(8,128)S(1)} fusion(f32[1,256,512]{2,1,0:T(8,128)S(1)} %collective-permute-done.2, f32[4,256,512]{2,1,0:T(8,128)S(1)} %add_divide_fusion, f32[1,256,512]{2,1,0:T(8,128)S(1)} %collective-permute-done.3), kind=kLoop, calls=%fused_computation.14 | loop fusion | flops 11935080 | bytes 6328416 | tf_op jit(solution)/shard_map/concatenate | solution.py:16
  114.3 7.0 %fusion.20 = f32[4,256,512]{2,1,0:T(8,128)} fusion(f32[6,258,514]{2,1,0:T(8,128)S(1)} %select_maximum_fusion, f32[4,256,512]{2,1,0:T(8,128)} %get-tuple-element.10, f32[4,256,512]{2,1,0:T(8,128)S(1)} %add_divide_fusion, f32[1,256,512]{2,1,0:T(8,128)S(1)} %collective-permute-done.3, f32[4,256,512]{2,1,0:T(8,128)} %copy-done.3, ...), kind=kLoop, calls=%fused_computation.39 | loop fusion | flops 15728640 | bytes 27262976 | tf_op jit(solution)/shard_map/div | solution.py:46
  (33 shorter events, 0.3 us)
Async XLA Ops:
  0.6 13.6 %copy-start.4 = (f32[128,128]{1,0:T(8,128)S(1)}, f32[128,128]{1,0:T(8,128)}, u32[]{:S(2)}) copy-start(f32[128,128]{1,0:T(8,128)} %param.15) | copy-start | bytes 196612
  0.6 13.8 %copy-start.13 = (s32[128]{0:T(128)S(1)}, s32[128]{0:T(128)}, u32[]{:S(2)}) copy-start(s32[128]{0:T(128)} %param.17) | copy-start | bytes 1540
  0.7 14.0 %copy-start.7 = (f32[128,128]{1,0:T(8,128)S(1)}, f32[128,128]{1,0:T(8,128)}, u32[]{:S(2)}) copy-start(f32[128,128]{1,0:T(8,128)} %param.14) | copy-start | bytes 196612
  0.7 14.2 %copy-start.10 = (f32[128]{0:T(128)S(1)}, f32[128]{0:T(128)}, u32[]{:S(2)}) copy-start(f32[128]{0:T(128)} %param.16) | copy-start | bytes 1540
  0.7 25.3 %copy-start.14 = (s32[128,1]{0,1:T(1,128)S(1)}, s32[128,1]{0,1:T(1,128)}, u32[]{:S(2)}) copy-start(s32[128,1]{0,1:T(1,128)} %param.21) | copy-start | bytes 1540
  0.7 25.5 %copy-start.11 = (s32[128]{0:T(128)S(1)}, s32[128]{0:T(128)}, u32[]{:S(2)}) copy-start(s32[128]{0:T(128)} %param.23) | copy-start | bytes 1540
  0.7 25.5 %copy-start.12 = (s32[128]{0:T(128)S(1)}, s32[128]{0:T(128)}, u32[]{:S(2)}) copy-start(s32[128]{0:T(128)} %param.22) | copy-start | bytes 1540
  3.8 68.3 %collective-permute-start = (f32[2,1,256,512]{3,2,1,0:T(8,128)}, f32[2,1,256,512]{3,2,1,0:T(8,128)S(1)}, u32[]{:S(2)}, u32[]{:S(2)}) collective-permute-start(f32[2,1,256,512]{3,2,1,0:T(8,128)} %get-tuple-element.18), channel_id=1, source_target_pairs={{1,0},{2,1},{3,2},{4,3},{5,4},{6,5},{7,6},{8,7},{9,8},{10,9},{11,1... | collective-permute-start | bytes 3145736 | tf_op jit(solution)/shard_map/ppermute | solution.py:20
  11.3 60.8 %collective-permute-start.1 = (f32[2,1,256,512]{3,2,1,0:T(8,128)}, f32[2,1,256,512]{3,2,1,0:T(8,128)}, u32[]{:S(2)}, u32[]{:S(2)}) collective-permute-start(f32[2,1,256,512]{3,2,1,0:T(8,128)} %get-tuple-element.17), channel_id=1, source_target_pairs={{0,1},{1,2},{2,3},{3,4},{4,5},{5,6},{6,7},{7,8},{8,9},{9,10},{10,1... | collective-permute-start | bytes 3145736 | tf_op jit(solution)/shard_map/ppermute | solution.py:18
  15.8 21.5 %all-to-all-start = ((f32[128,1,768]{2,1,0:T(1,128)}), f32[128,1,768]{2,1,0:T(1,128)S(1)}, u32[]{:S(2)}, u32[]{:S(2)}) async-start(f32[128,1,768]{2,1,0:T(1,128)} %broadcast_in_dim.118), calls=%async_computation | async-start | bytes 786432 | tf_op jit(solution)/shard_map/all_to_all | solution.py:113
  31.5 13.2 %copy-start.8 = (f32[128,128]{1,0:T(8,128)S(1)}, f32[128,128]{1,0:T(8,128)}, u32[]{:S(2)}) copy-start(f32[128,128]{1,0:T(8,128)} %param.19) | copy-start | bytes 196612
  31.5 13.2 %copy-start.9 = (f32[128,128]{1,0:T(8,128)S(1)}, f32[128,128]{1,0:T(8,128)}, u32[]{:S(2)}) copy-start(f32[128,128]{1,0:T(8,128)} %param.20) | copy-start | bytes 196612
  31.5 13.4 %copy-start.6 = (bf16[4,128,128]{2,1,0:T(8,128)(2,1)S(1)}, bf16[4,128,128]{2,1,0:T(8,128)(2,1)}, u32[]{:S(2)}) copy-start(bf16[4,128,128]{2,1,0:T(8,128)(2,1)} %param.24) | copy-start | bytes 393220
  37.3 14.7 %all-to-all-start.1 = ((f32[128,1,2]{2,1,0:T(1,128)}), f32[128,1,2]{2,1,0:T(1,128)S(1)}, u32[]{:S(2)}, u32[]{:S(2)}) async-start(f32[128,1,2]{2,1,0:T(1,128)} %bitcast.22), calls=%async_computation.1 | async-start | bytes 131072 | tf_op jit(solution)/shard_map/all_to_all | solution.py:155
  44.8 27.3 %copy-start.5 = (f32[128,128]{1,0:T(8,128)}, f32[128,128]{1,0:T(8,128)S(1)}, u32[]{:S(2)}) copy-start(f32[128,128]{1,0:T(8,128)S(1)} %multiply_add_fusion) | copy-start | bytes 196612
  51.9 14.2 %all-to-all-start.2 = ((f32[128,2,128]{2,1,0:T(2,128)}), f32[128,2,128]{2,1,0:T(2,128)S(1)}, u32[]{:S(2)}, u32[]{:S(2)}) async-start(f32[128,2,128]{2,1,0:T(2,128)} %bitcast.27), calls=%async_computation.2 | async-start | bytes 262144 | tf_op jit(solution)/shard_map/all_to_all | solution.py:152
  69.1 2.9 %copy-start = (f32[4,256,512]{2,1,0:T(8,128)S(1)}, f32[4,256,512]{2,1,0:T(8,128)}, u32[]{:S(2)}) copy-start(f32[4,256,512]{2,1,0:T(8,128)} %param.26) | copy-start | bytes 6291460
  74.3 2.4 %copy-start.1 = (f32[4,256,512]{2,1,0:T(8,128)S(1)}, f32[4,256,512]{2,1,0:T(8,128)}, u32[]{:S(2)}) copy-start(f32[4,256,512]{2,1,0:T(8,128)} %param.25) | copy-start | bytes 6291460
  81.1 9.2 %copy-start.3 = (f32[4,256,512]{2,1,0:T(8,128)}, f32[4,256,512]{2,1,0:T(8,128)S(1)}, u32[]{:S(2)}) copy-start(f32[4,256,512]{2,1,0:T(8,128)S(1)} %get-tuple-element.9) | copy-start | bytes 6291460
  81.1 9.2 %copy-start.2 = (f32[4,256,512]{2,1,0:T(8,128)S(1)}, f32[4,256,512]{2,1,0:T(8,128)}, u32[]{:S(2)}) copy-start(f32[4,256,512]{2,1,0:T(8,128)} %reshape.228) | copy-start | bytes 6291460
  93.4 10.6 %collective-permute-start.2 = (f32[1,256,512]{2,1,0:T(8,128)S(1)}, f32[1,256,512]{2,1,0:T(8,128)S(1)}, u32[]{:S(2)}, u32[]{:S(2)}) collective-permute-start(f32[1,256,512]{2,1,0:T(8,128)S(1)} %get-tuple-element.20), channel_id=1, source_target_pairs={{1,0},{2,1},{3,2},{4,3},{5,4},{6,5},{7,6},{8,7},{9,8},{10,9},{11,1... | collective-permute-start | bytes 1572872 | tf_op jit(solution)/shard_map/ppermute | solution.py:20
  97.3 14.7 %collective-permute-start.3 = (f32[1,256,512]{2,1,0:T(8,128)S(1)}, f32[1,256,512]{2,1,0:T(8,128)S(1)}, u32[]{:S(2)}, u32[]{:S(2)}) collective-permute-start(f32[1,256,512]{2,1,0:T(8,128)S(1)} %get-tuple-element.19), channel_id=1, source_target_pairs={{0,1},{1,2},{2,3},{3,4},{4,5},{5,6},{6,7},{7,8},{8,9},{9,10},{10,1... | collective-permute-start | bytes 1572872 | tf_op jit(solution)/shard_map/ppermute | solution.py:18

commit v6 on v5

--- a/solution.py
+++ b/solution.py
@@ -99,6 +99,16 @@
     exit_base = jnp.sum(last_row * fixed_rhs.astype(jnp.float32), axis=1)
     exit_col = last_row[:, 0]
     drive0 = drive[:, 0]
+    destination = owner[:, 0]
+    same = destination[:, None] == destination[None, :]
+    earlier = jnp.arange(nb)[None, :] < jnp.arange(nb)[:, None]
+    slot = jnp.sum((same & earlier).astype(jnp.int32), axis=1)
+    capacity = 2
+    row_of = destination * capacity + slot
+    slots = devices * capacity
+    onehot = row_of[None, :] == jnp.arange(slots, dtype=jnp.int32)[:, None]
+    kid_sent = jnp.sum(jnp.where(onehot, kernel_id[None, :], 0), axis=1)
+    tgt_sent = jnp.sum(jnp.where(onehot, target[None, :], 0), axis=1)
     packed = jnp.stack(
         [
             exit_base,
@@ -109,8 +119,16 @@
             parent.astype(jnp.float32),
         ]
     ).reshape(1, 6 * nb)
-    sent = jnp.broadcast_to(packed, (devices, 6 * nb))
-    got = lax.all_to_all(sent, AXES, 0, 0, tiled=True)
+    tgt_row = jnp.pad(
+        tgt_sent.astype(jnp.float32).reshape(devices, capacity),
+        ((0, 0), (0, seg - capacity)),
+    )
+    sent = jnp.concatenate(
+        [jnp.broadcast_to(packed, (devices, 6 * nb)), tgt_row], axis=1
+    )
+    got_all = lax.all_to_all(sent, AXES, 0, 0, tiled=True)
+    got = got_all[:, : 6 * nb]
+    got_index = got_all[:, 6 * nb : 6 * nb + capacity].reshape(slots).astype(jnp.int32)
     owners = jnp.arange(devices, dtype=jnp.int32)[None, :]
     within = jnp.arange(nb, dtype=jnp.int32)[None, :]
 
@@ -132,19 +150,9 @@
     r0 = bf16_round(drive0 + junction_gain * exit2)
     pressure = base + first_col * r0[:, None]
     leak = (wall_perm * (pressure - outside)).astype(jnp.bfloat16)
-    destination = owner[:, 0]
-    same = destination[:, None] == destination[None, :]
-    earlier = jnp.arange(nb)[None, :] < jnp.arange(nb)[:, None]
-    slot = jnp.sum((same & earlier).astype(jnp.int32), axis=1)
-    capacity = 2
-    row_of = destination * capacity + slot
-    slots = devices * capacity
-    onehot = row_of[None, :] == jnp.arange(slots, dtype=jnp.int32)[:, None]
     leak_sent = jnp.dot(
         onehot.astype(jnp.bfloat16), leak, preferred_element_type=jnp.float32
     ).astype(jnp.bfloat16)
-    kid_sent = jnp.sum(jnp.where(onehot, kernel_id[None, :], 0), axis=1)
-    tgt_sent = jnp.sum(jnp.where(onehot, target[None, :], 0), axis=1)
     cells = jnp.zeros((slots, seg), jnp.float32)
     for k in range(kernels.shape[0]):
         part = jnp.dot(leak_sent, kernels[k], preferred_element_type=jnp.float32)
@@ -152,9 +160,6 @@
     got_rows = lax.all_to_all(
         cells.reshape(devices, capacity, seg), AXES, 0, 0, tiled=True
     ).reshape(slots, seg)
-    got_index = lax.all_to_all(
-        tgt_sent.astype(jnp.float32).reshape(devices, 1, capacity), AXES, 0, 0, tiled=True
-    ).reshape(slots).astype(jnp.int32)
     cell_blocks = tissue_start.size // seg
     leakage = jax.ops.segment_sum(got_rows, got_index, num_segments=cell_blocks)
     leak_field = leakage.reshape(base_source.shape)

time: 122 us -> 112 us (0.918)
  starting transfers between devices: 36 us -> 30.6 us
  waiting for transfers between devices: 32.6 us -> 29 us
    all_to_all x2 -> x1, starting transfers between devices: 15.7 us -> 10 us  [on_device_body(): got_all = lax.all_to_all(sent, AXES, 0, 0, tiled=True)]
    all_to_all x2 -> x1, waiting for transfers between devices: 11.2 us -> 7.38 us  [on_device_body(): got_all = lax.all_to_all(sent, AXES, 0, 0, tiled=True)]
  transfers between devices with their start and end apart: 7 -> 6, of which waited for: 5 -> 4; matrix products, arithmetic and copies ran while one was open for 15% -> 15% of each run, Pallas kernels for 0% -> 0%
where the time goes in v6:
time: 112 us
  other arithmetic  35 us (31%)
  starting transfers between devices  30.6 us (27%)
  waiting for transfers between devices  29 us (26%)
  local copies, waits for them, and re-layouts  8.47 us (8%)
  matrix products  7.49 us (7%)
  between operations  1.15 us (1%)
    ppermute x2, starting transfers between devices, padded(): lax.ppermute(head, axis, [((i + 1) % count, i) for i in range(ends)])  11.3 us
    all_to_all x1, starting transfers between devices, on_device_body(): got_all = lax.all_to_all(sent, AXES, 0, 0, tiled=True)  10 us
    add x1, other arithmetic, relax_parts(): numerator = numerator + facing * p_side  9.22 us
    all_to_all x1, waiting for transfers between devices, on_device_body(): lax.all_to_all(cells.reshape(devices, capacity, seg), AXES, 0, 0, tiled=T...  8.82 us
    ppermute x2, waiting for transfers between devices, padded(): lax.ppermute(tail, axis, [(i, (i + 1) % count) for i in range(ends)])  8.04 us
    all_to_all x1, waiting for transfers between devices, on_device_body(): got_all = lax.all_to_all(sent, AXES, 0, 0, tiled=True)  7.38 us
    div x1, other arithmetic, relax(): return numerator / denominator  6.97 us
    all_to_all x1, starting transfers between devices, on_device_body(): lax.all_to_all(cells.reshape(devices, capacity, seg), AXES, 0, 0, tiled=T...  5.42 us
  transfers between devices with their start and end apart: 6, of which 4 were waited for; matrix products, arithmetic and copies ran while one was open for 15% of the time, Pallas kernels for 0%

profile of v6, /device:TPU:8, one launch (start us, length us, event | category | flops | bytes accessed | tf_op | source)
XLA Modules:
  0.0 111.7 jit_solution(5067575033285919735)
XLA Ops:
  0.6 0.0 copy-start.4
  0.6 0.0 copy-start.13
  0.7 0.0 copy-start.7
  0.7 0.0 copy-start.14
  0.7 0.0 copy-start.11
  0.7 0.0 copy-start.12
  0.7 0.0 copy-start.10
  0.7 3.1 %pad_maximum_fusion.7 = (f32[2,1,256,512]{3,2,1,0:T(8,128)}, f32[2,1,256,512]{3,2,1,0:T(8,128)}) fusion(f32[1,4,256,512]{3,2,1,0:T(8,128)} %bitcast.121, f32[1,4,256,512]{3,2,1,0:T(8,128)} %bitcast.125), kind=kLoop, calls=%fused_computation.76 | loop fusion | flops 524288 | bytes 6291456 | tf_op jit(solution)/shard_map/stack | solution.py:167
  3.8 7.5 %collective-permute-start = (f32[2,1,256,512]{3,2,1,0:T(8,128)}, f32[2,1,256,512]{3,2,1,0:T(8,128)S(1)}, u32[]{:S(2)}, u32[]{:S(2)}) collective-permute-start(f32[2,1,256,512]{3,2,1,0:T(8,128)} %get-tuple-element.18), channel_id=1, source_target_pairs={{1,0},{2,1},{3,2},{4,3},{5,4},{6,5},{7,6},{8,7},{9,8},{10,9},{11,1... | collective-permute-start | bytes 3145736 | tf_op jit(solution)/shard_map/ppermute | solution.py:20
  11.3 1.9 %collective-permute-start.1 = (f32[2,1,256,512]{3,2,1,0:T(8,128)}, f32[2,1,256,512]{3,2,1,0:T(8,128)}, u32[]{:S(2)}, u32[]{:S(2)}) collective-permute-start(f32[2,1,256,512]{3,2,1,0:T(8,128)} %get-tuple-element.17), channel_id=1, source_target_pairs={{0,1},{1,2},{2,3},{3,4},{4,5},{5,6},{6,7},{7,8},{8,9},{9,10},{10,1... | collective-permute-start | bytes 3145736 | tf_op jit(solution)/shard_map/ppermute | solution.py:18
  13.2 1.0 slice.184
  14.2 0.0 copy-done.4
  14.3 0.1 slice_reduce_fusion.2
  14.4 0.1 multiply_reduce_fusion
  14.5 0.0 copy-done.13
  14.5 0.1 slice_reduce_fusion
  14.6 0.2 slice_reduce_fusion.1
  14.8 0.0 copy-done.14
  14.8 0.2 convert_reduce_fusion
  15.0 0.0 copy-done.11
  15.0 0.0 copy-done.12
  15.0 0.1 select_reduce_fusion.3
  15.2 0.1 convert_element_type.118
  15.4 1.1 all_to_all.11
  16.5 10.0 %all-to-all-start = ((f32[128,1,896]{2,1,0:T(1,128)}), f32[128,1,896]{2,1,0:T(1,128)S(1)}, u32[]{:S(2)}, u32[]{:S(2)}) async-start(f32[128,1,896]{2,1,0:T(1,128)} %all_to_all.11), calls=%async_computation | async-start | bytes 917504 | tf_op jit(solution)/shard_map/all_to_all | solution.py:129
  26.6 0.1 copy.30
  26.7 4.4 %convolution_bitcast_fusion = f32[2,128,128]{2,0,1:T(2,128)S(1)} fusion(bf16[128,128,128]{2,1,0:T(8,128)(2,1)} %param.18, bf16[1,128,128]{2,0,1:T(2,128)(2,1)S(1)} %stack_broadcast_in_dim.2, bf16[1,128,128]{2,0,1:T(2,128)(2,1)S(1)} %copy.30), kind=kOutput, calls=%fused_computation.70 | convolution fusion | flops 8519680 | bytes 4390912 | tf_op jit(solution)/shard_map/bij,cbj->cbi/dot_general | solution.py:90
  31.2 0.1 fusion.78
  31.3 7.4 %all-to-all-done = f32[128,1,896]{2,1,0:T(1,128)S(1)} async-done(((f32[128,1,896]{2,1,0:T(1,128)}), f32[128,1,896]{2,1,0:T(1,128)S(1)}, u32[]{:S(2)}, u32[]{:S(2)}) %all-to-all-start) | async-done | bytes 458784 | tf_op jit(solution)/shard_map/all_to_all | solution.py:129
  38.7 0.0 copy-start.8
  38.7 0.0 copy-start.9
  38.7 0.0 copy-start.6
  38.7 0.5 fusion.47
  39.3 0.5 fusion.45
  40.0 0.5 fusion.43
  40.6 0.1 multiply_add_fusion
  40.7 0.0 copy-start.5
  40.7 0.2 convolution_convert_fusion
  40.9 0.1 fusion.56
  41.0 0.1 fusion.58
  41.2 0.1 fusion.60
  41.3 0.9 fusion.40
  42.2 5.4 %all-to-all-start.1 = ((f32[128,2,128]{2,1,0:T(2,128)}), f32[128,2,128]{2,1,0:T(2,128)S(1)}, u32[]{:S(2)}, u32[]{:S(2)}) async-start(f32[128,2,128]{2,1,0:T(2,128)} %bitcast.24), calls=%async_computation.1 | async-start | bytes 262144 | tf_op jit(solution)/shard_map/all_to_all | solution.py:160
  47.7 0.1 reshape.228
  47.8 8.8 %all-to-all-done.1 = f32[128,2,128]{2,1,0:T(2,128)S(1)} async-done(((f32[128,2,128]{2,1,0:T(2,128)}), f32[128,2,128]{2,1,0:T(2,128)S(1)}, u32[]{:S(2)}, u32[]{:S(2)}) %all-to-all-start.1) | async-done | bytes 131104 | tf_op jit(solution)/shard_map/all_to_all | solution.py:160
  56.6 3.0 %scatter_custom_fusion = f32[4096,128]{1,0:T(8,128)} fusion(s32[256]{0:T(256)S(1)} %reshape.228, f32[256,128]{1,0:T(8,128)S(1)} %bitcast.138, f32[]{:T(128)} %constant.59.clone.1), kind=kCustom, calls=%fused_computation.78 | custom fusion | flops 32768 | bytes 2097156 | tf_op jit(solution)/shard_map/scatter-add | solution.py:164
  59.6 2.9 %reshape.220 = f32[4,256,512]{2,1,0:T(8,128)} reshape(f32[4096,128]{1,0:T(8,128)} %scatter_custom_fusion) | data formatting | bytes 4194304 | tf_op jit(solution)/shard_map/reshape | solution.py:165
  62.6 0.0 copy-done.5
  62.6 0.0 collective-permute-done
  62.6 0.0 collective-permute-done.1
  62.6 0.0 copy-done
  62.6 2.2 %pad_maximum_fusion = f32[2,6,256,512]{3,2,1,0:T(8,128)S(1)} fusion(f32[2,1,256,512]{3,2,1,0:T(8,128)S(1)} %collective-permute-done, f32[1,4,256,512]{3,2,1,0:T(8,128)S(1)} %bitcast.122, f32[1,4,256,512]{3,2,1,0:T(8,128)} %bitcast.126, f32[2,1,256,512]{3,2,1,0:T(8,128)} %collective-permute-done.1), kind=kLoop, calls=%fused_computation.1 | loop fusion | flops 4718592 | bytes 12582912 | tf_op jit(solution)/shard_map/concatenate | solution.py:16
  64.8 0.0 copy-start.1
  64.8 2.4 %slice_bitcast_fusion.1 = (f32[6,256,512]{2,1,0:T(8,128)S(1)}, f32[6,256,512]{2,1,0:T(8,128)}) fusion(f32[2,6,256,512]{3,2,1,0:T(8,128)S(1)} %pad_maximum_fusion), kind=kLoop, calls=%fused_computation.20 | loop fusion | bytes 12582912 | tf_op jit(solution)/shard_map/squeeze | solution.py:169
  67.2 4.4 %add_add_fusion = (f32[4,256,512]{2,1,0:T(8,128)}, f32[4,256,512]{2,1,0:T(8,128)S(1)}, f32[4,256,512]{2,1,0:T(8,128)}) fusion(f32[4,256,512]{2,1,0:T(8,128)S(1)} %copy-done, f32[6,256,512]{2,1,0:T(8,128)S(1)} %get-tuple-element.15, f32[2,1,256,512]{3,2,1,0:T(8,128)S(1)} %collective-permute-done, f32[1,4,256,512]{3,2,1,0:T(8,128)S(1)} %bitcast.123, ...), kind=kLoop, calls=%fused_computation.69 | loop fusion | flops 11534336 | bytes 17825792 | tf_op jit(solution)/shard_map/add | solution.py:56
  71.6 9.2 %fusion.15 = f32[4,256,512]{2,1,0:T(8,128)} fusion(f32[6,256,512]{2,1,0:T(8,128)} %get-tuple-element.16, f32[4,256,512]{2,1,0:T(8,128)} %get-tuple-element.10, f32[2,1,256,512]{3,2,1,0:T(8,128)} %collective-permute-done.1, f32[1,4,256,512]{3,2,1,0:T(8,128)S(1)} %bitcast.124, f32[1,4,256,512]{3,2,1,0:T(8,128)S(1)} %bitcast.128, f32[4,256,512]{2,1,0:T(8,128)} %param.27, ...), kind=kLoop, calls=%fused_computation.33 | loop fusion | flops 12582912 | bytes 23068672 | tf_op jit(solution)/shard_map/add | solution.py:55
  80.8 3.0 %add_divide_fusion = f32[4,256,512]{2,1,0:T(8,128)S(1)} fusion(f32[4,256,512]{2,1,0:T(8,128)} %get-tuple-element.5, f32[4,256,512]{2,1,0:T(8,128)} %fusion.15, f32[4,256,512]{2,1,0:T(8,128)S(1)} %copy-done.2), kind=kLoop, calls=%fused_computation.68 | loop fusion | flops 1048576 | bytes 8388608 | tf_op jit(solution)/shard_map/div | solution.py:173
  83.8 0.1 fusion.77
  83.9 3.9 %collective-permute-start.2 = (f32[1,256,512]{2,1,0:T(8,128)S(1)}, f32[1,256,512]{2,1,0:T(8,128)S(1)}, u32[]{:S(2)}, u32[]{:S(2)}) collective-permute-start(f32[1,256,512]{2,1,0:T(8,128)S(1)} %get-tuple-element.20), channel_id=1, source_target_pairs={{1,0},{2,1},{3,2},{4,3},{5,4},{6,5},{7,6},{8,7},{9,8},{10,9},{11,1... | collective-permute-start | bytes 1572872 | tf_op jit(solution)/shard_map/ppermute | solution.py:20
  87.8 1.9 %collective-permute-start.3 = (f32[1,256,512]{2,1,0:T(8,128)S(1)}, f32[1,256,512]{2,1,0:T(8,128)S(1)}, u32[]{:S(2)}, u32[]{:S(2)}) collective-permute-start(f32[1,256,512]{2,1,0:T(8,128)S(1)} %get-tuple-element.19), channel_id=1, source_target_pairs={{0,1},{1,2},{2,3},{3,4},{4,5},{5,6},{6,7},{7,8},{8,9},{9,10},{10,1... | collective-permute-start | bytes 1572872 | tf_op jit(solution)/shard_map/ppermute | solution.py:18
  89.7 4.7 %collective-permute-done.2 = f32[1,256,512]{2,1,0:T(8,128)S(1)} collective-permute-done((f32[1,256,512]{2,1,0:T(8,128)S(1)}, f32[1,256,512]{2,1,0:T(8,128)S(1)}, u32[]{:S(2)}, u32[]{:S(2)}) %collective-permute-start.2) | collective-permute-done | bytes 524320 | tf_op jit(solution)/shard_map/ppermute | solution.py:20
  94.5 8.0 %collective-permute-done.3 = f32[1,256,512]{2,1,0:T(8,128)S(1)} collective-permute-done((f32[1,256,512]{2,1,0:T(8,128)S(1)}, f32[1,256,512]{2,1,0:T(8,128)S(1)}, u32[]{:S(2)}, u32[]{:S(2)}) %collective-permute-start.3) | collective-permute-done | bytes 524320 | tf_op jit(solution)/shard_map/ppermute | solution.py:18
  102.5 2.3 %select_maximum_fusion = f32[6,258,514]{2,1,0:T(8,128)S(1)} fusion(f32[1,256,512]{2,1,0:T(8,128)S(1)} %collective-permute-done.2, f32[4,256,512]{2,1,0:T(8,128)S(1)} %add_divide_fusion, f32[1,256,512]{2,1,0:T(8,128)S(1)} %collective-permute-done.3), kind=kLoop, calls=%fused_computation.14 | loop fusion | flops 11935080 | bytes 6328416 | tf_op jit(solution)/shard_map/concatenate | solution.py:16
  104.8 7.0 %fusion.20 = f32[4,256,512]{2,1,0:T(8,128)} fusion(f32[6,258,514]{2,1,0:T(8,128)S(1)} %select_maximum_fusion, f32[4,256,512]{2,1,0:T(8,128)} %get-tuple-element.10, f32[4,256,512]{2,1,0:T(8,128)S(1)} %add_divide_fusion, f32[1,256,512]{2,1,0:T(8,128)S(1)} %collective-permute-done.3, f32[4,256,512]{2,1,0:T(8,128)} %copy-done.3, ...), kind=kLoop, calls=%fused_computation.39 | loop fusion | flops 15728640 | bytes 27262976 | tf_op jit(solution)/shard_map/div | solution.py:46
  (36 shorter events, 0.5 us)
Async XLA Ops:
  0.6 13.6 %copy-start.4 = (f32[128,128]{1,0:T(8,128)S(1)}, f32[128,128]{1,0:T(8,128)}, u32[]{:S(2)}) copy-start(f32[128,128]{1,0:T(8,128)} %param.15) | copy-start | bytes 196612
  0.6 13.8 %copy-start.13 = (s32[128]{0:T(128)S(1)}, s32[128]{0:T(128)}, u32[]{:S(2)}) copy-start(s32[128]{0:T(128)} %param.17) | copy-start | bytes 1540
  0.7 14.0 %copy-start.7 = (f32[128,128]{1,0:T(8,128)S(1)}, f32[128,128]{1,0:T(8,128)}, u32[]{:S(2)}) copy-start(f32[128,128]{1,0:T(8,128)} %param.14) | copy-start | bytes 196612
  0.7 14.1 %copy-start.14 = (s32[128,1]{0,1:T(1,128)S(1)}, s32[128,1]{0,1:T(1,128)}, u32[]{:S(2)}) copy-start(s32[128,1]{0,1:T(1,128)} %param.21) | copy-start | bytes 1540
  0.7 14.3 %copy-start.11 = (s32[128]{0:T(128)S(1)}, s32[128]{0:T(128)}, u32[]{:S(2)}) copy-start(s32[128]{0:T(128)} %param.23) | copy-start | bytes 1540
  0.7 14.3 %copy-start.12 = (s32[128]{0:T(128)S(1)}, s32[128]{0:T(128)}, u32[]{:S(2)}) copy-start(s32[128]{0:T(128)} %param.22) | copy-start | bytes 1540
  0.7 14.6 %copy-start.10 = (f32[128]{0:T(128)S(1)}, f32[128]{0:T(128)}, u32[]{:S(2)}) copy-start(f32[128]{0:T(128)} %param.16) | copy-start | bytes 1540
  3.8 58.8 %collective-permute-start = (f32[2,1,256,512]{3,2,1,0:T(8,128)}, f32[2,1,256,512]{3,2,1,0:T(8,128)S(1)}, u32[]{:S(2)}, u32[]{:S(2)}) collective-permute-start(f32[2,1,256,512]{3,2,1,0:T(8,128)} %get-tuple-element.18), channel_id=1, source_target_pairs={{1,0},{2,1},{3,2},{4,3},{5,4},{6,5},{7,6},{8,7},{9,8},{10,9},{11,1... | collective-permute-start | bytes 3145736 | tf_op jit(solution)/shard_map/ppermute | solution.py:20
  11.3 51.3 %collective-permute-start.1 = (f32[2,1,256,512]{3,2,1,0:T(8,128)}, f32[2,1,256,512]{3,2,1,0:T(8,128)}, u32[]{:S(2)}, u32[]{:S(2)}) collective-permute-start(f32[2,1,256,512]{3,2,1,0:T(8,128)} %get-tuple-element.17), channel_id=1, source_target_pairs={{0,1},{1,2},{2,3},{3,4},{4,5},{5,6},{6,7},{7,8},{8,9},{9,10},{10,1... | collective-permute-start | bytes 3145736 | tf_op jit(solution)/shard_map/ppermute | solution.py:18
  16.5 22.1 %all-to-all-start = ((f32[128,1,896]{2,1,0:T(1,128)}), f32[128,1,896]{2,1,0:T(1,128)S(1)}, u32[]{:S(2)}, u32[]{:S(2)}) async-start(f32[128,1,896]{2,1,0:T(1,128)} %all_to_all.11), calls=%async_computation | async-start | bytes 917504 | tf_op jit(solution)/shard_map/all_to_all | solution.py:129
  38.7 2.0 %copy-start.8 = (f32[128,128]{1,0:T(8,128)S(1)}, f32[128,128]{1,0:T(8,128)}, u32[]{:S(2)}) copy-start(f32[128,128]{1,0:T(8,128)} %param.19) | copy-start | bytes 196612
  38.7 2.0 %copy-start.9 = (f32[128,128]{1,0:T(8,128)S(1)}, f32[128,128]{1,0:T(8,128)}, u32[]{:S(2)}) copy-start(f32[128,128]{1,0:T(8,128)} %param.20) | copy-start | bytes 196612
  38.7 2.2 %copy-start.6 = (bf16[4,128,128]{2,1,0:T(8,128)(2,1)S(1)}, bf16[4,128,128]{2,1,0:T(8,128)(2,1)}, u32[]{:S(2)}) copy-start(bf16[4,128,128]{2,1,0:T(8,128)(2,1)} %param.24) | copy-start | bytes 393220
  40.7 21.9 %copy-start.5 = (f32[128,128]{1,0:T(8,128)}, f32[128,128]{1,0:T(8,128)S(1)}, u32[]{:S(2)}) copy-start(f32[128,128]{1,0:T(8,128)S(1)} %multiply_add_fusion) | copy-start | bytes 196612
  42.2 14.4 %all-to-all-start.1 = ((f32[128,2,128]{2,1,0:T(2,128)}), f32[128,2,128]{2,1,0:T(2,128)S(1)}, u32[]{:S(2)}, u32[]{:S(2)}) async-start(f32[128,2,128]{2,1,0:T(2,128)} %bitcast.24), calls=%async_computation.1 | async-start | bytes 262144 | tf_op jit(solution)/shard_map/all_to_all | solution.py:160
  59.6 2.9 %copy-start = (f32[4,256,512]{2,1,0:T(8,128)S(1)}, f32[4,256,512]{2,1,0:T(8,128)}, u32[]{:S(2)}) copy-start(f32[4,256,512]{2,1,0:T(8,128)} %param.26) | copy-start | bytes 6291460
  64.8 2.4 %copy-start.1 = (f32[4,256,512]{2,1,0:T(8,128)S(1)}, f32[4,256,512]{2,1,0:T(8,128)}, u32[]{:S(2)}) copy-start(f32[4,256,512]{2,1,0:T(8,128)} %param.25) | copy-start | bytes 6291460
  71.6 9.2 %copy-start.3 = (f32[4,256,512]{2,1,0:T(8,128)}, f32[4,256,512]{2,1,0:T(8,128)S(1)}, u32[]{:S(2)}) copy-start(f32[4,256,512]{2,1,0:T(8,128)S(1)} %get-tuple-element.9) | copy-start | bytes 6291460
  71.6 9.2 %copy-start.2 = (f32[4,256,512]{2,1,0:T(8,128)S(1)}, f32[4,256,512]{2,1,0:T(8,128)}, u32[]{:S(2)}) copy-start(f32[4,256,512]{2,1,0:T(8,128)} %reshape.220) | copy-start | bytes 6291460
  83.9 10.6 %collective-permute-start.2 = (f32[1,256,512]{2,1,0:T(8,128)S(1)}, f32[1,256,512]{2,1,0:T(8,128)S(1)}, u32[]{:S(2)}, u32[]{:S(2)}) collective-permute-start(f32[1,256,512]{2,1,0:T(8,128)S(1)} %get-tuple-element.20), channel_id=1, source_target_pairs={{1,0},{2,1},{3,2},{4,3},{5,4},{6,5},{7,6},{8,7},{9,8},{10,9},{11,1... | collective-permute-start | bytes 1572872 | tf_op jit(solution)/shard_map/ppermute | solution.py:20
  87.8 14.7 %collective-permute-start.3 = (f32[1,256,512]{2,1,0:T(8,128)S(1)}, f32[1,256,512]{2,1,0:T(8,128)S(1)}, u32[]{:S(2)}, u32[]{:S(2)}) collective-permute-start(f32[1,256,512]{2,1,0:T(8,128)S(1)} %get-tuple-element.19), channel_id=1, source_target_pairs={{0,1},{1,2},{2,3},{3,4},{4,5},{5,6},{6,7},{7,8},{8,9},{9,10},{10,1... | collective-permute-start | bytes 1572872 | tf_op jit(solution)/shard_map/ppermute | solution.py:18

commit v7 on v5

--- a/solution.py
+++ b/solution.py
@@ -149,12 +149,14 @@
     for k in range(kernels.shape[0]):
         part = jnp.dot(leak_sent, kernels[k], preferred_element_type=jnp.float32)
         cells = jnp.where((kid_sent == k)[:, None], part, cells)
-    got_rows = lax.all_to_all(
-        cells.reshape(devices, capacity, seg), AXES, 0, 0, tiled=True
-    ).reshape(slots, seg)
-    got_index = lax.all_to_all(
-        tgt_sent.astype(jnp.float32).reshape(devices, 1, capacity), AXES, 0, 0, tiled=True
-    ).reshape(slots).astype(jnp.int32)
+    tgt_row = jnp.pad(
+        tgt_sent.astype(jnp.float32).reshape(devices, 1, capacity),
+        ((0, 0), (0, capacity - 1), (0, seg - capacity)),
+    )
+    send = jnp.concatenate([cells.reshape(devices, capacity, seg), tgt_row], axis=1)
+    recv = lax.all_to_all(send, AXES, 0, 0, tiled=True)
+    got_rows = recv[:, :capacity, :].reshape(slots, seg)
+    got_index = recv[:, capacity, :capacity].reshape(slots).astype(jnp.int32)
     cell_blocks = tissue_start.size // seg
     leakage = jax.ops.segment_sum(got_rows, got_index, num_segments=cell_blocks)
     leak_field = leakage.reshape(base_source.shape)

time: 122 us -> 111 us (0.910)
  blocking collectives: 0 us -> 15.4 us
  waiting for transfers between devices: 32.6 us -> 19 us
  starting transfers between devices: 36 us -> 25.1 us
    all_to_all x0 -> x1, blocking collectives: none -> 15.4 us  [on_device_body(): recv = lax.all_to_all(send, AXES, 0, 0, tiled=True)]
    all_to_all x2 -> x0, waiting for transfers between devices: 14.3 us -> none  [the longest x1 8.64 us: on_device_body(): lax.all_to_all(cells.reshape(devices, capacity, seg), AXES, 0, 0, tiled=T...]
    all_to_all x2 -> x0, starting transfers between devices: 10.8 us -> none  [the longest x1 5.66 us: on_device_body(): lax.all_to_all(tgt_sent.astype(jnp.float32).reshape(devices, 1, capacity)...]
  transfers between devices with their start and end apart: 7 -> 5, of which waited for: 5 -> 3; matrix products, arithmetic and copies ran while one was open for 15% -> 15% of each run, Pallas kernels for 0% -> 0%
where the time goes in v7:
time: 111 us
  other arithmetic  35.1 us (32%)
  starting transfers between devices  25.1 us (23%)
  waiting for transfers between devices  19 us (17%)
  blocking collectives  15.4 us (14%)
  local copies, waits for them, and re-layouts  8.92 us (8%)
  matrix products  6.45 us (6%)
  between operations  1.12 us (1%)
    all_to_all x1, blocking collectives, on_device_body(): recv = lax.all_to_all(send, AXES, 0, 0, tiled=True)  15.4 us
    ppermute x2, starting transfers between devices, padded(): lax.ppermute(head, axis, [((i + 1) % count, i) for i in range(ends)])  11.3 us
    all_to_all x1, starting transfers between devices, on_device_body(): got = lax.all_to_all(sent, AXES, 0, 0, tiled=True)  10 us
    add x1, other arithmetic, relax_parts(): numerator = numerator + facing * p_side  9.23 us
    ppermute x2, waiting for transfers between devices, padded(): lax.ppermute(tail, axis, [(i, (i + 1) % count) for i in range(ends)])  8.04 us
    div x1, other arithmetic, relax(): return numerator / denominator  6.97 us
    all_to_all x1, waiting for transfers between devices, on_device_body(): got = lax.all_to_all(sent, AXES, 0, 0, tiled=True)  6.17 us
    ppermute x2, waiting for transfers between devices, padded(): lax.ppermute(head, axis, [((i + 1) % count, i) for i in range(ends)])  4.75 us
  transfers between devices with their start and end apart: 5, of which 3 were waited for; matrix products, arithmetic and copies ran while one was open for 15% of the time, Pallas kernels for 0%

profile of v7, /device:TPU:8, one launch (start us, length us, event | category | flops | bytes accessed | tf_op | source)
XLA Modules:
  0.0 111.1 jit_solution(11936214908323589139)
XLA Ops:
  0.6 0.0 copy-start.4
  0.6 0.0 copy-start.13
  0.7 0.0 copy-start.7
  0.7 0.0 copy-start.10
  0.7 0.0 copy-start.14
  0.7 0.0 copy-start.11
  0.7 0.0 copy-start.12
  0.7 3.1 %pad_maximum_fusion.7 = (f32[2,1,256,512]{3,2,1,0:T(8,128)}, f32[2,1,256,512]{3,2,1,0:T(8,128)}) fusion(f32[1,4,256,512]{3,2,1,0:T(8,128)} %bitcast.133, f32[1,4,256,512]{3,2,1,0:T(8,128)} %bitcast.137), kind=kLoop, calls=%fused_computation.82 | loop fusion | flops 524288 | bytes 6291456 | tf_op jit(solution)/shard_map/stack | solution.py:164
  3.8 7.5 %collective-permute-start = (f32[2,1,256,512]{3,2,1,0:T(8,128)}, f32[2,1,256,512]{3,2,1,0:T(8,128)S(1)}, u32[]{:S(2)}, u32[]{:S(2)}) collective-permute-start(f32[2,1,256,512]{3,2,1,0:T(8,128)} %get-tuple-element.18), channel_id=1, source_target_pairs={{1,0},{2,1},{3,2},{4,3},{5,4},{6,5},{7,6},{8,7},{9,8},{10,9},{11,1... | collective-permute-start | bytes 3145736 | tf_op jit(solution)/shard_map/ppermute | solution.py:20
  11.3 1.9 %collective-permute-start.1 = (f32[2,1,256,512]{3,2,1,0:T(8,128)}, f32[2,1,256,512]{3,2,1,0:T(8,128)}, u32[]{:S(2)}, u32[]{:S(2)}) collective-permute-start(f32[2,1,256,512]{3,2,1,0:T(8,128)} %get-tuple-element.17), channel_id=1, source_target_pairs={{0,1},{1,2},{2,3},{3,4},{4,5},{5,6},{6,7},{7,8},{8,9},{9,10},{10,1... | collective-permute-start | bytes 3145736 | tf_op jit(solution)/shard_map/ppermute | solution.py:18
  13.2 1.0 slice.184
  14.3 0.0 copy-done.4
  14.3 0.1 slice_reduce_fusion.2
  14.4 0.1 multiply_reduce_fusion
  14.5 0.0 copy-done.13
  14.5 0.1 slice_reduce_fusion
  14.6 0.0 copy-done.7
  14.6 0.2 slice_reduce_fusion.1
  14.8 0.0 copy-done.10
  14.8 1.0 broadcast_in_dim.118
  15.8 10.0 %all-to-all-start = ((f32[128,1,768]{2,1,0:T(1,128)}), f32[128,1,768]{2,1,0:T(1,128)S(1)}, u32[]{:S(2)}, u32[]{:S(2)}) async-start(f32[128,1,768]{2,1,0:T(1,128)} %broadcast_in_dim.118), calls=%async_computation | async-start | bytes 786432 | tf_op jit(solution)/shard_map/all_to_all | solution.py:113
  25.9 0.1 copy.33
  25.9 0.0 copy-done.14
  25.9 0.2 convert_reduce_fusion
  26.1 0.0 copy-done.11
  26.2 0.1 select_reduce_fusion.1
  26.3 0.1 convert_element_type.137
  26.5 4.4 %convolution_bitcast_fusion = f32[2,128,128]{2,0,1:T(2,128)S(1)} fusion(bf16[128,128,128]{2,1,0:T(8,128)(2,1)} %param.18, bf16[1,128,128]{2,0,1:T(2,128)(2,1)S(1)} %stack_broadcast_in_dim.2, bf16[1,128,128]{2,0,1:T(2,128)(2,1)S(1)} %copy.33), kind=kOutput, calls=%fused_computation.76 | convolution fusion | flops 8519680 | bytes 4390912 | tf_op jit(solution)/shard_map/bij,cbj->cbi/dot_general | solution.py:90
  31.0 0.1 fusion.82
  31.1 6.2 %all-to-all-done = f32[128,1,768]{2,1,0:T(1,128)S(1)} async-done(((f32[128,1,768]{2,1,0:T(1,128)}), f32[128,1,768]{2,1,0:T(1,128)S(1)}, u32[]{:S(2)}, u32[]{:S(2)}) %all-to-all-start) | async-done | bytes 393248 | tf_op jit(solution)/shard_map/all_to_all | solution.py:113
  37.3 0.4 copy.42
  37.7 0.4 fusion.38
  38.1 0.4 fusion.39
  38.6 0.4 fusion.40
  39.0 0.1 multiply_add_fusion
  39.1 0.0 copy-start.5
  39.1 0.2 convolution_convert_fusion
  39.3 0.1 fusion.60
  39.4 0.1 fusion.62
  39.6 0.1 fusion.64
  39.7 0.2 fusion.43
  40.0 0.2 copy.38
  40.2 15.4 %all_to_all.14 = f32[128,4,128]{2,1,0:T(4,128)S(1)} all-to-all(f32[128,4,128]{2,1,0:T(4,128)S(1)} %copy.38), channel_id=1, replica_groups=mesh['grp'=4,'slab'=32] {'grp','slab'}, dimensions={0} | all-to-all | bytes 524288 | tf_op jit(solution)/shard_map/all_to_all | solution.py:157
  55.6 0.2 fusion.46
  55.9 0.1 reshape.235
  56.1 3.0 %scatter_custom_fusion = f32[4096,128]{1,0:T(8,128)} fusion(s32[256]{0:T(256)S(1)} %reshape.235, f32[256,128]{1,0:T(8,128)S(1)} %bitcast.147, f32[]{:T(128)} %constant.59.clone.1), kind=kCustom, calls=%fused_computation.84 | custom fusion | flops 32768 | bytes 2097156 | tf_op jit(solution)/shard_map/scatter-add | solution.py:161
  59.1 2.9 %reshape.227 = f32[4,256,512]{2,1,0:T(8,128)} reshape(f32[4096,128]{1,0:T(8,128)} %scatter_custom_fusion) | data formatting | bytes 4194304 | tf_op jit(solution)/shard_map/reshape | solution.py:162
  62.0 0.0 collective-permute-done
  62.0 0.0 collective-permute-done.1
  62.0 0.0 copy-done
  62.0 2.2 %pad_maximum_fusion = f32[2,6,256,512]{3,2,1,0:T(8,128)S(1)} fusion(f32[2,1,256,512]{3,2,1,0:T(8,128)S(1)} %collective-permute-done, f32[1,4,256,512]{3,2,1,0:T(8,128)S(1)} %bitcast.134, f32[1,4,256,512]{3,2,1,0:T(8,128)} %bitcast.138, f32[2,1,256,512]{3,2,1,0:T(8,128)} %collective-permute-done.1), kind=kLoop, calls=%fused_computation.1 | loop fusion | flops 4718592 | bytes 12582912 | tf_op jit(solution)/shard_map/concatenate | solution.py:16
  64.2 0.0 copy-start.1
  64.2 2.4 %slice_bitcast_fusion.1 = (f32[6,256,512]{2,1,0:T(8,128)S(1)}, f32[6,256,512]{2,1,0:T(8,128)}) fusion(f32[2,6,256,512]{3,2,1,0:T(8,128)S(1)} %pad_maximum_fusion), kind=kLoop, calls=%fused_computation.20 | loop fusion | bytes 12582912 | tf_op jit(solution)/shard_map/squeeze | solution.py:166
  66.6 4.4 %add_add_fusion = (f32[4,256,512]{2,1,0:T(8,128)}, f32[4,256,512]{2,1,0:T(8,128)S(1)}, f32[4,256,512]{2,1,0:T(8,128)}) fusion(f32[4,256,512]{2,1,0:T(8,128)S(1)} %copy-done, f32[6,256,512]{2,1,0:T(8,128)S(1)} %get-tuple-element.15, f32[2,1,256,512]{3,2,1,0:T(8,128)S(1)} %collective-permute-done, f32[1,4,256,512]{3,2,1,0:T(8,128)S(1)} %bitcast.135, ...), kind=kLoop, calls=%fused_computation.69 | loop fusion | flops 11534336 | bytes 17825792 | tf_op jit(solution)/shard_map/add | solution.py:56
  71.1 9.2 %fusion.15 = f32[4,256,512]{2,1,0:T(8,128)} fusion(f32[6,256,512]{2,1,0:T(8,128)} %get-tuple-element.16, f32[4,256,512]{2,1,0:T(8,128)} %get-tuple-element.10, f32[2,1,256,512]{3,2,1,0:T(8,128)} %collective-permute-done.1, f32[1,4,256,512]{3,2,1,0:T(8,128)S(1)} %bitcast.136, f32[1,4,256,512]{3,2,1,0:T(8,128)S(1)} %bitcast.140, f32[4,256,512]{2,1,0:T(8,128)} %param.27, ...), kind=kLoop, calls=%fused_computation.33 | loop fusion | flops 12582912 | bytes 23068672 | tf_op jit(solution)/shard_map/add | solution.py:55
  80.3 0.0 copy-done.3
  80.3 3.0 %add_divide_fusion = f32[4,256,512]{2,1,0:T(8,128)S(1)} fusion(f32[4,256,512]{2,1,0:T(8,128)} %get-tuple-element.5, f32[4,256,512]{2,1,0:T(8,128)} %fusion.15, f32[4,256,512]{2,1,0:T(8,128)S(1)} %copy-done.2), kind=kLoop, calls=%fused_computation.68 | loop fusion | flops 1048576 | bytes 8388608 | tf_op jit(solution)/shard_map/div | solution.py:170
  83.3 0.1 fusion.81
  83.3 3.8 %collective-permute-start.2 = (f32[1,256,512]{2,1,0:T(8,128)S(1)}, f32[1,256,512]{2,1,0:T(8,128)S(1)}, u32[]{:S(2)}, u32[]{:S(2)}) collective-permute-start(f32[1,256,512]{2,1,0:T(8,128)S(1)} %get-tuple-element.20), channel_id=1, source_target_pairs={{1,0},{2,1},{3,2},{4,3},{5,4},{6,5},{7,6},{8,7},{9,8},{10,9},{11,1... | collective-permute-start | bytes 1572872 | tf_op jit(solution)/shard_map/ppermute | solution.py:20
  87.1 1.9 %collective-permute-start.3 = (f32[1,256,512]{2,1,0:T(8,128)S(1)}, f32[1,256,512]{2,1,0:T(8,128)S(1)}, u32[]{:S(2)}, u32[]{:S(2)}) collective-permute-start(f32[1,256,512]{2,1,0:T(8,128)S(1)} %get-tuple-element.19), channel_id=1, source_target_pairs={{0,1},{1,2},{2,3},{3,4},{4,5},{5,6},{6,7},{7,8},{8,9},{9,10},{10,1... | collective-permute-start | bytes 1572872 | tf_op jit(solution)/shard_map/ppermute | solution.py:18
  89.1 4.7 %collective-permute-done.2 = f32[1,256,512]{2,1,0:T(8,128)S(1)} collective-permute-done((f32[1,256,512]{2,1,0:T(8,128)S(1)}, f32[1,256,512]{2,1,0:T(8,128)S(1)}, u32[]{:S(2)}, u32[]{:S(2)}) %collective-permute-start.2) | collective-permute-done | bytes 524320 | tf_op jit(solution)/shard_map/ppermute | solution.py:20
  93.8 8.0 %collective-permute-done.3 = f32[1,256,512]{2,1,0:T(8,128)S(1)} collective-permute-done((f32[1,256,512]{2,1,0:T(8,128)S(1)}, f32[1,256,512]{2,1,0:T(8,128)S(1)}, u32[]{:S(2)}, u32[]{:S(2)}) %collective-permute-start.3) | collective-permute-done | bytes 524320 | tf_op jit(solution)/shard_map/ppermute | solution.py:18
  101.9 2.3 %select_maximum_fusion = f32[6,258,514]{2,1,0:T(8,128)S(1)} fusion(f32[1,256,512]{2,1,0:T(8,128)S(1)} %collective-permute-done.2, f32[4,256,512]{2,1,0:T(8,128)S(1)} %add_divide_fusion, f32[1,256,512]{2,1,0:T(8,128)S(1)} %collective-permute-done.3), kind=kLoop, calls=%fused_computation.14 | loop fusion | flops 11935080 | bytes 6328416 | tf_op jit(solution)/shard_map/concatenate | solution.py:16
  104.1 7.0 %fusion.20 = f32[4,256,512]{2,1,0:T(8,128)} fusion(f32[6,258,514]{2,1,0:T(8,128)S(1)} %select_maximum_fusion, f32[4,256,512]{2,1,0:T(8,128)} %get-tuple-element.10, f32[4,256,512]{2,1,0:T(8,128)S(1)} %add_divide_fusion, f32[1,256,512]{2,1,0:T(8,128)S(1)} %collective-permute-done.3, f32[4,256,512]{2,1,0:T(8,128)} %copy-done.3, ...), kind=kLoop, calls=%fused_computation.39 | loop fusion | flops 15728640 | bytes 27262976 | tf_op jit(solution)/shard_map/div | solution.py:46
  (34 shorter events, 0.3 us)
Async XLA Ops:
  0.6 13.6 %copy-start.4 = (f32[128,128]{1,0:T(8,128)S(1)}, f32[128,128]{1,0:T(8,128)}, u32[]{:S(2)}) copy-start(f32[128,128]{1,0:T(8,128)} %param.15) | copy-start | bytes 196612
  0.6 13.8 %copy-start.13 = (s32[128]{0:T(128)S(1)}, s32[128]{0:T(128)}, u32[]{:S(2)}) copy-start(s32[128]{0:T(128)} %param.17) | copy-start | bytes 1540
  0.7 14.0 %copy-start.7 = (f32[128,128]{1,0:T(8,128)S(1)}, f32[128,128]{1,0:T(8,128)}, u32[]{:S(2)}) copy-start(f32[128,128]{1,0:T(8,128)} %param.14) | copy-start | bytes 196612
  0.7 14.2 %copy-start.10 = (f32[128]{0:T(128)S(1)}, f32[128]{0:T(128)}, u32[]{:S(2)}) copy-start(f32[128]{0:T(128)} %param.16) | copy-start | bytes 1540
  0.7 25.3 %copy-start.14 = (s32[128,1]{0,1:T(1,128)S(1)}, s32[128,1]{0,1:T(1,128)}, u32[]{:S(2)}) copy-start(s32[128,1]{0,1:T(1,128)} %param.21) | copy-start | bytes 1540
  0.7 25.5 %copy-start.11 = (s32[128]{0:T(128)S(1)}, s32[128]{0:T(128)}, u32[]{:S(2)}) copy-start(s32[128]{0:T(128)} %param.23) | copy-start | bytes 1540
  0.7 25.5 %copy-start.12 = (s32[128]{0:T(128)S(1)}, s32[128]{0:T(128)}, u32[]{:S(2)}) copy-start(s32[128]{0:T(128)} %param.22) | copy-start | bytes 1540
  3.8 58.2 %collective-permute-start = (f32[2,1,256,512]{3,2,1,0:T(8,128)}, f32[2,1,256,512]{3,2,1,0:T(8,128)S(1)}, u32[]{:S(2)}, u32[]{:S(2)}) collective-permute-start(f32[2,1,256,512]{3,2,1,0:T(8,128)} %get-tuple-element.18), channel_id=1, source_target_pairs={{1,0},{2,1},{3,2},{4,3},{5,4},{6,5},{7,6},{8,7},{9,8},{10,9},{11,1... | collective-permute-start | bytes 3145736 | tf_op jit(solution)/shard_map/ppermute | solution.py:20
  11.3 50.8 %collective-permute-start.1 = (f32[2,1,256,512]{3,2,1,0:T(8,128)}, f32[2,1,256,512]{3,2,1,0:T(8,128)}, u32[]{:S(2)}, u32[]{:S(2)}) collective-permute-start(f32[2,1,256,512]{3,2,1,0:T(8,128)} %get-tuple-element.17), channel_id=1, source_target_pairs={{0,1},{1,2},{2,3},{3,4},{4,5},{5,6},{6,7},{7,8},{8,9},{9,10},{10,1... | collective-permute-start | bytes 3145736 | tf_op jit(solution)/shard_map/ppermute | solution.py:18
  15.8 21.5 %all-to-all-start = ((f32[128,1,768]{2,1,0:T(1,128)}), f32[128,1,768]{2,1,0:T(1,128)S(1)}, u32[]{:S(2)}, u32[]{:S(2)}) async-start(f32[128,1,768]{2,1,0:T(1,128)} %broadcast_in_dim.118), calls=%async_computation | async-start | bytes 786432 | tf_op jit(solution)/shard_map/all_to_all | solution.py:113
  30.9 8.2 %copy-start.8 = (f32[128,128]{1,0:T(8,128)S(1)}, f32[128,128]{1,0:T(8,128)}, u32[]{:S(2)}) copy-start(f32[128,128]{1,0:T(8,128)} %param.19) | copy-start | bytes 196612
  30.9 8.2 %copy-start.9 = (f32[128,128]{1,0:T(8,128)S(1)}, f32[128,128]{1,0:T(8,128)}, u32[]{:S(2)}) copy-start(f32[128,128]{1,0:T(8,128)} %param.20) | copy-start | bytes 196612
  30.9 8.3 %copy-start.6 = (bf16[4,128,128]{2,1,0:T(8,128)(2,1)S(1)}, bf16[4,128,128]{2,1,0:T(8,128)(2,1)}, u32[]{:S(2)}) copy-start(bf16[4,128,128]{2,1,0:T(8,128)(2,1)} %param.24) | copy-start | bytes 393220
  39.1 20.0 %copy-start.5 = (f32[128,128]{1,0:T(8,128)}, f32[128,128]{1,0:T(8,128)S(1)}, u32[]{:S(2)}) copy-start(f32[128,128]{1,0:T(8,128)S(1)} %multiply_add_fusion) | copy-start | bytes 196612
  59.1 2.9 %copy-start = (f32[4,256,512]{2,1,0:T(8,128)S(1)}, f32[4,256,512]{2,1,0:T(8,128)}, u32[]{:S(2)}) copy-start(f32[4,256,512]{2,1,0:T(8,128)} %param.26) | copy-start | bytes 6291460
  64.2 2.4 %copy-start.1 = (f32[4,256,512]{2,1,0:T(8,128)S(1)}, f32[4,256,512]{2,1,0:T(8,128)}, u32[]{:S(2)}) copy-start(f32[4,256,512]{2,1,0:T(8,128)} %param.25) | copy-start | bytes 6291460
  71.0 9.2 %copy-start.3 = (f32[4,256,512]{2,1,0:T(8,128)}, f32[4,256,512]{2,1,0:T(8,128)S(1)}, u32[]{:S(2)}) copy-start(f32[4,256,512]{2,1,0:T(8,128)S(1)} %get-tuple-element.9) | copy-start | bytes 6291460
  71.0 9.2 %copy-start.2 = (f32[4,256,512]{2,1,0:T(8,128)S(1)}, f32[4,256,512]{2,1,0:T(8,128)}, u32[]{:S(2)}) copy-start(f32[4,256,512]{2,1,0:T(8,128)} %reshape.227) | copy-start | bytes 6291460
  83.3 10.5 %collective-permute-start.2 = (f32[1,256,512]{2,1,0:T(8,128)S(1)}, f32[1,256,512]{2,1,0:T(8,128)S(1)}, u32[]{:S(2)}, u32[]{:S(2)}) collective-permute-start(f32[1,256,512]{2,1,0:T(8,128)S(1)} %get-tuple-element.20), channel_id=1, source_target_pairs={{1,0},{2,1},{3,2},{4,3},{5,4},{6,5},{7,6},{8,7},{9,8},{10,9},{11,1... | collective-permute-start | bytes 1572872 | tf_op jit(solution)/shard_map/ppermute | solution.py:20
  87.1 14.7 %collective-permute-start.3 = (f32[1,256,512]{2,1,0:T(8,128)S(1)}, f32[1,256,512]{2,1,0:T(8,128)S(1)}, u32[]{:S(2)}, u32[]{:S(2)}) collective-permute-start(f32[1,256,512]{2,1,0:T(8,128)S(1)} %get-tuple-element.19), channel_id=1, source_target_pairs={{0,1},{1,2},{2,3},{3,4},{4,5},{5,6},{6,7},{7,8},{8,9},{9,10},{10,1... | collective-permute-start | bytes 1572872 | tf_op jit(solution)/shard_map/ppermute | solution.py:18

commit v8 on v4

--- a/solution.py
+++ b/solution.py
@@ -160,9 +160,16 @@
     ).reshape(devices, capacity + 1, seg)
     got_rows = recv[:, :capacity, :].reshape(slots, seg)
     got_index = recv[:, capacity, :capacity].reshape(slots).astype(jnp.int32)
-    cell_blocks = tissue_start.size // seg
-    leakage = jax.ops.segment_sum(got_rows, got_index, num_segments=cell_blocks)
-    leak_field = leakage.reshape(base_source.shape)
+    per_row = base_source.shape[2] // seg
+    plane_rows = base_source.shape[0] * base_source.shape[1]
+    spots = (got_index % per_row)[:, None] == jnp.arange(per_row, dtype=jnp.int32)[None, :]
+    placed = jnp.where(spots[:, :, None], got_rows[:, None, :], 0.0).reshape(
+        slots, per_row * seg
+    )
+    rows_hit = (got_index // per_row)[None, :] == jnp.arange(plane_rows, dtype=jnp.int32)[:, None]
+    leak_field = jnp.dot(
+        rows_hit.astype(jnp.float32), placed, precision=lax.Precision.HIGHEST
+    ).reshape(base_source.shape)
     source = base_source + leak_field
     stacked = jnp.stack([tissue_start, conduct])
     wide = padded(stacked, ((AXES, 1),), 1)

time: 104 us -> 111 us (1.067)
  blocking collectives: 15 us -> 0 us
  matrix products: 6.45 us -> 17.7 us
  waiting for transfers between devices: 6.5 us -> 16.8 us
  other arithmetic: 31.3 us -> 22.9 us
  starting transfers between devices: 30.2 us -> 37.1 us
    all_to_all x1 -> x0, blocking collectives: 15 us -> none  [on_device(): lax.all_to_all(send.reshape(devices, (capacity + 1) * seg), AXES, 0, 0, t...]
    dot_general x0 -> x1, matrix products: none -> 11.2 us  [on_device(): jnp.dot(rows_hit.astype(jnp.float32), placed, precision=lax.Precision.HIG...]
    div x1 -> x0, other arithmetic: 10 us -> none  [on_device(): first = (partial + leak_field) / denominator]
    all_to_all x0 -> x1, starting transfers between devices: none -> 6.59 us  [on_device(): lax.all_to_all(send.reshape(devices, (capacity + 1) * seg), AXES, 0, 0, t...]
    ppermute x2, waiting for transfers between devices: 4.74 us -> 9.89 us  [padded(): lax.ppermute(tail, axis, [(i, (i + 1) % count) for i in range(ends)])]
    all_to_all x1, waiting for transfers between devices: 0.01 us -> 3.19 us  [on_device(): got = lax.all_to_all(sent, AXES, 0, 0, tiled=True)]
    scatter-add x1 -> x0, other arithmetic: 3.03 us -> none  [on_device(): leakage = jax.ops.segment_sum(got_rows, got_index, num_segments=cell_blocks)]
    reshape x1 -> x0, local copies, waits for them, and re-layouts: 2.9 us -> none  [on_device(): leak_field = leakage.reshape(base_source.shape)]
  transfers between devices with their start and end apart: 5 -> 6, of which waited for: 2 -> 5; matrix products, arithmetic and copies ran while one was open for 17% -> 15% of each run, Pallas kernels for 0% -> 0%
where the time goes in v8:
time: 111 us; the launch traced here: 109 us
  starting transfers between devices  37.1 us (33%)
  other arithmetic  22.9 us (21%)
  matrix products  17.7 us (16%)
  waiting for transfers between devices  16.8 us (15%)
  local copies, waits for them, and re-layouts  13.9 us (13%)
    ppermute x2, starting transfers between devices, padded(): lax.ppermute(head, axis, [((i + 1) % count, i) for i in range(ends)])  16.1 us
    dot_general x1, matrix products, on_device(): jnp.dot(rows_hit.astype(jnp.float32), placed, precision=lax.Precision.HIG...  11.2 us
    all_to_all x1, starting transfers between devices, on_device(): got = lax.all_to_all(sent, AXES, 0, 0, tiled=True)  10.4 us
    ppermute x2, waiting for transfers between devices, padded(): lax.ppermute(tail, axis, [(i, (i + 1) % count) for i in range(ends)])  9.89 us
    div x1, other arithmetic, relax(): return numerator / denominator  8.43 us
    all_to_all x1, starting transfers between devices, on_device(): lax.all_to_all(send.reshape(devices, (capacity + 1) * seg), AXES, 0, 0, t...  6.59 us
    concatenate x2, other arithmetic, padded(): jnp.concatenate([lax.ppermute(tail, axis, [(i, (i + 1) % count) for i in...  4.47 us
    dot_general x1, matrix products, on_device(): jnp.einsum('bij,cbj->cbi', inverse_blocks, jnp.stack([fixed_rhs, unit]),...  4.43 us
  transfers between devices with their start and end apart: 6, of which 5 were waited for; matrix products, arithmetic and copies ran while one was open for 15% of the time, Pallas kernels for 0%

profile of v8, /device:TPU:8, one launch (start us, length us, event | category | flops | bytes accessed | tf_op | source)
XLA Modules:
  0.0 109.4 jit_solution(6117971371111981727)
XLA Ops:
  0.6 0.9 slice_reduce_fusion.2
  1.6 1.0 slice_reduce_fusion.1
  2.6 0.7 and_select_fusion.6
  3.4 1.0 slice.184
  4.4 0.9 multiply_reduce_fusion
  5.3 0.1 slice_reduce_fusion
  5.5 0.7 stack.32
  6.2 1.0 broadcast_in_dim.144
  7.1 10.4 %all-to-all-start = ((f32[128,1,768]{2,1,0:T(1,128)}), f32[128,1,768]{2,1,0:T(1,128)S(1)}, u32[]{:S(2)}, u32[]{:S(2)}) async-start(f32[128,1,768]{2,1,0:T(1,128)} %broadcast_in_dim.144), calls=%async_computation | async-start | bytes 786432 | tf_op jit(solution)/shard_map/all_to_all | solution.py:113
  17.6 0.9 fusion.76
  18.4 0.9 convert_reduce_fusion
  19.3 0.7 multiply_add_fusion.2
  20.0 0.8 select_reduce_fusion.1
  20.8 0.1 copy.41
  20.9 0.1 convert_element_type.133
  21.1 0.1 copy.46
  21.2 4.4 %convolution_bitcast_fusion = f32[2,128,128]{2,0,1:T(2,128)S(1)} fusion(bf16[128,128,128]{2,1,0:T(8,128)(2,1)} %param.18, bf16[1,128,128]{2,0,1:T(2,128)(2,1)S(1)} %stack_broadcast_in_dim.2, bf16[1,128,128]{2,0,1:T(2,128)(2,1)S(1)} %copy.41), kind=kOutput, calls=%fused_computation.76 | convolution fusion | flops 8519680 | bytes 4390912 | tf_op jit(solution)/shard_map/bij,cbj->cbi/dot_general | solution.py:90
  25.6 0.0 copy-start.5
  25.7 0.1 fusion.83
  25.8 3.2 %all-to-all-done = f32[128,1,768]{2,1,0:T(1,128)S(1)} async-done(((f32[128,1,768]{2,1,0:T(1,128)}), f32[128,1,768]{2,1,0:T(1,128)S(1)}, u32[]{:S(2)}, u32[]{:S(2)}) %all-to-all-start) | async-done | bytes 393248 | tf_op jit(solution)/shard_map/all_to_all | solution.py:113
  29.0 0.4 copy.54
  29.4 0.4 fusion.40
  29.8 0.0 copy-start
  29.9 0.4 fusion.41
  30.3 0.4 fusion.42
  30.7 0.0 copy-done.8
  30.8 0.1 multiply_add_fusion
  30.8 0.0 copy-start.4
  30.9 0.6 copy-done.4
  31.5 0.0 copy-done.6
  31.5 0.0 copy-done.7
  31.5 0.2 convolution_convert_fusion
  31.6 0.1 fusion.63
  31.8 0.1 fusion.65
  31.9 0.1 fusion.67
  32.1 0.2 fusion.45
  32.3 0.1 copy.45
  32.5 0.8 copy.47
  33.3 6.6 %all-to-all-start.1 = ((f32[128,1,384]{2,1,0:T(1,128)}), f32[128,1,384]{2,1,0:T(1,128)S(1)}, u32[]{:S(2)}, u32[]{:S(2)}) async-start(f32[128,1,384]{2,1,0:T(1,128)} %copy.47), calls=%async_computation.1 | async-start | bytes 393216 | tf_op jit(solution)/shard_map/all_to_all | solution.py:158
  39.9 2.7 %pad_maximum_fusion.7 = (f32[2,1,256,512]{3,2,1,0:T(8,128)}, f32[2,1,256,512]{3,2,1,0:T(8,128)}) fusion(f32[1,4,256,512]{3,2,1,0:T(8,128)S(1)} %bitcast.146, f32[1,4,256,512]{3,2,1,0:T(8,128)} %bitcast.150), kind=kLoop, calls=%fused_computation.82 | loop fusion | flops 524288 | bytes 6291456 | tf_op jit(solution)/shard_map/stack | solution.py:174
  42.6 2.0 %collective-permute-start.1 = (f32[2,1,256,512]{3,2,1,0:T(8,128)}, f32[2,1,256,512]{3,2,1,0:T(8,128)S(1)}, u32[]{:S(2)}, u32[]{:S(2)}) collective-permute-start(f32[2,1,256,512]{3,2,1,0:T(8,128)} %get-tuple-element.10), channel_id=1, source_target_pairs={{0,1},{1,2},{2,3},{3,4},{4,5},{5,6},{6,7},{7,8},{8,9},{9,10},{10,1... | collective-permute-start | bytes 3145736 | tf_op jit(solution)/shard_map/ppermute | solution.py:18
  44.6 7.8 %collective-permute-start = (f32[2,1,256,512]{3,2,1,0:T(8,128)}, f32[2,1,256,512]{3,2,1,0:T(8,128)}, u32[]{:S(2)}, u32[]{:S(2)}) collective-permute-start(f32[2,1,256,512]{3,2,1,0:T(8,128)} %get-tuple-element.11), channel_id=1, source_target_pairs={{1,0},{2,1},{3,2},{4,3},{5,4},{6,5},{7,6},{8,7},{9,8},{10,9},{11,1... | collective-permute-start | bytes 3145736 | tf_op jit(solution)/shard_map/ppermute | solution.py:20
  52.4 0.0 all-to-all-done.1
  52.4 0.2 copy.48
  52.6 0.7 copy.50
  53.3 0.1 copy.49
  53.4 0.1 convert_element_type.135
  53.6 0.1 iota_compare_fusion.4
  53.7 2.0 %broadcast_select_fusion = f32[256,4,128]{2,1,0:T(4,128)} fusion(f32[256,128]{1,0:T(8,128)} %bitcast.161, pred[256,4]{1,0:T(8,128)(4,1)S(1)} %iota_compare_fusion.4), kind=kLoop, calls=%fused_computation.88 | loop fusion | flops 131072 | bytes 656384 | tf_op jit(solution)/shard_map/jit(_where)/select_n | solution.py:166
  55.7 2.1 %reshape.307 = f32[256,512,1]{1,0,2:T(8,128)} reshape(f32[256,4,128]{2,1,0:T(4,128)} %broadcast_select_fusion) | data formatting | bytes 1048576 | tf_op jit(solution)/shard_map/jit(_where)/select_n | solution.py:166
  57.8 5.3 %collective-permute-done.1 = f32[2,1,256,512]{3,2,1,0:T(8,128)S(1)} collective-permute-done((f32[2,1,256,512]{3,2,1,0:T(8,128)}, f32[2,1,256,512]{3,2,1,0:T(8,128)S(1)}, u32[]{:S(2)}, u32[]{:S(2)}) %collective-permute-start.1) | collective-permute-done | bytes 1048608 | tf_op jit(solution)/shard_map/ppermute | solution.py:18
  63.1 1.9 %collective-permute-done = f32[2,1,256,512]{3,2,1,0:T(8,128)} collective-permute-done((f32[2,1,256,512]{3,2,1,0:T(8,128)}, f32[2,1,256,512]{3,2,1,0:T(8,128)}, u32[]{:S(2)}, u32[]{:S(2)}) %collective-permute-start) | collective-permute-done | bytes 1048608 | tf_op jit(solution)/shard_map/ppermute | solution.py:20
  65.0 2.2 %pad_maximum_fusion = f32[2,6,256,512]{3,2,1,0:T(8,128)S(1)} fusion(f32[2,1,256,512]{3,2,1,0:T(8,128)} %collective-permute-done, f32[1,4,256,512]{3,2,1,0:T(8,128)S(1)} %bitcast.147, f32[1,4,256,512]{3,2,1,0:T(8,128)} %bitcast.151, f32[2,1,256,512]{3,2,1,0:T(8,128)S(1)} %collective-permute-done.1), kind=kLoop, calls=%fused_computation | loop fusion | flops 4718592 | bytes 12582912 | tf_op jit(solution)/shard_map/concatenate | solution.py:16
  67.2 0.0 copy-done.2
  67.2 0.0 copy-start.1
  67.2 3.4 %slice_bitcast_fusion.1 = (f32[6,256,512]{2,1,0:T(8,128)}, f32[6,256,512]{2,1,0:T(8,128)}) fusion(f32[2,6,256,512]{3,2,1,0:T(8,128)S(1)} %pad_maximum_fusion), kind=kLoop, calls=%fused_computation.19 | loop fusion | bytes 12582912 | tf_op jit(solution)/shard_map/squeeze | solution.py:176
  70.6 11.2 %fusion.17 = (f32[4,256,512]{2,1,0:T(8,128)S(1)}, f32[4,256,512]{2,1,0:T(8,128)}) fusion(f32[6,256,512]{2,1,0:T(8,128)} %get-tuple-element.9, f32[2,1,256,512]{3,2,1,0:T(8,128)} %copy-done.2, f32[1,4,256,512]{3,2,1,0:T(8,128)S(1)} %bitcast.148, f32[1,4,256,512]{3,2,1,0:T(8,128)S(1)} %bitcast.152, f32[4,256,512]{2,1,0:T(8,128)} %param.27, ...), kind=kOutput, calls=%fused_computation.34 | convolution fusion | flops 1631846400 | bytes 21500928 | tf_op jit(solution)/shard_map/dot_general | solution.py:170
  81.8 0.1 fusion.82
  81.9 1.9 %collective-permute-start.3 = (f32[1,256,512]{2,1,0:T(8,128)S(1)}, f32[1,256,512]{2,1,0:T(8,128)S(1)}, u32[]{:S(2)}, u32[]{:S(2)}) collective-permute-start(f32[1,256,512]{2,1,0:T(8,128)S(1)} %get-tuple-element.12), channel_id=1, source_target_pairs={{0,1},{1,2},{2,3},{3,4},{4,5},{5,6},{6,7},{7,8},{8,9},{9,10},{10,1... | collective-permute-start | bytes 1572872 | tf_op jit(solution)/shard_map/ppermute | solution.py:18
  83.8 8.3 %collective-permute-start.2 = (f32[1,256,512]{2,1,0:T(8,128)S(1)}, f32[1,256,512]{2,1,0:T(8,128)S(1)}, u32[]{:S(2)}, u32[]{:S(2)}) collective-permute-start(f32[1,256,512]{2,1,0:T(8,128)S(1)} %get-tuple-element.13), channel_id=1, source_target_pairs={{1,0},{2,1},{3,2},{4,3},{5,4},{6,5},{7,6},{8,7},{9,8},{10,9},{11,1... | collective-permute-start | bytes 1572872 | tf_op jit(solution)/shard_map/ppermute | solution.py:20
  92.2 4.6 %collective-permute-done.3 = f32[1,256,512]{2,1,0:T(8,128)S(1)} collective-permute-done((f32[1,256,512]{2,1,0:T(8,128)S(1)}, f32[1,256,512]{2,1,0:T(8,128)S(1)}, u32[]{:S(2)}, u32[]{:S(2)}) %collective-permute-start.3) | collective-permute-done | bytes 524320 | tf_op jit(solution)/shard_map/ppermute | solution.py:18
  96.8 1.9 %collective-permute-done.2 = f32[1,256,512]{2,1,0:T(8,128)S(1)} collective-permute-done((f32[1,256,512]{2,1,0:T(8,128)S(1)}, f32[1,256,512]{2,1,0:T(8,128)S(1)}, u32[]{:S(2)}, u32[]{:S(2)}) %collective-permute-start.2) | collective-permute-done | bytes 524320 | tf_op jit(solution)/shard_map/ppermute | solution.py:20
  98.7 2.3 %select_maximum_fusion = f32[6,258,514]{2,1,0:T(8,128)S(1)} fusion(f32[1,256,512]{2,1,0:T(8,128)S(1)} %collective-permute-done.2, f32[4,256,512]{2,1,0:T(8,128)S(1)} %get-tuple-element.25, f32[1,256,512]{2,1,0:T(8,128)S(1)} %collective-permute-done.3), kind=kLoop, calls=%fused_computation.13 | loop fusion | flops 11935080 | bytes 6328416 | tf_op jit(solution)/shard_map/concatenate | solution.py:16
  101.0 8.4 %fusion.22 = f32[4,256,512]{2,1,0:T(8,128)} fusion(f32[6,258,514]{2,1,0:T(8,128)S(1)} %select_maximum_fusion, f32[4,256,512]{2,1,0:T(8,128)S(1)} %get-tuple-element.25, f32[1,256,512]{2,1,0:T(8,128)S(1)} %collective-permute-done.3, f32[1,256,512]{2,1,0:T(8,128)S(1)} %collective-permute-done.2, f32[4,256,512]{2,1,0:T(8,128)} %param.27, ...), kind=kLoop, calls=%fused_computation.40 | loop fusion | flops 19922944 | bytes 29360128 | tf_op jit(solution)/shard_map/div | solution.py:46
  (29 shorter events, 0.2 us)
Async XLA Ops:
  7.1 21.9 %all-to-all-start = ((f32[128,1,768]{2,1,0:T(1,128)}), f32[128,1,768]{2,1,0:T(1,128)S(1)}, u32[]{:S(2)}, u32[]{:S(2)}) async-start(f32[128,1,768]{2,1,0:T(1,128)} %broadcast_in_dim.144), calls=%async_computation | async-start | bytes 786432 | tf_op jit(solution)/shard_map/all_to_all | solution.py:113
  25.6 5.1 %copy-start.8 = (f32[128]{0:T(128)S(1)}, f32[128]{0:T(128)}, u32[]{:S(2)}) copy-start(f32[128]{0:T(128)} %param.16) | copy-start | bytes 1540
  25.6 5.8 %copy-start.6 = (f32[128,128]{1,0:T(8,128)S(1)}, f32[128,128]{1,0:T(8,128)}, u32[]{:S(2)}) copy-start(f32[128,128]{1,0:T(8,128)} %param.19) | copy-start | bytes 196612
  25.6 5.8 %copy-start.7 = (f32[128,128]{1,0:T(8,128)S(1)}, f32[128,128]{1,0:T(8,128)}, u32[]{:S(2)}) copy-start(f32[128,128]{1,0:T(8,128)} %param.20) | copy-start | bytes 196612
  25.6 6.0 %copy-start.5 = (bf16[4,128,128]{2,1,0:T(8,128)(2,1)S(1)}, bf16[4,128,128]{2,1,0:T(8,128)(2,1)}, u32[]{:S(2)}) copy-start(bf16[4,128,128]{2,1,0:T(8,128)(2,1)} %param.24) | copy-start | bytes 393220
  29.8 10.1 %copy-start = (f32[4,256,512]{2,1,0:T(8,128)S(1)}, f32[4,256,512]{2,1,0:T(8,128)}, u32[]{:S(2)}) copy-start(f32[4,256,512]{2,1,0:T(8,128)} %param.26) | copy-start | bytes 6291460
  30.8 0.6 copy-start.4
  33.3 19.1 %all-to-all-start.1 = ((f32[128,1,384]{2,1,0:T(1,128)}), f32[128,1,384]{2,1,0:T(1,128)S(1)}, u32[]{:S(2)}, u32[]{:S(2)}) async-start(f32[128,1,384]{2,1,0:T(1,128)} %copy.47), calls=%async_computation.1 | async-start | bytes 393216 | tf_op jit(solution)/shard_map/all_to_all | solution.py:158
  42.6 20.5 %collective-permute-start.1 = (f32[2,1,256,512]{3,2,1,0:T(8,128)}, f32[2,1,256,512]{3,2,1,0:T(8,128)S(1)}, u32[]{:S(2)}, u32[]{:S(2)}) collective-permute-start(f32[2,1,256,512]{3,2,1,0:T(8,128)} %get-tuple-element.10), channel_id=1, source_target_pairs={{0,1},{1,2},{2,3},{3,4},{4,5},{5,6},{6,7},{7,8},{8,9},{9,10},{10,1... | collective-permute-start | bytes 3145736 | tf_op jit(solution)/shard_map/ppermute | solution.py:18
  44.6 20.4 %collective-permute-start = (f32[2,1,256,512]{3,2,1,0:T(8,128)}, f32[2,1,256,512]{3,2,1,0:T(8,128)}, u32[]{:S(2)}, u32[]{:S(2)}) collective-permute-start(f32[2,1,256,512]{3,2,1,0:T(8,128)} %get-tuple-element.11), channel_id=1, source_target_pairs={{1,0},{2,1},{3,2},{4,3},{5,4},{6,5},{7,6},{8,7},{9,8},{10,9},{11,1... | collective-permute-start | bytes 3145736 | tf_op jit(solution)/shard_map/ppermute | solution.py:20
  63.1 4.1 %copy-start.2 = (f32[2,1,256,512]{3,2,1,0:T(8,128)}, f32[2,1,256,512]{3,2,1,0:T(8,128)S(1)}, u32[]{:S(2)}) copy-start(f32[2,1,256,512]{3,2,1,0:T(8,128)S(1)} %collective-permute-done.1) | copy-start | bytes 3145732
  67.2 3.4 %copy-start.1 = (f32[4,256,512]{2,1,0:T(8,128)S(1)}, f32[4,256,512]{2,1,0:T(8,128)}, u32[]{:S(2)}) copy-start(f32[4,256,512]{2,1,0:T(8,128)} %param.25) | copy-start | bytes 6291460
  81.9 14.9 %collective-permute-start.3 = (f32[1,256,512]{2,1,0:T(8,128)S(1)}, f32[1,256,512]{2,1,0:T(8,128)S(1)}, u32[]{:S(2)}, u32[]{:S(2)}) collective-permute-start(f32[1,256,512]{2,1,0:T(8,128)S(1)} %get-tuple-element.12), channel_id=1, source_target_pairs={{0,1},{1,2},{2,3},{3,4},{4,5},{5,6},{6,7},{7,8},{8,9},{9,10},{10,1... | collective-permute-start | bytes 1572872 | tf_op jit(solution)/shard_map/ppermute | solution.py:18
  83.8 17.2 %copy-start.3 = (f32[2,1,256,512]{3,2,1,0:T(8,128)S(1)}, f32[2,1,256,512]{3,2,1,0:T(8,128)}, u32[]{:S(2)}) copy-start(f32[2,1,256,512]{3,2,1,0:T(8,128)} %copy-done.2) | copy-start | bytes 3145732
  83.8 14.9 %collective-permute-start.2 = (f32[1,256,512]{2,1,0:T(8,128)S(1)}, f32[1,256,512]{2,1,0:T(8,128)S(1)}, u32[]{:S(2)}, u32[]{:S(2)}) collective-permute-start(f32[1,256,512]{2,1,0:T(8,128)S(1)} %get-tuple-element.13), channel_id=1, source_target_pairs={{1,0},{2,1},{3,2},{4,3},{5,4},{6,5},{7,6},{8,7},{9,8},{10,9},{11,1... | collective-permute-start | bytes 1572872 | tf_op jit(solution)/shard_map/ppermute | solution.py:20

commit v9 on v4

--- a/solution.py
+++ b/solution.py
@@ -24,19 +24,32 @@
     return cells
 
 
+def shifted(values, axis, step):
+    size = values.shape[axis]
+    widths = [(0, 0)] * values.ndim
+    if step > 0:
+        body = lax.slice_in_dim(values, 1, size, axis=axis)
+        widths[axis] = (0, 1)
+    else:
+        body = lax.slice_in_dim(values, 0, size - 1, axis=axis)
+        widths[axis] = (1, 0)
+    return jnp.pad(body, widths)
+
+
 def neighbours(values):
+    inner = values[1:-1]
     return [
-        values[2:, 1:-1, 1:-1],
-        values[:-2, 1:-1, 1:-1],
-        values[1:-1, 2:, 1:-1],
-        values[1:-1, :-2, 1:-1],
-        values[1:-1, 1:-1, 2:],
-        values[1:-1, 1:-1, :-2],
+        values[2:],
+        values[:-2],
+        shifted(inner, 1, 1),
+        shifted(inner, 1, -1),
+        shifted(inner, 2, 1),
+        shifted(inner, 2, -1),
     ]
 
 
 def relax(padded_p, padded_k, source):
-    centre = padded_k[1:-1, 1:-1, 1:-1]
+    centre = padded_k[1:-1]
     numerator = source
     denominator = jnp.full(centre.shape, UPTAKE, jnp.float32)
     for p_side, k_side in zip(neighbours(padded_p), neighbours(padded_k)):
@@ -47,7 +60,7 @@
 
 
 def relax_parts(padded_p, padded_k, source):
-    centre = padded_k[1:-1, 1:-1, 1:-1]
+    centre = padded_k[1:-1]
     numerator = source
     denominator = jnp.full(centre.shape, UPTAKE, jnp.float32)
     for p_side, k_side in zip(neighbours(padded_p), neighbours(padded_k)):
@@ -166,11 +179,11 @@
     source = base_source + leak_field
     stacked = jnp.stack([tissue_start, conduct])
     wide = padded(stacked, ((AXES, 1),), 1)
-    padded_k = pad_sides(wide[1])
-    partial, denominator = relax_parts(pad_sides(wide[0]), padded_k, base_source)
+    padded_k = wide[1]
+    partial, denominator = relax_parts(wide[0], padded_k, base_source)
     first = (partial + leak_field) / denominator
     second = padded(first, ((AXES, 0),), 1)
-    tissue = relax(pad_sides(second), padded_k, source)
+    tissue = relax(second, padded_k, source)
     return (pressure, tissue)
 
 

time: 104 us -> 117 us (1.12)
  local copies, waits for them, and re-layouts: 12.8 us -> 28.9 us
  blocking collectives: 15 us -> 0 us
  starting transfers between devices: 30.2 us -> 36.2 us
  waiting for transfers between devices: 6.5 us -> 10.4 us
  matrix products: 6.45 us -> 9.67 us
  other arithmetic: 31.3 us -> 29.9 us
    slice x1 -> x5, local copies, waits for them, and re-layouts: 0.07 us -> 15.8 us  [the longest x2 10.4 us: shifted(): body = lax.slice_in_dim(values, 0, size - 1, axis=axis)]
    all_to_all x1 -> x0, blocking collectives: 15 us -> none  [on_device(): lax.all_to_all(send.reshape(devices, (capacity + 1) * seg), AXES, 0, 0, t...]
    all_to_all x0 -> x1, starting transfers between devices: none -> 9.92 us  [on_device(): lax.all_to_all(send.reshape(devices, (capacity + 1) * seg), AXES, 0, 0, t...]
    concatenate x2 -> x0, other arithmetic: 4.48 us -> none  [padded(): jnp.concatenate([lax.ppermute(tail, axis, [(i, (i + 1) % count) for i in...]
    ppermute x2, starting transfers between devices: 15.8 us -> 11.6 us  [padded(): lax.ppermute(head, axis, [((i + 1) % count, i) for i in range(ends)])]
    squeeze x1 -> x0, local copies, waits for them, and re-layouts: 3.39 us -> none  [on_device(): padded_k = pad_sides(wide[1])]
    another operation x1 -> x0, other arithmetic: 3.07 us -> none  [on_device(): stacked = jnp.stack([tissue_start, conduct])]
    slice x0 -> x1, other arithmetic: none -> 3.05 us  [padded(): head = lax.slice_in_dim(cells, 0, width, axis=dim)]
  transfers between devices with their start and end apart: 5 -> 6, of which waited for: 2 -> 2; matrix products, arithmetic and copies ran while one was open for 17% -> 36% of each run, Pallas kernels for 0% -> 0%
where the time goes in v9:
time: 117 us; the launch traced here: 116 us
  starting transfers between devices  36.2 us (31%)
  other arithmetic  29.9 us (26%)
  local copies, waits for them, and re-layouts  28.9 us (25%)
  waiting for transfers between devices  10.4 us (9%)
  matrix products  9.67 us (8%)
  between operations  1.2 us (1%)
    ppermute x2, starting transfers between devices, padded(): lax.ppermute(head, axis, [((i + 1) % count, i) for i in range(ends)])  11.6 us
    all_to_all x1, starting transfers between devices, on_device(): got = lax.all_to_all(sent, AXES, 0, 0, tiled=True)  10.8 us
    div x1, other arithmetic, on_device(): first = (partial + leak_field) / denominator  10.6 us
    slice x2, local copies, waits for them, and re-layouts, shifted(): body = lax.slice_in_dim(values, 0, size - 1, axis=axis)  10.4 us
    all_to_all x1, starting transfers between devices, on_device(): lax.all_to_all(send.reshape(devices, (capacity + 1) * seg), AXES, 0, 0, t...  9.92 us
    div x1, other arithmetic, relax(): return numerator / denominator  7.98 us
    ppermute x2, waiting for transfers between devices, padded(): lax.ppermute(tail, axis, [(i, (i + 1) % count) for i in range(ends)])  7.57 us
    slice x2, local copies, waits for them, and re-layouts, shifted(): body = lax.slice_in_dim(values, 1, size, axis=axis)  5.29 us
  transfers between devices with their start and end apart: 6, of which 2 were waited for; matrix products, arithmetic and copies ran while one was open for 36% of the time, Pallas kernels for 0%

profile of v9, /device:TPU:8, one launch (start us, length us, event | category | flops | bytes accessed | tf_op | source)
XLA Modules:
  0.0 116.3 jit_solution(10692133424807825459)
XLA Ops:
  0.6 0.9 slice_reduce_fusion.2
  1.6 1.0 slice_reduce_fusion.1
  2.6 1.3 %and_select_fusion.4 = (s32[128]{0:T(128)}, s32[128]{0:T(128)S(1)}, f32[1,128]{1,0:T(1,128)S(1)}) fusion(s32[128]{0:T(128)} %param.17), kind=kLoop, calls=%fused_computation.104 | loop fusion | flops 2560 | bytes 2048 | tf_op jit(solution)/shard_map/jit(floor_divide)/jit(_where)/select_n | solution.py:131
  3.9 1.0 slice.179
  5.0 0.9 multiply_reduce_fusion
  5.9 0.1 slice_reduce_fusion
  6.0 0.7 stack.32
  6.7 1.0 broadcast_in_dim.121
  7.7 10.8 %all-to-all-start = ((f32[128,1,768]{2,1,0:T(1,128)}), f32[128,1,768]{2,1,0:T(1,128)}, u32[]{:S(2)}, u32[]{:S(2)}) async-start(f32[128,1,768]{2,1,0:T(1,128)} %broadcast_in_dim.121), calls=%async_computation | async-start | bytes 786432 | tf_op jit(solution)/shard_map/all_to_all | solution.py:126
  18.5 0.0 copy-start.9
  18.5 0.0 copy-start.21
  18.6 0.0 copy-start.19
  18.6 0.0 copy-start.20
  18.6 3.1 %pad_maximum_fusion.7 = (f32[2,1,256,512]{3,2,1,0:T(8,128)}, f32[2,1,256,512]{3,2,1,0:T(8,128)}) fusion(f32[1,4,256,512]{3,2,1,0:T(8,128)} %bitcast.151, f32[1,4,256,512]{3,2,1,0:T(8,128)} %bitcast.154), kind=kLoop, calls=%fused_computation.52 | loop fusion | flops 524288 | bytes 6291456 | tf_op jit(solution)/shard_map/slice | solution.py:14
  21.6 7.1 %collective-permute-start = (f32[2,1,256,512]{3,2,1,0:T(8,128)}, f32[2,1,256,512]{3,2,1,0:T(8,128)S(1)}, u32[]{:S(2)}, u32[]{:S(2)}) collective-permute-start(f32[2,1,256,512]{3,2,1,0:T(8,128)} %get-tuple-element.8), channel_id=1, source_target_pairs={{1,0},{2,1},{3,2},{4,3},{5,4},{6,5},{7,6},{8,7},{9,8},{10,9},{11,1... | collective-permute-start | bytes 3145736 | tf_op jit(solution)/shard_map/ppermute | solution.py:20
  28.8 1.9 %collective-permute-start.1 = (f32[2,1,256,512]{3,2,1,0:T(8,128)}, f32[2,1,256,512]{3,2,1,0:T(8,128)}, u32[]{:S(2)}, u32[]{:S(2)}) collective-permute-start(f32[2,1,256,512]{3,2,1,0:T(8,128)} %get-tuple-element.9), channel_id=1, source_target_pairs={{0,1},{1,2},{2,3},{3,4},{4,5},{5,6},{6,7},{7,8},{8,9},{9,10},{10,1... | collective-permute-start | bytes 3145736 | tf_op jit(solution)/shard_map/ppermute | solution.py:18
  30.7 0.2 convert_reduce_fusion
  31.0 0.1 select_reduce_fusion.1
  31.1 0.6 broadcast_compare_fusion.3
  31.7 0.1 copy.41
  31.8 0.1 convert_element_type.147
  31.9 0.7 copy.46
  32.7 0.0 copy-start
  32.7 0.0 copy-start.1
  32.7 4.6 %convolution_bitcast_fusion = f32[2,128,128]{2,0,1:T(2,128)S(1)} fusion(bf16[128,128,128]{2,1,0:T(8,128)(2,1)} %param.18, bf16[1,128,128]{2,0,1:T(2,128)(2,1)S(1)} %stack_broadcast_in_dim.2, bf16[1,128,128]{2,0,1:T(2,128)(2,1)S(1)} %copy.41), kind=kOutput, calls=%fused_computation.45 | convolution fusion | flops 8519680 | bytes 4390912 | tf_op jit(solution)/shard_map/bij,cbj->cbi/dot_general | solution.py:103
  37.3 0.8 fusion.72
  38.1 3.7 %fusion.69 = (f32[4,255,512]{2,1,0:T(8,128)}, f32[4,255,512]{2,1,0:T(8,128)}, f32[4,255,512]{2,1,0:T(8,128)}, f32[4,255,512]{2,1,0:T(8,128)}) fusion(f32[4,256,512]{2,1,0:T(8,128)S(1)} %copy-done, f32[4,256,512]{2,1,0:T(8,128)S(1)} %copy-done.1), kind=kLoop, calls=%fused_computation.137 | loop fusion | bytes 16711680 | tf_op jit(solution)/shard_map/slice | solution.py:34
  41.8 0.0 all-to-all-done
  41.8 1.2 %copy.54 = f32[128,1,768]{0,2,1:T(8,128)S(1)} copy(f32[128,1,768]{2,1,0:T(1,128)} %all-to-all-done) | data formatting | bytes 786432 | tf_op jit(solution)/shard_map/dot_general | solution.py:132
  43.0 0.0 copy-start.12
  43.0 1.1 fusion.25
  44.2 0.4 fusion.26
  44.7 0.4 fusion.27
  45.1 0.7 fusion.62
  45.8 0.9 multiply_add_fusion
  46.7 0.0 copy-start.10
  46.8 0.6 copy-done.10
  47.4 1.0 convolution_convert_fusion
  48.4 0.9 fusion.46
  49.3 0.9 fusion.48
  50.2 0.1 fusion.50
  50.4 0.2 fusion.30
  50.6 0.1 copy.45
  50.8 0.8 copy.47
  51.6 9.9 %all-to-all-start.1 = ((f32[128,1,384]{2,1,0:T(1,128)}), f32[128,1,384]{2,1,0:T(1,128)S(1)}, u32[]{:S(2)}, u32[]{:S(2)}) async-start(f32[128,1,384]{2,1,0:T(1,128)} %copy.47), calls=%async_computation.1 | async-start | bytes 393216 | tf_op jit(solution)/shard_map/all_to_all | solution.py:171
  61.5 6.7 %fusion.68 = (f32[4,256,511]{2,1,0:T(8,128)}, f32[4,256,511]{2,1,0:T(8,128)}, f32[4,256,511]{2,1,0:T(8,128)}, f32[4,256,511]{2,1,0:T(8,128)}) fusion(f32[4,256,512]{2,1,0:T(8,128)S(1)} %copy-done, f32[4,256,512]{2,1,0:T(8,128)} %param.25), kind=kLoop, calls=%fused_computation.136 | loop fusion | bytes 16744448 | tf_op jit(solution)/shard_map/slice | solution.py:34
  68.2 2.8 %all-to-all-done.1 = f32[128,1,384]{2,1,0:T(1,128)S(1)} async-done(((f32[128,1,384]{2,1,0:T(1,128)}), f32[128,1,384]{2,1,0:T(1,128)S(1)}, u32[]{:S(2)}, u32[]{:S(2)}) %all-to-all-start.1) | async-done | bytes 196640 | tf_op jit(solution)/shard_map/all_to_all | solution.py:171
  71.0 0.2 copy.48
  71.2 0.7 copy.50
  72.0 0.1 copy.49
  72.1 0.1 reshape.237
  72.2 3.4 %scatter_custom_fusion = f32[4096,128]{1,0:T(8,128)} fusion(s32[256]{0:T(256)S(1)} %reshape.237, f32[256,128]{1,0:T(8,128)} %bitcast.166, f32[]{:T(128)} %constant.59.clone.1), kind=kCustom, calls=%fused_computation.53 | custom fusion | flops 32768 | bytes 2097664 | tf_op jit(solution)/shard_map/scatter-add | solution.py:177
  75.6 2.7 %reshape.229 = f32[4,256,512]{2,1,0:T(8,128)} reshape(f32[4096,128]{1,0:T(8,128)} %scatter_custom_fusion) | data formatting | bytes 4194304 | tf_op jit(solution)/shard_map/reshape | solution.py:178
  78.3 0.0 collective-permute-done
  78.3 0.0 collective-permute-done.1
  78.3 10.6 %fusion.17 = f32[4,256,512]{2,1,0:T(8,128)S(1)} fusion(f32[4,256,512]{2,1,0:T(8,128)} %reshape.229, f32[2,1,256,512]{3,2,1,0:T(8,128)} %collective-permute-done.1, f32[1,4,256,512]{3,2,1,0:T(8,128)S(1)} %bitcast.152, f32[1,4,256,512]{3,2,1,0:T(8,128)} %bitcast.155, f32[4,256,512]{2,1,0:T(8,128)} %param.27, f32[2,1,256,512]{3,2,1,0:T(8,128)S(1)} %collective-permute-done, ...), kind=kLoop, calls=%fused_computation.21 | loop fusion | flops 20971520 | bytes 31408128 | tf_op jit(solution)/shard_map/div | solution.py:184
  88.9 0.1 fusion.67
  89.0 4.5 %collective-permute-start.2 = (f32[1,256,512]{2,1,0:T(8,128)S(1)}, f32[1,256,512]{2,1,0:T(8,128)S(1)}, u32[]{:S(2)}, u32[]{:S(2)}) collective-permute-start(f32[1,256,512]{2,1,0:T(8,128)S(1)} %get-tuple-element.14), channel_id=1, source_target_pairs={{1,0},{2,1},{3,2},{4,3},{5,4},{6,5},{7,6},{8,7},{9,8},{10,9},{11,1... | collective-permute-start | bytes 1572872 | tf_op jit(solution)/shard_map/ppermute | solution.py:20
  93.5 1.9 %collective-permute-start.3 = (f32[1,256,512]{2,1,0:T(8,128)S(1)}, f32[1,256,512]{2,1,0:T(8,128)}, u32[]{:S(2)}, u32[]{:S(2)}) collective-permute-start(f32[1,256,512]{2,1,0:T(8,128)S(1)} %get-tuple-element.15), channel_id=1, source_target_pairs={{0,1},{1,2},{2,3},{3,4},{4,5},{5,6},{6,7},{7,8},{8,9},{9,10},{10,1... | collective-permute-start | bytes 1572872 | tf_op jit(solution)/shard_map/ppermute | solution.py:18
  95.4 2.7 %fusion.66 = (f32[4,256,511]{2,1,0:T(8,128)}, f32[4,256,511]{2,1,0:T(8,128)}) fusion(f32[4,256,512]{2,1,0:T(8,128)S(1)} %fusion.17), kind=kLoop, calls=%fused_computation.134 | loop fusion | bytes 8372224 | tf_op jit(solution)/shard_map/slice | solution.py:31
  98.2 2.6 %fusion.65 = (f32[4,255,512]{2,1,0:T(8,128)}, f32[4,255,512]{2,1,0:T(8,128)}) fusion(f32[4,256,512]{2,1,0:T(8,128)S(1)} %fusion.17), kind=kLoop, calls=%fused_computation.133 | loop fusion | bytes 8355840 | tf_op jit(solution)/shard_map/slice | solution.py:31
  100.7 0.0 collective-permute-done.2
  100.7 7.6 %collective-permute-done.3 = f32[1,256,512]{2,1,0:T(8,128)} collective-permute-done((f32[1,256,512]{2,1,0:T(8,128)S(1)}, f32[1,256,512]{2,1,0:T(8,128)}, u32[]{:S(2)}, u32[]{:S(2)}) %collective-permute-start.3) | collective-permute-done | bytes 524320 | tf_op jit(solution)/shard_map/ppermute | solution.py:18
  108.4 8.0 %fusion.6 = f32[4,256,512]{2,1,0:T(8,128)} fusion(f32[4,256,512]{2,1,0:T(8,128)S(1)} %fusion.17, f32[1,256,512]{2,1,0:T(8,128)} %collective-permute-done.3, f32[1,256,512]{2,1,0:T(8,128)S(1)} %collective-permute-done.2, f32[4,256,511]{2,1,0:T(8,128)} %get-tuple-element.13, f32[4,256,511]{2,1,0:T(8,128)} %get-tuple-element.12, ...), kind=kLoop, calls=%fused_computation.8 | loop fusion | flops 19922944 | bytes 34553856 | tf_op jit(solution)/shard_map/div | solution.py:59
  (53 shorter events, 0.3 us)
Async XLA Ops:
  1.6 20.1 %copy-start.13 = (f32[128]{0:T(128)}, f32[128]{0:T(128)S(1)}, u32[]{:S(2)}) copy-start(f32[128]{0:T(128)S(1)} %slice_reduce_fusion.2) | copy-start | bytes 1540
  7.7 34.1 %all-to-all-start = ((f32[128,1,768]{2,1,0:T(1,128)}), f32[128,1,768]{2,1,0:T(1,128)}, u32[]{:S(2)}, u32[]{:S(2)}) async-start(f32[128,1,768]{2,1,0:T(1,128)} %broadcast_in_dim.121), calls=%async_computation | async-start | bytes 786432 | tf_op jit(solution)/shard_map/all_to_all | solution.py:126
  18.5 12.2 %copy-start.9 = (f32[128,128]{1,0:T(8,128)S(1)}, f32[128,128]{1,0:T(8,128)}, u32[]{:S(2)}) copy-start(f32[128,128]{1,0:T(8,128)} %param.15) | copy-start | bytes 196612
  18.5 12.2 %copy-start.21 = (s32[128,1]{0,1:T(1,128)S(1)}, s32[128,1]{0,1:T(1,128)}, u32[]{:S(2)}) copy-start(s32[128,1]{0,1:T(1,128)} %param.21) | copy-start | bytes 1540
  18.6 12.4 %copy-start.19 = (s32[128]{0:T(128)S(1)}, s32[128]{0:T(128)}, u32[]{:S(2)}) copy-start(s32[128]{0:T(128)} %param.23) | copy-start | bytes 1540
  18.6 12.4 %copy-start.20 = (s32[128]{0:T(128)S(1)}, s32[128]{0:T(128)}, u32[]{:S(2)}) copy-start(s32[128]{0:T(128)} %param.22) | copy-start | bytes 1540
  21.6 56.7 %collective-permute-start = (f32[2,1,256,512]{3,2,1,0:T(8,128)}, f32[2,1,256,512]{3,2,1,0:T(8,128)S(1)}, u32[]{:S(2)}, u32[]{:S(2)}) collective-permute-start(f32[2,1,256,512]{3,2,1,0:T(8,128)} %get-tuple-element.8), channel_id=1, source_target_pairs={{1,0},{2,1},{3,2},{4,3},{5,4},{6,5},{7,6},{8,7},{9,8},{10,9},{11,1... | collective-permute-start | bytes 3145736 | tf_op jit(solution)/shard_map/ppermute | solution.py:20
  28.8 49.6 %collective-permute-start.1 = (f32[2,1,256,512]{3,2,1,0:T(8,128)}, f32[2,1,256,512]{3,2,1,0:T(8,128)}, u32[]{:S(2)}, u32[]{:S(2)}) collective-permute-start(f32[2,1,256,512]{3,2,1,0:T(8,128)} %get-tuple-element.9), channel_id=1, source_target_pairs={{0,1},{1,2},{2,3},{3,4},{4,5},{5,6},{6,7},{7,8},{8,9},{9,10},{10,1... | collective-permute-start | bytes 3145736 | tf_op jit(solution)/shard_map/ppermute | solution.py:18
  30.9 0.7 copy-start.14
  32.7 5.4 %copy-start = (f32[4,256,512]{2,1,0:T(8,128)S(1)}, f32[4,256,512]{2,1,0:T(8,128)}, u32[]{:S(2)}) copy-start(f32[4,256,512]{2,1,0:T(8,128)} %param.26) | copy-start | bytes 6291460
  32.7 5.4 %copy-start.1 = (f32[4,256,512]{2,1,0:T(8,128)S(1)}, f32[4,256,512]{2,1,0:T(8,128)}, u32[]{:S(2)}) copy-start(f32[4,256,512]{2,1,0:T(8,128)} %param.25) | copy-start | bytes 6291460
  43.0 7.2 %copy-start.12 = (bf16[4,128,128]{2,1,0:T(8,128)(2,1)S(1)}, bf16[4,128,128]{2,1,0:T(8,128)(2,1)}, u32[]{:S(2)}) copy-start(bf16[4,128,128]{2,1,0:T(8,128)(2,1)} %param.24) | copy-start | bytes 393220
  43.0 7.4 %copy-start.15 = (pred[256]{0:T(512)(128)(4,1)S(1)}, pred[256]{0:T(512)(128)(4,1)}, u32[]{:S(2)}) copy-start(pred[256]{0:T(512)(128)(4,1)} %get-tuple-element.26) | copy-start | bytes 772
  43.0 7.4 %copy-start.16 = (pred[256]{0:T(512)(128)(4,1)S(1)}, pred[256]{0:T(512)(128)(4,1)}, u32[]{:S(2)}) copy-start(pred[256]{0:T(512)(128)(4,1)} %get-tuple-element.27) | copy-start | bytes 772
  43.0 7.4 %copy-start.17 = (pred[256]{0:T(512)(128)(4,1)S(1)}, pred[256]{0:T(512)(128)(4,1)}, u32[]{:S(2)}) copy-start(pred[256]{0:T(512)(128)(4,1)} %get-tuple-element.28) | copy-start | bytes 772
  43.0 7.4 %copy-start.18 = (pred[256]{0:T(512)(128)(4,1)S(1)}, pred[256]{0:T(512)(128)(4,1)}, u32[]{:S(2)}) copy-start(pred[256]{0:T(512)(128)(4,1)} %get-tuple-element.29) | copy-start | bytes 772
  45.1 5.7 %copy-start.11 = (f32[128,1,128]{0,2,1:T(8,128)S(1)}, f32[128,1,128]{0,2,1:T(8,128)}, u32[]{:S(2)}) copy-start(f32[128,1,128]{0,2,1:T(8,128)} %copy.46) | copy-start | bytes 196612
  46.7 0.6 copy-start.10
  51.6 19.4 %all-to-all-start.1 = ((f32[128,1,384]{2,1,0:T(1,128)}), f32[128,1,384]{2,1,0:T(1,128)S(1)}, u32[]{:S(2)}, u32[]{:S(2)}) async-start(f32[128,1,384]{2,1,0:T(1,128)} %copy.47), calls=%async_computation.1 | async-start | bytes 393216 | tf_op jit(solution)/shard_map/all_to_all | solution.py:171
  78.3 10.6 %copy-start.8 = (f32[2,1,256,512]{3,2,1,0:T(8,128)}, f32[2,1,256,512]{3,2,1,0:T(8,128)S(1)}, u32[]{:S(2)}) copy-start(f32[2,1,256,512]{3,2,1,0:T(8,128)S(1)} %collective-permute-done) | copy-start | bytes 3145732
  89.0 11.8 %collective-permute-start.2 = (f32[1,256,512]{2,1,0:T(8,128)S(1)}, f32[1,256,512]{2,1,0:T(8,128)S(1)}, u32[]{:S(2)}, u32[]{:S(2)}) collective-permute-start(f32[1,256,512]{2,1,0:T(8,128)S(1)} %get-tuple-element.14), channel_id=1, source_target_pairs={{1,0},{2,1},{3,2},{4,3},{5,4},{6,5},{7,6},{8,7},{9,8},{10,9},{11,1... | collective-permute-start | bytes 1572872 | tf_op jit(solution)/shard_map/ppermute | solution.py:20
  93.5 14.8 %collective-permute-start.3 = (f32[1,256,512]{2,1,0:T(8,128)S(1)}, f32[1,256,512]{2,1,0:T(8,128)}, u32[]{:S(2)}, u32[]{:S(2)}) collective-permute-start(f32[1,256,512]{2,1,0:T(8,128)S(1)} %get-tuple-element.15), channel_id=1, source_target_pairs={{0,1},{1,2},{2,3},{3,4},{4,5},{5,6},{6,7},{7,8},{8,9},{9,10},{10,1... | collective-permute-start | bytes 1572872 | tf_op jit(solution)/shard_map/ppermute | solution.py:18
  95.4 12.9 %copy-start.6 = (f32[4,256,511]{2,1,0:T(8,128)S(1)}, f32[4,256,511]{2,1,0:T(8,128)}, u32[]{:S(2)}) copy-start(f32[4,256,511]{2,1,0:T(8,128)} %get-tuple-element.16) | copy-start | bytes 6279172
  95.4 12.9 %copy-start.7 = (f32[4,256,511]{2,1,0:T(8,128)S(1)}, f32[4,256,511]{2,1,0:T(8,128)}, u32[]{:S(2)}) copy-start(f32[4,256,511]{2,1,0:T(8,128)} %get-tuple-element.17) | copy-start | bytes 6279172
  98.2 10.2 %copy-start.2 = (f32[4,256,512]{2,1,0:T(8,128)S(1)}, f32[4,256,512]{2,1,0:T(8,128)}, u32[]{:S(2)}) copy-start(f32[4,256,512]{2,1,0:T(8,128)} %param.25) | copy-start | bytes 6291460
  98.2 10.2 %copy-start.3 = (f32[4,256,512]{2,1,0:T(8,128)S(1)}, f32[4,256,512]{2,1,0:T(8,128)}, u32[]{:S(2)}) copy-start(f32[4,256,512]{2,1,0:T(8,128)} %reshape.229) | copy-start | bytes 6291460
  98.2 10.2 %copy-start.4 = (f32[4,255,512]{2,1,0:T(8,128)S(1)}, f32[4,255,512]{2,1,0:T(8,128)}, u32[]{:S(2)}) copy-start(f32[4,255,512]{2,1,0:T(8,128)} %get-tuple-element.18) | copy-start | bytes 6266884
  98.2 10.2 %copy-start.5 = (f32[4,255,512]{2,1,0:T(8,128)S(1)}, f32[4,255,512]{2,1,0:T(8,128)}, u32[]{:S(2)}) copy-start(f32[4,255,512]{2,1,0:T(8,128)} %get-tuple-element.19) | copy-start | bytes 6266884

commit v10 on v4

--- a/solution.py
+++ b/solution.py
@@ -2,6 +2,8 @@
 import jax.numpy as jnp
 from jax import lax
 from jax.sharding import PartitionSpec as P
+from jax.experimental import pallas as pl
+from jax.experimental.pallas import tpu as pltpu
 
 UPTAKE = 0.5
 AXES = ("grp", "slab")
@@ -55,6 +57,52 @@
         numerator = numerator + facing * p_side
         denominator = denominator + facing
     return numerator, denominator
+
+
+def _relax_kernel(pm, pc, pp, km, kc, kp, src, out):
+    p = pc[0]
+    k = kc[0]
+    rows, cols = p.shape
+    row = jax.lax.broadcasted_iota(jnp.int32, (rows, cols), 0)
+    col = jax.lax.broadcasted_iota(jnp.int32, (rows, cols), 1)
+
+    def side(v, axis, step, edge):
+        size = v.shape[axis]
+        moved = pltpu.roll(v, (size - step) % size, axis)
+        return jnp.where(edge, 0.0, moved)
+
+    x_hi = row == rows - 1
+    x_lo = row == 0
+    y_hi = col == cols - 1
+    y_lo = col == 0
+    sides = [
+        (pp[0], kp[0]),
+        (pm[0], km[0]),
+        (side(p, 0, 1, x_hi), side(k, 0, 1, x_hi)),
+        (side(p, 0, -1, x_lo), side(k, 0, -1, x_lo)),
+        (side(p, 1, 1, y_hi), side(k, 1, 1, y_hi)),
+        (side(p, 1, -1, y_lo), side(k, 1, -1, y_lo)),
+    ]
+    numerator = src[0]
+    denominator = jnp.full(p.shape, UPTAKE, jnp.float32)
+    for p_side, k_side in sides:
+        facing = 0.5 * (k + k_side)
+        numerator = numerator + facing * p_side
+        denominator = denominator + facing
+    out[0] = numerator / denominator
+
+
+def relax_sweep(p_halo, k_halo, source):
+    planes, rows, cols = source.shape
+    block = (1, rows, cols)
+    at = lambda shift: pl.BlockSpec(block, lambda z: (z + shift, 0, 0))
+    return pl.pallas_call(
+        _relax_kernel,
+        grid=(planes,),
+        in_specs=[at(0), at(1), at(2), at(0), at(1), at(2), at(0)],
+        out_specs=at(0),
+        out_shape=jax.ShapeDtypeStruct(source.shape, jnp.float32),
+    )(p_halo, p_halo, p_halo, k_halo, k_halo, k_halo, source)
 
 
 def pad_sides(values):
@@ -162,15 +210,12 @@
     got_index = recv[:, capacity, :capacity].reshape(slots).astype(jnp.int32)
     cell_blocks = tissue_start.size // seg
     leakage = jax.ops.segment_sum(got_rows, got_index, num_segments=cell_blocks)
-    leak_field = leakage.reshape(base_source.shape)
-    source = base_source + leak_field
+    source = base_source + leakage.reshape(base_source.shape)
     stacked = jnp.stack([tissue_start, conduct])
     wide = padded(stacked, ((AXES, 1),), 1)
-    padded_k = pad_sides(wide[1])
-    partial, denominator = relax_parts(pad_sides(wide[0]), padded_k, base_source)
-    first = (partial + leak_field) / denominator
+    first = relax_sweep(wide[0], wide[1], source)
     second = padded(first, ((AXES, 0),), 1)
-    tissue = relax(pad_sides(second), padded_k, source)
+    tissue = relax_sweep(second, wide[1], source)
     return (pressure, tissue)
 
 

time: 104 us -> 112 us (1.077)
  Pallas kernels: 0 us -> 17.3 us
  other arithmetic: 31.3 us -> 15.8 us
  waiting for transfers between devices: 6.5 us -> 12.8 us
  starting transfers between devices: 30.2 us -> 25.2 us
  blocking collectives: 15 us -> 19.4 us
    div x2 -> x0, other arithmetic: 18.4 us -> none  [the longest x1 10 us: on_device(): first = (partial + leak_field) / denominator]
    pallas_call x0 -> x2, Pallas kernels: none -> 17.3 us  [relax_sweep(): pl.pallas_call(_relax_kernel, grid=(planes,), in_specs=[at(0), at(1), at(...]
    ppermute x2, starting transfers between devices: 15.8 us -> 10.9 us  [padded(): lax.ppermute(head, axis, [((i + 1) % count, i) for i in range(ends)])]
    all_to_all x1, blocking collectives: 15 us -> 19.4 us  [on_device(): lax.all_to_all(send.reshape(devices, (capacity + 1) * seg), AXES, 0, 0, t...]
    add x0 -> x1, other arithmetic: none -> 3.59 us  [on_device(): source = base_source + leakage.reshape(base_source.shape)]
    ppermute x2, waiting for transfers between devices: 4.74 us -> 8.04 us  [padded(): lax.ppermute(tail, axis, [(i, (i + 1) % count) for i in range(ends)])]
    another operation x1 -> x0, other arithmetic: 3.07 us -> none  [on_device(): stacked = jnp.stack([tissue_start, conduct])]
    slice x0 -> x1, other arithmetic: none -> 3.07 us  [padded(): lax.slice_in_dim(cells, cells.shape[dim] - width, cells.shape[dim], axis=...]
  transfers between devices with their start and end apart: 5 -> 5, of which waited for: 2 -> 2; matrix products, arithmetic and copies ran while one was open for 17% -> 18% of each run, Pallas kernels for 0% -> 0%
where the time goes in v10:
time: 112 us; the launch traced here: 111 us
  starting transfers between devices  25.2 us (22%)
  blocking collectives  19.4 us (17%)
  Pallas kernels  17.3 us (15%)
  other arithmetic  15.8 us (14%)
  local copies, waits for them, and re-layouts  13 us (12%)
  waiting for transfers between devices  12.8 us (11%)
  matrix products  6.51 us (6%)
  between operations  1.14 us (1%)
    all_to_all x1, blocking collectives, on_device(): lax.all_to_all(send.reshape(devices, (capacity + 1) * seg), AXES, 0, 0, t...  19.4 us
    pallas_call x2, Pallas kernels, relax_sweep(): pl.pallas_call(_relax_kernel, grid=(planes,), in_specs=[at(0), at(1), at(...  17.3 us
    ppermute x2, starting transfers between devices, padded(): lax.ppermute(head, axis, [((i + 1) % count, i) for i in range(ends)])  10.9 us
    all_to_all x1, starting transfers between devices, on_device(): got = lax.all_to_all(sent, AXES, 0, 0, tiled=True)  10.4 us
    ppermute x2, waiting for transfers between devices, padded(): lax.ppermute(tail, axis, [(i, (i + 1) % count) for i in range(ends)])  8.04 us
    ppermute x2, waiting for transfers between devices, padded(): lax.ppermute(head, axis, [((i + 1) % count, i) for i in range(ends)])  4.75 us
    dot_general x1, matrix products, on_device(): jnp.einsum('bij,cbj->cbi', inverse_blocks, jnp.stack([fixed_rhs, unit]),...  4.48 us
    concatenate x2, other arithmetic, padded(): jnp.concatenate([lax.ppermute(tail, axis, [(i, (i + 1) % count) for i in...  3.9 us
  transfers between devices with their start and end apart: 5, of which 2 were waited for; matrix products, arithmetic and copies ran while one was open for 18% of the time, Pallas kernels for 0%

profile of v10, /device:TPU:8, one launch (start us, length us, event | category | flops | bytes accessed | tf_op | source)
XLA Modules:
  0.0 111.1 jit_solution(16653047966126860882)
XLA Ops:
  0.6 0.9 slice_reduce_fusion.2
  1.6 1.0 slice.91
  2.6 0.9 multiply_reduce_fusion
  3.6 0.1 slice_reduce_fusion
  3.7 1.0 slice_reduce_fusion.1
  4.7 0.7 and_select_fusion.4
  5.5 0.7 stack.32
  6.2 1.0 broadcast_in_dim.121
  7.1 10.4 %all-to-all-start = ((f32[128,1,768]{2,1,0:T(1,128)}), f32[128,1,768]{2,1,0:T(1,128)S(1)}, u32[]{:S(2)}, u32[]{:S(2)}) async-start(f32[128,1,768]{2,1,0:T(1,128)} %broadcast_in_dim.121), calls=%async_computation | async-start | bytes 786432 | tf_op jit(solution)/shard_map/all_to_all | solution.py:161
  17.6 0.0 copy-start.3
  17.6 0.0 copy-start.11
  17.6 0.0 copy-start.9
  17.6 0.0 copy-start.10
  17.6 3.1 %pad_maximum_fusion.3 = (f32[2,1,256,512]{3,2,1,0:T(8,128)}, f32[2,1,256,512]{3,2,1,0:T(8,128)}) fusion(f32[1,4,256,512]{3,2,1,0:T(8,128)} %bitcast.109, f32[1,4,256,512]{3,2,1,0:T(8,128)} %bitcast.111), kind=kLoop, calls=%fused_computation.18 | loop fusion | flops 524288 | bytes 6291456 | tf_op jit(solution)/shard_map/slice | solution.py:17
  20.7 7.1 %collective-permute-start.1 = (f32[2,1,256,512]{3,2,1,0:T(8,128)}, f32[2,1,256,512]{3,2,1,0:T(8,128)S(1)}, u32[]{:S(2)}, u32[]{:S(2)}) collective-permute-start(f32[2,1,256,512]{3,2,1,0:T(8,128)} %get-tuple-element.11), channel_id=1, source_target_pairs={{1,0},{2,1},{3,2},{4,3},{5,4},{6,5},{7,6},{8,7},{9,8},{10,9},{11,1... | collective-permute-start | bytes 3145736 | tf_op jit(solution)/shard_map/ppermute | solution.py:22
  27.8 1.9 %collective-permute-start = (f32[2,1,256,512]{3,2,1,0:T(8,128)}, f32[2,1,256,512]{3,2,1,0:T(8,128)}, u32[]{:S(2)}, u32[]{:S(2)}) collective-permute-start(f32[2,1,256,512]{3,2,1,0:T(8,128)} %get-tuple-element.10), channel_id=1, source_target_pairs={{0,1},{1,2},{2,3},{3,4},{4,5},{5,6},{6,7},{7,8},{8,9},{9,10},{10,1... | collective-permute-start | bytes 3145736 | tf_op jit(solution)/shard_map/ppermute | solution.py:20
  29.8 0.1 copy.41
  29.9 0.2 convert_reduce_fusion
  30.0 0.0 copy-done.9
  30.1 0.1 select_reduce_fusion.1
  30.2 0.1 convert_element_type.127
  30.4 0.1 copy.46
  30.5 0.0 copy-start.8
  30.5 0.0 copy-start.6
  30.6 0.0 copy-start.7
  30.6 0.0 copy-start.5
  30.6 4.5 %convolution_bitcast_fusion = f32[2,128,128]{2,0,1:T(2,128)S(1)} fusion(bf16[128,128,128]{2,1,0:T(8,128)(2,1)} %param.18, bf16[1,128,128]{2,0,1:T(2,128)(2,1)S(1)} %stack_broadcast_in_dim.2, bf16[1,128,128]{2,0,1:T(2,128)(2,1)S(1)} %copy.41), kind=kOutput, calls=%fused_computation.11 | convolution fusion | flops 8519680 | bytes 4390912 | tf_op jit(solution)/shard_map/bij,cbj->cbi/dot_general | solution.py:138
  35.1 0.1 fusion.41
  35.2 0.0 all-to-all-done
  35.2 0.4 copy.54
  35.6 0.4 fusion
  36.1 0.4 fusion.1
  36.5 0.4 fusion.2
  37.0 0.1 multiply_add_fusion
  37.1 0.0 copy-start.4
  37.1 0.2 convolution_convert_fusion
  37.3 0.1 fusion.25
  37.4 0.1 fusion.23
  37.6 0.1 fusion.21
  37.7 0.2 fusion.5
  37.9 0.1 copy.45
  38.1 0.2 copy.47
  38.2 19.4 %all_to_all.18 = f32[128,1,384]{2,1,0:T(1,128)S(1)} all-to-all(f32[128,1,384]{2,1,0:T(1,128)S(1)} %copy.47), channel_id=1, replica_groups=mesh['grp'=4,'slab'=32] {'grp','slab'}, dimensions={0} | all-to-all | bytes 393216 | tf_op jit(solution)/shard_map/all_to_all | solution.py:206
  57.6 0.2 copy.48
  57.8 0.1 copy.49
  57.9 0.1 reshape.229
  58.1 0.1 copy.50
  58.2 3.0 %scatter_custom_fusion = f32[4096,128]{1,0:T(8,128)} fusion(s32[256]{0:T(256)S(1)} %reshape.229, f32[256,128]{1,0:T(8,128)S(1)} %bitcast.122, f32[]{:T(128)} %constant.58.clone.1), kind=kCustom, calls=%fused_computation.19 | custom fusion | flops 32768 | bytes 2097156 | tf_op jit(solution)/shard_map/scatter-add | solution.py:212
  61.2 1.7 %reshape.221 = f32[4,256,512]{2,1,0:T(8,128)S(1)} reshape(f32[4096,128]{1,0:T(8,128)} %scatter_custom_fusion) | data formatting | bytes 4194304 | tf_op jit(solution)/shard_map/reshape | solution.py:213
  63.0 0.0 copy-start.1
  63.0 0.0 copy-start.2
  63.0 3.6 %add.76.src = f32[4,256,512]{2,1,0:T(8,128)} add(f32[4,256,512]{2,1,0:T(8,128)} %param.27, f32[4,256,512]{2,1,0:T(8,128)S(1)} %reshape.221) | non-fusion elementwise | flops 524288 | bytes 6291456 | tf_op jit(solution)/shard_map/add | solution.py:213
  66.6 0.0 collective-permute-done.1
  66.6 0.0 collective-permute-done
  66.6 1.8 %pad_maximum_fusion = f32[2,6,256,512]{3,2,1,0:T(8,128)S(1)} fusion(f32[2,1,256,512]{3,2,1,0:T(8,128)S(1)} %collective-permute-done.1, f32[1,4,256,512]{3,2,1,0:T(8,128)S(1)} %bitcast.110, f32[1,4,256,512]{3,2,1,0:T(8,128)S(1)} %bitcast.112, f32[2,1,256,512]{3,2,1,0:T(8,128)} %collective-permute-done), kind=kLoop, calls=%fused_computation.1 | loop fusion | flops 4718592 | bytes 12582912 | tf_op jit(solution)/shard_map/concatenate | solution.py:18
  68.4 3.4 %slice_bitcast_fusion = (f32[6,256,512]{2,1,0:T(8,128)}, f32[6,256,512]{2,1,0:T(8,128)}) fusion(f32[2,6,256,512]{3,2,1,0:T(8,128)S(1)} %pad_maximum_fusion), kind=kLoop, calls=%fused_computation.2 | loop fusion | bytes 12582912 | tf_op jit(solution)/shard_map/squeeze | solution.py:216
  71.8 8.7 %shard_map.149 = f32[4,256,512]{2,1,0:T(8,128)} custom-call(f32[6,256,512]{2,1,0:T(8,128)} %get-tuple-element.9.pm.pc.pp, f32[6,256,512]{2,1,0:T(8,128)} %get-tuple-element.9.pm.pc.pp, f32[6,256,512]{2,1,0:T(8,128)} %get-tuple-element.9.pm.pc.pp, f32[6,256,512]{2,1,0:T(8,128)} %get-tuple-element.8.km.kc.kp, f32[6,256,512]{2,1,0:T(8,128)} %get-tuple-element.8.km.kc.kp, ...), custom_call_target="tpu_custom_call" | custom-call | tf_op jit(solution)/shard_map/pallas_call | solution.py:99
  80.5 1.4 %fusion.40 = (f32[1,256,512]{2,1,0:T(8,128)S(1)}, f32[1,256,512]{2,1,0:T(8,128)S(1)}) fusion(f32[4,256,512]{2,1,0:T(8,128)} %shard_map.149), kind=kLoop, calls=%fused_computation.99 | loop fusion | bytes 2097152 | tf_op jit(solution)/shard_map/slice | solution.py:17
  81.9 3.8 %collective-permute-start.3 = (f32[1,256,512]{2,1,0:T(8,128)S(1)}, f32[1,256,512]{2,1,0:T(8,128)S(1)}, u32[]{:S(2)}, u32[]{:S(2)}) collective-permute-start(f32[1,256,512]{2,1,0:T(8,128)S(1)} %get-tuple-element.13), channel_id=1, source_target_pairs={{1,0},{2,1},{3,2},{4,3},{5,4},{6,5},{7,6},{8,7},{9,8},{10,9},{11,1... | collective-permute-start | bytes 1572872 | tf_op jit(solution)/shard_map/ppermute | solution.py:22
  85.7 1.9 %collective-permute-start.2 = (f32[1,256,512]{2,1,0:T(8,128)S(1)}, f32[1,256,512]{2,1,0:T(8,128)S(1)}, u32[]{:S(2)}, u32[]{:S(2)}) collective-permute-start(f32[1,256,512]{2,1,0:T(8,128)S(1)} %get-tuple-element.12), channel_id=1, source_target_pairs={{0,1},{1,2},{2,3},{3,4},{4,5},{5,6},{6,7},{7,8},{8,9},{9,10},{10,1... | collective-permute-start | bytes 1572872 | tf_op jit(solution)/shard_map/ppermute | solution.py:20
  87.6 4.7 %collective-permute-done.3 = f32[1,256,512]{2,1,0:T(8,128)S(1)} collective-permute-done((f32[1,256,512]{2,1,0:T(8,128)S(1)}, f32[1,256,512]{2,1,0:T(8,128)S(1)}, u32[]{:S(2)}, u32[]{:S(2)}) %collective-permute-start.3) | collective-permute-done | bytes 524320 | tf_op jit(solution)/shard_map/ppermute | solution.py:22
  92.3 8.0 %collective-permute-done.2 = f32[1,256,512]{2,1,0:T(8,128)S(1)} collective-permute-done((f32[1,256,512]{2,1,0:T(8,128)S(1)}, f32[1,256,512]{2,1,0:T(8,128)S(1)}, u32[]{:S(2)}, u32[]{:S(2)}) %collective-permute-start.2) | collective-permute-done | bytes 524320 | tf_op jit(solution)/shard_map/ppermute | solution.py:20
  100.4 2.1 %pad_maximum_fusion.1.pm.pc.pp = f32[6,256,512]{2,1,0:T(8,128)} fusion(f32[1,256,512]{2,1,0:T(8,128)S(1)} %collective-permute-done.3, f32[4,256,512]{2,1,0:T(8,128)S(1)} %copy-done, f32[1,256,512]{2,1,0:T(8,128)S(1)} %collective-permute-done.2), kind=kLoop, calls=%fused_computation.4 | loop fusion | flops 1572864 | bytes 6291456 | tf_op jit(solution)/shard_map/concatenate | solution.py:18
  102.5 8.7 %shard_map.150 = f32[4,256,512]{2,1,0:T(8,128)} custom-call(f32[6,256,512]{2,1,0:T(8,128)} %pad_maximum_fusion.1.pm.pc.pp, f32[6,256,512]{2,1,0:T(8,128)} %pad_maximum_fusion.1.pm.pc.pp, f32[6,256,512]{2,1,0:T(8,128)} %pad_maximum_fusion.1.pm.pc.pp, f32[6,256,512]{2,1,0:T(8,128)} %get-tuple-element.8.km.kc.kp, f32[6,256,512]{2,1,0:T(8,128)} %get-tuple-element.8.km.kc.kp, ...), custom_call_target="tpu_custom_call" | custom-call | tf_op jit(solution)/shard_map/pallas_call | solution.py:99
  (32 shorter events, 0.2 us)
Async XLA Ops:
  7.1 28.1 %all-to-all-start = ((f32[128,1,768]{2,1,0:T(1,128)}), f32[128,1,768]{2,1,0:T(1,128)S(1)}, u32[]{:S(2)}, u32[]{:S(2)}) async-start(f32[128,1,768]{2,1,0:T(1,128)} %broadcast_in_dim.121), calls=%async_computation | async-start | bytes 786432 | tf_op jit(solution)/shard_map/all_to_all | solution.py:161
  17.6 12.2 %copy-start.3 = (f32[128,128]{1,0:T(8,128)S(1)}, f32[128,128]{1,0:T(8,128)}, u32[]{:S(2)}) copy-start(f32[128,128]{1,0:T(8,128)} %param.15) | copy-start | bytes 196612
  17.6 12.3 %copy-start.11 = (s32[128,1]{0,1:T(1,128)S(1)}, s32[128,1]{0,1:T(1,128)}, u32[]{:S(2)}) copy-start(s32[128,1]{0,1:T(1,128)} %param.21) | copy-start | bytes 1540
  17.6 12.5 %copy-start.9 = (s32[128]{0:T(128)S(1)}, s32[128]{0:T(128)}, u32[]{:S(2)}) copy-start(s32[128]{0:T(128)} %param.23) | copy-start | bytes 1540
  17.6 12.5 %copy-start.10 = (s32[128]{0:T(128)S(1)}, s32[128]{0:T(128)}, u32[]{:S(2)}) copy-start(s32[128]{0:T(128)} %param.22) | copy-start | bytes 1540
  20.7 45.9 %collective-permute-start.1 = (f32[2,1,256,512]{3,2,1,0:T(8,128)}, f32[2,1,256,512]{3,2,1,0:T(8,128)S(1)}, u32[]{:S(2)}, u32[]{:S(2)}) collective-permute-start(f32[2,1,256,512]{3,2,1,0:T(8,128)} %get-tuple-element.11), channel_id=1, source_target_pairs={{1,0},{2,1},{3,2},{4,3},{5,4},{6,5},{7,6},{8,7},{9,8},{10,9},{11,1... | collective-permute-start | bytes 3145736 | tf_op jit(solution)/shard_map/ppermute | solution.py:22
  27.8 38.8 %collective-permute-start = (f32[2,1,256,512]{3,2,1,0:T(8,128)}, f32[2,1,256,512]{3,2,1,0:T(8,128)}, u32[]{:S(2)}, u32[]{:S(2)}) collective-permute-start(f32[2,1,256,512]{3,2,1,0:T(8,128)} %get-tuple-element.10), channel_id=1, source_target_pairs={{0,1},{1,2},{2,3},{3,4},{4,5},{5,6},{6,7},{7,8},{8,9},{9,10},{10,1... | collective-permute-start | bytes 3145736 | tf_op jit(solution)/shard_map/ppermute | solution.py:20
  30.5 6.4 %copy-start.8 = (f32[128]{0:T(128)S(1)}, f32[128]{0:T(128)}, u32[]{:S(2)}) copy-start(f32[128]{0:T(128)} %param.16) | copy-start | bytes 1540
  30.5 6.5 %copy-start.6 = (f32[128,128]{1,0:T(8,128)S(1)}, f32[128,128]{1,0:T(8,128)}, u32[]{:S(2)}) copy-start(f32[128,128]{1,0:T(8,128)} %param.19) | copy-start | bytes 196612
  30.6 6.5 %copy-start.7 = (f32[128,128]{1,0:T(8,128)S(1)}, f32[128,128]{1,0:T(8,128)}, u32[]{:S(2)}) copy-start(f32[128,128]{1,0:T(8,128)} %param.20) | copy-start | bytes 196612
  30.6 6.7 %copy-start.5 = (bf16[4,128,128]{2,1,0:T(8,128)(2,1)S(1)}, bf16[4,128,128]{2,1,0:T(8,128)(2,1)}, u32[]{:S(2)}) copy-start(bf16[4,128,128]{2,1,0:T(8,128)(2,1)} %param.24) | copy-start | bytes 393220
  37.1 25.9 %copy-start.4 = (f32[128,128]{1,0:T(8,128)}, f32[128,128]{1,0:T(8,128)S(1)}, u32[]{:S(2)}) copy-start(f32[128,128]{1,0:T(8,128)S(1)} %multiply_add_fusion) | copy-start | bytes 196612
  63.0 3.6 %copy-start.1 = (f32[4,256,512]{2,1,0:T(8,128)S(1)}, f32[4,256,512]{2,1,0:T(8,128)}, u32[]{:S(2)}) copy-start(f32[4,256,512]{2,1,0:T(8,128)} %param.26) | copy-start | bytes 6291460
  63.0 3.6 %copy-start.2 = (f32[4,256,512]{2,1,0:T(8,128)S(1)}, f32[4,256,512]{2,1,0:T(8,128)}, u32[]{:S(2)}) copy-start(f32[4,256,512]{2,1,0:T(8,128)} %param.25) | copy-start | bytes 6291460
  80.5 19.9 %copy-start = (f32[4,256,512]{2,1,0:T(8,128)S(1)}, f32[4,256,512]{2,1,0:T(8,128)}, u32[]{:S(2)}) copy-start(f32[4,256,512]{2,1,0:T(8,128)} %shard_map.149) | copy-start | bytes 6291460
  81.9 10.5 %collective-permute-start.3 = (f32[1,256,512]{2,1,0:T(8,128)S(1)}, f32[1,256,512]{2,1,0:T(8,128)S(1)}, u32[]{:S(2)}, u32[]{:S(2)}) collective-permute-start(f32[1,256,512]{2,1,0:T(8,128)S(1)} %get-tuple-element.13), channel_id=1, source_target_pairs={{1,0},{2,1},{3,2},{4,3},{5,4},{6,5},{7,6},{8,7},{9,8},{10,9},{11,1... | collective-permute-start | bytes 1572872 | tf_op jit(solution)/shard_map/ppermute | solution.py:22
  85.7 14.7 %collective-permute-start.2 = (f32[1,256,512]{2,1,0:T(8,128)S(1)}, f32[1,256,512]{2,1,0:T(8,128)S(1)}, u32[]{:S(2)}, u32[]{:S(2)}) collective-permute-start(f32[1,256,512]{2,1,0:T(8,128)S(1)} %get-tuple-element.12), channel_id=1, source_target_pairs={{0,1},{1,2},{2,3},{3,4},{4,5},{5,6},{6,7},{7,8},{8,9},{9,10},{10,1... | collective-permute-start | bytes 1572872 | tf_op jit(solution)/shard_map/ppermute | solution.py:20

commit v11 on v10

--- a/solution.py
+++ b/solution.py
@@ -59,9 +59,17 @@
     return numerator, denominator
 
 
-def _relax_kernel(pm, pc, pp, km, kc, kp, src, out):
-    p = pc[0]
-    k = kc[0]
+def _relax_kernel(p_ref, p_lo, p_hi, k_ref, k_lo, k_hi, base, leak, out):
+    z = pl.program_id(0)
+    top = p_ref.shape[0] - 1
+    p = p_ref[z]
+    k = k_ref[z]
+    up = jnp.minimum(z + 1, top)
+    down = jnp.maximum(z - 1, 0)
+    p_up = jnp.where(z == top, p_hi[0], p_ref[up])
+    k_up = jnp.where(z == top, k_hi[0], k_ref[up])
+    p_down = jnp.where(z == 0, p_lo[0], p_ref[down])
+    k_down = jnp.where(z == 0, k_lo[0], k_ref[down])
     rows, cols = p.shape
     row = jax.lax.broadcasted_iota(jnp.int32, (rows, cols), 0)
     col = jax.lax.broadcasted_iota(jnp.int32, (rows, cols), 1)
@@ -76,14 +84,14 @@
     y_hi = col == cols - 1
     y_lo = col == 0
     sides = [
-        (pp[0], kp[0]),
-        (pm[0], km[0]),
+        (p_up, k_up),
+        (p_down, k_down),
         (side(p, 0, 1, x_hi), side(k, 0, 1, x_hi)),
         (side(p, 0, -1, x_lo), side(k, 0, -1, x_lo)),
         (side(p, 1, 1, y_hi), side(k, 1, 1, y_hi)),
         (side(p, 1, -1, y_lo), side(k, 1, -1, y_lo)),
     ]
-    numerator = src[0]
+    numerator = base[0] + leak[0]
     denominator = jnp.full(p.shape, UPTAKE, jnp.float32)
     for p_side, k_side in sides:
         facing = 0.5 * (k + k_side)
@@ -92,17 +100,27 @@
     out[0] = numerator / denominator
 
 
-def relax_sweep(p_halo, k_halo, source):
-    planes, rows, cols = source.shape
-    block = (1, rows, cols)
-    at = lambda shift: pl.BlockSpec(block, lambda z: (z + shift, 0, 0))
+def relax_sweep(p, p_lo, p_hi, k, k_lo, k_hi, base, leak):
+    planes, rows, cols = base.shape
+    whole = pl.BlockSpec((planes, rows, cols), lambda z: (0, 0, 0))
+    one = pl.BlockSpec((1, rows, cols), lambda z: (0, 0, 0))
+    plane = pl.BlockSpec((1, rows, cols), lambda z: (z, 0, 0))
     return pl.pallas_call(
         _relax_kernel,
         grid=(planes,),
-        in_specs=[at(0), at(1), at(2), at(0), at(1), at(2), at(0)],
-        out_specs=at(0),
-        out_shape=jax.ShapeDtypeStruct(source.shape, jnp.float32),
-    )(p_halo, p_halo, p_halo, k_halo, k_halo, k_halo, source)
+        in_specs=[whole, one, one, whole, one, one, plane, plane],
+        out_specs=plane,
+        out_shape=jax.ShapeDtypeStruct(base.shape, jnp.float32),
+    )(p, p_lo, p_hi, k, k_lo, k_hi, base, leak)
+
+
+def halos(cells):
+    count = lax.axis_size(AXES)
+    ends = count - 1
+    last = cells.shape[1] - 1
+    lo = lax.ppermute(cells[:, last:], AXES, [(i, i + 1) for i in range(ends)])
+    hi = lax.ppermute(cells[:, :1], AXES, [(i + 1, i) for i in range(ends)])
+    return lo, hi
 
 
 def pad_sides(values):
@@ -210,12 +228,15 @@
     got_index = recv[:, capacity, :capacity].reshape(slots).astype(jnp.int32)
     cell_blocks = tissue_start.size // seg
     leakage = jax.ops.segment_sum(got_rows, got_index, num_segments=cell_blocks)
-    source = base_source + leakage.reshape(base_source.shape)
-    stacked = jnp.stack([tissue_start, conduct])
-    wide = padded(stacked, ((AXES, 1),), 1)
-    first = relax_sweep(wide[0], wide[1], source)
-    second = padded(first, ((AXES, 0),), 1)
-    tissue = relax_sweep(second, wide[1], source)
+    leak_field = leakage.reshape(base_source.shape)
+    lo, hi = halos(jnp.stack([tissue_start, conduct]))
+    first = relax_sweep(
+        tissue_start, lo[0], hi[0], conduct, lo[1], hi[1], base_source, leak_field
+    )
+    first_lo, first_hi = halos(first[None])
+    tissue = relax_sweep(
+        first, first_lo[0], first_hi[0], conduct, lo[1], hi[1], base_source, leak_field
+    )
     return (pressure, tissue)
 
 

time: 112 us -> 104 us (0.929)
  other arithmetic: 15.8 us -> 7.43 us
    concatenate x2 -> x0, other arithmetic: 3.9 us -> none  [padded(): jnp.concatenate([lax.ppermute(tail, axis, [(i, (i + 1) % count) for i in...]
    add x1 -> x0, other arithmetic: 3.59 us -> none  [on_device(): source = base_source + leakage.reshape(base_source.shape)]
    slice x1 -> x0, other arithmetic: 3.07 us -> none  [padded(): lax.slice_in_dim(cells, cells.shape[dim] - width, cells.shape[dim], axis=...]
    another operation x0 -> x1, other arithmetic: none -> 3.04 us  [on_device(): lo, hi = halos(jnp.stack([tissue_start, conduct]))]
    squeeze x1 -> x2, local copies, waits for them, and re-layouts: 3.37 us -> 3.27 us  [the longest x1 2.23 us: on_device(): hi[1]]
  transfers between devices with their start and end apart: 5 -> 5, of which waited for: 2 -> 2; matrix products, arithmetic and copies ran while one was open for 18% -> 17% of each run, Pallas kernels for 0% -> 0%
where the time goes in v11:
time: 104 us
  starting transfers between devices  25.2 us (24%)
  blocking collectives  19.4 us (19%)
  Pallas kernels  18.1 us (17%)
  local copies, waits for them, and re-layouts  13.3 us (13%)
  waiting for transfers between devices  12.8 us (12%)
  other arithmetic  7.43 us (7%)
  matrix products  6.45 us (6%)
  between operations  1.09 us (1%)
    all_to_all x1, blocking collectives, on_device(): lax.all_to_all(send.reshape(devices, (capacity + 1) * seg), AXES, 0, 0, t...  19.4 us
    pallas_call x2, Pallas kernels, relax_sweep(): pl.pallas_call(_relax_kernel, grid=(planes,), in_specs=[whole, one, one,...  18.1 us
    ppermute x2, starting transfers between devices, halos(): hi = lax.ppermute(cells[:, :1], AXES, [(i + 1, i) for i in range(ends)])  10.9 us
    all_to_all x1, starting transfers between devices, on_device(): got = lax.all_to_all(sent, AXES, 0, 0, tiled=True)  10.4 us
    ppermute x2, waiting for transfers between devices, halos(): lo = lax.ppermute(cells[:, last:], AXES, [(i, i + 1) for i in range(ends)])  8.04 us
    ppermute x2, waiting for transfers between devices, halos(): hi = lax.ppermute(cells[:, :1], AXES, [(i + 1, i) for i in range(ends)])  4.75 us
    dot_general x1, matrix products, on_device(): jnp.einsum('bij,cbj->cbi', inverse_blocks, jnp.stack([fixed_rhs, unit]),...  4.43 us
    ppermute x2, starting transfers between devices, halos(): lo = lax.ppermute(cells[:, last:], AXES, [(i, i + 1) for i in range(ends)])  3.84 us
  transfers between devices with their start and end apart: 5, of which 2 were waited for; matrix products, arithmetic and copies ran while one was open for 17% of the time, Pallas kernels for 0%

profile of v11, /device:TPU:8, one launch (start us, length us, event | category | flops | bytes accessed | tf_op | source)
XLA Modules:
  0.0 103.6 jit_solution(3685114103885851508)
XLA Ops:
  0.6 0.9 slice_reduce_fusion.2
  1.6 1.0 slice_reduce_fusion.1
  2.6 0.7 and_select_fusion.4
  3.4 1.0 slice.98
  4.4 0.9 multiply_reduce_fusion
  5.4 0.1 slice_reduce_fusion
  5.5 0.7 stack.32
  6.2 0.9 broadcast_in_dim.124
  7.1 10.4 %all-to-all-start = ((f32[128,1,768]{2,1,0:T(1,128)}), f32[128,1,768]{2,1,0:T(1,128)S(1)}, u32[]{:S(2)}, u32[]{:S(2)}) async-start(f32[128,1,768]{2,1,0:T(1,128)} %broadcast_in_dim.124), calls=%async_computation | async-start | bytes 786432 | tf_op jit(solution)/shard_map/all_to_all | solution.py:179
  17.6 0.0 copy-start
  17.6 0.0 copy-start.10
  17.6 0.0 copy-start.8
  17.6 0.0 copy-start.9
  17.6 3.0 %pad_maximum_fusion = (f32[2,1,256,512]{3,2,1,0:T(8,128)}, f32[2,1,256,512]{3,2,1,0:T(8,128)}) fusion(f32[1,4,256,512]{3,2,1,0:T(8,128)} %bitcast.116, f32[1,4,256,512]{3,2,1,0:T(8,128)} %bitcast.118), kind=kLoop, calls=%fused_computation.13 | loop fusion | flops 524288 | bytes 6291456 | tf_op jit(solution)/shard_map/stack | solution.py:232
  20.6 7.1 %collective-permute-start.1 = (f32[2,1,256,512]{3,2,1,0:T(8,128)}, f32[2,1,256,512]{3,2,1,0:T(8,128)}, u32[]{:S(2)}, u32[]{:S(2)}) collective-permute-start(f32[2,1,256,512]{3,2,1,0:T(8,128)} %get-tuple-element.8), channel_id=1, source_target_pairs={{1,0},{2,1},{3,2},{4,3},{5,4},{6,5},{7,6},{8,7},{9,8},{10,9},{11,1... | collective-permute-start | bytes 3145736 | tf_op jit(solution)/shard_map/ppermute | solution.py:122
  27.8 1.9 %collective-permute-start = (f32[2,1,256,512]{3,2,1,0:T(8,128)}, f32[2,1,256,512]{3,2,1,0:T(8,128)S(1)}, u32[]{:S(2)}, u32[]{:S(2)}) collective-permute-start(f32[2,1,256,512]{3,2,1,0:T(8,128)} %get-tuple-element.9), channel_id=1, source_target_pairs={{0,1},{1,2},{2,3},{3,4},{4,5},{5,6},{6,7},{7,8},{8,9},{9,10},{10,1... | collective-permute-start | bytes 3145736 | tf_op jit(solution)/shard_map/ppermute | solution.py:121
  29.7 0.0 copy-done
  29.7 0.0 copy-done.10
  29.7 0.2 convert_reduce_fusion
  29.9 0.0 copy-done.8
  30.0 0.1 select_reduce_fusion.1
  30.1 0.1 copy.41
  30.2 0.1 convert_element_type.127
  30.4 0.1 copy.46
  30.5 4.4 %convolution_bitcast_fusion = f32[2,128,128]{2,0,1:T(2,128)S(1)} fusion(bf16[128,128,128]{2,1,0:T(8,128)(2,1)} %param.18, bf16[1,128,128]{2,0,1:T(2,128)(2,1)S(1)} %stack_broadcast_in_dim.2, bf16[1,128,128]{2,0,1:T(2,128)(2,1)S(1)} %copy.41), kind=kOutput, calls=%fused_computation.7 | convolution fusion | flops 8519680 | bytes 4390912 | tf_op jit(solution)/shard_map/bij,cbj->cbi/dot_general | solution.py:156
  34.9 0.0 copy-start.4
  35.0 0.1 fusion.41
  35.1 0.0 all-to-all-done
  35.1 0.4 copy.54
  35.5 0.4 fusion
  36.0 0.4 fusion.1
  36.4 0.4 fusion.2
  36.8 0.0 copy-done.7
  36.9 0.1 multiply_add_fusion
  36.9 0.0 copy-done.5
  37.0 0.0 copy-done.6
  37.0 0.0 copy-start.3
  37.0 0.2 convolution_convert_fusion
  37.1 0.0 copy-done.4
  37.1 0.1 fusion.21
  37.3 0.1 fusion.23
  37.4 0.1 fusion.25
  37.6 0.2 fusion.5
  37.8 0.1 copy.45
  38.0 0.2 copy.47
  38.1 19.4 %all_to_all.18 = f32[128,1,384]{2,1,0:T(1,128)S(1)} all-to-all(f32[128,1,384]{2,1,0:T(1,128)S(1)} %copy.47), channel_id=1, replica_groups=mesh['grp'=4,'slab'=32] {'grp','slab'}, dimensions={0} | all-to-all | bytes 393216 | tf_op jit(solution)/shard_map/all_to_all | solution.py:224
  57.5 0.2 copy.48
  57.7 0.1 copy.50
  57.8 0.1 copy.49
  57.9 0.1 reshape.229
  58.1 2.1 %scatter_custom_fusion = f32[4096,128]{1,0:T(8,128)S(1)} fusion(s32[256]{0:T(256)S(1)} %reshape.229, f32[256,128]{1,0:T(8,128)S(1)} %bitcast.130, f32[]{:T(128)} %constant.58.clone.1), kind=kCustom, calls=%fused_computation.15 | custom fusion | flops 32768 | bytes 2097156 | tf_op jit(solution)/shard_map/scatter-add | solution.py:230
  60.2 1.5 %reshape.221.leak = f32[4,256,512]{2,1,0:T(8,128)} reshape(f32[4096,128]{1,0:T(8,128)S(1)} %scatter_custom_fusion) | data formatting | bytes 4194304 | tf_op jit(solution)/shard_map/reshape | solution.py:231
  61.7 0.0 collective-permute-done.1
  61.7 2.2 %slice_bitcast_fusion = (f32[1,256,512]{2,1,0:T(8,128)}, f32[1,256,512]{2,1,0:T(8,128)}) fusion(f32[2,1,256,512]{3,2,1,0:T(8,128)} %collective-permute-done.1), kind=kLoop, calls=%fused_computation.17 | loop fusion | bytes 2097152 | tf_op jit(solution)/shard_map/squeeze | solution.py:234
  64.0 0.0 collective-permute-done
  64.0 1.0 slice_bitcast_fusion.1
  65.0 9.0 %shard_map.149.p_ref = f32[4,256,512]{2,1,0:T(8,128)} custom-call(f32[4,256,512]{2,1,0:T(8,128)} %p_ref.1, f32[1,256,512]{2,1,0:T(8,128)} %get-tuple-element.15.p_lo, f32[1,256,512]{2,1,0:T(8,128)} %get-tuple-element.13.p_hi, f32[4,256,512]{2,1,0:T(8,128)} %k_ref.3, f32[1,256,512]{2,1,0:T(8,128)} %get-tuple-element.14.k_lo, ...), custom_call_target="tpu_custom_call" | custom-call | tf_op jit(solution)/shard_map/pallas_call | solution.py:108
  74.0 1.3 %fusion.40 = (f32[1,1,256,512]{3,2,1,0:T(8,128)S(1)}, f32[1,1,256,512]{3,2,1,0:T(8,128)S(1)}) fusion(f32[1,4,256,512]{3,2,1,0:T(8,128)} %bitcast.117), kind=kLoop, calls=%fused_computation.99 | loop fusion | bytes 2097152 | tf_op jit(solution)/shard_map/slice | solution.py:122
  75.3 3.8 %collective-permute-start.3 = (f32[1,1,256,512]{3,2,1,0:T(8,128)S(1)}, f32[1,1,256,512]{3,2,1,0:T(8,128)S(1)}, u32[]{:S(2)}, u32[]{:S(2)}) collective-permute-start(f32[1,1,256,512]{3,2,1,0:T(8,128)S(1)} %get-tuple-element.10), channel_id=1, source_target_pairs={{1,0},{2,1},{3,2},{4,3},{5,4},{6,5},{7,6},{8,7},{9,8},{10,9},{11,1... | collective-permute-start | bytes 1572872 | tf_op jit(solution)/shard_map/ppermute | solution.py:122
  79.1 1.9 %collective-permute-start.2 = (f32[1,1,256,512]{3,2,1,0:T(8,128)S(1)}, f32[1,1,256,512]{3,2,1,0:T(8,128)S(1)}, u32[]{:S(2)}, u32[]{:S(2)}) collective-permute-start(f32[1,1,256,512]{3,2,1,0:T(8,128)S(1)} %get-tuple-element.11), channel_id=1, source_target_pairs={{0,1},{1,2},{2,3},{3,4},{4,5},{5,6},{6,7},{7,8},{8,9},{9,10},{10,1... | collective-permute-start | bytes 1572872 | tf_op jit(solution)/shard_map/ppermute | solution.py:121
  81.0 4.7 %collective-permute-done.3 = f32[1,1,256,512]{3,2,1,0:T(8,128)S(1)} collective-permute-done((f32[1,1,256,512]{3,2,1,0:T(8,128)S(1)}, f32[1,1,256,512]{3,2,1,0:T(8,128)S(1)}, u32[]{:S(2)}, u32[]{:S(2)}) %collective-permute-start.3) | collective-permute-done | bytes 524320 | tf_op jit(solution)/shard_map/ppermute | solution.py:122
  85.8 8.0 %collective-permute-done.2 = f32[1,1,256,512]{3,2,1,0:T(8,128)S(1)} collective-permute-done((f32[1,1,256,512]{3,2,1,0:T(8,128)S(1)}, f32[1,1,256,512]{3,2,1,0:T(8,128)S(1)}, u32[]{:S(2)}, u32[]{:S(2)}) %collective-permute-start.2) | collective-permute-done | bytes 524320 | tf_op jit(solution)/shard_map/ppermute | solution.py:121
  93.8 0.8 copy-done.2
  94.6 9.0 %shard_map.150 = f32[4,256,512]{2,1,0:T(8,128)} custom-call(f32[4,256,512]{2,1,0:T(8,128)} %shard_map.149.p_ref, f32[1,256,512]{2,1,0:T(8,128)} %bitcast.126, f32[1,256,512]{2,1,0:T(8,128)} %bitcast.125, f32[4,256,512]{2,1,0:T(8,128)} %k_ref.3, f32[1,256,512]{2,1,0:T(8,128)} %get-tuple-element.14.k_lo, f32[1,256,512]{2,1,0:T(8,128)} %get-tuple-element.12.k_hi, ...), custom_call_target="tpu_custom_call" | custom-call | tf_op jit(solution)/shard_map/pallas_call | solution.py:108
  (28 shorter events, 0.2 us)
Async XLA Ops:
  7.1 28.0 %all-to-all-start = ((f32[128,1,768]{2,1,0:T(1,128)}), f32[128,1,768]{2,1,0:T(1,128)S(1)}, u32[]{:S(2)}, u32[]{:S(2)}) async-start(f32[128,1,768]{2,1,0:T(1,128)} %broadcast_in_dim.124), calls=%async_computation | async-start | bytes 786432 | tf_op jit(solution)/shard_map/all_to_all | solution.py:179
  17.6 12.2 %copy-start = (f32[128,128]{1,0:T(8,128)S(1)}, f32[128,128]{1,0:T(8,128)}, u32[]{:S(2)}) copy-start(f32[128,128]{1,0:T(8,128)} %param.15) | copy-start | bytes 196612
  17.6 12.2 %copy-start.10 = (s32[128,1]{0,1:T(1,128)S(1)}, s32[128,1]{0,1:T(1,128)}, u32[]{:S(2)}) copy-start(s32[128,1]{0,1:T(1,128)} %param.21) | copy-start | bytes 1540
  17.6 12.4 %copy-start.8 = (s32[128]{0:T(128)S(1)}, s32[128]{0:T(128)}, u32[]{:S(2)}) copy-start(s32[128]{0:T(128)} %param.23) | copy-start | bytes 1540
  17.6 12.4 %copy-start.9 = (s32[128]{0:T(128)S(1)}, s32[128]{0:T(128)}, u32[]{:S(2)}) copy-start(s32[128]{0:T(128)} %param.22) | copy-start | bytes 1540
  20.6 41.1 %collective-permute-start.1 = (f32[2,1,256,512]{3,2,1,0:T(8,128)}, f32[2,1,256,512]{3,2,1,0:T(8,128)}, u32[]{:S(2)}, u32[]{:S(2)}) collective-permute-start(f32[2,1,256,512]{3,2,1,0:T(8,128)} %get-tuple-element.8), channel_id=1, source_target_pairs={{1,0},{2,1},{3,2},{4,3},{5,4},{6,5},{7,6},{8,7},{9,8},{10,9},{11,1... | collective-permute-start | bytes 3145736 | tf_op jit(solution)/shard_map/ppermute | solution.py:122
  27.8 36.2 %collective-permute-start = (f32[2,1,256,512]{3,2,1,0:T(8,128)}, f32[2,1,256,512]{3,2,1,0:T(8,128)S(1)}, u32[]{:S(2)}, u32[]{:S(2)}) collective-permute-start(f32[2,1,256,512]{3,2,1,0:T(8,128)} %get-tuple-element.9), channel_id=1, source_target_pairs={{0,1},{1,2},{2,3},{3,4},{4,5},{5,6},{6,7},{7,8},{8,9},{9,10},{10,1... | collective-permute-start | bytes 3145736 | tf_op jit(solution)/shard_map/ppermute | solution.py:121
  34.9 1.9 %copy-start.7 = (f32[128]{0:T(128)S(1)}, f32[128]{0:T(128)}, u32[]{:S(2)}) copy-start(f32[128]{0:T(128)} %param.16) | copy-start | bytes 1540
  34.9 2.0 %copy-start.5 = (f32[128,128]{1,0:T(8,128)S(1)}, f32[128,128]{1,0:T(8,128)}, u32[]{:S(2)}) copy-start(f32[128,128]{1,0:T(8,128)} %param.19) | copy-start | bytes 196612
  34.9 2.0 %copy-start.6 = (f32[128,128]{1,0:T(8,128)S(1)}, f32[128,128]{1,0:T(8,128)}, u32[]{:S(2)}) copy-start(f32[128,128]{1,0:T(8,128)} %param.20) | copy-start | bytes 196612
  34.9 2.2 %copy-start.4 = (bf16[4,128,128]{2,1,0:T(8,128)(2,1)S(1)}, bf16[4,128,128]{2,1,0:T(8,128)(2,1)}, u32[]{:S(2)}) copy-start(bf16[4,128,128]{2,1,0:T(8,128)(2,1)} %param.24) | copy-start | bytes 393220
  37.0 23.2 %copy-start.3 = (f32[128,128]{1,0:T(8,128)}, f32[128,128]{1,0:T(8,128)S(1)}, u32[]{:S(2)}) copy-start(f32[128,128]{1,0:T(8,128)S(1)} %multiply_add_fusion) | copy-start | bytes 196612
  75.3 10.5 %collective-permute-start.3 = (f32[1,1,256,512]{3,2,1,0:T(8,128)S(1)}, f32[1,1,256,512]{3,2,1,0:T(8,128)S(1)}, u32[]{:S(2)}, u32[]{:S(2)}) collective-permute-start(f32[1,1,256,512]{3,2,1,0:T(8,128)S(1)} %get-tuple-element.10), channel_id=1, source_target_pairs={{1,0},{2,1},{3,2},{4,3},{5,4},{6,5},{7,6},{8,7},{9,8},{10,9},{11,1... | collective-permute-start | bytes 1572872 | tf_op jit(solution)/shard_map/ppermute | solution.py:122
  79.1 14.7 %collective-permute-start.2 = (f32[1,1,256,512]{3,2,1,0:T(8,128)S(1)}, f32[1,1,256,512]{3,2,1,0:T(8,128)S(1)}, u32[]{:S(2)}, u32[]{:S(2)}) collective-permute-start(f32[1,1,256,512]{3,2,1,0:T(8,128)S(1)} %get-tuple-element.11), channel_id=1, source_target_pairs={{0,1},{1,2},{2,3},{3,4},{4,5},{5,6},{6,7},{7,8},{8,9},{9,10},{10,1... | collective-permute-start | bytes 1572872 | tf_op jit(solution)/shard_map/ppermute | solution.py:121
  85.8 8.0 %copy-start.1 = (f32[1,1,256,512]{3,2,1,0:T(8,128)}, f32[1,1,256,512]{3,2,1,0:T(8,128)S(1)}, u32[]{:S(2)}) copy-start(f32[1,1,256,512]{3,2,1,0:T(8,128)S(1)} %collective-permute-done.3) | copy-start | bytes 1572868
  93.8 0.8 copy-start.2

commit v12 on v11

--- a/solution.py
+++ b/solution.py
@@ -100,15 +100,18 @@
     out[0] = numerator / denominator
 
 
-def relax_sweep(p, p_lo, p_hi, k, k_lo, k_hi, base, leak):
+def relax_sweep(p, p_lo, p_hi, p_at, k, k_lo, k_hi, k_at, base, leak):
     planes, rows, cols = base.shape
     whole = pl.BlockSpec((planes, rows, cols), lambda z: (0, 0, 0))
-    one = pl.BlockSpec((1, rows, cols), lambda z: (0, 0, 0))
     plane = pl.BlockSpec((1, rows, cols), lambda z: (z, 0, 0))
+
+    def edge(at):
+        return pl.BlockSpec((None, 1, rows, cols), lambda z: (at, 0, 0, 0))
+
     return pl.pallas_call(
         _relax_kernel,
         grid=(planes,),
-        in_specs=[whole, one, one, whole, one, one, plane, plane],
+        in_specs=[whole, edge(p_at), edge(p_at), whole, edge(k_at), edge(k_at), plane, plane],
         out_specs=plane,
         out_shape=jax.ShapeDtypeStruct(base.shape, jnp.float32),
     )(p, p_lo, p_hi, k, k_lo, k_hi, base, leak)
@@ -231,11 +234,11 @@
     leak_field = leakage.reshape(base_source.shape)
     lo, hi = halos(jnp.stack([tissue_start, conduct]))
     first = relax_sweep(
-        tissue_start, lo[0], hi[0], conduct, lo[1], hi[1], base_source, leak_field
+        tissue_start, lo, hi, 0, conduct, lo, hi, 1, base_source, leak_field
     )
     first_lo, first_hi = halos(first[None])
     tissue = relax_sweep(
-        first, first_lo[0], first_hi[0], conduct, lo[1], hi[1], base_source, leak_field
+        first, first_lo, first_hi, 0, conduct, lo, hi, 1, base_source, leak_field
     )
     return (pressure, tissue)
 

time: 104 us -> 105 us (level)
    squeeze x2 -> x0, local copies, waits for them, and re-layouts: 3.27 us -> none  [the longest x1 2.23 us: on_device(): hi[1]]
    unnamed x22 -> x26, local copies, waits for them, and re-layouts: 0.88 us -> 2.87 us
    reshape x1, local copies, waits for them, and re-layouts: 1.53 us -> 2.76 us  [on_device(): leak_field = leakage.reshape(base_source.shape)]
where the time goes in v12:
time: 105 us; the launch traced here: 104 us
  starting transfers between devices  25.2 us (24%)
  blocking collectives  19.4 us (18%)
  Pallas kernels  18.1 us (17%)
  local copies, waits for them, and re-layouts  13.2 us (13%)
  waiting for transfers between devices  12.8 us (12%)
  other arithmetic  8.3 us (8%)
  matrix products  6.45 us (6%)
  between operations  1.08 us (1%)
    all_to_all x1, blocking collectives, on_device(): lax.all_to_all(send.reshape(devices, (capacity + 1) * seg), AXES, 0, 0, t...  19.4 us
    pallas_call x2, Pallas kernels, relax_sweep(): pl.pallas_call(_relax_kernel, grid=(planes,), in_specs=[whole, edge(p_at)...  18.1 us
    ppermute x2, starting transfers between devices, halos(): hi = lax.ppermute(cells[:, :1], AXES, [(i + 1, i) for i in range(ends)])  10.9 us
    all_to_all x1, starting transfers between devices, on_device(): got = lax.all_to_all(sent, AXES, 0, 0, tiled=True)  10.4 us
    ppermute x2, waiting for transfers between devices, halos(): lo = lax.ppermute(cells[:, last:], AXES, [(i, i + 1) for i in range(ends)])  8.04 us
    ppermute x2, waiting for transfers between devices, halos(): hi = lax.ppermute(cells[:, :1], AXES, [(i + 1, i) for i in range(ends)])  4.75 us
    dot_general x1, matrix products, on_device(): jnp.einsum('bij,cbj->cbi', inverse_blocks, jnp.stack([fixed_rhs, unit]),...  4.43 us
    ppermute x2, starting transfers between devices, halos(): lo = lax.ppermute(cells[:, last:], AXES, [(i, i + 1) for i in range(ends)])  3.84 us
  transfers between devices with their start and end apart: 5, of which 2 were waited for; matrix products, arithmetic and copies ran while one was open for 17% of the time, Pallas kernels for 0%

profile of v12, /device:TPU:8, one launch (start us, length us, event | category | flops | bytes accessed | tf_op | source)
XLA Modules:
  0.0 104.5 jit_solution(12976793056497740250)
XLA Ops:
  0.6 0.9 slice_reduce_fusion.2
  1.6 1.0 slice_reduce_fusion.1
  2.6 0.7 and_select_fusion.4
  3.4 1.0 slice.84
  4.4 0.9 multiply_reduce_fusion
  5.3 0.1 slice_reduce_fusion
  5.5 0.7 stack.32
  6.2 1.0 broadcast_in_dim.124
  7.1 10.4 %all-to-all-start = ((f32[128,1,768]{2,1,0:T(1,128)}), f32[128,1,768]{2,1,0:T(1,128)S(1)}, u32[]{:S(2)}, u32[]{:S(2)}) async-start(f32[128,1,768]{2,1,0:T(1,128)} %broadcast_in_dim.124), calls=%async_computation | async-start | bytes 786432 | tf_op jit(solution)/shard_map/all_to_all | solution.py:182
  17.6 0.0 copy-start.2
  17.6 0.0 copy-start.12
  17.6 0.0 copy-start.10
  17.6 0.0 copy-start.11
  17.6 3.0 %pad_maximum_fusion = (f32[2,1,256,512]{3,2,1,0:T(8,128)}, f32[2,1,256,512]{3,2,1,0:T(8,128)}) fusion(f32[1,4,256,512]{3,2,1,0:T(8,128)} %bitcast.106, f32[1,4,256,512]{3,2,1,0:T(8,128)} %bitcast.108), kind=kLoop, calls=%fused_computation.13 | loop fusion | flops 524288 | bytes 6291456 | tf_op jit(solution)/shard_map/stack | solution.py:235
  20.6 7.1 %collective-permute-start.1 = (f32[2,1,256,512]{3,2,1,0:T(8,128)}, f32[2,1,256,512]{3,2,1,0:T(8,128)S(1)}, u32[]{:S(2)}, u32[]{:S(2)}) collective-permute-start(f32[2,1,256,512]{3,2,1,0:T(8,128)} %get-tuple-element.8), channel_id=1, source_target_pairs={{1,0},{2,1},{3,2},{4,3},{5,4},{6,5},{7,6},{8,7},{9,8},{10,9},{11,1... | collective-permute-start | bytes 3145736 | tf_op jit(solution)/shard_map/ppermute | solution.py:125
  27.7 1.9 %collective-permute-start = (f32[2,1,256,512]{3,2,1,0:T(8,128)}, f32[2,1,256,512]{3,2,1,0:T(8,128)S(1)}, u32[]{:S(2)}, u32[]{:S(2)}) collective-permute-start(f32[2,1,256,512]{3,2,1,0:T(8,128)} %get-tuple-element.9), channel_id=1, source_target_pairs={{0,1},{1,2},{2,3},{3,4},{4,5},{5,6},{6,7},{7,8},{8,9},{9,10},{10,1... | collective-permute-start | bytes 3145736 | tf_op jit(solution)/shard_map/ppermute | solution.py:124
  29.7 0.0 copy-done.2
  29.7 0.0 copy-done.12
  29.7 0.2 convert_reduce_fusion
  29.9 0.0 copy-done.10
  29.9 0.0 copy-done.11
  29.9 0.1 select_reduce_fusion.1
  30.1 0.1 copy.41
  30.2 0.1 convert_element_type.127
  30.3 0.1 copy.46
  30.5 4.4 %convolution_bitcast_fusion = f32[2,128,128]{2,0,1:T(2,128)S(1)} fusion(bf16[128,128,128]{2,1,0:T(8,128)(2,1)} %param.18, bf16[1,128,128]{2,0,1:T(2,128)(2,1)S(1)} %stack_broadcast_in_dim.2, bf16[1,128,128]{2,0,1:T(2,128)(2,1)S(1)} %copy.41), kind=kOutput, calls=%fused_computation.7 | convolution fusion | flops 8519680 | bytes 4390912 | tf_op jit(solution)/shard_map/bij,cbj->cbi/dot_general | solution.py:159
  34.9 0.0 copy-start.6
  35.0 0.1 fusion.41
  35.1 0.0 all-to-all-done
  35.1 0.4 copy.54
  35.5 0.4 fusion
  35.9 0.4 fusion.1
  36.4 0.4 fusion.2
  36.8 0.0 copy-done.9
  36.8 0.1 multiply_add_fusion
  36.9 0.0 copy-done.7
  36.9 0.0 copy-start.5
  37.0 0.2 convolution_convert_fusion
  37.1 0.1 fusion.21
  37.3 0.1 fusion.23
  37.4 0.1 fusion.25
  37.6 0.2 fusion.5
  37.8 0.1 copy.45
  37.9 0.2 copy.47
  38.1 19.4 %all_to_all.18 = f32[128,1,384]{2,1,0:T(1,128)S(1)} all-to-all(f32[128,1,384]{2,1,0:T(1,128)S(1)} %copy.47), channel_id=1, replica_groups=mesh['grp'=4,'slab'=32] {'grp','slab'}, dimensions={0} | all-to-all | bytes 393216 | tf_op jit(solution)/shard_map/all_to_all | solution.py:227
  57.5 0.2 copy.48
  57.7 0.1 copy.50
  57.8 0.1 copy.49
  57.9 0.1 reshape.229
  58.0 3.0 %scatter_custom_fusion = f32[4096,128]{1,0:T(8,128)} fusion(s32[256]{0:T(256)S(1)} %reshape.229, f32[256,128]{1,0:T(8,128)S(1)} %bitcast.118, f32[]{:T(128)} %constant.58.clone.1), kind=kCustom, calls=%fused_computation.15 | custom fusion | flops 32768 | bytes 2097156 | tf_op jit(solution)/shard_map/scatter-add | solution.py:233
  61.1 0.0 copy-done.5
  61.1 2.8 %reshape.221.leak = f32[4,256,512]{2,1,0:T(8,128)} reshape(f32[4096,128]{1,0:T(8,128)} %scatter_custom_fusion) | data formatting | bytes 4194304 | tf_op jit(solution)/shard_map/reshape | solution.py:234
  63.8 0.0 collective-permute-done.1.p_hi.k_hi
  63.8 0.0 collective-permute-done.p_lo.k_lo
  63.8 1.0 copy-done
  64.8 1.0 copy-done.1
  65.8 9.0 %shard_map.149.p_ref = f32[4,256,512]{2,1,0:T(8,128)} custom-call(f32[4,256,512]{2,1,0:T(8,128)} %p_ref.1, f32[2,1,256,512]{3,2,1,0:T(8,128)} %copy-done.1, f32[2,1,256,512]{3,2,1,0:T(8,128)} %copy-done, f32[4,256,512]{2,1,0:T(8,128)} %k_ref.3, f32[2,1,256,512]{3,2,1,0:T(8,128)} %copy-done.1, f32[2,1,256,512]{3,2,1,0:T(8,128)} %copy-done, ...), custom_call_target="tpu_custom_call" | custom-call | tf_op jit(solution)/shard_map/pallas_call | solution.py:111
  74.9 1.3 %fusion.40 = (f32[1,1,256,512]{3,2,1,0:T(8,128)S(1)}, f32[1,1,256,512]{3,2,1,0:T(8,128)S(1)}) fusion(f32[1,4,256,512]{3,2,1,0:T(8,128)} %bitcast.107), kind=kLoop, calls=%fused_computation.95 | loop fusion | bytes 2097152 | tf_op jit(solution)/shard_map/slice | solution.py:125
  76.1 3.8 %collective-permute-start.3 = (f32[1,1,256,512]{3,2,1,0:T(8,128)S(1)}, f32[1,1,256,512]{3,2,1,0:T(8,128)S(1)}, u32[]{:S(2)}, u32[]{:S(2)}) collective-permute-start(f32[1,1,256,512]{3,2,1,0:T(8,128)S(1)} %get-tuple-element.10), channel_id=1, source_target_pairs={{1,0},{2,1},{3,2},{4,3},{5,4},{6,5},{7,6},{8,7},{9,8},{10,9},{11,1... | collective-permute-start | bytes 1572872 | tf_op jit(solution)/shard_map/ppermute | solution.py:125
  79.9 1.9 %collective-permute-start.2 = (f32[1,1,256,512]{3,2,1,0:T(8,128)S(1)}, f32[1,1,256,512]{3,2,1,0:T(8,128)S(1)}, u32[]{:S(2)}, u32[]{:S(2)}) collective-permute-start(f32[1,1,256,512]{3,2,1,0:T(8,128)S(1)} %get-tuple-element.11), channel_id=1, source_target_pairs={{0,1},{1,2},{2,3},{3,4},{4,5},{5,6},{6,7},{7,8},{8,9},{9,10},{10,1... | collective-permute-start | bytes 1572872 | tf_op jit(solution)/shard_map/ppermute | solution.py:124
  81.8 4.7 %collective-permute-done.3.p_hi = f32[1,1,256,512]{3,2,1,0:T(8,128)S(1)} collective-permute-done((f32[1,1,256,512]{3,2,1,0:T(8,128)S(1)}, f32[1,1,256,512]{3,2,1,0:T(8,128)S(1)}, u32[]{:S(2)}, u32[]{:S(2)}) %collective-permute-start.3) | collective-permute-done | bytes 524320 | tf_op jit(solution)/shard_map/ppermute | solution.py:125
  86.6 8.0 %collective-permute-done.2.p_lo = f32[1,1,256,512]{3,2,1,0:T(8,128)S(1)} collective-permute-done((f32[1,1,256,512]{3,2,1,0:T(8,128)S(1)}, f32[1,1,256,512]{3,2,1,0:T(8,128)S(1)}, u32[]{:S(2)}, u32[]{:S(2)}) %collective-permute-start.2) | collective-permute-done | bytes 524320 | tf_op jit(solution)/shard_map/ppermute | solution.py:124
  94.6 0.8 copy-done.4
  95.4 9.0 %shard_map.150 = f32[4,256,512]{2,1,0:T(8,128)} custom-call(f32[4,256,512]{2,1,0:T(8,128)} %shard_map.149.p_ref, f32[1,1,256,512]{3,2,1,0:T(8,128)} %copy-done.4, f32[1,1,256,512]{3,2,1,0:T(8,128)} %copy-done.3, f32[4,256,512]{2,1,0:T(8,128)} %k_ref.3, f32[2,1,256,512]{3,2,1,0:T(8,128)} %copy-done.1, f32[2,1,256,512]{3,2,1,0:T(8,128)} %copy-done, ...), custom_call_target="tpu_custom_call" | custom-call | tf_op jit(solution)/shard_map/pallas_call | solution.py:111
  (30 shorter events, 0.2 us)
Async XLA Ops:
  7.1 28.0 %all-to-all-start = ((f32[128,1,768]{2,1,0:T(1,128)}), f32[128,1,768]{2,1,0:T(1,128)S(1)}, u32[]{:S(2)}, u32[]{:S(2)}) async-start(f32[128,1,768]{2,1,0:T(1,128)} %broadcast_in_dim.124), calls=%async_computation | async-start | bytes 786432 | tf_op jit(solution)/shard_map/all_to_all | solution.py:182
  17.6 12.1 %copy-start.2 = (f32[128,128]{1,0:T(8,128)S(1)}, f32[128,128]{1,0:T(8,128)}, u32[]{:S(2)}) copy-start(f32[128,128]{1,0:T(8,128)} %param.15) | copy-start | bytes 196612
  17.6 12.1 %copy-start.12 = (s32[128,1]{0,1:T(1,128)S(1)}, s32[128,1]{0,1:T(1,128)}, u32[]{:S(2)}) copy-start(s32[128,1]{0,1:T(1,128)} %param.21) | copy-start | bytes 1540
  17.6 12.3 %copy-start.10 = (s32[128]{0:T(128)S(1)}, s32[128]{0:T(128)}, u32[]{:S(2)}) copy-start(s32[128]{0:T(128)} %param.23) | copy-start | bytes 1540
  17.6 12.3 %copy-start.11 = (s32[128]{0:T(128)S(1)}, s32[128]{0:T(128)}, u32[]{:S(2)}) copy-start(s32[128]{0:T(128)} %param.22) | copy-start | bytes 1540
  20.6 43.2 %collective-permute-start.1 = (f32[2,1,256,512]{3,2,1,0:T(8,128)}, f32[2,1,256,512]{3,2,1,0:T(8,128)S(1)}, u32[]{:S(2)}, u32[]{:S(2)}) collective-permute-start(f32[2,1,256,512]{3,2,1,0:T(8,128)} %get-tuple-element.8), channel_id=1, source_target_pairs={{1,0},{2,1},{3,2},{4,3},{5,4},{6,5},{7,6},{8,7},{9,8},{10,9},{11,1... | collective-permute-start | bytes 3145736 | tf_op jit(solution)/shard_map/ppermute | solution.py:125
  27.7 36.1 %collective-permute-start = (f32[2,1,256,512]{3,2,1,0:T(8,128)}, f32[2,1,256,512]{3,2,1,0:T(8,128)S(1)}, u32[]{:S(2)}, u32[]{:S(2)}) collective-permute-start(f32[2,1,256,512]{3,2,1,0:T(8,128)} %get-tuple-element.9), channel_id=1, source_target_pairs={{0,1},{1,2},{2,3},{3,4},{4,5},{5,6},{6,7},{7,8},{8,9},{9,10},{10,1... | collective-permute-start | bytes 3145736 | tf_op jit(solution)/shard_map/ppermute | solution.py:124
  34.9 1.9 %copy-start.9 = (f32[128]{0:T(128)S(1)}, f32[128]{0:T(128)}, u32[]{:S(2)}) copy-start(f32[128]{0:T(128)} %param.16) | copy-start | bytes 1540
  34.9 2.0 %copy-start.7 = (f32[128,128]{1,0:T(8,128)S(1)}, f32[128,128]{1,0:T(8,128)}, u32[]{:S(2)}) copy-start(f32[128,128]{1,0:T(8,128)} %param.19) | copy-start | bytes 196612
  34.9 2.0 %copy-start.8 = (f32[128,128]{1,0:T(8,128)S(1)}, f32[128,128]{1,0:T(8,128)}, u32[]{:S(2)}) copy-start(f32[128,128]{1,0:T(8,128)} %param.20) | copy-start | bytes 196612
  34.9 2.2 %copy-start.6 = (bf16[4,128,128]{2,1,0:T(8,128)(2,1)S(1)}, bf16[4,128,128]{2,1,0:T(8,128)(2,1)}, u32[]{:S(2)}) copy-start(bf16[4,128,128]{2,1,0:T(8,128)(2,1)} %param.24) | copy-start | bytes 393220
  36.9 24.1 %copy-start.5 = (f32[128,128]{1,0:T(8,128)}, f32[128,128]{1,0:T(8,128)S(1)}, u32[]{:S(2)}) copy-start(f32[128,128]{1,0:T(8,128)S(1)} %multiply_add_fusion) | copy-start | bytes 196612
  63.8 1.0 copy-start
  64.8 1.0 copy-start.1
  76.1 10.5 %collective-permute-start.3 = (f32[1,1,256,512]{3,2,1,0:T(8,128)S(1)}, f32[1,1,256,512]{3,2,1,0:T(8,128)S(1)}, u32[]{:S(2)}, u32[]{:S(2)}) collective-permute-start(f32[1,1,256,512]{3,2,1,0:T(8,128)S(1)} %get-tuple-element.10), channel_id=1, source_target_pairs={{1,0},{2,1},{3,2},{4,3},{5,4},{6,5},{7,6},{8,7},{9,8},{10,9},{11,1... | collective-permute-start | bytes 1572872 | tf_op jit(solution)/shard_map/ppermute | solution.py:125
  79.9 14.7 %collective-permute-start.2 = (f32[1,1,256,512]{3,2,1,0:T(8,128)S(1)}, f32[1,1,256,512]{3,2,1,0:T(8,128)S(1)}, u32[]{:S(2)}, u32[]{:S(2)}) collective-permute-start(f32[1,1,256,512]{3,2,1,0:T(8,128)S(1)} %get-tuple-element.11), channel_id=1, source_target_pairs={{0,1},{1,2},{2,3},{3,4},{4,5},{5,6},{6,7},{7,8},{8,9},{9,10},{10,1... | collective-permute-start | bytes 1572872 | tf_op jit(solution)/shard_map/ppermute | solution.py:124
  86.6 8.0 %copy-start.3 = (f32[1,1,256,512]{3,2,1,0:T(8,128)}, f32[1,1,256,512]{3,2,1,0:T(8,128)S(1)}, u32[]{:S(2)}) copy-start(f32[1,1,256,512]{3,2,1,0:T(8,128)S(1)} %collective-permute-done.3.p_hi) | copy-start | bytes 1572868
  94.6 0.8 copy-start.4

commit v13 on v12

--- a/solution.py
+++ b/solution.py
@@ -1,3 +1,5 @@
+import functools
+
 import jax
 import jax.numpy as jnp
 from jax import lax
@@ -59,8 +61,8 @@
     return numerator, denominator
 
 
-def _relax_kernel(p_ref, p_lo, p_hi, k_ref, k_lo, k_hi, base, leak, out):
-    z = pl.program_id(0)
+def _relax_kernel(plane_of, p_ref, p_lo, p_hi, k_ref, k_lo, k_hi, base, leak, out):
+    z = plane_of(pl.program_id(0))
     top = p_ref.shape[0] - 1
     p = p_ref[z]
     k = k_ref[z]
@@ -100,20 +102,21 @@
     out[0] = numerator / denominator
 
 
-def relax_sweep(p, p_lo, p_hi, p_at, k, k_lo, k_hi, k_at, base, leak):
+def relax_sweep(p, p_lo, p_hi, p_at, k, k_lo, k_hi, k_at, base, leak, plane_of, count):
     planes, rows, cols = base.shape
     whole = pl.BlockSpec((planes, rows, cols), lambda z: (0, 0, 0))
-    plane = pl.BlockSpec((1, rows, cols), lambda z: (z, 0, 0))
+    plane = pl.BlockSpec((1, rows, cols), lambda z: (plane_of(z), 0, 0))
+    step = pl.BlockSpec((1, rows, cols), lambda z: (z, 0, 0))
 
     def edge(at):
         return pl.BlockSpec((None, 1, rows, cols), lambda z: (at, 0, 0, 0))
 
     return pl.pallas_call(
-        _relax_kernel,
-        grid=(planes,),
+        functools.partial(_relax_kernel, plane_of),
+        grid=(count,),
         in_specs=[whole, edge(p_at), edge(p_at), whole, edge(k_at), edge(k_at), plane, plane],
-        out_specs=plane,
-        out_shape=jax.ShapeDtypeStruct(base.shape, jnp.float32),
+        out_specs=step,
+        out_shape=jax.ShapeDtypeStruct((count, rows, cols), jnp.float32),
     )(p, p_lo, p_hi, k, k_lo, k_hi, base, leak)
 
 
@@ -233,12 +236,15 @@
     leakage = jax.ops.segment_sum(got_rows, got_index, num_segments=cell_blocks)
     leak_field = leakage.reshape(base_source.shape)
     lo, hi = halos(jnp.stack([tissue_start, conduct]))
-    first = relax_sweep(
-        tissue_start, lo, hi, 0, conduct, lo, hi, 1, base_source, leak_field
-    )
-    first_lo, first_hi = halos(first[None])
+    planes = base_source.shape[0]
+    args = (tissue_start, lo, hi, 0, conduct, lo, hi, 1, base_source, leak_field)
+    ends = relax_sweep(*args, lambda z: z * (planes - 1), 2)
+    first_lo, first_hi = halos(ends[None])
+    inner = relax_sweep(*args, lambda z: z + 1, planes - 2)
+    first = jnp.concatenate([ends[0:1], inner, ends[1:2]], axis=0)
     tissue = relax_sweep(
-        first, first_lo, first_hi, 0, conduct, lo, hi, 1, base_source, leak_field
+        first, first_lo, first_hi, 0, conduct, lo, hi, 1, base_source, leak_field,
+        lambda z: z, planes,
     )
     return (pressure, tissue)
 

time: 105 us -> 102 us (0.971)
  waiting for transfers between devices: 12.8 us -> 3.58 us
  Pallas kernels: 18.1 us -> 21.8 us
  other arithmetic: 8.3 us -> 9.6 us
    ppermute x2, waiting for transfers between devices: 4.75 us -> 0.01 us  [halos(): hi = lax.ppermute(cells[:, :1], AXES, [(i + 1, i) for i in range(ends)])]
    ppermute x2, waiting for transfers between devices: 8.04 us -> 3.57 us  [halos(): lo = lax.ppermute(cells[:, last:], AXES, [(i, i + 1) for i in range(ends)])]
    pallas_call x2 -> x3, Pallas kernels: 18.1 us -> 21.8 us  [relax_sweep(): pl.pallas_call(functools.partial(_relax_kernel, plane_of), grid=(count,),...]
    concatenate x0 -> x1, other arithmetic: none -> 1.5 us  [on_device(): first = jnp.concatenate([ends[0:1], inner, ends[1:2]], axis=0)]
  transfers between devices with their start and end apart: 5 -> 5, of which waited for: 2 -> 1; matrix products, arithmetic and copies ran while one was open for 17% -> 19% of each run, Pallas kernels for 0% -> 6%
where the time goes in v13:
time: 102 us; the launch traced here: 101 us
  starting transfers between devices  25.6 us (25%)
  Pallas kernels  21.8 us (21%)
  blocking collectives  19.4 us (19%)
  local copies, waits for them, and re-layouts  13.6 us (13%)
  other arithmetic  9.6 us (9%)
  matrix products  6.45 us (6%)
  waiting for transfers between devices  3.58 us (4%)
  between operations  1.1 us (1%)
    pallas_call x3, Pallas kernels, relax_sweep(): pl.pallas_call(functools.partial(_relax_kernel, plane_of), grid=(count,),...  21.8 us
    all_to_all x1, blocking collectives, on_device(): lax.all_to_all(send.reshape(devices, (capacity + 1) * seg), AXES, 0, 0, t...  19.4 us
    ppermute x2, starting transfers between devices, halos(): hi = lax.ppermute(cells[:, :1], AXES, [(i + 1, i) for i in range(ends)])  11 us
    all_to_all x1, starting transfers between devices, on_device(): got = lax.all_to_all(sent, AXES, 0, 0, tiled=True)  10.4 us
    dot_general x1, matrix products, on_device(): jnp.einsum('bij,cbj->cbi', inverse_blocks, jnp.stack([fixed_rhs, unit]),...  4.43 us
    ppermute x2, starting transfers between devices, halos(): lo = lax.ppermute(cells[:, last:], AXES, [(i, i + 1) for i in range(ends)])  4.15 us
    ppermute x2, waiting for transfers between devices, halos(): lo = lax.ppermute(cells[:, last:], AXES, [(i, i + 1) for i in range(ends)])  3.57 us
    unnamed x26, local copies, waits for them, and re-layouts  3.21 us
  transfers between devices with their start and end apart: 5, of which 1 were waited for; matrix products, arithmetic and copies ran while one was open for 19% of the time, Pallas kernels for 6%

profile of v13, /device:TPU:8, one launch (start us, length us, event | category | flops | bytes accessed | tf_op | source)
XLA Modules:
  0.0 101.1 jit_solution(15729953766038135830)
XLA Ops:
  0.6 0.9 slice_reduce_fusion.2
  1.6 1.0 %slice_reduce_fusion.1 = f32[128]{0:T(128)S(1)} fusion(f32[128,128]{1,0:T(8,128)} %param.14), kind=kLoop, calls=%fused_computation.36 | loop fusion | bytes 1024 | tf_op jit(solution)/shard_map/slice | solution.py:180
  2.6 0.7 and_select_fusion.4
  3.4 1.0 %slice.90 = bf16[128,1,128]{2,1,0:T(2,128)(2,1)S(1)} slice(bf16[128,128,128]{2,1,0:T(8,128)(2,1)} %param.18), slice={[0:128], [127:128], [0:128]} | slice | bytes 65536 | tf_op jit(solution)/shard_map/slice | solution.py:170
  4.4 0.9 multiply_reduce_fusion
  5.3 0.1 slice_reduce_fusion
  5.5 0.7 stack.32
  6.2 1.0 broadcast_in_dim.124
  7.1 10.4 %all-to-all-start = ((f32[128,1,768]{2,1,0:T(1,128)}), f32[128,1,768]{2,1,0:T(1,128)S(1)}, u32[]{:S(2)}, u32[]{:S(2)}) async-start(f32[128,1,768]{2,1,0:T(1,128)} %broadcast_in_dim.124), calls=%async_computation | async-start | bytes 786432 | tf_op jit(solution)/shard_map/all_to_all | solution.py:185
  17.6 0.0 copy-start.4
  17.6 0.0 copy-start.12
  17.6 0.0 copy-start.10
  17.6 0.0 copy-start.11
  17.6 3.0 %pad_maximum_fusion.1 = (f32[2,1,256,512]{3,2,1,0:T(8,128)}, f32[2,1,256,512]{3,2,1,0:T(8,128)}) fusion(f32[1,4,256,512]{3,2,1,0:T(8,128)} %bitcast.106, f32[1,4,256,512]{3,2,1,0:T(8,128)} %bitcast.107), kind=kLoop, calls=%fused_computation.14 | loop fusion | flops 524288 | bytes 6291456 | tf_op jit(solution)/shard_map/stack | solution.py:238
  20.6 7.1 %collective-permute-start.1 = (f32[2,1,256,512]{3,2,1,0:T(8,128)}, f32[2,1,256,512]{3,2,1,0:T(8,128)S(1)}, u32[]{:S(2)}, u32[]{:S(2)}) collective-permute-start(f32[2,1,256,512]{3,2,1,0:T(8,128)} %get-tuple-element.8), channel_id=1, source_target_pairs={{1,0},{2,1},{3,2},{4,3},{5,4},{6,5},{7,6},{8,7},{9,8},{10,9},{11,1... | collective-permute-start | bytes 3145736 | tf_op jit(solution)/shard_map/ppermute | solution.py:128
  27.7 1.9 %collective-permute-start = (f32[2,1,256,512]{3,2,1,0:T(8,128)}, f32[2,1,256,512]{3,2,1,0:T(8,128)S(1)}, u32[]{:S(2)}, u32[]{:S(2)}) collective-permute-start(f32[2,1,256,512]{3,2,1,0:T(8,128)} %get-tuple-element.9), channel_id=1, source_target_pairs={{0,1},{1,2},{2,3},{3,4},{4,5},{5,6},{6,7},{7,8},{8,9},{9,10},{10,1... | collective-permute-start | bytes 3145736 | tf_op jit(solution)/shard_map/ppermute | solution.py:127
  29.7 0.0 copy-done.12
  29.7 0.2 convert_reduce_fusion
  29.9 0.1 select_reduce_fusion.1
  30.1 0.1 copy.41
  30.2 0.1 convert_element_type.127
  30.3 0.1 copy.46
  30.5 4.4 %convolution_bitcast_fusion = f32[2,128,128]{2,0,1:T(2,128)S(1)} fusion(bf16[128,128,128]{2,1,0:T(8,128)(2,1)} %param.18, bf16[1,128,128]{2,0,1:T(2,128)(2,1)S(1)} %stack_broadcast_in_dim.2, bf16[1,128,128]{2,0,1:T(2,128)(2,1)S(1)} %copy.41), kind=kOutput, calls=%fused_computation.8 | convolution fusion | flops 8519680 | bytes 4390912 | tf_op jit(solution)/shard_map/bij,cbj->cbi/dot_general | solution.py:162
  34.9 0.0 copy-start.6
  35.0 0.1 fusion.42
  35.1 0.0 all-to-all-done
  35.1 0.4 copy.54
  35.5 0.4 fusion
  35.9 0.4 fusion.1
  36.4 0.4 fusion.2
  36.8 0.1 multiply_add_fusion
  36.9 0.0 copy-done.7
  36.9 0.0 copy-done.8
  36.9 0.0 copy-start.5
  37.0 0.2 convolution_convert_fusion
  37.1 0.1 fusion.21
  37.3 0.1 fusion.23
  37.4 0.1 fusion.25
  37.6 0.2 fusion.5
  37.8 0.1 copy.45
  37.9 0.2 copy.47
  38.1 19.4 %all_to_all.18 = f32[128,1,384]{2,1,0:T(1,128)S(1)} all-to-all(f32[128,1,384]{2,1,0:T(1,128)S(1)} %copy.47), channel_id=1, replica_groups=mesh['grp'=4,'slab'=32] {'grp','slab'}, dimensions={0} | all-to-all | bytes 393216 | tf_op jit(solution)/shard_map/all_to_all | solution.py:230
  57.5 0.2 copy.48
  57.7 0.1 copy.50
  57.8 0.1 copy.49
  57.9 0.1 reshape.229
  58.0 2.8 %scatter_custom_fusion = f32[4096,128]{1,0:T(8,128)} fusion(s32[256]{0:T(256)S(1)} %reshape.229, f32[256,128]{1,0:T(8,128)S(1)} %bitcast.118, f32[]{:T(128)} %constant.58.clone.1), kind=kCustom, calls=%fused_computation.16 | custom fusion | flops 32768 | bytes 2097156 | tf_op jit(solution)/shard_map/scatter-add | solution.py:236
  60.9 2.8 %reshape.221.leak = f32[4,256,512]{2,1,0:T(8,128)} reshape(f32[4096,128]{1,0:T(8,128)} %scatter_custom_fusion) | data formatting | bytes 4194304 | tf_op jit(solution)/shard_map/reshape | solution.py:237
  63.6 0.0 collective-permute-done.1.p_hi.k_hi
  63.6 0.0 collective-permute-done.p_lo.k_lo
  63.6 1.0 copy-done
  64.6 1.0 %copy-done.1 = f32[2,1,256,512]{3,2,1,0:T(8,128)} copy-done((f32[2,1,256,512]{3,2,1,0:T(8,128)}, f32[2,1,256,512]{3,2,1,0:T(8,128)S(1)}, u32[]{:S(2)}) %copy-start.1) | copy-done | bytes 1048600
  65.6 6.4 %shard_map.149 = f32[2,256,512]{2,1,0:T(8,128)} custom-call(f32[4,256,512]{2,1,0:T(8,128)} %p_ref.3, f32[2,1,256,512]{3,2,1,0:T(8,128)} %copy-done.1, f32[2,1,256,512]{3,2,1,0:T(8,128)} %copy-done, f32[4,256,512]{2,1,0:T(8,128)} %k_ref.5, f32[2,1,256,512]{3,2,1,0:T(8,128)} %copy-done.1, f32[2,1,256,512]{3,2,1,0:T(8,128)} %copy-done, f32[4,256,512]{2,1,0:T(8,128)} %base.5, ...), custom_call_target="tpu_custom_call" | custom-call | tf_op jit(solution)/shard_map/pallas_call | solution.py:114
  72.0 1.3 %fusion.40 = (f32[1,1,256,512]{3,2,1,0:T(8,128)S(1)}, f32[1,1,256,512]{3,2,1,0:T(8,128)S(1)}) fusion(f32[1,2,256,512]{3,2,1,0:T(8,128)} %bitcast.108), kind=kLoop, calls=%fused_computation.96 | loop fusion | bytes 2097152 | tf_op jit(solution)/shard_map/slice | solution.py:128
  73.3 3.9 %collective-permute-start.3 = (f32[1,1,256,512]{3,2,1,0:T(8,128)S(1)}, f32[1,1,256,512]{3,2,1,0:T(8,128)}, u32[]{:S(2)}, u32[]{:S(2)}) collective-permute-start(f32[1,1,256,512]{3,2,1,0:T(8,128)S(1)} %get-tuple-element.10), channel_id=1, source_target_pairs={{1,0},{2,1},{3,2},{4,3},{5,4},{6,5},{7,6},{8,7},{9,8},{10,9},{11,1... | collective-permute-start | bytes 1572872 | tf_op jit(solution)/shard_map/ppermute | solution.py:128
  77.1 0.0 copy-start.2
  77.1 2.2 %collective-permute-start.2 = (f32[1,1,256,512]{3,2,1,0:T(8,128)S(1)}, f32[1,1,256,512]{3,2,1,0:T(8,128)}, u32[]{:S(2)}, u32[]{:S(2)}) collective-permute-start(f32[1,1,256,512]{3,2,1,0:T(8,128)S(1)} %get-tuple-element.11), channel_id=1, source_target_pairs={{0,1},{1,2},{2,3},{3,4},{4,5},{5,6},{6,7},{7,8},{8,9},{9,10},{10,1... | collective-permute-start | bytes 1572872 | tf_op jit(solution)/shard_map/ppermute | solution.py:127
  79.4 6.4 %shard_map.150 = f32[2,256,512]{2,1,0:T(8,128)} custom-call(f32[4,256,512]{2,1,0:T(8,128)} %p_ref.3, f32[2,1,256,512]{3,2,1,0:T(8,128)} %copy-done.1, f32[2,1,256,512]{3,2,1,0:T(8,128)} %copy-done, f32[4,256,512]{2,1,0:T(8,128)} %k_ref.5, f32[2,1,256,512]{3,2,1,0:T(8,128)} %copy-done.1, f32[2,1,256,512]{3,2,1,0:T(8,128)} %copy-done, f32[4,256,512]{2,1,0:T(8,128)} %base.5, ...), custom_call_target="tpu_custom_call" | custom-call | tf_op jit(solution)/shard_map/pallas_call | solution.py:114
  85.8 0.1 fusion.41
  85.9 1.1 %copy-done.3 = f32[2,256,512]{2,1,0:T(8,128)S(1)} copy-done((f32[2,256,512]{2,1,0:T(8,128)S(1)}, f32[2,256,512]{2,1,0:T(8,128)}, u32[]{:S(2)}) %copy-start.3) | copy-done | bytes 1048600
  87.0 1.5 %pad_maximum_fusion.p_ref = f32[4,256,512]{2,1,0:T(8,128)} fusion(f32[1,256,512]{2,1,0:T(8,128)S(1)} %get-tuple-element.13, f32[2,256,512]{2,1,0:T(8,128)S(1)} %copy-done.3, f32[1,256,512]{2,1,0:T(8,128)S(1)} %get-tuple-element.12), kind=kLoop, calls=%fused_computation.1 | loop fusion | flops 1048576 | bytes 4194304 | tf_op jit(solution)/shard_map/concatenate | solution.py:244
  88.5 0.0 collective-permute-done.3.p_hi
  88.5 3.6 %collective-permute-done.2.p_lo = f32[1,1,256,512]{3,2,1,0:T(8,128)} collective-permute-done((f32[1,1,256,512]{3,2,1,0:T(8,128)S(1)}, f32[1,1,256,512]{3,2,1,0:T(8,128)}, u32[]{:S(2)}, u32[]{:S(2)}) %collective-permute-start.2) | collective-permute-done | bytes 524320 | tf_op jit(solution)/shard_map/ppermute | solution.py:127
  92.1 9.0 %shard_map.151 = f32[4,256,512]{2,1,0:T(8,128)} custom-call(f32[4,256,512]{2,1,0:T(8,128)} %pad_maximum_fusion.p_ref, f32[1,1,256,512]{3,2,1,0:T(8,128)} %collective-permute-done.2.p_lo, f32[1,1,256,512]{3,2,1,0:T(8,128)} %collective-permute-done.3.p_hi, f32[4,256,512]{2,1,0:T(8,128)} %k_ref.5, f32[2,1,256,512]{3,2,1,0:T(8,128)} %copy-done.1, ...), custom_call_target="tpu_custom_call" | custom-call | tf_op jit(solution)/shard_map/pallas_call | solution.py:114
  (33 shorter events, 0.2 us)
Async XLA Ops:
  7.1 28.0 %all-to-all-start = ((f32[128,1,768]{2,1,0:T(1,128)}), f32[128,1,768]{2,1,0:T(1,128)S(1)}, u32[]{:S(2)}, u32[]{:S(2)}) async-start(f32[128,1,768]{2,1,0:T(1,128)} %broadcast_in_dim.124), calls=%async_computation | async-start | bytes 786432 | tf_op jit(solution)/shard_map/all_to_all | solution.py:185
  17.6 12.1 %copy-start.4 = (f32[128,128]{1,0:T(8,128)S(1)}, f32[128,128]{1,0:T(8,128)}, u32[]{:S(2)}) copy-start(f32[128,128]{1,0:T(8,128)} %param.15) | copy-start | bytes 196612
  17.6 12.1 %copy-start.12 = (s32[128,1]{0,1:T(1,128)S(1)}, s32[128,1]{0,1:T(1,128)}, u32[]{:S(2)}) copy-start(s32[128,1]{0,1:T(1,128)} %param.21) | copy-start | bytes 1540
  17.6 12.3 %copy-start.10 = (s32[128]{0:T(128)S(1)}, s32[128]{0:T(128)}, u32[]{:S(2)}) copy-start(s32[128]{0:T(128)} %param.23) | copy-start | bytes 1540
  17.6 12.3 %copy-start.11 = (s32[128]{0:T(128)S(1)}, s32[128]{0:T(128)}, u32[]{:S(2)}) copy-start(s32[128]{0:T(128)} %param.22) | copy-start | bytes 1540
  20.6 43.0 %collective-permute-start.1 = (f32[2,1,256,512]{3,2,1,0:T(8,128)}, f32[2,1,256,512]{3,2,1,0:T(8,128)S(1)}, u32[]{:S(2)}, u32[]{:S(2)}) collective-permute-start(f32[2,1,256,512]{3,2,1,0:T(8,128)} %get-tuple-element.8), channel_id=1, source_target_pairs={{1,0},{2,1},{3,2},{4,3},{5,4},{6,5},{7,6},{8,7},{9,8},{10,9},{11,1... | collective-permute-start | bytes 3145736 | tf_op jit(solution)/shard_map/ppermute | solution.py:128
  27.7 35.9 %collective-permute-start = (f32[2,1,256,512]{3,2,1,0:T(8,128)}, f32[2,1,256,512]{3,2,1,0:T(8,128)S(1)}, u32[]{:S(2)}, u32[]{:S(2)}) collective-permute-start(f32[2,1,256,512]{3,2,1,0:T(8,128)} %get-tuple-element.9), channel_id=1, source_target_pairs={{0,1},{1,2},{2,3},{3,4},{4,5},{5,6},{6,7},{7,8},{8,9},{9,10},{10,1... | collective-permute-start | bytes 3145736 | tf_op jit(solution)/shard_map/ppermute | solution.py:127
  34.9 1.9 %copy-start.9 = (f32[128]{0:T(128)S(1)}, f32[128]{0:T(128)}, u32[]{:S(2)}) copy-start(f32[128]{0:T(128)} %param.16) | copy-start | bytes 1540
  34.9 2.0 %copy-start.7 = (f32[128,128]{1,0:T(8,128)S(1)}, f32[128,128]{1,0:T(8,128)}, u32[]{:S(2)}) copy-start(f32[128,128]{1,0:T(8,128)} %param.19) | copy-start | bytes 196612
  34.9 2.0 %copy-start.8 = (f32[128,128]{1,0:T(8,128)S(1)}, f32[128,128]{1,0:T(8,128)}, u32[]{:S(2)}) copy-start(f32[128,128]{1,0:T(8,128)} %param.20) | copy-start | bytes 196612
  34.9 2.2 %copy-start.6 = (bf16[4,128,128]{2,1,0:T(8,128)(2,1)S(1)}, bf16[4,128,128]{2,1,0:T(8,128)(2,1)}, u32[]{:S(2)}) copy-start(bf16[4,128,128]{2,1,0:T(8,128)(2,1)} %param.24) | copy-start | bytes 393220
  36.9 23.9 %copy-start.5 = (f32[128,128]{1,0:T(8,128)}, f32[128,128]{1,0:T(8,128)S(1)}, u32[]{:S(2)}) copy-start(f32[128,128]{1,0:T(8,128)S(1)} %multiply_add_fusion) | copy-start | bytes 196612
  63.6 1.0 copy-start
  64.6 1.0 %copy-start.1 = (f32[2,1,256,512]{3,2,1,0:T(8,128)}, f32[2,1,256,512]{3,2,1,0:T(8,128)S(1)}, u32[]{:S(2)}) copy-start(f32[2,1,256,512]{3,2,1,0:T(8,128)S(1)} %collective-permute-done.p_lo.k_lo) | copy-start | bytes 3145732
  73.3 15.3 %collective-permute-start.3 = (f32[1,1,256,512]{3,2,1,0:T(8,128)S(1)}, f32[1,1,256,512]{3,2,1,0:T(8,128)}, u32[]{:S(2)}, u32[]{:S(2)}) collective-permute-start(f32[1,1,256,512]{3,2,1,0:T(8,128)S(1)} %get-tuple-element.10), channel_id=1, source_target_pairs={{1,0},{2,1},{3,2},{4,3},{5,4},{6,5},{7,6},{8,7},{9,8},{10,9},{11,1... | collective-permute-start | bytes 1572872 | tf_op jit(solution)/shard_map/ppermute | solution.py:128
  77.1 8.7 %copy-start.2 = (f32[2,256,512]{2,1,0:T(8,128)S(1)}, f32[2,256,512]{2,1,0:T(8,128)}, u32[]{:S(2)}) copy-start(f32[2,256,512]{2,1,0:T(8,128)} %shard_map.149) | copy-start | bytes 3145732
  77.1 15.0 %collective-permute-start.2 = (f32[1,1,256,512]{3,2,1,0:T(8,128)S(1)}, f32[1,1,256,512]{3,2,1,0:T(8,128)}, u32[]{:S(2)}, u32[]{:S(2)}) collective-permute-start(f32[1,1,256,512]{3,2,1,0:T(8,128)S(1)} %get-tuple-element.11), channel_id=1, source_target_pairs={{0,1},{1,2},{2,3},{3,4},{4,5},{5,6},{6,7},{7,8},{8,9},{9,10},{10,1... | collective-permute-start | bytes 1572872 | tf_op jit(solution)/shard_map/ppermute | solution.py:127
  85.8 1.2 %copy-start.3 = (f32[2,256,512]{2,1,0:T(8,128)S(1)}, f32[2,256,512]{2,1,0:T(8,128)}, u32[]{:S(2)}) copy-start(f32[2,256,512]{2,1,0:T(8,128)} %shard_map.150) | copy-start | bytes 3145732

commit v14 on v13

--- a/solution.py
+++ b/solution.py
@@ -61,7 +61,7 @@
     return numerator, denominator
 
 
-def _relax_kernel(plane_of, p_ref, p_lo, p_hi, k_ref, k_lo, k_hi, base, leak, out):
+def _relax_kernel(plane_of, mode, p_ref, p_lo, p_hi, k_ref, k_lo, k_hi, base, leak, *rest):
     z = plane_of(pl.program_id(0))
     top = p_ref.shape[0] - 1
     p = p_ref[z]
@@ -98,11 +98,19 @@
     for p_side, k_side in sides:
         facing = 0.5 * (k + k_side)
         numerator = numerator + facing * p_side
-        denominator = denominator + facing
+        if mode == 0:
+            denominator = denominator + facing
+    if mode == 0:
+        out, den = rest
+        den[0] = denominator
+    else:
+        den_ends, den_inner, out = rest
+        on_edge = (z == 0) | (z == top)
+        denominator = jnp.where(on_edge, den_ends[0], den_inner[0])
     out[0] = numerator / denominator
 
 
-def relax_sweep(p, p_lo, p_hi, p_at, k, k_lo, k_hi, k_at, base, leak, plane_of, count):
+def relax_sweep(p, p_lo, p_hi, p_at, k, k_lo, k_hi, k_at, base, leak, plane_of, count, dens=None):
     planes, rows, cols = base.shape
     whole = pl.BlockSpec((planes, rows, cols), lambda z: (0, 0, 0))
     plane = pl.BlockSpec((1, rows, cols), lambda z: (plane_of(z), 0, 0))
@@ -111,13 +119,29 @@
     def edge(at):
         return pl.BlockSpec((None, 1, rows, cols), lambda z: (at, 0, 0, 0))
 
+    specs = [whole, edge(p_at), edge(p_at), whole, edge(k_at), edge(k_at), plane, plane]
+    shape = jax.ShapeDtypeStruct((count, rows, cols), jnp.float32)
+    operands = (p, p_lo, p_hi, k, k_lo, k_hi, base, leak)
+    if dens is None:
+        return pl.pallas_call(
+            functools.partial(_relax_kernel, plane_of, 0),
+            grid=(count,),
+            in_specs=specs,
+            out_specs=(step, step),
+            out_shape=(shape, shape),
+        )(*operands)
+    top = planes - 1
+    end_at = pl.BlockSpec((1, rows, cols), lambda z: (jnp.minimum(plane_of(z), 1), 0, 0))
+    inner_at = pl.BlockSpec(
+        (1, rows, cols), lambda z: (jnp.clip(plane_of(z) - 1, 0, top - 2), 0, 0)
+    )
     return pl.pallas_call(
-        functools.partial(_relax_kernel, plane_of),
+        functools.partial(_relax_kernel, plane_of, 1),
         grid=(count,),
-        in_specs=[whole, edge(p_at), edge(p_at), whole, edge(k_at), edge(k_at), plane, plane],
+        in_specs=specs + [end_at, inner_at],
         out_specs=step,
-        out_shape=jax.ShapeDtypeStruct((count, rows, cols), jnp.float32),
-    )(p, p_lo, p_hi, k, k_lo, k_hi, base, leak)
+        out_shape=shape,
+    )(*operands, *dens)
 
 
 def halos(cells):
@@ -238,13 +262,13 @@
     lo, hi = halos(jnp.stack([tissue_start, conduct]))
     planes = base_source.shape[0]
     args = (tissue_start, lo, hi, 0, conduct, lo, hi, 1, base_source, leak_field)
-    ends = relax_sweep(*args, lambda z: z * (planes - 1), 2)
+    ends, den_ends = relax_sweep(*args, lambda z: z * (planes - 1), 2)
     first_lo, first_hi = halos(ends[None])
-    inner = relax_sweep(*args, lambda z: z + 1, planes - 2)
+    inner, den_inner = relax_sweep(*args, lambda z: z + 1, planes - 2)
     first = jnp.concatenate([ends[0:1], inner, ends[1:2]], axis=0)
     tissue = relax_sweep(
         first, first_lo, first_hi, 0, conduct, lo, hi, 1, base_source, leak_field,
-        lambda z: z, planes,
+        lambda z: z, planes, (den_ends, den_inner),
     )
     return (pressure, tissue)
 

time: 102 us -> 105 us (1.029)
  local copies, waits for them, and re-layouts: 13.6 us -> 15.6 us
  Pallas kernels: 21.8 us -> 22.9 us
    pallas_call x3, Pallas kernels: 21.8 us -> 22.9 us  [the longest x2 13.3 us: relax_sweep(): pl.pallas_call(functools.partial(_relax_kernel, plane_of, 0), grid=(count...]
    slice x1, local copies, waits for them, and re-layouts: 1.27 us -> 2.34 us  [halos(): hi = lax.ppermute(cells[:, :1], AXES, [(i + 1, i) for i in range(ends)])]
    unnamed x26 -> x30, local copies, waits for them, and re-layouts: 3.21 us -> 4.07 us
  transfers between devices with their start and end apart: 5 -> 5, of which waited for: 1 -> 1; matrix products, arithmetic and copies ran while one was open for 19% -> 18% of each run, Pallas kernels for 6% -> 6%
where the time goes in v14:
time: 105 us; the launch traced here: 104 us
  starting transfers between devices  25.5 us (24%)
  Pallas kernels  22.9 us (22%)
  blocking collectives  19.4 us (18%)
  local copies, waits for them, and re-layouts  15.6 us (15%)
  other arithmetic  9.77 us (9%)
  matrix products  6.45 us (6%)
  waiting for transfers between devices  3.41 us (3%)
  between operations  1.11 us (1%)
    all_to_all x1, blocking collectives, on_device(): lax.all_to_all(send.reshape(devices, (capacity + 1) * seg), AXES, 0, 0, t...  19.4 us
    pallas_call x2, Pallas kernels, relax_sweep(): pl.pallas_call(functools.partial(_relax_kernel, plane_of, 0), grid=(count...  13.3 us
    ppermute x2, starting transfers between devices, halos(): hi = lax.ppermute(cells[:, :1], AXES, [(i + 1, i) for i in range(ends)])  10.9 us
    all_to_all x1, starting transfers between devices, on_device(): got = lax.all_to_all(sent, AXES, 0, 0, tiled=True)  10.4 us
    pallas_call x1, Pallas kernels, relax_sweep(): pl.pallas_call(functools.partial(_relax_kernel, plane_of, 1), grid=(count...  9.61 us
    dot_general x1, matrix products, on_device(): jnp.einsum('bij,cbj->cbi', inverse_blocks, jnp.stack([fixed_rhs, unit]),...  4.43 us
    ppermute x2, starting transfers between devices, halos(): lo = lax.ppermute(cells[:, last:], AXES, [(i, i + 1) for i in range(ends)])  4.15 us
    unnamed x30, local copies, waits for them, and re-layouts  4.07 us
  transfers between devices with their start and end apart: 5, of which 1 were waited for; matrix products, arithmetic and copies ran while one was open for 18% of the time, Pallas kernels for 6%

profile of v14, /device:TPU:8, one launch (start us, length us, event | category | flops | bytes accessed | tf_op | source)
XLA Modules:
  0.0 104.1 jit_solution(2572291651992969798)
XLA Ops:
  0.6 0.9 slice_reduce_fusion.2
  1.6 1.0 slice_reduce_fusion.1
  2.6 0.7 and_select_fusion.4
  3.4 1.0 slice.90
  4.4 0.9 multiply_reduce_fusion
  5.3 0.1 slice_reduce_fusion
  5.5 0.7 stack.32
  6.2 1.0 broadcast_in_dim.124
  7.1 10.4 %all-to-all-start = ((f32[128,1,768]{2,1,0:T(1,128)}), f32[128,1,768]{2,1,0:T(1,128)S(1)}, u32[]{:S(2)}, u32[]{:S(2)}) async-start(f32[128,1,768]{2,1,0:T(1,128)} %broadcast_in_dim.124), calls=%async_computation | async-start | bytes 786432 | tf_op jit(solution)/shard_map/all_to_all | solution.py:209
  17.6 0.0 copy-start.4
  17.6 0.0 copy-start.14
  17.6 0.0 copy-start.12
  17.6 0.0 copy-start.13
  17.6 3.0 %pad_maximum_fusion.1 = (f32[2,1,256,512]{3,2,1,0:T(8,128)}, f32[2,1,256,512]{3,2,1,0:T(8,128)}) fusion(f32[1,4,256,512]{3,2,1,0:T(8,128)} %bitcast.106, f32[1,4,256,512]{3,2,1,0:T(8,128)} %bitcast.107), kind=kLoop, calls=%fused_computation.14 | loop fusion | flops 524288 | bytes 6291456 | tf_op jit(solution)/shard_map/stack | solution.py:262
  20.6 7.1 %collective-permute-start.1 = (f32[2,1,256,512]{3,2,1,0:T(8,128)}, f32[2,1,256,512]{3,2,1,0:T(8,128)S(1)}, u32[]{:S(2)}, u32[]{:S(2)}) collective-permute-start(f32[2,1,256,512]{3,2,1,0:T(8,128)} %get-tuple-element.16), channel_id=1, source_target_pairs={{1,0},{2,1},{3,2},{4,3},{5,4},{6,5},{7,6},{8,7},{9,8},{10,9},{11,1... | collective-permute-start | bytes 3145736 | tf_op jit(solution)/shard_map/ppermute | solution.py:152
  27.7 1.9 %collective-permute-start = (f32[2,1,256,512]{3,2,1,0:T(8,128)}, f32[2,1,256,512]{3,2,1,0:T(8,128)S(1)}, u32[]{:S(2)}, u32[]{:S(2)}) collective-permute-start(f32[2,1,256,512]{3,2,1,0:T(8,128)} %get-tuple-element.17), channel_id=1, source_target_pairs={{0,1},{1,2},{2,3},{3,4},{4,5},{5,6},{6,7},{7,8},{8,9},{9,10},{10,1... | collective-permute-start | bytes 3145736 | tf_op jit(solution)/shard_map/ppermute | solution.py:151
  29.7 0.0 copy-done.14
  29.7 0.2 convert_reduce_fusion
  29.9 0.1 select_reduce_fusion.1
  30.1 0.1 copy.41
  30.2 0.1 convert_element_type.127
  30.3 0.1 copy.46
  30.5 4.4 %convolution_bitcast_fusion = f32[2,128,128]{2,0,1:T(2,128)S(1)} fusion(bf16[128,128,128]{2,1,0:T(8,128)(2,1)} %param.18, bf16[1,128,128]{2,0,1:T(2,128)(2,1)S(1)} %stack_broadcast_in_dim.2, bf16[1,128,128]{2,0,1:T(2,128)(2,1)S(1)} %copy.41), kind=kOutput, calls=%fused_computation.8 | convolution fusion | flops 8519680 | bytes 4390912 | tf_op jit(solution)/shard_map/bij,cbj->cbi/dot_general | solution.py:186
  34.9 0.0 copy-start.8
  35.0 0.1 fusion.42
  35.1 0.0 all-to-all-done
  35.1 0.4 copy.54
  35.5 0.4 fusion
  35.9 0.4 fusion.1
  36.4 0.4 fusion.2
  36.8 0.1 multiply_add_fusion
  36.9 0.0 copy-done.9
  36.9 0.0 copy-start.7
  37.0 0.2 convolution_convert_fusion
  37.1 0.1 fusion.21
  37.3 0.1 fusion.23
  37.4 0.1 fusion.25
  37.6 0.2 fusion.5
  37.8 0.1 copy.45
  37.9 0.2 copy.47
  38.1 19.4 %all_to_all.18 = f32[128,1,384]{2,1,0:T(1,128)S(1)} all-to-all(f32[128,1,384]{2,1,0:T(1,128)S(1)} %copy.47), channel_id=1, replica_groups=mesh['grp'=4,'slab'=32] {'grp','slab'}, dimensions={0} | all-to-all | bytes 393216 | tf_op jit(solution)/shard_map/all_to_all | solution.py:254
  57.5 0.2 copy.48
  57.7 0.1 copy.50
  57.8 0.1 copy.49
  57.9 0.1 reshape.229
  58.0 3.0 %scatter_custom_fusion = f32[4096,128]{1,0:T(8,128)} fusion(s32[256]{0:T(256)S(1)} %reshape.229, f32[256,128]{1,0:T(8,128)S(1)} %bitcast.118, f32[]{:T(128)} %constant.58.clone.1), kind=kCustom, calls=%fused_computation.16 | custom fusion | flops 32768 | bytes 2097156 | tf_op jit(solution)/shard_map/scatter-add | solution.py:260
  61.0 2.8 %reshape.221.leak = f32[4,256,512]{2,1,0:T(8,128)} reshape(f32[4096,128]{1,0:T(8,128)} %scatter_custom_fusion) | data formatting | bytes 4194304 | tf_op jit(solution)/shard_map/reshape | solution.py:261
  63.8 0.0 collective-permute-done.1.p_hi.k_hi
  63.8 0.0 collective-permute-done.p_lo.k_lo
  63.8 1.0 copy-done
  64.8 1.0 copy-done.1
  65.8 6.6 %shard_map.149 = (f32[2,256,512]{2,1,0:T(8,128)}, f32[2,256,512]{2,1,0:T(8,128)}) custom-call(f32[4,256,512]{2,1,0:T(8,128)} %p_ref.3, f32[2,1,256,512]{3,2,1,0:T(8,128)} %copy-done.1, f32[2,1,256,512]{3,2,1,0:T(8,128)} %copy-done, f32[4,256,512]{2,1,0:T(8,128)} %k_ref.5, f32[2,1,256,512]{3,2,1,0:T(8,128)} %copy-done.1, f32[2,1,256,512]{3,2,1,0:T(8,128)} %copy-done, ...), custom_call_target="tpu_custom_call" | custom-call | tf_op jit(solution)/shard_map/pallas_call | solution.py:126
  72.4 2.3 %fusion.40 = (f32[1,1,256,512]{3,2,1,0:T(8,128)}, f32[1,1,256,512]{3,2,1,0:T(8,128)}) fusion(f32[1,2,256,512]{3,2,1,0:T(8,128)} %bitcast.111), kind=kLoop, calls=%fused_computation.96 | loop fusion | bytes 2097152 | tf_op jit(solution)/shard_map/slice | solution.py:152
  74.7 3.8 %collective-permute-start.3 = (f32[1,1,256,512]{3,2,1,0:T(8,128)}, f32[1,1,256,512]{3,2,1,0:T(8,128)S(1)}, u32[]{:S(2)}, u32[]{:S(2)}) collective-permute-start(f32[1,1,256,512]{3,2,1,0:T(8,128)} %get-tuple-element.18), channel_id=1, source_target_pairs={{1,0},{2,1},{3,2},{4,3},{5,4},{6,5},{7,6},{8,7},{9,8},{10,9},{11,1... | collective-permute-start | bytes 1572872 | tf_op jit(solution)/shard_map/ppermute | solution.py:152
  78.5 0.0 copy-start.2
  78.5 2.2 %collective-permute-start.2 = (f32[1,1,256,512]{3,2,1,0:T(8,128)}, f32[1,1,256,512]{3,2,1,0:T(8,128)S(1)}, u32[]{:S(2)}, u32[]{:S(2)}) collective-permute-start(f32[1,1,256,512]{3,2,1,0:T(8,128)} %get-tuple-element.19), channel_id=1, source_target_pairs={{0,1},{1,2},{2,3},{3,4},{4,5},{5,6},{6,7},{7,8},{8,9},{9,10},{10,1... | collective-permute-start | bytes 1572872 | tf_op jit(solution)/shard_map/ppermute | solution.py:151
  80.8 6.7 %shard_map.150 = (f32[2,256,512]{2,1,0:T(8,128)}, f32[2,256,512]{2,1,0:T(8,128)}) custom-call(f32[4,256,512]{2,1,0:T(8,128)} %p_ref.3, f32[2,1,256,512]{3,2,1,0:T(8,128)} %copy-done.1, f32[2,1,256,512]{3,2,1,0:T(8,128)} %copy-done, f32[4,256,512]{2,1,0:T(8,128)} %k_ref.5, f32[2,1,256,512]{3,2,1,0:T(8,128)} %copy-done.1, f32[2,1,256,512]{3,2,1,0:T(8,128)} %copy-done, ...), custom_call_target="tpu_custom_call" | custom-call | tf_op jit(solution)/shard_map/pallas_call | solution.py:126
  87.5 0.1 fusion.41
  87.6 1.1 %copy-done.3 = f32[2,256,512]{2,1,0:T(8,128)S(1)} copy-done((f32[2,256,512]{2,1,0:T(8,128)S(1)}, f32[2,256,512]{2,1,0:T(8,128)}, u32[]{:S(2)}) %copy-start.3) | copy-done | bytes 1048600
  88.7 1.5 %pad_maximum_fusion.p_ref = f32[4,256,512]{2,1,0:T(8,128)} fusion(f32[1,256,512]{2,1,0:T(8,128)S(1)} %get-tuple-element.21, f32[2,256,512]{2,1,0:T(8,128)S(1)} %copy-done.3, f32[1,256,512]{2,1,0:T(8,128)S(1)} %get-tuple-element.20), kind=kLoop, calls=%fused_computation.1 | loop fusion | flops 1048576 | bytes 4194304 | tf_op jit(solution)/shard_map/concatenate | solution.py:268
  90.2 0.0 collective-permute-done.3.p_hi
  90.2 3.4 %collective-permute-done.2.p_lo = f32[1,1,256,512]{3,2,1,0:T(8,128)S(1)} collective-permute-done((f32[1,1,256,512]{3,2,1,0:T(8,128)}, f32[1,1,256,512]{3,2,1,0:T(8,128)S(1)}, u32[]{:S(2)}, u32[]{:S(2)}) %collective-permute-start.2) | collective-permute-done | bytes 524320 | tf_op jit(solution)/shard_map/ppermute | solution.py:151
  93.6 0.9 copy-done.6
  94.5 9.6 %shard_map.151 = f32[4,256,512]{2,1,0:T(8,128)} custom-call(f32[4,256,512]{2,1,0:T(8,128)} %pad_maximum_fusion.p_ref, f32[1,1,256,512]{3,2,1,0:T(8,128)} %copy-done.6, f32[1,1,256,512]{3,2,1,0:T(8,128)} %copy-done.5, f32[4,256,512]{2,1,0:T(8,128)} %k_ref.5, f32[2,1,256,512]{3,2,1,0:T(8,128)} %copy-done.1, f32[2,1,256,512]{3,2,1,0:T(8,128)} %copy-done, ...), custom_call_target="tpu_custom_call" | custom-call | tf_op jit(solution)/shard_map/pallas_call | solution.py:138
  (37 shorter events, 0.3 us)
Async XLA Ops:
  7.1 28.0 %all-to-all-start = ((f32[128,1,768]{2,1,0:T(1,128)}), f32[128,1,768]{2,1,0:T(1,128)S(1)}, u32[]{:S(2)}, u32[]{:S(2)}) async-start(f32[128,1,768]{2,1,0:T(1,128)} %broadcast_in_dim.124), calls=%async_computation | async-start | bytes 786432 | tf_op jit(solution)/shard_map/all_to_all | solution.py:209
  17.6 12.1 %copy-start.4 = (f32[128,128]{1,0:T(8,128)S(1)}, f32[128,128]{1,0:T(8,128)}, u32[]{:S(2)}) copy-start(f32[128,128]{1,0:T(8,128)} %param.15) | copy-start | bytes 196612
  17.6 12.1 %copy-start.14 = (s32[128,1]{0,1:T(1,128)S(1)}, s32[128,1]{0,1:T(1,128)}, u32[]{:S(2)}) copy-start(s32[128,1]{0,1:T(1,128)} %param.21) | copy-start | bytes 1540
  17.6 12.3 %copy-start.12 = (s32[128]{0:T(128)S(1)}, s32[128]{0:T(128)}, u32[]{:S(2)}) copy-start(s32[128]{0:T(128)} %param.23) | copy-start | bytes 1540
  17.6 12.3 %copy-start.13 = (s32[128]{0:T(128)S(1)}, s32[128]{0:T(128)}, u32[]{:S(2)}) copy-start(s32[128]{0:T(128)} %param.22) | copy-start | bytes 1540
  20.6 43.2 %collective-permute-start.1 = (f32[2,1,256,512]{3,2,1,0:T(8,128)}, f32[2,1,256,512]{3,2,1,0:T(8,128)S(1)}, u32[]{:S(2)}, u32[]{:S(2)}) collective-permute-start(f32[2,1,256,512]{3,2,1,0:T(8,128)} %get-tuple-element.16), channel_id=1, source_target_pairs={{1,0},{2,1},{3,2},{4,3},{5,4},{6,5},{7,6},{8,7},{9,8},{10,9},{11,1... | collective-permute-start | bytes 3145736 | tf_op jit(solution)/shard_map/ppermute | solution.py:152
  27.7 36.1 %collective-permute-start = (f32[2,1,256,512]{3,2,1,0:T(8,128)}, f32[2,1,256,512]{3,2,1,0:T(8,128)S(1)}, u32[]{:S(2)}, u32[]{:S(2)}) collective-permute-start(f32[2,1,256,512]{3,2,1,0:T(8,128)} %get-tuple-element.17), channel_id=1, source_target_pairs={{0,1},{1,2},{2,3},{3,4},{4,5},{5,6},{6,7},{7,8},{8,9},{9,10},{10,1... | collective-permute-start | bytes 3145736 | tf_op jit(solution)/shard_map/ppermute | solution.py:151
  34.9 1.9 %copy-start.11 = (f32[128]{0:T(128)S(1)}, f32[128]{0:T(128)}, u32[]{:S(2)}) copy-start(f32[128]{0:T(128)} %param.16) | copy-start | bytes 1540
  34.9 2.0 %copy-start.9 = (f32[128,128]{1,0:T(8,128)S(1)}, f32[128,128]{1,0:T(8,128)}, u32[]{:S(2)}) copy-start(f32[128,128]{1,0:T(8,128)} %param.19) | copy-start | bytes 196612
  34.9 2.0 %copy-start.10 = (f32[128,128]{1,0:T(8,128)S(1)}, f32[128,128]{1,0:T(8,128)}, u32[]{:S(2)}) copy-start(f32[128,128]{1,0:T(8,128)} %param.20) | copy-start | bytes 196612
  34.9 2.2 %copy-start.8 = (bf16[4,128,128]{2,1,0:T(8,128)(2,1)S(1)}, bf16[4,128,128]{2,1,0:T(8,128)(2,1)}, u32[]{:S(2)}) copy-start(bf16[4,128,128]{2,1,0:T(8,128)(2,1)} %param.24) | copy-start | bytes 393220
  36.9 24.1 %copy-start.7 = (f32[128,128]{1,0:T(8,128)}, f32[128,128]{1,0:T(8,128)S(1)}, u32[]{:S(2)}) copy-start(f32[128,128]{1,0:T(8,128)S(1)} %multiply_add_fusion) | copy-start | bytes 196612
  63.8 1.0 copy-start
  64.8 1.0 copy-start.1
  74.7 15.5 %collective-permute-start.3 = (f32[1,1,256,512]{3,2,1,0:T(8,128)}, f32[1,1,256,512]{3,2,1,0:T(8,128)S(1)}, u32[]{:S(2)}, u32[]{:S(2)}) collective-permute-start(f32[1,1,256,512]{3,2,1,0:T(8,128)} %get-tuple-element.18), channel_id=1, source_target_pairs={{1,0},{2,1},{3,2},{4,3},{5,4},{6,5},{7,6},{8,7},{9,8},{10,9},{11,1... | collective-permute-start | bytes 1572872 | tf_op jit(solution)/shard_map/ppermute | solution.py:152
  78.5 8.9 %copy-start.2 = (f32[2,256,512]{2,1,0:T(8,128)S(1)}, f32[2,256,512]{2,1,0:T(8,128)}, u32[]{:S(2)}) copy-start(f32[2,256,512]{2,1,0:T(8,128)} %get-tuple-element.6) | copy-start | bytes 3145732
  78.5 15.1 %collective-permute-start.2 = (f32[1,1,256,512]{3,2,1,0:T(8,128)}, f32[1,1,256,512]{3,2,1,0:T(8,128)S(1)}, u32[]{:S(2)}, u32[]{:S(2)}) collective-permute-start(f32[1,1,256,512]{3,2,1,0:T(8,128)} %get-tuple-element.19), channel_id=1, source_target_pairs={{0,1},{1,2},{2,3},{3,4},{4,5},{5,6},{6,7},{7,8},{8,9},{9,10},{10,1... | collective-permute-start | bytes 1572872 | tf_op jit(solution)/shard_map/ppermute | solution.py:151
  87.5 1.2 %copy-start.3 = (f32[2,256,512]{2,1,0:T(8,128)S(1)}, f32[2,256,512]{2,1,0:T(8,128)}, u32[]{:S(2)}) copy-start(f32[2,256,512]{2,1,0:T(8,128)} %get-tuple-element.7) | copy-start | bytes 3145732
  90.2 3.4 %copy-start.5 = (f32[1,1,256,512]{3,2,1,0:T(8,128)}, f32[1,1,256,512]{3,2,1,0:T(8,128)S(1)}, u32[]{:S(2)}) copy-start(f32[1,1,256,512]{3,2,1,0:T(8,128)S(1)} %collective-permute-done.3.p_hi) | copy-start | bytes 1572868
  93.6 0.9 copy-start.6

commit v15 on v13

--- a/solution.py
+++ b/solution.py
@@ -61,7 +61,8 @@
     return numerator, denominator
 
 
-def _relax_kernel(plane_of, p_ref, p_lo, p_hi, k_ref, k_lo, k_hi, base, leak, out):
+def _relax_kernel(plane_of, p_ref, p_lo, p_hi, k_ref, k_lo, k_hi, base, leak, *rest):
+    out = rest[-1]
     z = plane_of(pl.program_id(0))
     top = p_ref.shape[0] - 1
     p = p_ref[z]
@@ -102,22 +103,29 @@
     out[0] = numerator / denominator
 
 
-def relax_sweep(p, p_lo, p_hi, p_at, k, k_lo, k_hi, k_at, base, leak, plane_of, count):
+def relax_sweep(p, p_lo, p_hi, p_at, k, k_lo, k_hi, k_at, base, leak, plane_of, count, into=None):
     planes, rows, cols = base.shape
     whole = pl.BlockSpec((planes, rows, cols), lambda z: (0, 0, 0))
     plane = pl.BlockSpec((1, rows, cols), lambda z: (plane_of(z), 0, 0))
-    step = pl.BlockSpec((1, rows, cols), lambda z: (z, 0, 0))
 
     def edge(at):
         return pl.BlockSpec((None, 1, rows, cols), lambda z: (at, 0, 0, 0))
 
+    specs = [whole, edge(p_at), edge(p_at), whole, edge(k_at), edge(k_at), plane, plane]
+    operands = [p, p_lo, p_hi, k, k_lo, k_hi, base, leak]
+    aliases = {}
+    if into is not None:
+        specs.append(pl.BlockSpec(memory_space=pl.ANY))
+        operands.append(into)
+        aliases = {len(operands) - 1: 0}
     return pl.pallas_call(
         functools.partial(_relax_kernel, plane_of),
         grid=(count,),
-        in_specs=[whole, edge(p_at), edge(p_at), whole, edge(k_at), edge(k_at), plane, plane],
-        out_specs=step,
-        out_shape=jax.ShapeDtypeStruct((count, rows, cols), jnp.float32),
-    )(p, p_lo, p_hi, k, k_lo, k_hi, base, leak)
+        in_specs=specs,
+        out_specs=plane,
+        out_shape=jax.ShapeDtypeStruct(base.shape, jnp.float32),
+        input_output_aliases=aliases,
+    )(*operands)
 
 
 def halos(cells):
@@ -240,8 +248,7 @@
     args = (tissue_start, lo, hi, 0, conduct, lo, hi, 1, base_source, leak_field)
     ends = relax_sweep(*args, lambda z: z * (planes - 1), 2)
     first_lo, first_hi = halos(ends[None])
-    inner = relax_sweep(*args, lambda z: z + 1, planes - 2)
-    first = jnp.concatenate([ends[0:1], inner, ends[1:2]], axis=0)
+    first = relax_sweep(*args, lambda z: z + 1, planes - 2, into=ends)
     tissue = relax_sweep(
         first, first_lo, first_hi, 0, conduct, lo, hi, 1, base_source, leak_field,
         lambda z: z, planes,

time: 102 us -> 102 us (level)
  waiting for transfers between devices: 3.58 us -> 6.41 us
  other arithmetic: 9.6 us -> 8.3 us
    ppermute x2, waiting for transfers between devices: 3.57 us -> 6.4 us  [halos(): lo = lax.ppermute(cells[:, last:], AXES, [(i, i + 1) for i in range(ends)])]
    concatenate x1 -> x0, other arithmetic: 1.5 us -> none  [on_device(): first = jnp.concatenate([ends[0:1], inner, ends[1:2]], axis=0)]
  transfers between devices with their start and end apart: 5 -> 5, of which waited for: 1 -> 1; matrix products, arithmetic and copies ran while one was open for 19% -> 17% of each run, Pallas kernels for 6% -> 6%
where the time goes in v15:
time: 102 us
  starting transfers between devices  25.2 us (25%)
  Pallas kernels  21.8 us (21%)
  blocking collectives  19.4 us (19%)
  local copies, waits for them, and re-layouts  13.2 us (13%)
  other arithmetic  8.3 us (8%)
  matrix products  6.45 us (6%)
  waiting for transfers between devices  6.41 us (6%)
  between operations  1.08 us (1%)
    pallas_call x3, Pallas kernels, relax_sweep(): pl.pallas_call(functools.partial(_relax_kernel, plane_of), grid=(count,),...  21.8 us
    all_to_all x1, blocking collectives, on_device(): lax.all_to_all(send.reshape(devices, (capacity + 1) * seg), AXES, 0, 0, t...  19.4 us
    ppermute x2, starting transfers between devices, halos(): hi = lax.ppermute(cells[:, :1], AXES, [(i + 1, i) for i in range(ends)])  10.9 us
    all_to_all x1, starting transfers between devices, on_device(): got = lax.all_to_all(sent, AXES, 0, 0, tiled=True)  10.4 us
    ppermute x2, waiting for transfers between devices, halos(): lo = lax.ppermute(cells[:, last:], AXES, [(i, i + 1) for i in range(ends)])  6.4 us
    dot_general x1, matrix products, on_device(): jnp.einsum('bij,cbj->cbi', inverse_blocks, jnp.stack([fixed_rhs, unit]),...  4.43 us
    ppermute x2, starting transfers between devices, halos(): lo = lax.ppermute(cells[:, last:], AXES, [(i, i + 1) for i in range(ends)])  3.84 us
    scatter-add x1, other arithmetic, on_device(): leakage = jax.ops.segment_sum(got_rows, got_index, num_segments=cell_blocks)  3.03 us
  transfers between devices with their start and end apart: 5, of which 1 were waited for; matrix products, arithmetic and copies ran while one was open for 17% of the time, Pallas kernels for 6%

profile of v15, /device:TPU:8, one launch (start us, length us, event | category | flops | bytes accessed | tf_op | source)
XLA Modules:
  0.0 101.8 jit_solution(10214497278995694690)
XLA Ops:
  0.6 0.9 slice_reduce_fusion.2
  1.6 1.0 %slice_reduce_fusion.1 = f32[128]{0:T(128)S(1)} fusion(f32[128,128]{1,0:T(8,128)} %param.14), kind=kLoop, calls=%fused_computation.35 | loop fusion | bytes 1024 | tf_op jit(solution)/shard_map/slice | solution.py:188
  2.6 0.7 and_select_fusion.4
  3.4 1.0 %slice.84 = bf16[128,1,128]{2,1,0:T(2,128)(2,1)S(1)} slice(bf16[128,128,128]{2,1,0:T(8,128)(2,1)} %param.18), slice={[0:128], [127:128], [0:128]} | slice | bytes 65536 | tf_op jit(solution)/shard_map/slice | solution.py:178
  4.4 0.9 multiply_reduce_fusion
  5.4 0.1 slice_reduce_fusion
  5.5 0.7 stack.32
  6.2 1.0 broadcast_in_dim.124
  7.1 10.4 %all-to-all-start = ((f32[128,1,768]{2,1,0:T(1,128)}), f32[128,1,768]{2,1,0:T(1,128)S(1)}, u32[]{:S(2)}, u32[]{:S(2)}) async-start(f32[128,1,768]{2,1,0:T(1,128)} %broadcast_in_dim.124), calls=%async_computation | async-start | bytes 786432 | tf_op jit(solution)/shard_map/all_to_all | solution.py:193
  17.6 0.0 copy-start.2
  17.6 0.0 copy-start.12
  17.6 0.0 copy-start.10
  17.6 0.0 copy-start.11
  17.6 3.0 %pad_maximum_fusion = (f32[2,1,256,512]{3,2,1,0:T(8,128)}, f32[2,1,256,512]{3,2,1,0:T(8,128)}) fusion(f32[1,4,256,512]{3,2,1,0:T(8,128)} %bitcast.106, f32[1,4,256,512]{3,2,1,0:T(8,128)} %bitcast.108), kind=kLoop, calls=%fused_computation.13 | loop fusion | flops 524288 | bytes 6291456 | tf_op jit(solution)/shard_map/stack | solution.py:246
  20.6 7.1 %collective-permute-start.1 = (f32[2,1,256,512]{3,2,1,0:T(8,128)}, f32[2,1,256,512]{3,2,1,0:T(8,128)S(1)}, u32[]{:S(2)}, u32[]{:S(2)}) collective-permute-start(f32[2,1,256,512]{3,2,1,0:T(8,128)} %get-tuple-element.8), channel_id=1, source_target_pairs={{1,0},{2,1},{3,2},{4,3},{5,4},{6,5},{7,6},{8,7},{9,8},{10,9},{11,1... | collective-permute-start | bytes 3145736 | tf_op jit(solution)/shard_map/ppermute | solution.py:136
  27.7 1.9 %collective-permute-start = (f32[2,1,256,512]{3,2,1,0:T(8,128)}, f32[2,1,256,512]{3,2,1,0:T(8,128)S(1)}, u32[]{:S(2)}, u32[]{:S(2)}) collective-permute-start(f32[2,1,256,512]{3,2,1,0:T(8,128)} %get-tuple-element.9), channel_id=1, source_target_pairs={{0,1},{1,2},{2,3},{3,4},{4,5},{5,6},{6,7},{7,8},{8,9},{9,10},{10,1... | collective-permute-start | bytes 3145736 | tf_op jit(solution)/shard_map/ppermute | solution.py:135
  29.7 0.0 copy-done.2
  29.7 0.0 copy-done.12
  29.7 0.2 convert_reduce_fusion
  29.9 0.0 copy-done.10
  29.9 0.0 copy-done.11
  29.9 0.1 select_reduce_fusion.1
  30.1 0.1 copy.42
  30.2 0.1 convert_element_type.127
  30.3 0.1 copy.47
  30.5 4.4 %convolution_bitcast_fusion = f32[2,128,128]{2,0,1:T(2,128)S(1)} fusion(bf16[128,128,128]{2,1,0:T(8,128)(2,1)} %param.18, bf16[1,128,128]{2,0,1:T(2,128)(2,1)S(1)} %stack_broadcast_in_dim.2, bf16[1,128,128]{2,0,1:T(2,128)(2,1)S(1)} %copy.42), kind=kOutput, calls=%fused_computation.7 | convolution fusion | flops 8519680 | bytes 4390912 | tf_op jit(solution)/shard_map/bij,cbj->cbi/dot_general | solution.py:170
  34.9 0.0 copy-start.6
  35.0 0.1 fusion.41
  35.1 0.0 all-to-all-done
  35.1 0.4 copy.55
  35.5 0.4 fusion
  35.9 0.4 fusion.1
  36.4 0.4 fusion.2
  36.8 0.1 multiply_add_fusion
  36.9 0.0 copy-done.7
  36.9 0.0 copy-done.8
  36.9 0.0 copy-start.5
  37.0 0.2 convolution_convert_fusion
  37.1 0.1 fusion.21
  37.3 0.1 fusion.23
  37.4 0.1 fusion.25
  37.6 0.2 fusion.5
  37.8 0.1 copy.46
  37.9 0.2 copy.48
  38.1 19.4 %all_to_all.18 = f32[128,1,384]{2,1,0:T(1,128)S(1)} all-to-all(f32[128,1,384]{2,1,0:T(1,128)S(1)} %copy.48), channel_id=1, replica_groups=mesh['grp'=4,'slab'=32] {'grp','slab'}, dimensions={0} | all-to-all | bytes 393216 | tf_op jit(solution)/shard_map/all_to_all | solution.py:238
  57.5 0.2 copy.49
  57.7 0.1 copy.51
  57.8 0.1 copy.50
  57.9 0.1 reshape.229
  58.0 3.0 %scatter_custom_fusion = f32[4096,128]{1,0:T(8,128)} fusion(s32[256]{0:T(256)S(1)} %reshape.229, f32[256,128]{1,0:T(8,128)S(1)} %bitcast.118, f32[]{:T(128)} %constant.58.clone.1), kind=kCustom, calls=%fused_computation.15 | custom fusion | flops 32768 | bytes 2097156 | tf_op jit(solution)/shard_map/scatter-add | solution.py:244
  61.1 2.8 %reshape.221.leak = f32[4,256,512]{2,1,0:T(8,128)} reshape(f32[4096,128]{1,0:T(8,128)} %scatter_custom_fusion) | data formatting | bytes 4194304 | tf_op jit(solution)/shard_map/reshape | solution.py:245
  63.8 0.0 collective-permute-done.1.p_hi.k_hi
  63.8 0.0 collective-permute-done.p_lo.k_lo
  63.8 1.0 copy-done
  64.8 1.0 copy-done.1
  65.8 6.4 %shard_map.149.rest_0_ = f32[4,256,512]{2,1,0:T(8,128)} custom-call(f32[4,256,512]{2,1,0:T(8,128)} %p_ref.3, f32[2,1,256,512]{3,2,1,0:T(8,128)} %copy-done.1, f32[2,1,256,512]{3,2,1,0:T(8,128)} %copy-done, f32[4,256,512]{2,1,0:T(8,128)} %k_ref.5, f32[2,1,256,512]{3,2,1,0:T(8,128)} %copy-done.1, f32[2,1,256,512]{3,2,1,0:T(8,128)} %copy-done, ...), custom_call_target="tpu_custom_call" | custom-call | tf_op jit(solution)/shard_map/pallas_call | solution.py:121
  72.2 1.3 %fusion.40 = (f32[1,1,256,512]{3,2,1,0:T(8,128)S(1)}, f32[1,1,256,512]{3,2,1,0:T(8,128)S(1)}) fusion(f32[1,4,256,512]{3,2,1,0:T(8,128)} %bitcast.107), kind=kLoop, calls=%fused_computation.95 | loop fusion | bytes 2097152 | tf_op jit(solution)/shard_map/slice | solution.py:136
  73.5 3.8 %collective-permute-start.3 = (f32[1,1,256,512]{3,2,1,0:T(8,128)S(1)}, f32[1,1,256,512]{3,2,1,0:T(8,128)S(1)}, u32[]{:S(2)}, u32[]{:S(2)}) collective-permute-start(f32[1,1,256,512]{3,2,1,0:T(8,128)S(1)} %get-tuple-element.10), channel_id=1, source_target_pairs={{1,0},{2,1},{3,2},{4,3},{5,4},{6,5},{7,6},{8,7},{9,8},{10,9},{11,1... | collective-permute-start | bytes 1572872 | tf_op jit(solution)/shard_map/ppermute | solution.py:136
  77.3 1.9 %collective-permute-start.2 = (f32[1,1,256,512]{3,2,1,0:T(8,128)S(1)}, f32[1,1,256,512]{3,2,1,0:T(8,128)S(1)}, u32[]{:S(2)}, u32[]{:S(2)}) collective-permute-start(f32[1,1,256,512]{3,2,1,0:T(8,128)S(1)} %get-tuple-element.11), channel_id=1, source_target_pairs={{0,1},{1,2},{2,3},{3,4},{4,5},{5,6},{6,7},{7,8},{8,9},{9,10},{10,1... | collective-permute-start | bytes 1572872 | tf_op jit(solution)/shard_map/ppermute | solution.py:135
  79.2 6.4 %shard_map.150.p_ref = f32[4,256,512]{2,1,0:T(8,128)} custom-call(f32[4,256,512]{2,1,0:T(8,128)} %p_ref.3, f32[2,1,256,512]{3,2,1,0:T(8,128)} %copy-done.1, f32[2,1,256,512]{3,2,1,0:T(8,128)} %copy-done, f32[4,256,512]{2,1,0:T(8,128)} %k_ref.5, f32[2,1,256,512]{3,2,1,0:T(8,128)} %copy-done.1, ...), custom_call_target="tpu_custom_call", output_to_operand_aliasing={{}: (8, {})} | custom-call | tf_op jit(solution)/shard_map/pallas_call | solution.py:121
  85.6 0.0 collective-permute-done.3.p_hi
  85.6 6.4 %collective-permute-done.2.p_lo = f32[1,1,256,512]{3,2,1,0:T(8,128)S(1)} collective-permute-done((f32[1,1,256,512]{3,2,1,0:T(8,128)S(1)}, f32[1,1,256,512]{3,2,1,0:T(8,128)S(1)}, u32[]{:S(2)}, u32[]{:S(2)}) %collective-permute-start.2) | collective-permute-done | bytes 524320 | tf_op jit(solution)/shard_map/ppermute | solution.py:135
  92.0 0.8 copy-done.4
  92.8 9.0 %shard_map.151 = f32[4,256,512]{2,1,0:T(8,128)} custom-call(f32[4,256,512]{2,1,0:T(8,128)} %shard_map.150.p_ref, f32[1,1,256,512]{3,2,1,0:T(8,128)} %copy-done.4, f32[1,1,256,512]{3,2,1,0:T(8,128)} %copy-done.3, f32[4,256,512]{2,1,0:T(8,128)} %k_ref.5, f32[2,1,256,512]{3,2,1,0:T(8,128)} %copy-done.1, f32[2,1,256,512]{3,2,1,0:T(8,128)} %copy-done, ...), custom_call_target="tpu_custom_call" | custom-call | tf_op jit(solution)/shard_map/pallas_call | solution.py:121
  (31 shorter events, 0.2 us)
Async XLA Ops:
  7.1 28.0 %all-to-all-start = ((f32[128,1,768]{2,1,0:T(1,128)}), f32[128,1,768]{2,1,0:T(1,128)S(1)}, u32[]{:S(2)}, u32[]{:S(2)}) async-start(f32[128,1,768]{2,1,0:T(1,128)} %broadcast_in_dim.124), calls=%async_computation | async-start | bytes 786432 | tf_op jit(solution)/shard_map/all_to_all | solution.py:193
  17.6 12.1 %copy-start.2 = (f32[128,128]{1,0:T(8,128)S(1)}, f32[128,128]{1,0:T(8,128)}, u32[]{:S(2)}) copy-start(f32[128,128]{1,0:T(8,128)} %param.15) | copy-start | bytes 196612
  17.6 12.1 %copy-start.12 = (s32[128,1]{0,1:T(1,128)S(1)}, s32[128,1]{0,1:T(1,128)}, u32[]{:S(2)}) copy-start(s32[128,1]{0,1:T(1,128)} %param.21) | copy-start | bytes 1540
  17.6 12.3 %copy-start.10 = (s32[128]{0:T(128)S(1)}, s32[128]{0:T(128)}, u32[]{:S(2)}) copy-start(s32[128]{0:T(128)} %param.23) | copy-start | bytes 1540
  17.6 12.3 %copy-start.11 = (s32[128]{0:T(128)S(1)}, s32[128]{0:T(128)}, u32[]{:S(2)}) copy-start(s32[128]{0:T(128)} %param.22) | copy-start | bytes 1540
  20.6 43.2 %collective-permute-start.1 = (f32[2,1,256,512]{3,2,1,0:T(8,128)}, f32[2,1,256,512]{3,2,1,0:T(8,128)S(1)}, u32[]{:S(2)}, u32[]{:S(2)}) collective-permute-start(f32[2,1,256,512]{3,2,1,0:T(8,128)} %get-tuple-element.8), channel_id=1, source_target_pairs={{1,0},{2,1},{3,2},{4,3},{5,4},{6,5},{7,6},{8,7},{9,8},{10,9},{11,1... | collective-permute-start | bytes 3145736 | tf_op jit(solution)/shard_map/ppermute | solution.py:136
  27.7 36.1 %collective-permute-start = (f32[2,1,256,512]{3,2,1,0:T(8,128)}, f32[2,1,256,512]{3,2,1,0:T(8,128)S(1)}, u32[]{:S(2)}, u32[]{:S(2)}) collective-permute-start(f32[2,1,256,512]{3,2,1,0:T(8,128)} %get-tuple-element.9), channel_id=1, source_target_pairs={{0,1},{1,2},{2,3},{3,4},{4,5},{5,6},{6,7},{7,8},{8,9},{9,10},{10,1... | collective-permute-start | bytes 3145736 | tf_op jit(solution)/shard_map/ppermute | solution.py:135
  34.9 1.9 %copy-start.9 = (f32[128]{0:T(128)S(1)}, f32[128]{0:T(128)}, u32[]{:S(2)}) copy-start(f32[128]{0:T(128)} %param.16) | copy-start | bytes 1540
  34.9 2.0 %copy-start.7 = (f32[128,128]{1,0:T(8,128)S(1)}, f32[128,128]{1,0:T(8,128)}, u32[]{:S(2)}) copy-start(f32[128,128]{1,0:T(8,128)} %param.19) | copy-start | bytes 196612
  34.9 2.0 %copy-start.8 = (f32[128,128]{1,0:T(8,128)S(1)}, f32[128,128]{1,0:T(8,128)}, u32[]{:S(2)}) copy-start(f32[128,128]{1,0:T(8,128)} %param.20) | copy-start | bytes 196612
  34.9 2.2 %copy-start.6 = (bf16[4,128,128]{2,1,0:T(8,128)(2,1)S(1)}, bf16[4,128,128]{2,1,0:T(8,128)(2,1)}, u32[]{:S(2)}) copy-start(bf16[4,128,128]{2,1,0:T(8,128)(2,1)} %param.24) | copy-start | bytes 393220
  36.9 24.1 %copy-start.5 = (f32[128,128]{1,0:T(8,128)}, f32[128,128]{1,0:T(8,128)S(1)}, u32[]{:S(2)}) copy-start(f32[128,128]{1,0:T(8,128)S(1)} %multiply_add_fusion) | copy-start | bytes 196612
  63.8 1.0 copy-start
  64.8 1.0 copy-start.1
  73.5 12.1 %collective-permute-start.3 = (f32[1,1,256,512]{3,2,1,0:T(8,128)S(1)}, f32[1,1,256,512]{3,2,1,0:T(8,128)S(1)}, u32[]{:S(2)}, u32[]{:S(2)}) collective-permute-start(f32[1,1,256,512]{3,2,1,0:T(8,128)S(1)} %get-tuple-element.10), channel_id=1, source_target_pairs={{1,0},{2,1},{3,2},{4,3},{5,4},{6,5},{7,6},{8,7},{9,8},{10,9},{11,1... | collective-permute-start | bytes 1572872 | tf_op jit(solution)/shard_map/ppermute | solution.py:136
  77.3 14.7 %collective-permute-start.2 = (f32[1,1,256,512]{3,2,1,0:T(8,128)S(1)}, f32[1,1,256,512]{3,2,1,0:T(8,128)S(1)}, u32[]{:S(2)}, u32[]{:S(2)}) collective-permute-start(f32[1,1,256,512]{3,2,1,0:T(8,128)S(1)} %get-tuple-element.11), channel_id=1, source_target_pairs={{0,1},{1,2},{2,3},{3,4},{4,5},{5,6},{6,7},{7,8},{8,9},{9,10},{10,1... | collective-permute-start | bytes 1572872 | tf_op jit(solution)/shard_map/ppermute | solution.py:135
  85.6 6.4 %copy-start.3 = (f32[1,1,256,512]{3,2,1,0:T(8,128)}, f32[1,1,256,512]{3,2,1,0:T(8,128)S(1)}, u32[]{:S(2)}) copy-start(f32[1,1,256,512]{3,2,1,0:T(8,128)S(1)} %collective-permute-done.3.p_hi) | copy-start | bytes 1572868
  92.0 0.8 copy-start.4
